TPU v7x, 256 devices: a whole 4x4x8 slice. The times are simulated.
256 devices in a mesh: dp: 16 (over z, core), seq: 16 (over y, x).
Axes of the slice: x: 4, y: 4, z: 8, core: 2. Of those that a mesh axis runs over, the one named last changes fastest.
Arguments:
- queries: bfloat16 [16, 16, 144, 1536], P('dp', 'seq'), may hold values from -32 to 32
- keys: bfloat16 [16, 16, 144, 1536], P('dp', 'seq'), may hold values from -32 to 32
- values: bfloat16 [16, 16, 144, 1536], P('dp', 'seq'), may hold values from -6 to 6
- cotangent: bfloat16 [16, 16, 144, 1536], P('dp', 'seq'), may hold values from -6 to 6
- spatial_count: int32 [16, 16], P('dp', 'seq'), may hold values from 72 to 144, as said below
- clip_ids: int32 [16, 16], P('dp'), may hold values from 0 to 1, never falling along the last dimension, each value on 1 to 12 neighbouring positions
- time_bias: float32 [12, 16], replicated, may hold values from -4 to 4
Outputs:
- attended: bfloat16 [16, 16, 144, 1536], P('dp', 'seq')
- query_grad: bfloat16 [16, 16, 144, 1536], P('dp', 'seq')
- key_grad: bfloat16 [16, 16, 144, 1536], P('dp', 'seq')
- value_grad: bfloat16 [16, 16, 144, 1536], P('dp', 'seq')
- bias_grad: float32 [12, 16], replicated
Inputs may be any that keep to these rules, and one draw needn't show every extreme that they name: The live spatial tokens of a frame are its first spatial_count positions; in each group some frame has all 144 live. `clip_ids`: frames of one clip are consecutive; a clip has at most 12 frames.
All inputs are finite; a program needn't handle non-finite values.
Results may differ from a plain program's by a relative error of at most 0.0059.
Values may be sent and summed in bfloat16 or wider, within the bound.
No kernel may reach another device: no remote copies, remote signals or barrier semaphores. Data moves between devices by JAX's collectives and lax.ppermute only.
A program may use at most 64 MiB of HBM per device.

v0:
```python
import math

import jax
import jax.numpy as jnp
from jax import lax
from jax.sharding import PartitionSpec as P

SPACE_PATTERNS = ("bfihe,bfjhe->bfhij", "bfhij,bfjhe->bfihe", "bfhij,bfihe->bfjhe")
TIME_PATTERNS = ("biphe,bjphe->bphij", "bphij,bjphe->biphe", "bphij,biphe->bjphe")


def split_heads(tensor, head_count):
    return tensor.reshape(tensor.shape[:-1] + (head_count, tensor.shape[-1] // head_count))


def join_heads(tensor):
    return tensor.reshape(tensor.shape[:-2] + (tensor.shape[-2] * tensor.shape[-1],))


def attend_forward(patterns, query_part, key_part, value_part, bias, allowed):
    scaling = 1.0 / math.sqrt(query_part.shape[-1])
    scores = (
        jnp.einsum(patterns[0], query_part, key_part, preferred_element_type=jnp.float32) * scaling
        + bias
    )
    scores = jnp.where(allowed, scores, -1e30)
    row_peak = jnp.max(scores, axis=-1, keepdims=True)
    weights = jnp.exp(scores - row_peak)
    shares = weights / jnp.sum(weights, axis=-1, keepdims=True)
    shares_half = shares.astype(jnp.bfloat16)
    result = jnp.einsum(patterns[1], shares_half, value_part, preferred_element_type=jnp.float32)
    return (shares, shares_half, result)


def attend_backward(
    patterns, query_part, key_part, value_part, cotangent_part, shares, shares_half
):
    scaling = 1.0 / math.sqrt(query_part.shape[-1])
    value_grad = jnp.einsum(
        patterns[2], shares_half, cotangent_part, preferred_element_type=jnp.float32
    )
    share_grad = jnp.einsum(
        patterns[0], cotangent_part, value_part, preferred_element_type=jnp.float32
    )
    spread = jnp.sum(shares * share_grad, axis=-1, keepdims=True)
    score_grad = shares * (share_grad - spread)
    score_half = score_grad.astype(jnp.bfloat16)
    query_grad = (
        jnp.einsum(patterns[1], score_half, key_part, preferred_element_type=jnp.float32) * scaling
    )
    key_grad = (
        jnp.einsum(patterns[2], score_half, query_part, preferred_element_type=jnp.float32)
        * scaling
    )
    return (query_grad, key_grad, value_grad, score_grad)


def butterfly_sum(value, axis, size):
    step = 1
    while step < size:
        pairs = [(index, index ^ step) for index in range(size)]
        value = value + lax.ppermute(value, axis, pairs)
        step *= 2
    return value


def on_device(queries, keys, values, cotangent, spatial_count, clip_ids, time_bias):
    head_count, frames_all = time_bias.shape
    positions = queries.shape[2]
    width = queries.shape[3]
    seq_size = lax.axis_size("seq")
    dp_size = lax.axis_size("dp")
    row_index = lax.broadcasted_iota(jnp.int32, (frames_all, frames_all), 0)
    col_index = lax.broadcasted_iota(jnp.int32, (frames_all, frames_all), 1)
    distance = jnp.abs(row_index - col_index)
    lag_index = lax.broadcasted_iota(jnp.int32, (frames_all, frames_all, frames_all), 0)
    onehot = (lag_index == distance[None]).astype(jnp.float32)
    bias_table = jnp.tensordot(time_bias, onehot, axes=1, precision=lax.Precision.HIGHEST)[
        None, None
    ]
    same_clip = (clip_ids[:, :, None] == clip_ids[:, None, :])[:, None, None]
    position = lax.broadcasted_iota(jnp.int32, (1, 1, 1, 1, positions), 4)
    live_keys = position < spatial_count[:, :, None, None, None]

    block = positions // seq_size
    stacked = jnp.stack([queries[0, 0], keys[0, 0], values[0, 0], cotangent[0, 0]])
    stacked = stacked.reshape(4, seq_size, block, width)
    rows = lax.all_to_all(stacked, "seq", split_axis=1, concat_axis=1, tiled=True)
    query_part = split_heads(rows[0][None], head_count)
    key_part = split_heads(rows[1][None], head_count)
    value_part = split_heads(rows[2][None], head_count)
    slope_part = split_heads(rows[3][None], head_count)
    shares, shares_half, result = attend_forward(
        TIME_PATTERNS, query_part, key_part, value_part, bias_table, same_clip
    )
    time_grads = attend_backward(
        TIME_PATTERNS, query_part, key_part, value_part, slope_part, shares, shares_half
    )
    bias_part = jnp.tensordot(
        jnp.sum(time_grads[3], axis=(0, 1)),
        onehot,
        axes=((1, 2), (1, 2)),
        precision=lax.Precision.HIGHEST,
    )
    summed = butterfly_sum(butterfly_sum(bias_part, "seq", seq_size), "dp", dp_size)
    bias_grad = summed / math.sqrt(dp_size * queries.shape[0] * frames_all * positions)

    back_rows = jnp.stack(
        [
            join_heads(result[0]).astype(jnp.bfloat16),
            join_heads(time_grads[0][0]).astype(jnp.bfloat16),
            join_heads(time_grads[1][0]).astype(jnp.bfloat16),
            join_heads(time_grads[2][0]).astype(jnp.bfloat16),
        ]
    )
    back = lax.all_to_all(back_rows, "seq", split_axis=1, concat_axis=2, tiled=True)
    back = back.reshape(4, 1, 1, positions, width).astype(jnp.float32)

    space_query = split_heads(queries, head_count)
    space_key = split_heads(keys, head_count)
    space_value = split_heads(values, head_count)
    space_slope = split_heads(cotangent, head_count)
    space_shares, space_half, space_out = attend_forward(
        SPACE_PATTERNS, space_query, space_key, space_value, 0.0, live_keys
    )
    space_grads = attend_backward(
        SPACE_PATTERNS, space_query, space_key, space_value, space_slope, space_shares, space_half
    )
    attended = (join_heads(space_out) + back[0]).astype(jnp.bfloat16)
    query_grad = (join_heads(space_grads[0]) + back[1]).astype(jnp.bfloat16)
    key_grad = (join_heads(space_grads[1]) + back[2]).astype(jnp.bfloat16)
    value_grad = (join_heads(space_grads[2]) + back[3]).astype(jnp.bfloat16)
    return (attended, query_grad, key_grad, value_grad, bias_grad)


def solution(mesh):
    return jax.shard_map(
        on_device,
        mesh=mesh,
        in_specs=(
            P("dp", "seq", None, None),
            P("dp", "seq", None, None),
            P("dp", "seq", None, None),
            P("dp", "seq", None, None),
            P("dp", "seq"),
            P("dp", None),
            P(),
        ),
        out_specs=(
            P("dp", "seq", None, None),
            P("dp", "seq", None, None),
            P("dp", "seq", None, None),
            P("dp", "seq", None, None),
            P(),
        ),
        check_vma=False,
    )
```

profile of v0, /device:TPU:4, one launch (start us, length us, event | category | flops | bytes accessed | tf_op | source)
XLA Modules:
  0.0 122.4 jit_solution(15696889758372611251)
XLA Ops:
  0.7 1.2 %stack.18 = bf16[1,16,9,1536]{3,2,1,0:T(8,128)(2,1)S(1)} reshape(bf16[1,1,144,1536]{3,2,1,0:T(8,128)(2,1)} %param.7) | data formatting | bytes 884736 | tf_op jit(solution)/shard_map/stack | solution.py:86
  1.9 1.2 stack.19
  3.1 0.2 stack.20
  3.3 1.2 stack.21
  4.5 0.6 pad_maximum_fusion
  5.1 2.8 %copy.114 = bf16[4,16,9,1536]{3,0,2,1:T(4,128)(2,1)} copy(bf16[4,16,9,1536]{3,2,1,0:T(8,128)(2,1)S(1)} %pad_maximum_fusion) | data formatting | bytes 3538944 | tf_op jit(solution)/shard_map/stack | solution.py:86
  7.9 7.6 %all-to-all-start = ((bf16[4,16,9,1536]{3,0,2,1:T(4,128)(2,1)}), bf16[4,16,9,1536]{3,0,2,1:T(4,128)(2,1)S(1)}, u32[]{:S(2)}, u32[]{:S(2)}) async-start(bf16[4,16,9,1536]{3,0,2,1:T(4,128)(2,1)} %copy.114), calls=%async_computation | async-start | bytes 3538944 | tf_op jit(solution)/shard_map/all_to_all | solution.py:88
  15.5 0.3 reshape.406
  15.9 0.3 reshape.407
  16.2 1.5 %reshape.408 = bf16[144,12,128]{2,1,0:T(8,128)(2,1)S(1)} reshape(bf16[1,1,144,1536]{3,2,1,0:T(8,128)(2,1)} %param.9) | data formatting | bytes 884736 | tf_op jit(solution)/shard_map/reshape.7
  17.7 2.4 %reshape.414 = bf16[144,12,128]{2,1,0:T(8,128)(2,1)} reshape(bf16[1,1,144,1536]{3,2,1,0:T(8,128)(2,1)} %param.10) | data formatting | bytes 884736 | tf_op jit(solution)/shard_map/reshape.55
  20.8 0.9 convolution_bitcast_fusion.2
  21.7 1.7 %copy.121 = f32[12,16,16]{1,2,0:T(8,128)} copy(f32[12,16,16]{0,2,1:T(8,128)} %convolution_bitcast_fusion.2) | data formatting | bytes 24576 | tf_op jit(solution)/shard_map/dot_general | solution.py:78
  23.4 0.5 iota_compare_fusion.2
  23.9 1.4 %broadcast_compare_fusion = pred[16,16]{0,1:T(8,128)(4,1)} fusion(s32[16]{0:T(128)} %bitcast.111), kind=kLoop, calls=%fused_computation.87 | loop fusion | flops 256 | bytes 320 | tf_op jit(solution)/shard_map/eq | solution.py:81
  25.3 3.2 %fusion.67 = (f32[12,144]{1,0:T(8,128)}, f32[12,144,144]{1,2,0:T(8,128)}) fusion(pred[144]{0:T(512)(128)(4,1)} %iota_compare_fusion.2, bf16[144,12,128]{2,1,0:T(8,128)(2,1)S(1)} %reshape.407, bf16[144,12,128]{2,1,0:T(8,128)(2,1)S(1)} %reshape.406), kind=kOutput, calls=%fused_computation.92 | convolution fusion | flops 64696464 | bytes 1887120 | tf_op jit(solution)/shard_map/sub | solution.py:28
  28.6 3.9 %multiply_reduce_fusion = (f32[12,144]{1,0:T(8,128)}, f32[12,144,144]{1,2,0:T(8,128)}) fusion(f32[12,144,144]{1,2,0:T(8,128)} %get-tuple-element.16, f32[12,144]{1,0:T(8,128)} %get-tuple-element.15, bf16[144,12,128]{2,1,0:T(8,128)(2,1)S(1)} %reshape.408, bf16[144,12,128]{2,1,0:T(8,128)(2,1)} %reshape.414), kind=kOutput, calls=%fused_computation.5 | convolution fusion | flops 64445760 | bytes 2889216 | tf_op jit(solution)/shard_map/bfihe,bfjhe->bfhij/dot_general | solution.py:42
  32.5 6.2 %all-to-all-done = bf16[4,16,9,1536]{3,0,2,1:T(4,128)(2,1)S(1)} async-done(((bf16[4,16,9,1536]{3,0,2,1:T(4,128)(2,1)}), bf16[4,16,9,1536]{3,0,2,1:T(4,128)(2,1)S(1)}, u32[]{:S(2)}, u32[]{:S(2)}) %all-to-all-start) | async-done | bytes 1769504 | tf_op jit(solution)/shard_map/all_to_all | solution.py:88
  38.7 9.1 %slice_reduce_fusion.3 = (bf16[16,9,1536]{2,1,0:T(8,128)(2,1)}, bf16[16,9,1536]{2,1,0:T(8,128)(2,1)}, bf16[16,9,1536]{2,1,0:T(8,128)(2,1)S(1)}, bf16[16,9,1536]{2,1,0:T(8,128)(2,1)S(1)}) fusion(bf16[4,16,9,1536]{3,0,2,1:T(4,128)(2,1)S(1)} %all-to-all-done), kind=kLoop, calls=%fused_computation.43 | loop fusion | bytes 3538944 | tf_op jit(solution)/shard_map/slice | solution.py:91
  47.8 2.3 %reshape.420 = bf16[16,9,12,128]{3,2,1,0:T(8,128)(2,1)} reshape(bf16[16,9,1536]{2,1,0:T(8,128)(2,1)} %get-tuple-element.5) | data formatting | bytes 884736 | tf_op jit(solution)/shard_map/reshape.34
  50.1 1.2 reshape.423
  51.3 0.4 reshape.422
  51.7 0.4 reshape.421
  52.0 0.7 fusion.72
  52.7 0.4 copy-done.16
  53.1 0.4 fusion.14
  53.5 0.7 copy-done.15
  54.2 0.4 multiply_reduce_fusion.1
  54.6 0.3 fusion.13
  54.9 1.2 fusion.43
  56.1 0.3 fusion.12
  56.4 0.1 copy.149
  56.5 0.2 convolution_bitcast_fusion.3
  56.7 0.9 collective-permute-start
  57.6 0.1 copy_bitcast_fusion.2
  57.7 0.4 fusion.11
  58.1 2.6 %collective-permute-done = f32[12,16]{1,0:T(8,128)S(1)} collective-permute-done((f32[12,16]{1,0:T(8,128)S(1)}, f32[12,16]{1,0:T(8,128)S(1)}, u32[]{:S(2)}, u32[]{:S(2)}) %collective-permute-start) | collective-permute-done | bytes 800 | tf_op jit(solution)/shard_map/ppermute | solution.py:62
  60.7 4.0 %collective-permute-start.1 = (f32[12,16]{1,0:T(8,128)S(1)}, f32[12,16]{1,0:T(8,128)S(1)}, u32[]{:S(2)}, u32[]{:S(2)}) collective-permute-start(f32[12,16]{1,0:T(8,128)S(1)} %add.83), channel_id=1, source_target_pairs={{0,2},{1,3},{2,0},{3,1},{4,6},{5,7},{6,4},{7,5},{8,10},{9,11},{10,... | collective-permute-start | bytes 2312 | tf_op jit(solution)/shard_map/ppermute | solution.py:62
  64.7 1.6 %collective-permute-done.1 = f32[12,16]{1,0:T(8,128)S(1)} collective-permute-done((f32[12,16]{1,0:T(8,128)S(1)}, f32[12,16]{1,0:T(8,128)S(1)}, u32[]{:S(2)}, u32[]{:S(2)}) %collective-permute-start.1) | collective-permute-done | bytes 800 | tf_op jit(solution)/shard_map/ppermute | solution.py:62
  66.3 1.6 %collective-permute-start.2 = (f32[12,16]{1,0:T(8,128)S(1)}, f32[12,16]{1,0:T(8,128)}, u32[]{:S(2)}, u32[]{:S(2)}) collective-permute-start(f32[12,16]{1,0:T(8,128)S(1)} %add.84), channel_id=1, source_target_pairs={{0,4},{1,5},{2,6},{3,7},{4,0},{5,1},{6,2},{7,3},{8,12},{9,13},{10,... | collective-permute-start | bytes 2312 | tf_op jit(solution)/shard_map/ppermute | solution.py:62
  67.9 0.2 pad_maximum_fusion.1
  68.1 2.6 %copy.135 = bf16[4,16,9,1536]{3,0,2,1:T(4,128)(2,1)} copy(bf16[4,16,9,1536]{3,1,2,0:T(8,128)(2,1)S(1)} %pad_maximum_fusion.1) | data formatting | bytes 3538944 | tf_op jit(solution)/shard_map/stack | solution.py:108
  70.7 6.2 %all-to-all-start.1 = ((bf16[4,16,9,1536]{3,0,2,1:T(4,128)(2,1)}), bf16[4,16,9,1536]{3,0,2,1:T(4,128)(2,1)S(1)}, u32[]{:S(2)}, u32[]{:S(2)}) async-start(bf16[4,16,9,1536]{3,0,2,1:T(4,128)(2,1)} %copy.135), calls=%async_computation.1 | async-start | bytes 3538944 | tf_op jit(solution)/shard_map/all_to_all | solution.py:116
  76.9 0.7 add.85
  77.6 3.0 %collective-permute-start.3 = (f32[12,16]{1,0:T(8,128)S(1)}, f32[12,16]{1,0:T(8,128)S(1)}, u32[]{:S(2)}, u32[]{:S(2)}) collective-permute-start(f32[12,16]{1,0:T(8,128)S(1)} %add.85), channel_id=1, source_target_pairs={{0,8},{1,9},{2,10},{3,11},{4,12},{5,13},{6,14},{7,15},{8,0},{9,1},... | collective-permute-start | bytes 2312 | tf_op jit(solution)/shard_map/ppermute | solution.py:62
  80.6 2.0 %multiply_convert_fusion = bf16[12,144,144]{1,2,0:T(8,128)(2,1)S(1)} fusion(f32[12,144,144]{1,2,0:T(8,128)} %get-tuple-element.22, f32[12,144]{1,0:T(8,128)} %get-tuple-element.21, f32[12,144,144]{1,2,0:T(8,128)S(1)} %copy-done.6, f32[12,144]{1,0:T(8,128)} %get-tuple-element.15), kind=kLoop, calls=%fused_computation.4 | loop fusion | flops 995328 | bytes 2502144 | tf_op jit(solution)/shard_map/convert_element_type | solution.py:47
  82.6 14.3 %collective-permute-done.3 = f32[12,16]{1,0:T(8,128)S(1)} collective-permute-done((f32[12,16]{1,0:T(8,128)S(1)}, f32[12,16]{1,0:T(8,128)S(1)}, u32[]{:S(2)}, u32[]{:S(2)}) %collective-permute-start.3) | collective-permute-done | bytes 800 | tf_op jit(solution)/shard_map/ppermute | solution.py:62
  97.0 1.3 %convolution_bitcast_fusion = f32[1,1,12,18,8,128]{5,4,3,2,1,0:T(8,128)} fusion(bf16[144,12,128]{2,1,0:T(8,128)(2,1)S(1)} %copy-done.14, f32[12,144,144]{1,2,0:T(8,128)S(1)} %copy-done.6, f32[12,144]{1,0:T(8,128)S(1)} %copy-done.19), kind=kOutput, calls=%fused_computation.20 | convolution fusion | flops 64198656 | bytes 2329344 | tf_op jit(solution)/shard_map/bfhij,bfihe->bfjhe/dot_general | solution.py:39
  98.3 2.0 %collective-permute-start.5 = (f32[12,16]{1,0:T(8,128)S(1)}, f32[12,16]{1,0:T(8,128)S(1)}, u32[]{:S(2)}, u32[]{:S(2)}) collective-permute-start(f32[12,16]{1,0:T(8,128)S(1)} %add.87), channel_id=1, source_target_pairs={{0,32},{16,48},{32,0},{48,16},{64,96},{80,112},{96,64},{112,80},{1... | collective-permute-start | bytes 2312 | tf_op jit(solution)/shard_map/ppermute | solution.py:62
  100.3 1.5 %convolution_bitcast_fusion.1 = f32[1,1,12,18,8,128]{5,4,3,2,1,0:T(8,128)} fusion(bf16[144,12,128]{2,1,0:T(8,128)(2,1)S(1)} %copy-done.13, f32[12,144,144]{1,2,0:T(8,128)S(1)} %copy-done.6, f32[12,144]{1,0:T(8,128)S(1)} %copy-done.19), kind=kOutput, calls=%fused_computation.21 | convolution fusion | flops 64198656 | bytes 2329344 | tf_op jit(solution)/shard_map/bfhij,bfjhe->bfihe/dot_general | solution.py:31
  101.8 0.2 collective-permute-done.5
  102.1 3.3 %collective-permute-start.6 = (f32[12,16]{1,0:T(8,128)S(1)}, f32[12,16]{1,0:T(8,128)S(1)}, u32[]{:S(2)}, u32[]{:S(2)}) collective-permute-start(f32[12,16]{1,0:T(8,128)S(1)} %add.88), channel_id=1, source_target_pairs={{0,64},{16,80},{32,96},{48,112},{64,0},{80,16},{96,32},{112,48},{1... | collective-permute-start | bytes 2312 | tf_op jit(solution)/shard_map/ppermute | solution.py:62
  105.3 0.4 fusion.5
  105.7 1.3 %collective-permute-done.6 = f32[12,16]{1,0:T(8,128)S(1)} collective-permute-done((f32[12,16]{1,0:T(8,128)S(1)}, f32[12,16]{1,0:T(8,128)S(1)}, u32[]{:S(2)}, u32[]{:S(2)}) %collective-permute-start.6) | collective-permute-done | bytes 800 | tf_op jit(solution)/shard_map/ppermute | solution.py:62
  107.0 6.8 %collective-permute-start.7 = (f32[12,16]{1,0:T(8,128)S(1)}, f32[12,16]{1,0:T(8,128)S(1)}, u32[]{:S(2)}, u32[]{:S(2)}) collective-permute-start(f32[12,16]{1,0:T(8,128)S(1)} %add.89), channel_id=1, source_target_pairs={{0,128},{16,144},{32,160},{48,176},{64,192},{80,208},{96,224},{112... | collective-permute-start | bytes 2312 | tf_op jit(solution)/shard_map/ppermute | solution.py:62
  113.8 0.6 fusion.4
  114.4 1.0 collective-permute-done.7
  115.4 0.6 add_multiply_fusion
  116.0 2.5 %fusion.66 = (f32[1,16,9,1536]{3,0,2,1:T(1,128)S(1)}, f32[1,16,9,1536]{3,0,2,1:T(1,128)S(1)}, f32[1,16,9,1536]{3,0,2,1:T(1,128)S(1)}, f32[1,16,9,1536]{3,0,2,1:T(1,128)S(1)}) fusion(bf16[4,16,9,1536]{3,0,2,1:T(4,128)(2,1)S(1)} %all-to-all-done.1), kind=kLoop, calls=%fused_computation.91 | loop fusion | bytes 7077888 | tf_op jit(solution)/shard_map/slice | solution.py:132
  118.5 0.9 fusion.15
  119.4 0.4 copy-done.11
  119.8 0.9 fusion.18
  120.7 0.9 fusion.16
  121.5 0.9 fusion.17
  (51 shorter events, 0.2 us)
Async XLA Ops:
  0.6 20.1 %copy-start = (f32[12,16]{1,0:T(8,128)S(1)}, f32[12,16]{1,0:T(8,128)}, u32[]{:S(2)}) copy-start(f32[12,16]{1,0:T(8,128)} %param.13) | copy-start | bytes 2308
  0.6 2.5 %copy-start.9 = (bf16[1,1,144,1536]{3,2,1,0:T(8,128)(2,1)S(1)}, bf16[1,1,144,1536]{3,2,1,0:T(8,128)(2,1)}, u32[]{:S(2)}) copy-start(bf16[1,1,144,1536]{3,2,1,0:T(8,128)(2,1)} %param.9) | copy-start | bytes 1327108
  7.9 7.6 %copy-start.7 = (bf16[1,1,144,1536]{3,2,1,0:T(8,128)(2,1)S(1)}, bf16[1,1,144,1536]{3,2,1,0:T(8,128)(2,1)}, u32[]{:S(2)}) copy-start(bf16[1,1,144,1536]{3,2,1,0:T(8,128)(2,1)} %param.7) | copy-start | bytes 1327108
  7.9 7.9 %copy-start.8 = (bf16[1,1,144,1536]{3,2,1,0:T(8,128)(2,1)S(1)}, bf16[1,1,144,1536]{3,2,1,0:T(8,128)(2,1)}, u32[]{:S(2)}) copy-start(bf16[1,1,144,1536]{3,2,1,0:T(8,128)(2,1)} %param.8) | copy-start | bytes 1327108
  7.9 30.8 %all-to-all-start = ((bf16[4,16,9,1536]{3,0,2,1:T(4,128)(2,1)}), bf16[4,16,9,1536]{3,0,2,1:T(4,128)(2,1)S(1)}, u32[]{:S(2)}, u32[]{:S(2)}) async-start(bf16[4,16,9,1536]{3,0,2,1:T(4,128)(2,1)} %copy.114), calls=%async_computation | async-start | bytes 3538944 | tf_op jit(solution)/shard_map/all_to_all | solution.py:88
  15.9 12.7 %copy-start.4 = (bf16[144,12,128]{2,1,0:T(8,128)(2,1)}, bf16[144,12,128]{2,1,0:T(8,128)(2,1)S(1)}, u32[]{:S(2)}) copy-start(bf16[144,12,128]{2,1,0:T(8,128)(2,1)S(1)} %reshape.406) | copy-start | bytes 1327108
  16.2 12.4 %copy-start.2 = (bf16[144,12,128]{2,1,0:T(8,128)(2,1)}, bf16[144,12,128]{2,1,0:T(8,128)(2,1)S(1)}, u32[]{:S(2)}) copy-start(bf16[144,12,128]{2,1,0:T(8,128)(2,1)S(1)} %reshape.407) | copy-start | bytes 1327108
  17.7 10.8 %copy-start.12 = (bf16[144,12,128]{2,1,0:T(8,128)(2,1)}, bf16[144,12,128]{2,1,0:T(8,128)(2,1)S(1)}, u32[]{:S(2)}) copy-start(bf16[144,12,128]{2,1,0:T(8,128)(2,1)S(1)} %reshape.408) | copy-start | bytes 1327108
  47.8 2.3 %copy-start.1 = (bf16[16,9,1536]{2,1,0:T(8,128)(2,1)S(1)}, bf16[16,9,1536]{2,1,0:T(8,128)(2,1)}, u32[]{:S(2)}) copy-start(bf16[16,9,1536]{2,1,0:T(8,128)(2,1)} %get-tuple-element.6) | copy-start | bytes 1327108
  50.1 1.9 %copy-start.17 = (f32[12,16,16]{1,2,0:T(8,128)S(1)}, f32[12,16,16]{1,2,0:T(8,128)}, u32[]{:S(2)}) copy-start(f32[12,16,16]{1,2,0:T(8,128)} %copy.121) | copy-start | bytes 36868
  50.1 1.9 %copy-start.20 = (pred[16,16]{0,1:T(8,128)(4,1)S(1)}, pred[16,16]{0,1:T(8,128)(4,1)}, u32[]{:S(2)}) copy-start(pred[16,16]{0,1:T(8,128)(4,1)} %broadcast_compare_fusion) | copy-start | bytes 772
  52.0 1.1 copy-start.16
  52.7 1.9 %copy-start.18 = (f32[9,12,16]{2,1,0:T(8,128)}, f32[9,12,16]{2,1,0:T(8,128)S(1)}, u32[]{:S(2)}) copy-start(f32[9,12,16]{2,1,0:T(8,128)S(1)} %get-tuple-element.17) | copy-start | bytes 20740
  53.1 1.1 copy-start.15
  56.7 3.9 %collective-permute-start = (f32[12,16]{1,0:T(8,128)S(1)}, f32[12,16]{1,0:T(8,128)S(1)}, u32[]{:S(2)}, u32[]{:S(2)}) collective-permute-start(f32[12,16]{1,0:T(8,128)S(1)} %convolution_bitcast_fusion.3), channel_id=1, source_target_pairs={{0,1},{1,0},{2,3},{3,2},{4,5},{5,4},{6,7},{7,6},{8,9},{9,8},{10,11... | collective-permute-start | bytes 2312 | tf_op jit(solution)/shard_map/ppermute | solution.py:62
  60.7 5.6 %collective-permute-start.1 = (f32[12,16]{1,0:T(8,128)S(1)}, f32[12,16]{1,0:T(8,128)S(1)}, u32[]{:S(2)}, u32[]{:S(2)}) collective-permute-start(f32[12,16]{1,0:T(8,128)S(1)} %add.83), channel_id=1, source_target_pairs={{0,2},{1,3},{2,0},{3,1},{4,6},{5,7},{6,4},{7,5},{8,10},{9,11},{10,... | collective-permute-start | bytes 2312 | tf_op jit(solution)/shard_map/ppermute | solution.py:62
  66.3 10.6 %collective-permute-start.2 = (f32[12,16]{1,0:T(8,128)S(1)}, f32[12,16]{1,0:T(8,128)}, u32[]{:S(2)}, u32[]{:S(2)}) collective-permute-start(f32[12,16]{1,0:T(8,128)S(1)} %add.84), channel_id=1, source_target_pairs={{0,4},{1,5},{2,6},{3,7},{4,0},{5,1},{6,2},{7,3},{8,12},{9,13},{10,... | collective-permute-start | bytes 2312 | tf_op jit(solution)/shard_map/ppermute | solution.py:62
  70.7 9.9 %copy-start.6 = (f32[12,144,144]{1,2,0:T(8,128)S(1)}, f32[12,144,144]{1,2,0:T(8,128)}, u32[]{:S(2)}) copy-start(f32[12,144,144]{1,2,0:T(8,128)} %get-tuple-element.16) | copy-start | bytes 2985988
  70.7 45.3 %all-to-all-start.1 = ((bf16[4,16,9,1536]{3,0,2,1:T(4,128)(2,1)}), bf16[4,16,9,1536]{3,0,2,1:T(4,128)(2,1)S(1)}, u32[]{:S(2)}, u32[]{:S(2)}) async-start(bf16[4,16,9,1536]{3,0,2,1:T(4,128)(2,1)} %copy.135), calls=%async_computation.1 | async-start | bytes 3538944 | tf_op jit(solution)/shard_map/all_to_all | solution.py:116
  77.6 19.3 %collective-permute-start.3 = (f32[12,16]{1,0:T(8,128)S(1)}, f32[12,16]{1,0:T(8,128)S(1)}, u32[]{:S(2)}, u32[]{:S(2)}) collective-permute-start(f32[12,16]{1,0:T(8,128)S(1)} %add.85), channel_id=1, source_target_pairs={{0,8},{1,9},{2,10},{3,11},{4,12},{5,13},{6,14},{7,15},{8,0},{9,1},... | collective-permute-start | bytes 2312 | tf_op jit(solution)/shard_map/ppermute | solution.py:62
  80.6 16.4 %copy-start.14 = (bf16[144,12,128]{2,1,0:T(8,128)(2,1)S(1)}, bf16[144,12,128]{2,1,0:T(8,128)(2,1)}, u32[]{:S(2)}) copy-start(bf16[144,12,128]{2,1,0:T(8,128)(2,1)} %reshape.414) | copy-start | bytes 1327108
  80.6 16.4 %copy-start.19 = (f32[12,144]{1,0:T(8,128)S(1)}, f32[12,144]{1,0:T(8,128)}, u32[]{:S(2)}) copy-start(f32[12,144]{1,0:T(8,128)} %get-tuple-element.15) | copy-start | bytes 20740
  96.9 3.4 %copy-start.13 = (bf16[144,12,128]{2,1,0:T(8,128)(2,1)S(1)}, bf16[144,12,128]{2,1,0:T(8,128)(2,1)}, u32[]{:S(2)}) copy-start(bf16[144,12,128]{2,1,0:T(8,128)(2,1)} %copy-done.12) | copy-start | bytes 1327108
  96.9 1.4 %collective-permute-start.4 = (f32[12,16]{1,0:T(8,128)S(1)}, f32[12,16]{1,0:T(8,128)S(1)}, u32[]{:S(2)}, u32[]{:S(2)}) collective-permute-start(f32[12,16]{1,0:T(8,128)S(1)} %add.86), channel_id=1, source_target_pairs={{0,16},{16,0},{32,48},{48,32},{64,80},{80,64},{96,112},{112,96},{1... | collective-permute-start | bytes 2312 | tf_op jit(solution)/shard_map/ppermute | solution.py:62
  98.3 7.0 %copy-start.5 = (bf16[144,12,128]{2,1,0:T(8,128)(2,1)S(1)}, bf16[144,12,128]{2,1,0:T(8,128)(2,1)}, u32[]{:S(2)}) copy-start(bf16[144,12,128]{2,1,0:T(8,128)(2,1)} %copy-done.4) | copy-start | bytes 1327108
  98.3 3.7 %collective-permute-start.5 = (f32[12,16]{1,0:T(8,128)S(1)}, f32[12,16]{1,0:T(8,128)S(1)}, u32[]{:S(2)}, u32[]{:S(2)}) collective-permute-start(f32[12,16]{1,0:T(8,128)S(1)} %add.87), channel_id=1, source_target_pairs={{0,32},{16,48},{32,0},{48,16},{64,96},{80,112},{96,64},{112,80},{1... | collective-permute-start | bytes 2312 | tf_op jit(solution)/shard_map/ppermute | solution.py:62
  101.8 12.0 %copy-start.3 = (bf16[144,12,128]{2,1,0:T(8,128)(2,1)S(1)}, bf16[144,12,128]{2,1,0:T(8,128)(2,1)}, u32[]{:S(2)}) copy-start(bf16[144,12,128]{2,1,0:T(8,128)(2,1)} %copy-done.2) | copy-start | bytes 1327108
  102.1 5.0 %collective-permute-start.6 = (f32[12,16]{1,0:T(8,128)S(1)}, f32[12,16]{1,0:T(8,128)S(1)}, u32[]{:S(2)}, u32[]{:S(2)}) collective-permute-start(f32[12,16]{1,0:T(8,128)S(1)} %add.88), channel_id=1, source_target_pairs={{0,64},{16,80},{32,96},{48,112},{64,0},{80,16},{96,32},{112,48},{1... | collective-permute-start | bytes 2312 | tf_op jit(solution)/shard_map/ppermute | solution.py:62
  107.0 8.4 %collective-permute-start.7 = (f32[12,16]{1,0:T(8,128)S(1)}, f32[12,16]{1,0:T(8,128)S(1)}, u32[]{:S(2)}, u32[]{:S(2)}) collective-permute-start(f32[12,16]{1,0:T(8,128)S(1)} %add.89), channel_id=1, source_target_pairs={{0,128},{16,144},{32,160},{48,176},{64,192},{80,208},{96,224},{112... | collective-permute-start | bytes 2312 | tf_op jit(solution)/shard_map/ppermute | solution.py:62
  116.0 2.5 %copy-start.10 = (f32[1,1,12,18,8,128]{5,4,3,2,1,0:T(8,128)S(1)}, f32[1,1,12,18,8,128]{5,4,3,2,1,0:T(8,128)}, u32[]{:S(2)}) copy-start(f32[1,1,12,18,8,128]{5,4,3,2,1,0:T(8,128)} %convolution_bitcast_fusion) | copy-start | bytes 2654212
  118.5 1.3 %copy-start.11 = (f32[1,1,12,18,8,128]{5,4,3,2,1,0:T(8,128)S(1)}, f32[1,1,12,18,8,128]{5,4,3,2,1,0:T(8,128)}, u32[]{:S(2)}) copy-start(f32[1,1,12,18,8,128]{5,4,3,2,1,0:T(8,128)} %convolution_bitcast_fusion.1) | copy-start | bytes 2654212
where the time goes:
time: 123 us; the launch traced here: 122 us
  starting transfers between devices  35.3 us (29%)
  local copies, waits for them, and re-layouts  33 us (27%)
  waiting for transfers between devices  27.3 us (22%)
  matrix products  14.5 us (12%)
  other arithmetic  10.7 us (9%)
  between operations  1.61 us (1%)
    ppermute x8, starting transfers between devices, butterfly_sum(): value = value + lax.ppermute(value, axis, pairs)  21.5 us
    ppermute x8, waiting for transfers between devices, butterfly_sum(): value = value + lax.ppermute(value, axis, pairs)  21 us
    slice x1, local copies, waits for them, and re-layouts, on_device(): value_part = split_heads(rows[2][None], head_count)  9.11 us
    another operation x8, local copies, waits for them, and re-layouts  8.69 us
    all_to_all x1, starting transfers between devices, on_device(): lax.all_to_all(stacked, 'seq', split_axis=1, concat_axis=1, tiled=True)  7.58 us
    another operation x5, local copies, waits for them, and re-layouts, on_device(): jnp.stack([queries[0, 0], keys[0, 0], values[0, 0], cotangent[0, 0]])  6.62 us
    all_to_all x1, waiting for transfers between devices, on_device(): lax.all_to_all(stacked, 'seq', split_axis=1, concat_axis=1, tiled=True)  6.24 us
    all_to_all x1, starting transfers between devices, on_device(): lax.all_to_all(back_rows, 'seq', split_axis=1, concat_axis=2, tiled=True)  6.22 us
  transfers between devices with their start and end apart: 10, of which 7 were waited for; matrix products, arithmetic and copies ran while one was open for 22% of the time, Pallas kernels for 0%

commit v1 on v0

--- a/solution.py
+++ b/solution.py
@@ -55,12 +55,15 @@
     return (query_grad, key_grad, value_grad, score_grad)
 
 
-def butterfly_sum(value, axis, size):
+def quad_sum(value, axis, size):
     step = 1
     while step < size:
-        pairs = [(index, index ^ step) for index in range(size)]
-        value = value + lax.ppermute(value, axis, pairs)
-        step *= 2
+        received = [
+            lax.ppermute(value, axis, [(index, index ^ (part * step)) for index in range(size)])
+            for part in (1, 2, 3)
+        ]
+        value = (value + received[0]) + (received[1] + received[2])
+        step *= 4
     return value
 
 
@@ -102,7 +105,7 @@
         axes=((1, 2), (1, 2)),
         precision=lax.Precision.HIGHEST,
     )
-    summed = butterfly_sum(butterfly_sum(bias_part, "seq", seq_size), "dp", dp_size)
+    summed = quad_sum(quad_sum(bias_part, "seq", seq_size), "dp", dp_size)
     bias_grad = summed / math.sqrt(dp_size * queries.shape[0] * frames_all * positions)
 
     back_rows = jnp.stack(

time: 123 us -> 123 us (level)
  other arithmetic: 10.7 us -> 6.15 us
  matrix products: 14.5 us -> 17.1 us
  local copies, waits for them, and re-layouts: 33 us -> 34.7 us
  waiting for transfers between devices: 27.3 us -> 28.9 us
  starting transfers between devices: 35.3 us -> 33.8 us
    all_to_all x1, waiting for transfers between devices: 6.24 us -> 10.2 us  [on_device(): lax.all_to_all(stacked, 'seq', split_axis=1, concat_axis=1, tiled=True)]
    dot_general x2, matrix products: 1.7 us -> 5.25 us  [attend_backward(): jnp.einsum(patterns[2], shares_half, cotangent_part, preferred_element_ty...]
    another operation x8, local copies, waits for them, and re-layouts: 8.69 us -> 11.5 us
    ppermute x8 -> x12, waiting for transfers between devices: 21 us -> 18.7 us  [quad_sum(): lax.ppermute(value, axis, [(index, index ^ part * step) for index in rang...]
    ppermute x8 -> x12, starting transfers between devices: 21.5 us -> 19.7 us  [quad_sum(): lax.ppermute(value, axis, [(index, index ^ part * step) for index in rang...]
    convert_element_type x1, other arithmetic: 2.02 us -> 0.32 us  [attend_backward(): score_half = score_grad.astype(jnp.bfloat16)]
    dot_general x1, local copies, waits for them, and re-layouts: 1.72 us -> 0.19 us  [on_device(): jnp.tensordot(time_bias, onehot, axes=1, precision=lax.Precision.HIGHEST)]
    dot_general x2, matrix products: 4.34 us -> 2.84 us  [attend_backward(): jnp.einsum(patterns[0], cotangent_part, value_part, preferred_element_typ...]
  transfers between devices with their start and end apart: 10 -> 14, of which waited for: 7 -> 6; matrix products, arithmetic and copies ran while one was open for 22% -> 19% of each run, Pallas kernels for 0% -> 0%
where the time goes in v1:
time: 123 us; the launch traced here: 122 us
  local copies, waits for them, and re-layouts  34.7 us (28%)
  starting transfers between devices  33.8 us (27%)
  waiting for transfers between devices  28.9 us (23%)
  matrix products  17.1 us (14%)
  other arithmetic  6.15 us (5%)
  between operations  1.62 us (1%)
    ppermute x12, starting transfers between devices, quad_sum(): lax.ppermute(value, axis, [(index, index ^ part * step) for index in rang...  19.7 us
    ppermute x12, waiting for transfers between devices, quad_sum(): lax.ppermute(value, axis, [(index, index ^ part * step) for index in rang...  18.7 us
    another operation x8, local copies, waits for them, and re-layouts  11.5 us
    all_to_all x1, waiting for transfers between devices, on_device(): lax.all_to_all(stacked, 'seq', split_axis=1, concat_axis=1, tiled=True)  10.2 us
    slice x1, local copies, waits for them, and re-layouts, on_device(): value_part = split_heads(rows[2][None], head_count)  9.38 us
    all_to_all x1, starting transfers between devices, on_device(): lax.all_to_all(stacked, 'seq', split_axis=1, concat_axis=1, tiled=True)  7.58 us
    another operation x5, local copies, waits for them, and re-layouts, on_device(): jnp.stack([queries[0, 0], keys[0, 0], values[0, 0], cotangent[0, 0]])  6.64 us
    all_to_all x1, starting transfers between devices, on_device(): lax.all_to_all(back_rows, 'seq', split_axis=1, concat_axis=2, tiled=True)  6.56 us
  transfers between devices with their start and end apart: 14, of which 6 were waited for; matrix products, arithmetic and copies ran while one was open for 19% of the time, Pallas kernels for 0%

profile of v1, /device:TPU:4, one launch (start us, length us, event | category | flops | bytes accessed | tf_op | source)
XLA Modules:
  0.0 122.2 jit_solution(16076429180634993890)
XLA Ops:
  0.7 1.2 %stack.18 = bf16[1,16,9,1536]{3,2,1,0:T(8,128)(2,1)S(1)} reshape(bf16[1,1,144,1536]{3,2,1,0:T(8,128)(2,1)} %param.7) | data formatting | bytes 884736 | tf_op jit(solution)/shard_map/stack | solution.py:89
  1.9 1.2 stack.19
  3.1 0.2 stack.20
  3.3 1.2 stack.21
  4.5 0.6 pad_maximum_fusion
  5.1 2.8 %copy.114 = bf16[4,16,9,1536]{3,0,2,1:T(4,128)(2,1)} copy(bf16[4,16,9,1536]{3,2,1,0:T(8,128)(2,1)S(1)} %pad_maximum_fusion) | data formatting | bytes 3538944 | tf_op jit(solution)/shard_map/stack | solution.py:89
  8.0 7.6 %all-to-all-start = ((bf16[4,16,9,1536]{3,0,2,1:T(4,128)(2,1)}), bf16[4,16,9,1536]{3,0,2,1:T(4,128)(2,1)S(1)}, u32[]{:S(2)}, u32[]{:S(2)}) async-start(bf16[4,16,9,1536]{3,0,2,1:T(4,128)(2,1)} %copy.114), calls=%async_computation | async-start | bytes 3538944 | tf_op jit(solution)/shard_map/all_to_all | solution.py:91
  15.6 0.3 reshape.406
  15.9 1.5 %reshape.407 = bf16[144,12,128]{2,1,0:T(8,128)(2,1)S(1)} reshape(bf16[1,1,144,1536]{3,2,1,0:T(8,128)(2,1)} %param.8) | data formatting | bytes 884736 | tf_op jit(solution)/shard_map/reshape.3
  17.5 2.4 %reshape.408 = bf16[144,12,128]{2,1,0:T(8,128)(2,1)} reshape(bf16[1,1,144,1536]{3,2,1,0:T(8,128)(2,1)} %param.9) | data formatting | bytes 884736 | tf_op jit(solution)/shard_map/reshape.7
  19.8 2.1 %reshape.414 = bf16[144,12,128]{2,1,0:T(8,128)(2,1)} reshape(bf16[1,1,144,1536]{3,2,1,0:T(8,128)(2,1)} %param.10) | data formatting | bytes 884736 | tf_op jit(solution)/shard_map/reshape.55
  22.6 0.3 convolution_bitcast_fusion.2
  22.9 0.2 copy.121
  23.1 0.7 broadcast_compare_fusion
  23.7 2.0 %fusion.67 = (f32[12,144]{1,0:T(8,128)S(1)}, f32[12,144,144]{1,2,0:T(8,128)}) fusion(pred[144]{0:T(512)(128)(4,1)S(1)} %iota_compare_fusion.2, bf16[144,12,128]{2,1,0:T(8,128)(2,1)S(1)} %reshape.407, bf16[144,12,128]{2,1,0:T(8,128)(2,1)S(1)} %reshape.406), kind=kOutput, calls=%fused_computation.95 | convolution fusion | flops 64696464 | bytes 1887120 | tf_op jit(solution)/shard_map/sub | solution.py:28
  25.8 2.4 %multiply_reduce_fusion = (f32[12,144]{1,0:T(8,128)S(1)}, f32[12,144,144]{1,2,0:T(8,128)S(1)}) fusion(f32[12,144,144]{1,2,0:T(8,128)} %get-tuple-element.16, f32[12,144]{1,0:T(8,128)S(1)} %get-tuple-element.15, bf16[144,12,128]{2,1,0:T(8,128)(2,1)} %reshape.408, bf16[144,12,128]{2,1,0:T(8,128)(2,1)} %reshape.414), kind=kOutput, calls=%fused_computation.5 | convolution fusion | flops 64445760 | bytes 2889216 | tf_op jit(solution)/shard_map/bfihe,bfjhe->bfhij/dot_general | solution.py:42
  28.2 0.3 multiply_convert_fusion
  28.5 10.2 %all-to-all-done = bf16[4,16,9,1536]{3,0,2,1:T(4,128)(2,1)S(1)} async-done(((bf16[4,16,9,1536]{3,0,2,1:T(4,128)(2,1)}), bf16[4,16,9,1536]{3,0,2,1:T(4,128)(2,1)S(1)}, u32[]{:S(2)}, u32[]{:S(2)}) %all-to-all-start) | async-done | bytes 1769504 | tf_op jit(solution)/shard_map/all_to_all | solution.py:91
  38.7 9.4 %slice_reduce_fusion.3 = (bf16[16,9,1536]{2,1,0:T(8,128)(2,1)}, bf16[16,9,1536]{2,1,0:T(8,128)(2,1)}, bf16[16,9,1536]{2,1,0:T(8,128)(2,1)}, bf16[16,9,1536]{2,1,0:T(8,128)(2,1)S(1)}) fusion(bf16[4,16,9,1536]{3,0,2,1:T(4,128)(2,1)S(1)} %all-to-all-done), kind=kLoop, calls=%fused_computation.43 | loop fusion | bytes 3538944 | tf_op jit(solution)/shard_map/slice | solution.py:94
  48.1 2.3 %reshape.420 = bf16[16,9,12,128]{3,2,1,0:T(8,128)(2,1)} reshape(bf16[16,9,1536]{2,1,0:T(8,128)(2,1)} %get-tuple-element.5) | data formatting | bytes 884736 | tf_op jit(solution)/shard_map/reshape.34
  50.4 2.2 %reshape.423 = bf16[16,9,12,128]{3,2,1,0:T(8,128)(2,1)} reshape(bf16[16,9,1536]{2,1,0:T(8,128)(2,1)} %get-tuple-element.6) | data formatting | bytes 884736 | tf_op jit(solution)/shard_map/reshape.37
  52.6 0.4 reshape.422
  52.9 0.4 reshape.421
  53.3 1.3 %fusion.72 = (f32[9,12,16]{2,1,0:T(8,128)S(1)}, f32[9,12,16,16]{2,3,1,0:T(8,128)S(1)}) fusion(f32[12,16,16]{1,2,0:T(8,128)S(1)} %copy.121, pred[16,16]{0,1:T(8,128)(4,1)} %broadcast_compare_fusion, bf16[16,9,12,128]{3,2,1,0:T(8,128)(2,1)S(1)} %reshape.422, bf16[16,9,12,128]{3,2,1,0:T(8,128)(2,1)S(1)} %reshape.421), kind=kOutput, calls=%fused_computation.96 | convolution fusion | flops 7216143 | bytes 1014784 | tf_op jit(solution)/shard_map/sub | solution.py:28
  54.7 2.3 %fusion.14 = bf16[1,9,12,2,8,128]{5,4,3,2,1,0:T(8,128)(2,1)} fusion(bf16[16,9,12,128]{3,2,1,0:T(8,128)(2,1)} %reshape.423, f32[9,12,16,16]{2,3,1,0:T(8,128)S(1)} %get-tuple-element.18, f32[9,12,16]{2,1,0:T(8,128)S(1)} %get-tuple-element.17), kind=kOutput, calls=%fused_computation.29 | convolution fusion | flops 7354368 | bytes 1002240 | tf_op jit(solution)/shard_map/bphij,biphe->bjphe/dot_general | solution.py:39
  57.0 0.4 multiply_reduce_fusion.1
  57.4 1.1 fusion.13
  58.5 0.3 fusion.43
  58.8 0.4 fusion.11
  59.1 0.3 fusion.12
  59.5 0.1 copy.149
  59.6 0.2 convolution_bitcast_fusion.3
  59.8 1.0 collective-permute-start.2
  60.8 3.1 %collective-permute-start.1 = (f32[12,16]{1,0:T(8,128)S(1)}, f32[12,16]{1,0:T(8,128)S(1)}, u32[]{:S(2)}, u32[]{:S(2)}) collective-permute-start(f32[12,16]{1,0:T(8,128)S(1)} %convolution_bitcast_fusion.3), channel_id=1, source_target_pairs={{0,2},{1,3},{2,0},{3,1},{4,6},{5,7},{6,4},{7,5},{8,10},{9,11},{10,... | collective-permute-start | bytes 2312 | tf_op jit(solution)/shard_map/ppermute | solution.py:62
  63.9 1.1 collective-permute-start
  65.0 1.1 copy_bitcast_fusion.2
  66.1 0.1 copy_bitcast_fusion
  66.2 0.2 pad_maximum_fusion.1
  66.4 2.6 %copy.135 = bf16[4,16,9,1536]{3,0,2,1:T(4,128)(2,1)} copy(bf16[4,16,9,1536]{3,1,2,0:T(8,128)(2,1)S(1)} %pad_maximum_fusion.1) | data formatting | bytes 3538944 | tf_op jit(solution)/shard_map/stack | solution.py:111
  69.1 6.6 %all-to-all-start.1 = ((bf16[4,16,9,1536]{3,0,2,1:T(4,128)(2,1)}), bf16[4,16,9,1536]{3,0,2,1:T(4,128)(2,1)S(1)}, u32[]{:S(2)}, u32[]{:S(2)}) async-start(bf16[4,16,9,1536]{3,0,2,1:T(4,128)(2,1)} %copy.135), calls=%async_computation.1 | async-start | bytes 3538944 | tf_op jit(solution)/shard_map/all_to_all | solution.py:119
  75.7 3.0 %convolution_bitcast_fusion = f32[1,1,12,18,8,128]{5,4,3,2,1,0:T(8,128)} fusion(bf16[144,12,128]{2,1,0:T(8,128)(2,1)S(1)} %copy-done.14, f32[12,144,144]{1,2,0:T(8,128)} %get-tuple-element.16, f32[12,144]{1,0:T(8,128)S(1)} %copy-done.19), kind=kOutput, calls=%fused_computation.20 | convolution fusion | flops 64198656 | bytes 2329344 | tf_op jit(solution)/shard_map/bfhij,bfihe->bfjhe/dot_general | solution.py:39
  78.6 2.8 %collective-permute-start.5 = (f32[12,16]{1,0:T(8,128)S(1)}, f32[12,16]{1,0:T(8,128)S(1)}, u32[]{:S(2)}, u32[]{:S(2)}) collective-permute-start(f32[12,16]{1,0:T(8,128)S(1)} %add_add_fusion.2), channel_id=1, source_target_pairs={{0,12},{1,13},{2,14},{3,15},{4,8},{5,9},{6,10},{7,11},{8,4},{9,5},... | collective-permute-start | bytes 2312 | tf_op jit(solution)/shard_map/ppermute | solution.py:62
  81.5 0.8 collective-permute-start.4
  82.3 0.5 collective-permute-start.3
  82.8 1.5 %convolution_bitcast_fusion.1 = f32[1,1,12,18,8,128]{5,4,3,2,1,0:T(8,128)} fusion(bf16[144,12,128]{2,1,0:T(8,128)(2,1)S(1)} %copy-done.13, f32[12,144,144]{1,2,0:T(8,128)S(1)} %copy-done.8, f32[12,144]{1,0:T(8,128)S(1)} %copy-done.19), kind=kOutput, calls=%fused_computation.21 | convolution fusion | flops 64198656 | bytes 2329344 | tf_op jit(solution)/shard_map/bfhij,bfjhe->bfihe/dot_general | solution.py:31
  84.4 6.8 %collective-permute-done.5 = f32[12,16]{1,0:T(8,128)S(1)} collective-permute-done((f32[12,16]{1,0:T(8,128)S(1)}, f32[12,16]{1,0:T(8,128)S(1)}, u32[]{:S(2)}, u32[]{:S(2)}) %collective-permute-start.5) | collective-permute-done | bytes 800 | tf_op jit(solution)/shard_map/ppermute | solution.py:62
  91.2 5.8 %collective-permute-done.4 = f32[12,16]{1,0:T(8,128)S(1)} collective-permute-done((f32[12,16]{1,0:T(8,128)S(1)}, f32[12,16]{1,0:T(8,128)S(1)}, u32[]{:S(2)}, u32[]{:S(2)}) %collective-permute-start.4) | collective-permute-done | bytes 800 | tf_op jit(solution)/shard_map/ppermute | solution.py:62
  97.0 1.4 %collective-permute-start.8 = (f32[12,16]{1,0:T(8,128)S(1)}, f32[12,16]{1,0:T(8,128)S(1)}, u32[]{:S(2)}, u32[]{:S(2)}) collective-permute-start(f32[12,16]{1,0:T(8,128)S(1)} %add_add_fusion.1), channel_id=1, source_target_pairs={{0,48},{16,32},{32,16},{48,0},{64,112},{80,96},{96,80},{112,64},{1... | collective-permute-start | bytes 2312 | tf_op jit(solution)/shard_map/ppermute | solution.py:62
  98.4 0.7 collective-permute-start.7
  99.1 0.4 fusion.5
  99.5 0.7 collective-permute-done.8
  100.1 1.9 %collective-permute-done.7 = f32[12,16]{1,0:T(8,128)S(1)} collective-permute-done((f32[12,16]{1,0:T(8,128)S(1)}, f32[12,16]{1,0:T(8,128)S(1)}, u32[]{:S(2)}, u32[]{:S(2)}) %collective-permute-start.7) | collective-permute-done | bytes 800 | tf_op jit(solution)/shard_map/ppermute | solution.py:62
  102.0 5.7 %collective-permute-start.11 = (f32[12,16]{1,0:T(8,128)S(1)}, f32[12,16]{1,0:T(8,128)S(1)}, u32[]{:S(2)}, u32[]{:S(2)}) collective-permute-start(f32[12,16]{1,0:T(8,128)S(1)} %add_add_fusion), channel_id=1, source_target_pairs={{0,192},{16,208},{32,224},{48,240},{64,128},{80,144},{96,160},{112... | collective-permute-start | bytes 2312 | tf_op jit(solution)/shard_map/ppermute | solution.py:62
  107.7 1.5 %collective-permute-start.10 = (f32[12,16]{1,0:T(8,128)S(1)}, f32[12,16]{1,0:T(8,128)S(1)}, u32[]{:S(2)}, u32[]{:S(2)}) collective-permute-start(f32[12,16]{1,0:T(8,128)S(1)} %add_add_fusion), channel_id=1, source_target_pairs={{0,128},{16,144},{32,160},{48,176},{64,192},{80,208},{96,224},{112... | collective-permute-start | bytes 2312 | tf_op jit(solution)/shard_map/ppermute | solution.py:62
  109.2 1.0 collective-permute-start.9
  110.2 1.5 %fusion.4 = f32[1,1,12,18,8,128]{5,4,3,2,1,0:T(8,128)} fusion(bf16[12,144,144]{1,2,0:T(8,128)(2,1)S(1)} %multiply_convert_fusion, bf16[144,12,128]{2,1,0:T(8,128)(2,1)S(1)} %copy-done.4), kind=kOutput, calls=%fused_computation.12 | convolution fusion | flops 63922176 | bytes 1824768 | tf_op jit(solution)/shard_map/bfhij,bfjhe->bfihe/dot_general | solution.py:49
  111.7 3.6 %collective-permute-done.10 = f32[12,16]{1,0:T(8,128)S(1)} collective-permute-done((f32[12,16]{1,0:T(8,128)S(1)}, f32[12,16]{1,0:T(8,128)S(1)}, u32[]{:S(2)}, u32[]{:S(2)}) %collective-permute-start.10) | collective-permute-done | bytes 800 | tf_op jit(solution)/shard_map/ppermute | solution.py:62
  115.3 0.6 add_multiply_fusion
  115.9 2.5 %fusion.66 = (f32[1,16,9,1536]{3,0,2,1:T(1,128)S(1)}, f32[1,16,9,1536]{3,0,2,1:T(1,128)S(1)}, f32[1,16,9,1536]{3,0,2,1:T(1,128)S(1)}, f32[1,16,9,1536]{3,0,2,1:T(1,128)S(1)}) fusion(bf16[4,16,9,1536]{3,0,2,1:T(4,128)(2,1)S(1)} %all-to-all-done.1), kind=kLoop, calls=%fused_computation.94 | loop fusion | bytes 7077888 | tf_op jit(solution)/shard_map/slice | solution.py:135
  118.3 0.9 fusion.15
  119.2 0.4 copy-done.12
  119.7 0.9 fusion.18
  120.5 0.9 fusion.16
  121.4 0.9 fusion.17
  (55 shorter events, 0.2 us)
Async XLA Ops:
  0.6 22.0 %copy-start = (f32[12,16]{1,0:T(8,128)S(1)}, f32[12,16]{1,0:T(8,128)}, u32[]{:S(2)}) copy-start(f32[12,16]{1,0:T(8,128)} %param.13) | copy-start | bytes 2308
  0.6 2.5 %copy-start.10 = (bf16[1,1,144,1536]{3,2,1,0:T(8,128)(2,1)S(1)}, bf16[1,1,144,1536]{3,2,1,0:T(8,128)(2,1)}, u32[]{:S(2)}) copy-start(bf16[1,1,144,1536]{3,2,1,0:T(8,128)(2,1)} %param.9) | copy-start | bytes 1327108
  8.0 7.6 %copy-start.9 = (bf16[1,1,144,1536]{3,2,1,0:T(8,128)(2,1)S(1)}, bf16[1,1,144,1536]{3,2,1,0:T(8,128)(2,1)}, u32[]{:S(2)}) copy-start(bf16[1,1,144,1536]{3,2,1,0:T(8,128)(2,1)} %param.7) | copy-start | bytes 1327108
  8.0 30.8 %all-to-all-start = ((bf16[4,16,9,1536]{3,0,2,1:T(4,128)(2,1)}), bf16[4,16,9,1536]{3,0,2,1:T(4,128)(2,1)S(1)}, u32[]{:S(2)}, u32[]{:S(2)}) async-start(bf16[4,16,9,1536]{3,0,2,1:T(4,128)(2,1)} %copy.114), calls=%async_computation | async-start | bytes 3538944 | tf_op jit(solution)/shard_map/all_to_all | solution.py:91
  15.9 9.9 %copy-start.5 = (bf16[144,12,128]{2,1,0:T(8,128)(2,1)}, bf16[144,12,128]{2,1,0:T(8,128)(2,1)S(1)}, u32[]{:S(2)}) copy-start(bf16[144,12,128]{2,1,0:T(8,128)(2,1)S(1)} %reshape.406) | copy-start | bytes 1327108
  15.9 7.2 %copy-start.20 = (s32[1,16]{1,0:T(1,128)S(1)}, s32[1,16]{1,0:T(1,128)}, u32[]{:S(2)}) copy-start(s32[1,16]{1,0:T(1,128)} %param.12) | copy-start | bytes 196
  17.4 8.3 %copy-start.3 = (bf16[144,12,128]{2,1,0:T(8,128)(2,1)}, bf16[144,12,128]{2,1,0:T(8,128)(2,1)S(1)}, u32[]{:S(2)}) copy-start(bf16[144,12,128]{2,1,0:T(8,128)(2,1)S(1)} %reshape.407) | copy-start | bytes 1327108
  25.8 2.4 %copy-start.18 = (f32[12,144]{1,0:T(8,128)}, f32[12,144]{1,0:T(8,128)S(1)}, u32[]{:S(2)}) copy-start(f32[12,144]{1,0:T(8,128)S(1)} %get-tuple-element.15) | copy-start | bytes 20740
  25.8 2.4 %copy-start.7 = (f32[12,144,144]{1,2,0:T(8,128)S(1)}, f32[12,144,144]{1,2,0:T(8,128)}, u32[]{:S(2)}) copy-start(f32[12,144,144]{1,2,0:T(8,128)} %get-tuple-element.16) | copy-start | bytes 2985988
  48.1 4.5 %copy-start.2 = (bf16[16,9,1536]{2,1,0:T(8,128)(2,1)S(1)}, bf16[16,9,1536]{2,1,0:T(8,128)(2,1)}, u32[]{:S(2)}) copy-start(bf16[16,9,1536]{2,1,0:T(8,128)(2,1)} %get-tuple-element.7) | copy-start | bytes 1327108
  54.6 2.3 %copy-start.15 = (bf16[16,9,12,128]{3,2,1,0:T(8,128)(2,1)S(1)}, bf16[16,9,12,128]{3,2,1,0:T(8,128)(2,1)}, u32[]{:S(2)}) copy-start(bf16[16,9,12,128]{3,2,1,0:T(8,128)(2,1)} %reshape.420) | copy-start | bytes 1327108
  54.7 2.3 %copy-start.16 = (bf16[16,9,12,128]{3,2,1,0:T(8,128)(2,1)S(1)}, bf16[16,9,12,128]{3,2,1,0:T(8,128)(2,1)}, u32[]{:S(2)}) copy-start(bf16[16,9,12,128]{3,2,1,0:T(8,128)(2,1)} %reshape.423) | copy-start | bytes 1327108
  59.1 7.0 %copy-start.17 = (bf16[1,9,12,2,8,128]{5,4,3,2,1,0:T(8,128)(2,1)S(1)}, bf16[1,9,12,2,8,128]{5,4,3,2,1,0:T(8,128)(2,1)}, u32[]{:S(2)}) copy-start(bf16[1,9,12,2,8,128]{5,4,3,2,1,0:T(8,128)(2,1)} %fusion.14) | copy-start | bytes 1327108
  59.8 18.8 %collective-permute-start.2 = (f32[12,16]{1,0:T(8,128)S(1)}, f32[12,16]{1,0:T(8,128)S(1)}, u32[]{:S(2)}, u32[]{:S(2)}) collective-permute-start(f32[12,16]{1,0:T(8,128)S(1)} %convolution_bitcast_fusion.3), channel_id=1, source_target_pairs={{0,3},{1,2},{2,1},{3,0},{4,7},{5,6},{6,5},{7,4},{8,11},{9,10},{10,... | collective-permute-start | bytes 2312 | tf_op jit(solution)/shard_map/ppermute | solution.py:62
  60.8 17.8 %collective-permute-start.1 = (f32[12,16]{1,0:T(8,128)S(1)}, f32[12,16]{1,0:T(8,128)S(1)}, u32[]{:S(2)}, u32[]{:S(2)}) collective-permute-start(f32[12,16]{1,0:T(8,128)S(1)} %convolution_bitcast_fusion.3), channel_id=1, source_target_pairs={{0,2},{1,3},{2,0},{3,1},{4,6},{5,7},{6,4},{7,5},{8,10},{9,11},{10,... | collective-permute-start | bytes 2312 | tf_op jit(solution)/shard_map/ppermute | solution.py:62
  63.9 14.7 %collective-permute-start = (f32[12,16]{1,0:T(8,128)S(1)}, f32[12,16]{1,0:T(8,128)S(1)}, u32[]{:S(2)}, u32[]{:S(2)}) collective-permute-start(f32[12,16]{1,0:T(8,128)S(1)} %convolution_bitcast_fusion.3), channel_id=1, source_target_pairs={{0,1},{1,0},{2,3},{3,2},{4,5},{5,4},{6,7},{7,6},{8,9},{9,8},{10,11... | collective-permute-start | bytes 2312 | tf_op jit(solution)/shard_map/ppermute | solution.py:62
  69.1 6.6 %copy-start.14 = (bf16[144,12,128]{2,1,0:T(8,128)(2,1)S(1)}, bf16[144,12,128]{2,1,0:T(8,128)(2,1)}, u32[]{:S(2)}) copy-start(bf16[144,12,128]{2,1,0:T(8,128)(2,1)} %reshape.414) | copy-start | bytes 1327108
  69.1 6.6 %copy-start.19 = (f32[12,144]{1,0:T(8,128)S(1)}, f32[12,144]{1,0:T(8,128)}, u32[]{:S(2)}) copy-start(f32[12,144]{1,0:T(8,128)} %copy-done.18) | copy-start | bytes 20740
  69.1 46.8 %all-to-all-start.1 = ((bf16[4,16,9,1536]{3,0,2,1:T(4,128)(2,1)}), bf16[4,16,9,1536]{3,0,2,1:T(4,128)(2,1)S(1)}, u32[]{:S(2)}, u32[]{:S(2)}) async-start(bf16[4,16,9,1536]{3,0,2,1:T(4,128)(2,1)} %copy.135), calls=%async_computation.1 | async-start | bytes 3538944 | tf_op jit(solution)/shard_map/all_to_all | solution.py:119
  75.6 7.2 %copy-start.8 = (f32[12,144,144]{1,2,0:T(8,128)S(1)}, f32[12,144,144]{1,2,0:T(8,128)}, u32[]{:S(2)}) copy-start(f32[12,144,144]{1,2,0:T(8,128)} %get-tuple-element.16) | copy-start | bytes 2985988
  75.6 7.2 %copy-start.13 = (bf16[144,12,128]{2,1,0:T(8,128)(2,1)S(1)}, bf16[144,12,128]{2,1,0:T(8,128)(2,1)}, u32[]{:S(2)}) copy-start(bf16[144,12,128]{2,1,0:T(8,128)(2,1)} %reshape.408) | copy-start | bytes 1327108
  78.6 20.5 %copy-start.6 = (bf16[144,12,128]{2,1,0:T(8,128)(2,1)S(1)}, bf16[144,12,128]{2,1,0:T(8,128)(2,1)}, u32[]{:S(2)}) copy-start(bf16[144,12,128]{2,1,0:T(8,128)(2,1)} %copy-done.5) | copy-start | bytes 1327108
  78.6 12.5 %collective-permute-start.5 = (f32[12,16]{1,0:T(8,128)S(1)}, f32[12,16]{1,0:T(8,128)S(1)}, u32[]{:S(2)}, u32[]{:S(2)}) collective-permute-start(f32[12,16]{1,0:T(8,128)S(1)} %add_add_fusion.2), channel_id=1, source_target_pairs={{0,12},{1,13},{2,14},{3,15},{4,8},{5,9},{6,10},{7,11},{8,4},{9,5},... | collective-permute-start | bytes 2312 | tf_op jit(solution)/shard_map/ppermute | solution.py:62
  81.5 15.5 %collective-permute-start.4 = (f32[12,16]{1,0:T(8,128)S(1)}, f32[12,16]{1,0:T(8,128)S(1)}, u32[]{:S(2)}, u32[]{:S(2)}) collective-permute-start(f32[12,16]{1,0:T(8,128)S(1)} %add_add_fusion.2), channel_id=1, source_target_pairs={{0,8},{1,9},{2,10},{3,11},{4,12},{5,13},{6,14},{7,15},{8,0},{9,1},... | collective-permute-start | bytes 2312 | tf_op jit(solution)/shard_map/ppermute | solution.py:62
  82.3 14.7 %collective-permute-start.3 = (f32[12,16]{1,0:T(8,128)S(1)}, f32[12,16]{1,0:T(8,128)S(1)}, u32[]{:S(2)}, u32[]{:S(2)}) collective-permute-start(f32[12,16]{1,0:T(8,128)S(1)} %add_add_fusion.2), channel_id=1, source_target_pairs={{0,4},{1,5},{2,6},{3,7},{4,0},{5,1},{6,2},{7,3},{8,12},{9,13},{10,... | collective-permute-start | bytes 2312 | tf_op jit(solution)/shard_map/ppermute | solution.py:62
  84.4 25.8 %copy-start.4 = (bf16[144,12,128]{2,1,0:T(8,128)(2,1)S(1)}, bf16[144,12,128]{2,1,0:T(8,128)(2,1)}, u32[]{:S(2)}) copy-start(bf16[144,12,128]{2,1,0:T(8,128)(2,1)} %copy-done.3) | copy-start | bytes 1327108
  97.0 3.2 %collective-permute-start.8 = (f32[12,16]{1,0:T(8,128)S(1)}, f32[12,16]{1,0:T(8,128)S(1)}, u32[]{:S(2)}, u32[]{:S(2)}) collective-permute-start(f32[12,16]{1,0:T(8,128)S(1)} %add_add_fusion.1), channel_id=1, source_target_pairs={{0,48},{16,32},{32,16},{48,0},{64,112},{80,96},{96,80},{112,64},{1... | collective-permute-start | bytes 2312 | tf_op jit(solution)/shard_map/ppermute | solution.py:62
  98.4 3.7 %collective-permute-start.7 = (f32[12,16]{1,0:T(8,128)S(1)}, f32[12,16]{1,0:T(8,128)S(1)}, u32[]{:S(2)}, u32[]{:S(2)}) collective-permute-start(f32[12,16]{1,0:T(8,128)S(1)} %add_add_fusion.1), channel_id=1, source_target_pairs={{0,32},{16,48},{32,0},{48,16},{64,96},{80,112},{96,64},{112,80},{1... | collective-permute-start | bytes 2312 | tf_op jit(solution)/shard_map/ppermute | solution.py:62
  99.1 2.9 %collective-permute-start.6 = (f32[12,16]{1,0:T(8,128)S(1)}, f32[12,16]{1,0:T(8,128)S(1)}, u32[]{:S(2)}, u32[]{:S(2)}) collective-permute-start(f32[12,16]{1,0:T(8,128)S(1)} %add_add_fusion.1), channel_id=1, source_target_pairs={{0,16},{16,0},{32,48},{48,32},{64,80},{80,64},{96,112},{112,96},{1... | collective-permute-start | bytes 2312 | tf_op jit(solution)/shard_map/ppermute | solution.py:62
  102.0 9.7 %collective-permute-start.11 = (f32[12,16]{1,0:T(8,128)S(1)}, f32[12,16]{1,0:T(8,128)S(1)}, u32[]{:S(2)}, u32[]{:S(2)}) collective-permute-start(f32[12,16]{1,0:T(8,128)S(1)} %add_add_fusion), channel_id=1, source_target_pairs={{0,192},{16,208},{32,224},{48,240},{64,128},{80,144},{96,160},{112... | collective-permute-start | bytes 2312 | tf_op jit(solution)/shard_map/ppermute | solution.py:62
  107.7 7.6 %collective-permute-start.10 = (f32[12,16]{1,0:T(8,128)S(1)}, f32[12,16]{1,0:T(8,128)S(1)}, u32[]{:S(2)}, u32[]{:S(2)}) collective-permute-start(f32[12,16]{1,0:T(8,128)S(1)} %add_add_fusion), channel_id=1, source_target_pairs={{0,128},{16,144},{32,160},{48,176},{64,192},{80,208},{96,224},{112... | collective-permute-start | bytes 2312 | tf_op jit(solution)/shard_map/ppermute | solution.py:62
  109.2 6.1 %collective-permute-start.9 = (f32[12,16]{1,0:T(8,128)S(1)}, f32[12,16]{1,0:T(8,128)S(1)}, u32[]{:S(2)}, u32[]{:S(2)}) collective-permute-start(f32[12,16]{1,0:T(8,128)S(1)} %add_add_fusion), channel_id=1, source_target_pairs={{0,64},{16,80},{32,96},{48,112},{64,0},{80,16},{96,32},{112,48},{1... | collective-permute-start | bytes 2312 | tf_op jit(solution)/shard_map/ppermute | solution.py:62
  115.9 2.5 %copy-start.11 = (f32[1,1,12,18,8,128]{5,4,3,2,1,0:T(8,128)S(1)}, f32[1,1,12,18,8,128]{5,4,3,2,1,0:T(8,128)}, u32[]{:S(2)}) copy-start(f32[1,1,12,18,8,128]{5,4,3,2,1,0:T(8,128)} %convolution_bitcast_fusion) | copy-start | bytes 2654212
  118.3 1.3 %copy-start.12 = (f32[1,1,12,18,8,128]{5,4,3,2,1,0:T(8,128)S(1)}, f32[1,1,12,18,8,128]{5,4,3,2,1,0:T(8,128)}, u32[]{:S(2)}) copy-start(f32[1,1,12,18,8,128]{5,4,3,2,1,0:T(8,128)} %convolution_bitcast_fusion.1) | copy-start | bytes 2654212
  119.7 1.7 %copy-start.1 = (f32[1,1,12,18,8,128]{5,4,3,2,1,0:T(8,128)S(1)}, f32[1,1,12,18,8,128]{5,4,3,2,1,0:T(8,128)}, u32[]{:S(2)}) copy-start(f32[1,1,12,18,8,128]{5,4,3,2,1,0:T(8,128)} %fusion.4) | copy-start | bytes 2654212

commit v2 on v1

--- a/solution.py
+++ b/solution.py
@@ -6,7 +6,7 @@
 from jax.sharding import PartitionSpec as P
 
 SPACE_PATTERNS = ("bfihe,bfjhe->bfhij", "bfhij,bfjhe->bfihe", "bfhij,bfihe->bfjhe")
-TIME_PATTERNS = ("biphe,bjphe->bphij", "bphij,bjphe->biphe", "bphij,biphe->bjphe")
+TIME_PATTERNS = ("phie,phje->phij", "phij,phje->phie", "phij,phie->phje")
 
 
 def split_heads(tensor, head_count):
@@ -86,21 +86,25 @@
     live_keys = position < spatial_count[:, :, None, None, None]
 
     block = positions // seq_size
-    stacked = jnp.stack([queries[0, 0], keys[0, 0], values[0, 0], cotangent[0, 0]])
-    stacked = stacked.reshape(4, seq_size, block, width)
-    rows = lax.all_to_all(stacked, "seq", split_axis=1, concat_axis=1, tiled=True)
-    query_part = split_heads(rows[0][None], head_count)
-    key_part = split_heads(rows[1][None], head_count)
-    value_part = split_heads(rows[2][None], head_count)
-    slope_part = split_heads(rows[3][None], head_count)
+    stacked = jnp.stack(
+        [
+            tensor.reshape(seq_size, block, width)
+            for tensor in (queries, keys, values, cotangent)
+        ],
+        axis=2,
+    )
+    rows = lax.all_to_all(stacked, "seq", split_axis=0, concat_axis=0, tiled=True)
+    rows = rows.reshape(seq_size, block, 4, head_count, width // head_count)
+    rows = jnp.transpose(rows, (2, 1, 3, 0, 4))
+    query_part, key_part, value_part, slope_part = rows[0], rows[1], rows[2], rows[3]
     shares, shares_half, result = attend_forward(
-        TIME_PATTERNS, query_part, key_part, value_part, bias_table, same_clip
+        TIME_PATTERNS, query_part, key_part, value_part, bias_table[0], same_clip[0]
     )
     time_grads = attend_backward(
         TIME_PATTERNS, query_part, key_part, value_part, slope_part, shares, shares_half
     )
     bias_part = jnp.tensordot(
-        jnp.sum(time_grads[3], axis=(0, 1)),
+        jnp.sum(time_grads[3], axis=0),
         onehot,
         axes=((1, 2), (1, 2)),
         precision=lax.Precision.HIGHEST,
@@ -110,14 +114,13 @@
 
     back_rows = jnp.stack(
         [
-            join_heads(result[0]).astype(jnp.bfloat16),
-            join_heads(time_grads[0][0]).astype(jnp.bfloat16),
-            join_heads(time_grads[1][0]).astype(jnp.bfloat16),
-            join_heads(time_grads[2][0]).astype(jnp.bfloat16),
-        ]
+            jnp.transpose(tensor.astype(jnp.bfloat16), (2, 0, 1, 3)).reshape(seq_size, block, width)
+            for tensor in (result, time_grads[0], time_grads[1], time_grads[2])
+        ],
+        axis=2,
     )
-    back = lax.all_to_all(back_rows, "seq", split_axis=1, concat_axis=2, tiled=True)
-    back = back.reshape(4, 1, 1, positions, width).astype(jnp.float32)
+    back = lax.all_to_all(back_rows, "seq", split_axis=0, concat_axis=0, tiled=True)
+    back = jnp.moveaxis(back, 2, 0).reshape(4, 1, 1, positions, width).astype(jnp.float32)
 
     space_query = split_heads(queries, head_count)
     space_key = split_heads(keys, head_count)

time: 123 us -> 120 us (0.976)
  local copies, waits for them, and re-layouts: 34.7 us -> 25.6 us
  other arithmetic: 6.15 us -> 9.03 us
  waiting for transfers between devices: 28.9 us -> 31.2 us
    slice x1 -> x0, local copies, waits for them, and re-layouts: 9.38 us -> none  [on_device(): value_part = split_heads(rows[2][None], head_count)]
    another operation x14, local copies, waits for them, and re-layouts: 20.8 us -> 13.4 us  [the longest x5 6.65 us: on_device(): jnp.stack([tensor.reshape(seq_size, block, width) for tensor in (queries,...]
    reshape x0 -> x2, local copies, waits for them, and re-layouts: none -> 5.45 us  [on_device(): rows = rows.reshape(seq_size, block, 4, head_count, width // head_count)]
    all_to_all x2, waiting for transfers between devices: 10.2 us -> 15.2 us  [the longest x1 15.2 us: on_device(): lax.all_to_all(stacked, 'seq', split_axis=0, concat_axis=0, tiled=True)]
    sub x0 -> x1, other arithmetic: none -> 3.37 us  [attend_forward(): weights = jnp.exp(scores - row_peak)]
    ppermute x12, waiting for transfers between devices: 18.7 us -> 16 us  [quad_sum(): lax.ppermute(value, axis, [(index, index ^ part * step) for index in rang...]
    sub x2 -> x1, matrix products: 3.33 us -> 0.77 us  [attend_forward(): weights = jnp.exp(scores - row_peak)]
    unnamed x42 -> x50, local copies, waits for them, and re-layouts: 0.54 us -> 2.33 us
  transfers between devices with their start and end apart: 14 -> 14, of which waited for: 6 -> 6; matrix products, arithmetic and copies ran while one was open for 19% -> 23% of each run, Pallas kernels for 0% -> 0%
where the time goes in v2:
time: 120 us
  starting transfers between devices  34.4 us (29%)
  waiting for transfers between devices  31.2 us (26%)
  local copies, waits for them, and re-layouts  25.6 us (21%)
  matrix products  17.7 us (15%)
  other arithmetic  9.03 us (8%)
  between operations  1.79 us (1%)
    ppermute x12, starting transfers between devices, quad_sum(): lax.ppermute(value, axis, [(index, index ^ part * step) for index in rang...  19.2 us
    ppermute x12, waiting for transfers between devices, quad_sum(): lax.ppermute(value, axis, [(index, index ^ part * step) for index in rang...  16 us
    all_to_all x1, waiting for transfers between devices, on_device(): lax.all_to_all(stacked, 'seq', split_axis=0, concat_axis=0, tiled=True)  15.2 us
    all_to_all x1, starting transfers between devices, on_device(): lax.all_to_all(back_rows, 'seq', split_axis=0, concat_axis=0, tiled=True)  7.64 us
    all_to_all x1, starting transfers between devices, on_device(): lax.all_to_all(stacked, 'seq', split_axis=0, concat_axis=0, tiled=True)  7.58 us
    another operation x5, local copies, waits for them, and re-layouts, on_device(): jnp.stack([tensor.reshape(seq_size, block, width) for tensor in (queries,...  6.65 us
    reshape x2, local copies, waits for them, and re-layouts, on_device(): rows = rows.reshape(seq_size, block, 4, head_count, width // head_count)  5.45 us
    dot_general x2, matrix products, attend_backward(): jnp.einsum(patterns[2], shares_half, cotangent_part, preferred_element_ty...  4.87 us
  transfers between devices with their start and end apart: 14, of which 6 were waited for; matrix products, arithmetic and copies ran while one was open for 23% of the time, Pallas kernels for 0%

profile of v2, /device:TPU:4, one launch (start us, length us, event | category | flops | bytes accessed | tf_op | source)
XLA Modules:
  0.0 119.8 jit_solution(10276809334186244180)
XLA Ops:
  0.7 1.2 %stack_reshape.24 = bf16[16,9,1,1536]{3,1,0,2:T(8,128)(2,1)S(1)} reshape(bf16[1,1,144,1536]{3,2,1,0:T(8,128)(2,1)} %param.7) | data formatting | bytes 884736 | tf_op jit(solution)/shard_map/stack;reshape | solution.py:89
  1.9 1.2 stack_reshape.25
  3.1 0.2 stack_reshape.26
  3.3 1.2 stack_reshape.27
  4.5 0.6 pad_maximum_fusion
  5.1 2.8 %copy.94 = bf16[16,9,4,1536]{3,2,1,0:T(4,128)(2,1)} copy(bf16[16,9,4,1536]{3,1,0,2:T(8,128)(2,1)S(1)} %pad_maximum_fusion) | data formatting | bytes 3538944 | tf_op jit(solution)/shard_map/stack | solution.py:89
  8.0 7.6 %all-to-all-start = ((bf16[16,9,4,1536]{3,2,1,0:T(4,128)(2,1)}), bf16[16,9,4,1536]{3,2,1,0:T(4,128)(2,1)}, u32[]{:S(2)}, u32[]{:S(2)}) async-start(bf16[16,9,4,1536]{3,2,1,0:T(4,128)(2,1)} %copy.94), calls=%async_computation | async-start | bytes 3538944 | tf_op jit(solution)/shard_map/all_to_all | solution.py:96
  15.6 0.3 reshape.278
  15.9 0.3 reshape.279
  16.3 0.3 copy-done.14
  16.6 1.1 reshape.280
  17.7 1.1 reshape.283
  18.8 0.3 convolution_bitcast_fusion.2
  19.1 0.2 copy.98
  20.0 0.8 fusion.59
  20.9 2.4 %multiply_reduce_fusion = (f32[12,144]{1,0:T(8,128)S(1)}, f32[12,144,144]{1,2,0:T(8,128)S(1)}) fusion(f32[12,144,144]{1,2,0:T(8,128)S(1)} %get-tuple-element.12, f32[12,144]{1,0:T(8,128)S(1)} %get-tuple-element.11, bf16[144,12,128]{2,1,0:T(8,128)(2,1)} %reshape.280, bf16[144,12,128]{2,1,0:T(8,128)(2,1)} %reshape.283), kind=kOutput, calls=%fused_computation.7 | convolution fusion | flops 64445760 | bytes 2889216 | tf_op jit(solution)/shard_map/bfihe,bfjhe->bfhij/dot_general | solution.py:42
  23.2 0.4 multiply_convert_fusion
  23.6 15.2 %all-to-all-done = bf16[16,9,4,1536]{3,2,1,0:T(4,128)(2,1)} async-done(((bf16[16,9,4,1536]{3,2,1,0:T(4,128)(2,1)}), bf16[16,9,4,1536]{3,2,1,0:T(4,128)(2,1)}, u32[]{:S(2)}, u32[]{:S(2)}) %all-to-all-start) | async-done | bytes 1769504 | tf_op jit(solution)/shard_map/all_to_all | solution.py:96
  38.8 3.4 %reshape.289 = bf16[16,9,4,12,128]{4,3,2,1,0:T(8,128)(2,1)S(1)} reshape(bf16[16,9,4,1536]{3,2,1,0:T(4,128)(2,1)} %all-to-all-done) | data formatting | bytes 3538944 | tf_op jit(solution)/shard_map/reshape | solution.py:97
  42.2 2.1 %copy.176 = bf16[16,9,4,12,128]{4,0,3,1,2:T(8,128)(2,1)S(1)} copy(bf16[16,9,4,12,128]{4,3,2,1,0:T(8,128)(2,1)S(1)} %reshape.289) | data formatting | bytes 3538944 | tf_op jit(solution)/shard_map/reshape | solution.py:97
  44.3 0.4 fusion.8
  44.7 1.1 copy-done.17
  45.8 3.4 %fusion.64 = (f32[9,12,16]{2,1,0:T(8,128)S(1)}, f32[9,12,16,16]{2,3,1,0:T(8,128)S(1)}) fusion(f32[9,12,16,16]{2,3,1,0:T(8,128)S(1)} %fusion.8), kind=kOutput, calls=%fused_computation.86 | output fusion | flops 55311 | bytes 228096 | tf_op jit(solution)/shard_map/sub | solution.py:28
  49.2 0.4 multiply_reduce_fusion.1
  49.6 0.2 copy-done.21
  49.8 0.3 fusion.35
  50.4 0.7 collective-permute-start
  51.1 3.4 %collective-permute-start.1 = (f32[12,16]{1,0:T(8,128)S(1)}, f32[12,16]{1,0:T(8,128)}, u32[]{:S(2)}, u32[]{:S(2)}) collective-permute-start(f32[12,16]{1,0:T(8,128)S(1)} %convolution_bitcast_fusion.3), channel_id=1, source_target_pairs={{0,2},{1,3},{2,0},{3,1},{4,6},{5,7},{6,4},{7,5},{8,10},{9,11},{10,... | collective-permute-start | bytes 2312 | tf_op jit(solution)/shard_map/ppermute | solution.py:62
  54.5 0.5 collective-permute-start.2
  55.0 1.1 fusion.12
  56.1 0.4 fusion.11
  56.4 2.7 %fusion.13 = bf16[16,9,12,128]{3,0,2,1:T(8,128)(2,1)} fusion(bf16[4,9,12,16,128]{4,3,2,1,0:T(8,128)(2,1)S(1)} %bitcast.127, f32[9,12,16]{2,1,0:T(8,128)} %copy-done.21, f32[9,12,16,16]{2,3,1,0:T(8,128)} %copy-done.17), kind=kOutput, calls=%fused_computation.30 | convolution fusion | flops 7383759 | bytes 2727936 | tf_op jit(solution)/shard_map/phij,phje->phie/dot_general | solution.py:31
  59.2 2.7 %fusion.14 = bf16[16,9,12,128]{3,0,2,1:T(8,128)(2,1)} fusion(bf16[4,9,12,16,128]{4,3,2,1,0:T(8,128)(2,1)S(1)} %bitcast.128, f32[9,12,16]{2,1,0:T(8,128)} %copy-done.21, f32[9,12,16,16]{2,3,1,0:T(8,128)} %copy-done.17), kind=kOutput, calls=%fused_computation.31 | convolution fusion | flops 7383759 | bytes 2727936 | tf_op jit(solution)/shard_map/phij,phie->phje/dot_general | solution.py:39
  62.0 0.3 stack_reshape.29
  62.5 0.3 stack_reshape.30
  62.8 1.2 copy.100
  63.9 0.3 stack_reshape.28
  64.4 0.3 stack_reshape.31
  64.7 0.2 pad_maximum_fusion.1
  65.0 2.6 %copy.105 = bf16[16,9,4,1536]{3,2,1,0:T(4,128)(2,1)} copy(bf16[16,9,4,1536]{3,0,1,2:T(8,128)(2,1)S(1)} %pad_maximum_fusion.1) | data formatting | bytes 3538944 | tf_op jit(solution)/shard_map/stack | solution.py:115
  67.5 7.6 %all-to-all-start.1 = ((bf16[16,9,4,1536]{3,2,1,0:T(4,128)(2,1)}), bf16[16,9,4,1536]{3,2,1,0:T(4,128)(2,1)S(1)}, u32[]{:S(2)}, u32[]{:S(2)}) async-start(bf16[16,9,4,1536]{3,2,1,0:T(4,128)(2,1)} %copy.105), calls=%async_computation.1 | async-start | bytes 3538944 | tf_op jit(solution)/shard_map/all_to_all | solution.py:122
  75.2 2.2 %convolution_bitcast_fusion = f32[1,1,12,18,8,128]{5,4,3,2,1,0:T(8,128)S(1)} fusion(bf16[144,12,128]{2,1,0:T(8,128)(2,1)} %reshape.283, f32[12,144,144]{1,2,0:T(8,128)} %copy-done.9, f32[12,144]{1,0:T(8,128)} %copy-done.22), kind=kOutput, calls=%fused_computation.22 | convolution fusion | flops 64198656 | bytes 2329344 | tf_op jit(solution)/shard_map/bfhij,bfihe->bfjhe/dot_general | solution.py:39
  77.4 0.7 add_add_fusion.2
  78.1 1.5 %collective-permute-start.3 = (f32[12,16]{1,0:T(8,128)S(1)}, f32[12,16]{1,0:T(8,128)S(1)}, u32[]{:S(2)}, u32[]{:S(2)}) collective-permute-start(f32[12,16]{1,0:T(8,128)S(1)} %add_add_fusion.2), channel_id=1, source_target_pairs={{0,4},{1,5},{2,6},{3,7},{4,0},{5,1},{6,2},{7,3},{8,12},{9,13},{10,... | collective-permute-start | bytes 2312 | tf_op jit(solution)/shard_map/ppermute | solution.py:62
  79.6 2.7 %collective-permute-start.4 = (f32[12,16]{1,0:T(8,128)S(1)}, f32[12,16]{1,0:T(8,128)S(1)}, u32[]{:S(2)}, u32[]{:S(2)}) collective-permute-start(f32[12,16]{1,0:T(8,128)S(1)} %add_add_fusion.2), channel_id=1, source_target_pairs={{0,8},{1,9},{2,10},{3,11},{4,12},{5,13},{6,14},{7,15},{8,0},{9,1},... | collective-permute-start | bytes 2312 | tf_op jit(solution)/shard_map/ppermute | solution.py:62
  82.4 0.5 collective-permute-start.5
  82.9 1.5 %convolution_bitcast_fusion.1 = f32[1,1,12,18,8,128]{5,4,3,2,1,0:T(8,128)} fusion(bf16[144,12,128]{2,1,0:T(8,128)(2,1)S(1)} %copy-done.19, f32[12,144,144]{1,2,0:T(8,128)S(1)} %copy-done.10, f32[12,144]{1,0:T(8,128)S(1)} %copy-done.23), kind=kOutput, calls=%fused_computation.23 | convolution fusion | flops 64198656 | bytes 2329344 | tf_op jit(solution)/shard_map/bfhij,bfjhe->bfihe/dot_general | solution.py:31
  84.4 9.8 %collective-permute-done.3 = f32[12,16]{1,0:T(8,128)S(1)} collective-permute-done((f32[12,16]{1,0:T(8,128)S(1)}, f32[12,16]{1,0:T(8,128)S(1)}, u32[]{:S(2)}, u32[]{:S(2)}) %collective-permute-start.3) | collective-permute-done | bytes 800 | tf_op jit(solution)/shard_map/ppermute | solution.py:62
  94.2 1.7 %collective-permute-done.4 = f32[12,16]{1,0:T(8,128)S(1)} collective-permute-done((f32[12,16]{1,0:T(8,128)S(1)}, f32[12,16]{1,0:T(8,128)S(1)}, u32[]{:S(2)}, u32[]{:S(2)}) %collective-permute-start.4) | collective-permute-done | bytes 800 | tf_op jit(solution)/shard_map/ppermute | solution.py:62
  96.0 2.0 %collective-permute-start.7 = (f32[12,16]{1,0:T(8,128)S(1)}, f32[12,16]{1,0:T(8,128)S(1)}, u32[]{:S(2)}, u32[]{:S(2)}) collective-permute-start(f32[12,16]{1,0:T(8,128)S(1)} %add_add_fusion.1), channel_id=1, source_target_pairs={{0,32},{16,48},{32,0},{48,16},{64,96},{80,112},{96,64},{112,80},{1... | collective-permute-start | bytes 2312 | tf_op jit(solution)/shard_map/ppermute | solution.py:62
  98.0 1.3 %fusion.5 = f32[1,1,12,18,8,128]{5,4,3,2,1,0:T(8,128)} fusion(bf16[12,144,144]{1,2,0:T(8,128)(2,1)S(1)} %multiply_convert_fusion, bf16[144,12,128]{2,1,0:T(8,128)(2,1)S(1)} %copy-done.8), kind=kOutput, calls=%fused_computation.15 | convolution fusion | flops 63922176 | bytes 1824768 | tf_op jit(solution)/shard_map/bfhij,bfihe->bfjhe/dot_general | solution.py:52
  99.4 0.4 collective-permute-done.7
  99.7 1.3 %collective-permute-done.8 = f32[12,16]{1,0:T(8,128)S(1)} collective-permute-done((f32[12,16]{1,0:T(8,128)S(1)}, f32[12,16]{1,0:T(8,128)S(1)}, u32[]{:S(2)}, u32[]{:S(2)}) %collective-permute-start.8) | collective-permute-done | bytes 800 | tf_op jit(solution)/shard_map/ppermute | solution.py:62
  101.1 6.3 %collective-permute-start.10 = (f32[12,16]{1,0:T(8,128)S(1)}, f32[12,16]{1,0:T(8,128)S(1)}, u32[]{:S(2)}, u32[]{:S(2)}) collective-permute-start(f32[12,16]{1,0:T(8,128)S(1)} %add_add_fusion), channel_id=1, source_target_pairs={{0,128},{16,144},{32,160},{48,176},{64,192},{80,208},{96,224},{112... | collective-permute-start | bytes 2312 | tf_op jit(solution)/shard_map/ppermute | solution.py:62
  107.4 0.6 collective-permute-start.11
  107.9 0.9 collective-permute-start.9
  108.8 1.5 %fusion.4 = f32[1,1,12,18,8,128]{5,4,3,2,1,0:T(8,128)} fusion(bf16[12,144,144]{1,2,0:T(8,128)(2,1)S(1)} %multiply_convert_fusion, bf16[144,12,128]{2,1,0:T(8,128)(2,1)S(1)} %copy-done.6), kind=kOutput, calls=%fused_computation.14 | convolution fusion | flops 63922176 | bytes 1824768 | tf_op jit(solution)/shard_map/bfhij,bfjhe->bfihe/dot_general | solution.py:49
  110.4 2.8 %collective-permute-done.11 = f32[12,16]{1,0:T(8,128)S(1)} collective-permute-done((f32[12,16]{1,0:T(8,128)S(1)}, f32[12,16]{1,0:T(8,128)S(1)}, u32[]{:S(2)}, u32[]{:S(2)}) %collective-permute-start.11) | collective-permute-done | bytes 800 | tf_op jit(solution)/shard_map/ppermute | solution.py:62
  113.1 0.6 add_multiply_fusion
  113.7 0.5 convert_bitcast_fusion
  114.2 2.6 %fusion.58 = (f32[1,16,9,1536]{3,0,2,1:T(1,128)S(1)}, f32[1,16,9,1536]{3,0,2,1:T(1,128)S(1)}, f32[1,16,9,1536]{3,0,2,1:T(1,128)S(1)}, f32[1,16,9,1536]{3,0,2,1:T(1,128)S(1)}) fusion(f32[4,16,9,1536]{3,0,2,1:T(4,128)S(1)} %convert_bitcast_fusion), kind=kLoop, calls=%fused_computation.84 | loop fusion | bytes 7077888 | tf_op jit(solution)/shard_map/slice | solution.py:138
  116.9 1.1 fusion.15
  118.1 0.6 copy-done.18
  118.7 1.1 fusion.17
  (66 shorter events, 1.1 us)
Async XLA Ops:
  0.6 18.2 %copy-start = (f32[12,16]{1,0:T(8,128)S(1)}, f32[12,16]{1,0:T(8,128)}, u32[]{:S(2)}) copy-start(f32[12,16]{1,0:T(8,128)} %param.13) | copy-start | bytes 2308
  0.6 2.5 %copy-start.13 = (bf16[1,1,144,1536]{3,2,1,0:T(8,128)(2,1)S(1)}, bf16[1,1,144,1536]{3,2,1,0:T(8,128)(2,1)}, u32[]{:S(2)}) copy-start(bf16[1,1,144,1536]{3,2,1,0:T(8,128)(2,1)} %param.9) | copy-start | bytes 1327108
  8.0 7.6 %copy-start.11 = (bf16[1,1,144,1536]{3,2,1,0:T(8,128)(2,1)S(1)}, bf16[1,1,144,1536]{3,2,1,0:T(8,128)(2,1)}, u32[]{:S(2)}) copy-start(bf16[1,1,144,1536]{3,2,1,0:T(8,128)(2,1)} %param.7) | copy-start | bytes 1327108
  8.0 7.9 %copy-start.12 = (bf16[1,1,144,1536]{3,2,1,0:T(8,128)(2,1)S(1)}, bf16[1,1,144,1536]{3,2,1,0:T(8,128)(2,1)}, u32[]{:S(2)}) copy-start(bf16[1,1,144,1536]{3,2,1,0:T(8,128)(2,1)} %param.8) | copy-start | bytes 1327108
  8.0 30.9 %all-to-all-start = ((bf16[16,9,4,1536]{3,2,1,0:T(4,128)(2,1)}), bf16[16,9,4,1536]{3,2,1,0:T(4,128)(2,1)}, u32[]{:S(2)}, u32[]{:S(2)}) async-start(bf16[16,9,4,1536]{3,2,1,0:T(4,128)(2,1)} %copy.94), calls=%async_computation | async-start | bytes 3538944 | tf_op jit(solution)/shard_map/all_to_all | solution.py:96
  15.5 1.0 copy-start.14
  15.5 2.2 %copy-start.15 = (bf16[1,1,144,1536]{3,2,1,0:T(8,128)(2,1)S(1)}, bf16[1,1,144,1536]{3,2,1,0:T(8,128)(2,1)}, u32[]{:S(2)}) copy-start(bf16[1,1,144,1536]{3,2,1,0:T(8,128)(2,1)} %param.10) | copy-start | bytes 1327108
  15.9 4.9 %copy-start.7 = (bf16[144,12,128]{2,1,0:T(8,128)(2,1)}, bf16[144,12,128]{2,1,0:T(8,128)(2,1)S(1)}, u32[]{:S(2)}) copy-start(bf16[144,12,128]{2,1,0:T(8,128)(2,1)S(1)} %reshape.278) | copy-start | bytes 1327108
  15.9 4.0 %copy-start.24 = (s32[1,16]{1,0:T(1,128)S(1)}, s32[1,16]{1,0:T(1,128)}, u32[]{:S(2)}) copy-start(s32[1,16]{1,0:T(1,128)} %param.12) | copy-start | bytes 196
  16.6 4.3 %copy-start.5 = (bf16[144,12,128]{2,1,0:T(8,128)(2,1)}, bf16[144,12,128]{2,1,0:T(8,128)(2,1)S(1)}, u32[]{:S(2)}) copy-start(bf16[144,12,128]{2,1,0:T(8,128)(2,1)S(1)} %reshape.279) | copy-start | bytes 1327108
  20.8 2.4 %copy-start.9 = (f32[12,144,144]{1,2,0:T(8,128)}, f32[12,144,144]{1,2,0:T(8,128)S(1)}, u32[]{:S(2)}) copy-start(f32[12,144,144]{1,2,0:T(8,128)S(1)} %get-tuple-element.12) | copy-start | bytes 2985988
  20.8 2.4 %copy-start.22 = (f32[12,144]{1,0:T(8,128)}, f32[12,144]{1,0:T(8,128)S(1)}, u32[]{:S(2)}) copy-start(f32[12,144]{1,0:T(8,128)S(1)} %get-tuple-element.11) | copy-start | bytes 20740
  44.3 4.9 %copy-start.1 = (bf16[16,9,4,12,128]{4,0,3,1,2:T(8,128)(2,1)}, bf16[16,9,4,12,128]{4,0,3,1,2:T(8,128)(2,1)S(1)}, u32[]{:S(2)}) copy-start(bf16[16,9,4,12,128]{4,0,3,1,2:T(8,128)(2,1)S(1)} %copy.176) | copy-start | bytes 5308420
  44.7 1.1 copy-start.17
  49.2 0.6 copy-start.21
  49.6 5.4 %copy-start.2 = (bf16[16,9,4,12,128]{4,0,3,1,2:T(8,128)(2,1)S(1)}, bf16[16,9,4,12,128]{4,0,3,1,2:T(8,128)(2,1)}, u32[]{:S(2)}) copy-start(bf16[16,9,4,12,128]{4,0,3,1,2:T(8,128)(2,1)} %copy-done.1) | copy-start | bytes 5308420
  50.4 27.0 %collective-permute-start = (f32[12,16]{1,0:T(8,128)S(1)}, f32[12,16]{1,0:T(8,128)}, u32[]{:S(2)}, u32[]{:S(2)}) collective-permute-start(f32[12,16]{1,0:T(8,128)S(1)} %convolution_bitcast_fusion.3), channel_id=1, source_target_pairs={{0,1},{1,0},{2,3},{3,2},{4,5},{5,4},{6,7},{7,6},{8,9},{9,8},{10,11... | collective-permute-start | bytes 2312 | tf_op jit(solution)/shard_map/ppermute | solution.py:62
  51.1 26.3 %collective-permute-start.1 = (f32[12,16]{1,0:T(8,128)S(1)}, f32[12,16]{1,0:T(8,128)}, u32[]{:S(2)}, u32[]{:S(2)}) collective-permute-start(f32[12,16]{1,0:T(8,128)S(1)} %convolution_bitcast_fusion.3), channel_id=1, source_target_pairs={{0,2},{1,3},{2,0},{3,1},{4,6},{5,7},{6,4},{7,5},{8,10},{9,11},{10,... | collective-permute-start | bytes 2312 | tf_op jit(solution)/shard_map/ppermute | solution.py:62
  54.5 22.9 %collective-permute-start.2 = (f32[12,16]{1,0:T(8,128)S(1)}, f32[12,16]{1,0:T(8,128)}, u32[]{:S(2)}, u32[]{:S(2)}) collective-permute-start(f32[12,16]{1,0:T(8,128)S(1)} %convolution_bitcast_fusion.3), channel_id=1, source_target_pairs={{0,3},{1,2},{2,1},{3,0},{4,7},{5,6},{6,5},{7,4},{8,11},{9,10},{10,... | collective-permute-start | bytes 2312 | tf_op jit(solution)/shard_map/ppermute | solution.py:62
  59.2 2.7 %copy-start.16 = (bf16[16,9,12,128]{3,0,2,1:T(8,128)(2,1)S(1)}, bf16[16,9,12,128]{3,0,2,1:T(8,128)(2,1)}, u32[]{:S(2)}) copy-start(bf16[16,9,12,128]{3,0,2,1:T(8,128)(2,1)} %fusion.12) | copy-start | bytes 1327108
  62.5 1.8 %copy-start.20 = (bf16[16,9,12,128]{3,0,2,1:T(8,128)(2,1)S(1)}, bf16[16,9,12,128]{3,0,2,1:T(8,128)(2,1)}, u32[]{:S(2)}) copy-start(bf16[16,9,12,128]{3,0,2,1:T(8,128)(2,1)} %fusion.14) | copy-start | bytes 1327108
  67.5 46.2 %all-to-all-start.1 = ((bf16[16,9,4,1536]{3,2,1,0:T(4,128)(2,1)}), bf16[16,9,4,1536]{3,2,1,0:T(4,128)(2,1)S(1)}, u32[]{:S(2)}, u32[]{:S(2)}) async-start(bf16[16,9,4,1536]{3,2,1,0:T(4,128)(2,1)} %copy.105), calls=%async_computation.1 | async-start | bytes 3538944 | tf_op jit(solution)/shard_map/all_to_all | solution.py:122
  75.2 7.7 %copy-start.10 = (f32[12,144,144]{1,2,0:T(8,128)S(1)}, f32[12,144,144]{1,2,0:T(8,128)}, u32[]{:S(2)}) copy-start(f32[12,144,144]{1,2,0:T(8,128)} %copy-done.9) | copy-start | bytes 2985988
  75.2 7.7 %copy-start.19 = (bf16[144,12,128]{2,1,0:T(8,128)(2,1)S(1)}, bf16[144,12,128]{2,1,0:T(8,128)(2,1)}, u32[]{:S(2)}) copy-start(bf16[144,12,128]{2,1,0:T(8,128)(2,1)} %reshape.280) | copy-start | bytes 1327108
  75.2 7.7 %copy-start.23 = (f32[12,144]{1,0:T(8,128)S(1)}, f32[12,144]{1,0:T(8,128)}, u32[]{:S(2)}) copy-start(f32[12,144]{1,0:T(8,128)} %copy-done.22) | copy-start | bytes 20740
  78.1 19.9 %copy-start.8 = (bf16[144,12,128]{2,1,0:T(8,128)(2,1)S(1)}, bf16[144,12,128]{2,1,0:T(8,128)(2,1)}, u32[]{:S(2)}) copy-start(bf16[144,12,128]{2,1,0:T(8,128)(2,1)} %copy-done.7) | copy-start | bytes 1327108
  78.1 16.1 %collective-permute-start.3 = (f32[12,16]{1,0:T(8,128)S(1)}, f32[12,16]{1,0:T(8,128)S(1)}, u32[]{:S(2)}, u32[]{:S(2)}) collective-permute-start(f32[12,16]{1,0:T(8,128)S(1)} %add_add_fusion.2), channel_id=1, source_target_pairs={{0,4},{1,5},{2,6},{3,7},{4,0},{5,1},{6,2},{7,3},{8,12},{9,13},{10,... | collective-permute-start | bytes 2312 | tf_op jit(solution)/shard_map/ppermute | solution.py:62
  79.6 16.2 %collective-permute-start.4 = (f32[12,16]{1,0:T(8,128)S(1)}, f32[12,16]{1,0:T(8,128)S(1)}, u32[]{:S(2)}, u32[]{:S(2)}) collective-permute-start(f32[12,16]{1,0:T(8,128)S(1)} %add_add_fusion.2), channel_id=1, source_target_pairs={{0,8},{1,9},{2,10},{3,11},{4,12},{5,13},{6,14},{7,15},{8,0},{9,1},... | collective-permute-start | bytes 2312 | tf_op jit(solution)/shard_map/ppermute | solution.py:62
  82.4 13.5 %collective-permute-start.5 = (f32[12,16]{1,0:T(8,128)S(1)}, f32[12,16]{1,0:T(8,128)S(1)}, u32[]{:S(2)}, u32[]{:S(2)}) collective-permute-start(f32[12,16]{1,0:T(8,128)S(1)} %add_add_fusion.2), channel_id=1, source_target_pairs={{0,12},{1,13},{2,14},{3,15},{4,8},{5,9},{6,10},{7,11},{8,4},{9,5},... | collective-permute-start | bytes 2312 | tf_op jit(solution)/shard_map/ppermute | solution.py:62
  84.4 24.5 %copy-start.6 = (bf16[144,12,128]{2,1,0:T(8,128)(2,1)S(1)}, bf16[144,12,128]{2,1,0:T(8,128)(2,1)}, u32[]{:S(2)}) copy-start(bf16[144,12,128]{2,1,0:T(8,128)(2,1)} %copy-done.5) | copy-start | bytes 1327108
  95.9 3.5 %collective-permute-start.6 = (f32[12,16]{1,0:T(8,128)S(1)}, f32[12,16]{1,0:T(8,128)S(1)}, u32[]{:S(2)}, u32[]{:S(2)}) collective-permute-start(f32[12,16]{1,0:T(8,128)S(1)} %add_add_fusion.1), channel_id=1, source_target_pairs={{0,16},{16,0},{32,48},{48,32},{64,80},{80,64},{96,112},{112,96},{1... | collective-permute-start | bytes 2312 | tf_op jit(solution)/shard_map/ppermute | solution.py:62
  96.0 3.7 %collective-permute-start.7 = (f32[12,16]{1,0:T(8,128)S(1)}, f32[12,16]{1,0:T(8,128)S(1)}, u32[]{:S(2)}, u32[]{:S(2)}) collective-permute-start(f32[12,16]{1,0:T(8,128)S(1)} %add_add_fusion.1), channel_id=1, source_target_pairs={{0,32},{16,48},{32,0},{48,16},{64,96},{80,112},{96,64},{112,80},{1... | collective-permute-start | bytes 2312 | tf_op jit(solution)/shard_map/ppermute | solution.py:62
  98.0 3.1 %collective-permute-start.8 = (f32[12,16]{1,0:T(8,128)S(1)}, f32[12,16]{1,0:T(8,128)S(1)}, u32[]{:S(2)}, u32[]{:S(2)}) collective-permute-start(f32[12,16]{1,0:T(8,128)S(1)} %add_add_fusion.1), channel_id=1, source_target_pairs={{0,48},{16,32},{32,16},{48,0},{64,112},{80,96},{96,80},{112,64},{1... | collective-permute-start | bytes 2312 | tf_op jit(solution)/shard_map/ppermute | solution.py:62
  101.1 9.3 %collective-permute-start.10 = (f32[12,16]{1,0:T(8,128)S(1)}, f32[12,16]{1,0:T(8,128)S(1)}, u32[]{:S(2)}, u32[]{:S(2)}) collective-permute-start(f32[12,16]{1,0:T(8,128)S(1)} %add_add_fusion), channel_id=1, source_target_pairs={{0,128},{16,144},{32,160},{48,176},{64,192},{80,208},{96,224},{112... | collective-permute-start | bytes 2312 | tf_op jit(solution)/shard_map/ppermute | solution.py:62
  107.4 5.8 %collective-permute-start.11 = (f32[12,16]{1,0:T(8,128)S(1)}, f32[12,16]{1,0:T(8,128)S(1)}, u32[]{:S(2)}, u32[]{:S(2)}) collective-permute-start(f32[12,16]{1,0:T(8,128)S(1)} %add_add_fusion), channel_id=1, source_target_pairs={{0,192},{16,208},{32,224},{48,240},{64,128},{80,144},{96,160},{112... | collective-permute-start | bytes 2312 | tf_op jit(solution)/shard_map/ppermute | solution.py:62
  107.9 5.2 %collective-permute-start.9 = (f32[12,16]{1,0:T(8,128)S(1)}, f32[12,16]{1,0:T(8,128)S(1)}, u32[]{:S(2)}, u32[]{:S(2)}) collective-permute-start(f32[12,16]{1,0:T(8,128)S(1)} %add_add_fusion), channel_id=1, source_target_pairs={{0,64},{16,80},{32,96},{48,112},{64,0},{80,16},{96,32},{112,48},{1... | collective-permute-start | bytes 2312 | tf_op jit(solution)/shard_map/ppermute | solution.py:62
  114.2 2.7 %copy-start.3 = (f32[1,1,12,18,8,128]{5,4,3,2,1,0:T(8,128)S(1)}, f32[1,1,12,18,8,128]{5,4,3,2,1,0:T(8,128)}, u32[]{:S(2)}) copy-start(f32[1,1,12,18,8,128]{5,4,3,2,1,0:T(8,128)} %fusion.5) | copy-start | bytes 2654212
  116.9 1.2 copy-start.4
  116.9 1.7 %copy-start.18 = (f32[1,1,12,18,8,128]{5,4,3,2,1,0:T(8,128)S(1)}, f32[1,1,12,18,8,128]{5,4,3,2,1,0:T(8,128)}, u32[]{:S(2)}) copy-start(f32[1,1,12,18,8,128]{5,4,3,2,1,0:T(8,128)} %convolution_bitcast_fusion.1) | copy-start | bytes 2654212

commit v3 on v2

--- a/solution.py
+++ b/solution.py
@@ -55,16 +55,12 @@
     return (query_grad, key_grad, value_grad, score_grad)
 
 
-def quad_sum(value, axis, size):
-    step = 1
-    while step < size:
-        received = [
-            lax.ppermute(value, axis, [(index, index ^ (part * step)) for index in range(size)])
-            for part in (1, 2, 3)
-        ]
-        value = (value + received[0]) + (received[1] + received[2])
-        step *= 4
-    return value
+def quad_step(value, axis, size, step):
+    received = [
+        lax.ppermute(value, axis, [(index, index ^ (part * step)) for index in range(size)])
+        for part in (1, 2, 3)
+    ]
+    return (value + received[0]) + (received[1] + received[2])
 
 
 def on_device(queries, keys, values, cotangent, spatial_count, clip_ids, time_bias):
@@ -97,28 +93,60 @@
     rows = rows.reshape(seq_size, block, 4, head_count, width // head_count)
     rows = jnp.transpose(rows, (2, 1, 3, 0, 4))
     query_part, key_part, value_part, slope_part = rows[0], rows[1], rows[2], rows[3]
-    shares, shares_half, result = attend_forward(
-        TIME_PATTERNS, query_part, key_part, value_part, bias_table[0], same_clip[0]
+    scaling = 1.0 / math.sqrt(query_part.shape[-1])
+    scores = (
+        jnp.einsum(TIME_PATTERNS[0], query_part, key_part, preferred_element_type=jnp.float32)
+        * scaling
+        + bias_table[0]
     )
-    time_grads = attend_backward(
-        TIME_PATTERNS, query_part, key_part, value_part, slope_part, shares, shares_half
+    scores = jnp.where(same_clip[0], scores, -1e30)
+    row_peak = jnp.max(scores, axis=-1, keepdims=True)
+    weights = jnp.exp(scores - row_peak)
+    shares = weights / jnp.sum(weights, axis=-1, keepdims=True)
+    share_grad = jnp.einsum(
+        TIME_PATTERNS[0], slope_part, value_part, preferred_element_type=jnp.float32
     )
+    spread = jnp.sum(shares * share_grad, axis=-1, keepdims=True)
+    score_grad = shares * (share_grad - spread)
     bias_part = jnp.tensordot(
-        jnp.sum(time_grads[3], axis=0),
+        jnp.sum(score_grad, axis=0),
         onehot,
         axes=((1, 2), (1, 2)),
         precision=lax.Precision.HIGHEST,
     )
-    summed = quad_sum(quad_sum(bias_part, "seq", seq_size), "dp", dp_size)
-    bias_grad = summed / math.sqrt(dp_size * queries.shape[0] * frames_all * positions)
-
+    partial = quad_step(bias_part, "seq", seq_size, 1)
+    partial, shares, score_grad, query_part, key_part, value_part, slope_part = (
+        lax.optimization_barrier(
+            (partial, shares, score_grad, query_part, key_part, value_part, slope_part)
+        )
+    )
+    shares_half = shares.astype(jnp.bfloat16)
+    score_half = score_grad.astype(jnp.bfloat16)
+    result = jnp.einsum(
+        TIME_PATTERNS[1], shares_half, value_part, preferred_element_type=jnp.float32
+    )
+    time_value_grad = jnp.einsum(
+        TIME_PATTERNS[2], shares_half, slope_part, preferred_element_type=jnp.float32
+    )
+    time_query_grad = (
+        jnp.einsum(TIME_PATTERNS[1], score_half, key_part, preferred_element_type=jnp.float32)
+        * scaling
+    )
+    time_key_grad = (
+        jnp.einsum(TIME_PATTERNS[2], score_half, query_part, preferred_element_type=jnp.float32)
+        * scaling
+    )
+    partial = quad_step(partial, "seq", seq_size, 4)
     back_rows = jnp.stack(
         [
             jnp.transpose(tensor.astype(jnp.bfloat16), (2, 0, 1, 3)).reshape(seq_size, block, width)
-            for tensor in (result, time_grads[0], time_grads[1], time_grads[2])
+            for tensor in (result, time_query_grad, time_key_grad, time_value_grad)
         ],
         axis=2,
     )
+    partial, back_rows = lax.optimization_barrier((partial, back_rows))
+    summed = quad_step(quad_step(partial, "dp", dp_size, 1), "dp", dp_size, 4)
+    bias_grad = summed / math.sqrt(dp_size * queries.shape[0] * frames_all * positions)
     back = lax.all_to_all(back_rows, "seq", split_axis=0, concat_axis=0, tiled=True)
     back = jnp.moveaxis(back, 2, 0).reshape(4, 1, 1, positions, width).astype(jnp.float32)
 

time: 120 us -> 106 us (0.88)
  waiting for transfers between devices: 31.2 us -> 15.8 us
  local copies, waits for them, and re-layouts: 25.6 us -> 28.3 us
  matrix products: 17.7 us -> 15.6 us
    ppermute x12, waiting for transfers between devices: 16 us -> 8.27 us  [quad_step(): lax.ppermute(value, axis, [(index, index ^ part * step) for index in rang...]
    all_to_all x1, waiting for transfers between devices: 15.2 us -> 7.55 us  [on_device(): lax.all_to_all(stacked, 'seq', split_axis=0, concat_axis=0, tiled=True)]
    dot_general x2 -> x6, matrix products: 0.55 us -> 3.84 us  [the longest x1 1.38 us: on_device(): jnp.einsum(TIME_PATTERNS[2], score_half, query_part, preferred_element_ty...]
    optimization_barrier x0 -> x1, local copies, waits for them, and re-layouts: none -> 2.61 us  [on_device(): partial, back_rows = lax.optimization_barrier((partial, back_rows))]
    sub x1, matrix products: 0.77 us -> 3.27 us  [attend_forward(): weights = jnp.exp(scores - row_peak)]
    dot_general x2 -> x1, matrix products: 2.73 us -> 0.48 us  [attend_backward(): jnp.einsum(patterns[0], cotangent_part, value_part, preferred_element_typ...]
    dot_general x2 -> x1, matrix products: 4.87 us -> 2.79 us  [attend_backward(): jnp.einsum(patterns[2], shares_half, cotangent_part, preferred_element_ty...]
    unnamed x50 -> x38, local copies, waits for them, and re-layouts: 2.33 us -> 0.29 us
  transfers between devices with their start and end apart: 14 -> 14, of which waited for: 6 -> 5; matrix products, arithmetic and copies ran while one was open for 23% -> 25% of each run, Pallas kernels for 0% -> 0%
where the time goes in v3:
time: 106 us; the launch traced here: 105 us
  starting transfers between devices  34.8 us (33%)
  local copies, waits for them, and re-layouts  28.3 us (27%)
  waiting for transfers between devices  15.8 us (15%)
  matrix products  15.6 us (15%)
  other arithmetic  8.34 us (8%)
  between operations  1.71 us (2%)
    ppermute x12, starting transfers between devices, quad_step(): lax.ppermute(value, axis, [(index, index ^ part * step) for index in rang...  19.3 us
    ppermute x12, waiting for transfers between devices, quad_step(): lax.ppermute(value, axis, [(index, index ^ part * step) for index in rang...  8.27 us
    all_to_all x1, starting transfers between devices, on_device(): lax.all_to_all(back_rows, 'seq', split_axis=0, concat_axis=0, tiled=True)  8 us
    all_to_all x1, starting transfers between devices, on_device(): lax.all_to_all(stacked, 'seq', split_axis=0, concat_axis=0, tiled=True)  7.58 us
    all_to_all x1, waiting for transfers between devices, on_device(): lax.all_to_all(stacked, 'seq', split_axis=0, concat_axis=0, tiled=True)  7.55 us
    another operation x5, local copies, waits for them, and re-layouts, on_device(): jnp.stack([tensor.reshape(seq_size, block, width) for tensor in (queries,...  6.64 us
    reshape x2, local copies, waits for them, and re-layouts, on_device(): rows = rows.reshape(seq_size, block, 4, head_count, width // head_count)  6.25 us
    another operation x4, local copies, waits for them, and re-layouts  4.31 us
  transfers between devices with their start and end apart: 14, of which 5 were waited for; matrix products, arithmetic and copies ran while one was open for 25% of the time, Pallas kernels for 0%

profile of v3, /device:TPU:4, one launch (start us, length us, event | category | flops | bytes accessed | tf_op | source)
XLA Modules:
  0.0 104.6 jit_solution(4872899570261673832)
XLA Ops:
  0.7 1.2 %stack_reshape.24 = bf16[16,9,1,1536]{3,1,0,2:T(8,128)(2,1)S(1)} reshape(bf16[1,1,144,1536]{3,2,1,0:T(8,128)(2,1)} %param.7) | data formatting | bytes 884736 | tf_op jit(solution)/shard_map/stack;reshape | solution.py:85
  1.9 1.2 %stack_reshape.25 = bf16[16,9,1,1536]{3,1,0,2:T(8,128)(2,1)S(1)} reshape(bf16[1,1,144,1536]{3,2,1,0:T(8,128)(2,1)} %param.8) | data formatting | bytes 884736 | tf_op jit(solution)/shard_map/stack;reshape | solution.py:85
  3.1 0.2 stack_reshape.26
  3.3 1.2 %stack_reshape.27 = bf16[16,9,1,1536]{3,1,0,2:T(8,128)(2,1)S(1)} reshape(bf16[1,1,144,1536]{3,2,1,0:T(8,128)(2,1)} %param.10) | data formatting | bytes 884736 | tf_op jit(solution)/shard_map/stack;reshape | solution.py:85
  4.5 0.6 pad_maximum_fusion
  5.1 2.8 %copy.94 = bf16[16,9,4,1536]{3,2,1,0:T(4,128)(2,1)} copy(bf16[16,9,4,1536]{3,1,0,2:T(8,128)(2,1)S(1)} %pad_maximum_fusion) | data formatting | bytes 3538944 | tf_op jit(solution)/shard_map/stack | solution.py:85
  7.9 7.6 %all-to-all-start = ((bf16[16,9,4,1536]{3,2,1,0:T(4,128)(2,1)}), bf16[16,9,4,1536]{3,2,1,0:T(4,128)(2,1)S(1)}, u32[]{:S(2)}, u32[]{:S(2)}) async-start(bf16[16,9,4,1536]{3,2,1,0:T(4,128)(2,1)} %copy.94), calls=%async_computation | async-start | bytes 3538944 | tf_op jit(solution)/shard_map/all_to_all | solution.py:92
  15.5 0.3 reshape.278
  15.9 0.3 reshape.279
  16.2 2.4 %reshape.280 = bf16[144,12,128]{2,1,0:T(8,128)(2,1)} reshape(bf16[1,1,144,1536]{3,2,1,0:T(8,128)(2,1)} %param.9) | data formatting | bytes 884736 | tf_op jit(solution)/shard_map/reshape.7
  18.6 1.3 %reshape.283 = bf16[144,12,128]{2,1,0:T(8,128)(2,1)S(1)} reshape(bf16[1,1,144,1536]{3,2,1,0:T(8,128)(2,1)} %param.10) | data formatting | bytes 884736 | tf_op jit(solution)/shard_map/reshape.22
  19.9 0.9 convolution_bitcast_fusion.2
  20.8 1.7 %copy.98 = f32[12,16,16]{1,2,0:T(8,128)} copy(f32[12,16,16]{0,2,1:T(8,128)} %convolution_bitcast_fusion.2) | data formatting | bytes 24576 | tf_op jit(solution)/shard_map/dot_general | solution.py:77
  23.2 0.5 iota_compare_fusion.2
  23.7 1.4 %broadcast_compare_fusion = pred[16,16]{0,1:T(8,128)(4,1)} fusion(s32[16]{0:T(128)} %bitcast.131), kind=kLoop, calls=%fused_computation.83 | loop fusion | flops 256 | bytes 320 | tf_op jit(solution)/shard_map/eq | solution.py:80
  25.1 3.3 %fusion.66 = (f32[12,144]{1,0:T(8,128)}, f32[12,144,144]{1,2,0:T(8,128)}) fusion(pred[144]{0:T(512)(128)(4,1)} %iota_compare_fusion.2, bf16[144,12,128]{2,1,0:T(8,128)(2,1)S(1)} %reshape.279, bf16[144,12,128]{2,1,0:T(8,128)(2,1)S(1)} %reshape.278), kind=kOutput, calls=%fused_computation.90 | convolution fusion | flops 64696464 | bytes 1887120 | tf_op jit(solution)/shard_map/sub | solution.py:28
  28.4 2.8 %convolution_bitcast_fusion = f32[1,1,12,18,8,128]{5,4,3,2,1,0:T(8,128)} fusion(bf16[144,12,128]{2,1,0:T(8,128)(2,1)S(1)} %reshape.283, f32[12,144,144]{1,2,0:T(8,128)} %get-tuple-element.32, f32[12,144]{1,0:T(8,128)} %get-tuple-element.31), kind=kOutput, calls=%fused_computation.27 | convolution fusion | flops 64198656 | bytes 2329344 | tf_op jit(solution)/shard_map/bfhij,bfihe->bfjhe/dot_general | solution.py:39
  31.2 7.6 %all-to-all-done = bf16[16,9,4,1536]{3,2,1,0:T(4,128)(2,1)S(1)} async-done(((bf16[16,9,4,1536]{3,2,1,0:T(4,128)(2,1)}), bf16[16,9,4,1536]{3,2,1,0:T(4,128)(2,1)S(1)}, u32[]{:S(2)}, u32[]{:S(2)}) %all-to-all-start) | async-done | bytes 1769504 | tf_op jit(solution)/shard_map/all_to_all | solution.py:92
  38.7 2.5 %reshape.289 = bf16[16,9,4,12,128]{4,3,2,1,0:T(8,128)(2,1)} reshape(bf16[16,9,4,1536]{3,2,1,0:T(4,128)(2,1)S(1)} %all-to-all-done) | data formatting | bytes 3538944 | tf_op jit(solution)/shard_map/reshape | solution.py:93
  41.3 3.7 %copy.176 = bf16[16,9,4,12,128]{4,0,3,1,2:T(8,128)(2,1)S(1)} copy(bf16[16,9,4,12,128]{4,3,2,1,0:T(8,128)(2,1)} %reshape.289) | data formatting | bytes 3538944 | tf_op jit(solution)/shard_map/reshape | solution.py:93
  45.0 1.3 %fusion.64 = f32[9,12,16,16]{2,3,1,0:T(8,128)} fusion(bf16[4,9,12,16,128]{4,3,2,1,0:T(8,128)(2,1)S(1)} %bitcast.124), kind=kOutput, calls=%fused_computation.88 | convolution fusion | flops 7077888 | bytes 995328 | tf_op jit(solution)/shard_map/phie,phje->phij/dot_general | solution.py:106
  46.3 0.6 fusion.6
  46.9 1.8 %fusion.71 = (f32[12,16,16]{1,2,0:T(8,128)S(1)}, bf16[9,12,16,16]{2,3,1,0:T(8,128)(2,1)S(1)}) fusion(f32[9,12,16,16]{2,3,1,0:T(8,128)S(1)} %fusion.6, f32[9,12,16,16]{2,3,1,0:T(8,128)} %fusion.64), kind=kOutput, calls=%fused_computation.91 | output fusion | flops 136911 | bytes 288768 | tf_op jit(solution)/shard_map/sub | solution.py:110
  48.8 0.2 convolution_bitcast_fusion.3
  49.0 0.7 collective-permute-start
  49.7 3.5 %collective-permute-start.1 = (f32[12,16]{1,0:T(8,128)S(1)}, f32[12,16]{1,0:T(8,128)S(1)}, u32[]{:S(2)}, u32[]{:S(2)}) collective-permute-start(f32[12,16]{1,0:T(8,128)S(1)} %convolution_bitcast_fusion.3), channel_id=1, source_target_pairs={{0,2},{1,3},{2,0},{3,1},{4,6},{5,7},{6,4},{7,5},{8,10},{9,11},{10,... | collective-permute-start | bytes 2312 | tf_op jit(solution)/shard_map/ppermute | solution.py:60
  53.1 0.5 collective-permute-start.2
  53.6 1.3 %slice_bitcast_fusion.1 = (bf16[9,12,16,128]{3,2,1,0:T(8,128)(2,1)S(1)}, bf16[9,12,16,128]{3,2,1,0:T(8,128)(2,1)S(1)}, bf16[9,12,16,128]{3,2,1,0:T(8,128)(2,1)}, bf16[9,12,16,128]{3,2,1,0:T(8,128)(2,1)}) fusion(bf16[4,9,12,16,128]{4,3,2,1,0:T(8,128)(2,1)S(1)} %bitcast.126), kind=kLoop, calls=%fused_computation.54 | loop fusion | bytes 3538944 | tf_op jit(solution)/shard_map/squeeze | solution.py:95
  54.9 1.9 %collective-permute-done.2 = f32[12,16]{1,0:T(8,128)S(1)} collective-permute-done((f32[12,16]{1,0:T(8,128)S(1)}, f32[12,16]{1,0:T(8,128)S(1)}, u32[]{:S(2)}, u32[]{:S(2)}) %collective-permute-start.2) | collective-permute-done | bytes 800 | tf_op jit(solution)/shard_map/ppermute | solution.py:60
  56.8 0.2 collective-permute-start.3
  57.0 2.6 %collective-permute-start.4 = (f32[12,16]{1,0:T(8,128)S(1)}, f32[12,16]{1,0:T(8,128)S(1)}, u32[]{:S(2)}, u32[]{:S(2)}) collective-permute-start(f32[12,16]{1,0:T(8,128)S(1)} %add_add_fusion.2), channel_id=1, source_target_pairs={{0,8},{1,9},{2,10},{3,11},{4,12},{5,13},{6,14},{7,15},{8,0},{9,1},... | collective-permute-start | bytes 2312 | tf_op jit(solution)/shard_map/ppermute | solution.py:60
  59.6 1.9 %collective-permute-start.5 = (f32[12,16]{1,0:T(8,128)S(1)}, f32[12,16]{1,0:T(8,128)S(1)}, u32[]{:S(2)}, u32[]{:S(2)}) collective-permute-start(f32[12,16]{1,0:T(8,128)S(1)} %add_add_fusion.2), channel_id=1, source_target_pairs={{0,12},{1,13},{2,14},{3,15},{4,8},{5,9},{6,10},{7,11},{8,4},{9,5},... | collective-permute-start | bytes 2312 | tf_op jit(solution)/shard_map/ppermute | solution.py:60
  61.5 0.3 fusion.18
  61.8 0.1 copy.101
  62.0 0.3 stack_reshape.28
  62.3 0.3 fusion.17
  62.6 0.1 copy.103
  62.8 0.3 stack_reshape.29
  63.1 1.4 %fusion.16 = bf16[16,9,12,128]{3,0,2,1:T(8,128)(2,1)S(1)} fusion(bf16[9,12,16,128]{3,2,1,0:T(8,128)(2,1)} %get-tuple-element.19, bf16[9,12,16,16]{2,3,1,0:T(8,128)(2,1)S(1)} %get-tuple-element.17), kind=kOutput, calls=%fused_computation.33 | convolution fusion | flops 7520256 | bytes 940032 | tf_op jit(solution)/shard_map/phij,phie->phje/dot_general | solution.py:136
  64.6 1.1 %stack_reshape.30 = bf16[16,9,1,1536]{3,0,1,2:T(8,128)(2,1)} reshape(bf16[16,9,12,128]{3,2,0,1:T(8,128)(2,1)S(1)} %copy.104) | data formatting | bytes 884736 | tf_op jit(solution)/shard_map/stack;reshape | solution.py:140
  65.7 0.4 fusion.19
  66.0 0.1 copy.105
  66.2 0.3 stack_reshape.31
  66.5 0.2 copy-done.9
  66.7 0.2 pad_maximum_fusion.1
  66.9 2.6 %copy.106 = bf16[16,9,4,1536]{3,2,1,0:T(4,128)(2,1)} copy(bf16[16,9,4,1536]{3,0,1,2:T(8,128)(2,1)S(1)} %pad_maximum_fusion.1) | data formatting | bytes 3538944 | tf_op jit(solution)/shard_map/optimization_barrier | solution.py:147
  69.6 8.0 %all-to-all-start.1 = ((bf16[16,9,4,1536]{3,2,1,0:T(4,128)(2,1)}), bf16[16,9,4,1536]{3,2,1,0:T(4,128)(2,1)S(1)}, u32[]{:S(2)}, u32[]{:S(2)}) async-start(bf16[16,9,4,1536]{3,2,1,0:T(4,128)(2,1)} %copy.106), calls=%async_computation.1 | async-start | bytes 3538944 | tf_op jit(solution)/shard_map/all_to_all | solution.py:150
  77.6 2.7 %convolution_bitcast_fusion.1 = f32[1,1,12,18,8,128]{5,4,3,2,1,0:T(8,128)} fusion(bf16[144,12,128]{2,1,0:T(8,128)(2,1)} %reshape.280, f32[12,144,144]{1,2,0:T(8,128)S(1)} %copy-done.5, f32[12,144]{1,0:T(8,128)} %get-tuple-element.31), kind=kOutput, calls=%fused_computation.28 | convolution fusion | flops 64198656 | bytes 2329344 | tf_op jit(solution)/shard_map/bfhij,bfjhe->bfihe/dot_general | solution.py:31
  80.3 0.5 multiply_reduce_fusion
  80.8 0.4 multiply_convert_fusion
  81.3 2.0 %collective-permute-start.7 = (f32[12,16]{1,0:T(8,128)S(1)}, f32[12,16]{1,0:T(8,128)S(1)}, u32[]{:S(2)}, u32[]{:S(2)}) collective-permute-start(f32[12,16]{1,0:T(8,128)S(1)} %add_add_fusion.1), channel_id=1, source_target_pairs={{0,32},{16,48},{32,0},{48,16},{64,96},{80,112},{96,64},{112,80},{1... | collective-permute-start | bytes 2312 | tf_op jit(solution)/shard_map/ppermute | solution.py:60
  83.3 0.4 fusion.8
  83.7 1.3 %collective-permute-done.7 = f32[12,16]{1,0:T(8,128)S(1)} collective-permute-done((f32[12,16]{1,0:T(8,128)S(1)}, f32[12,16]{1,0:T(8,128)S(1)}, u32[]{:S(2)}, u32[]{:S(2)}) %collective-permute-start.7) | collective-permute-done | bytes 800 | tf_op jit(solution)/shard_map/ppermute | solution.py:60
  85.1 1.3 %collective-permute-done.8 = f32[12,16]{1,0:T(8,128)S(1)} collective-permute-done((f32[12,16]{1,0:T(8,128)S(1)}, f32[12,16]{1,0:T(8,128)S(1)}, u32[]{:S(2)}, u32[]{:S(2)}) %collective-permute-start.8) | collective-permute-done | bytes 800 | tf_op jit(solution)/shard_map/ppermute | solution.py:60
  86.4 6.4 %collective-permute-start.10 = (f32[12,16]{1,0:T(8,128)S(1)}, f32[12,16]{1,0:T(8,128)S(1)}, u32[]{:S(2)}, u32[]{:S(2)}) collective-permute-start(f32[12,16]{1,0:T(8,128)S(1)} %add_add_fusion), channel_id=1, source_target_pairs={{0,128},{16,144},{32,160},{48,176},{64,192},{80,208},{96,224},{112... | collective-permute-start | bytes 2312 | tf_op jit(solution)/shard_map/ppermute | solution.py:60
  92.8 0.5 collective-permute-start.11
  93.2 1.0 collective-permute-start.9
  94.2 0.6 fusion.7
  94.8 3.7 %collective-permute-done.11 = f32[12,16]{1,0:T(8,128)S(1)} collective-permute-done((f32[12,16]{1,0:T(8,128)S(1)}, f32[12,16]{1,0:T(8,128)S(1)}, u32[]{:S(2)}, u32[]{:S(2)}) %collective-permute-start.11) | collective-permute-done | bytes 800 | tf_op jit(solution)/shard_map/ppermute | solution.py:60
  98.5 0.6 add_multiply_fusion
  99.1 0.5 convert_bitcast_fusion
  99.6 2.6 %fusion.65 = (f32[1,16,9,1536]{3,0,2,1:T(1,128)S(1)}, f32[1,16,9,1536]{3,0,2,1:T(1,128)S(1)}, f32[1,16,9,1536]{3,0,2,1:T(1,128)S(1)}, f32[1,16,9,1536]{3,0,2,1:T(1,128)S(1)}) fusion(f32[4,16,9,1536]{3,0,2,1:T(4,128)S(1)} %convert_bitcast_fusion), kind=kLoop, calls=%fused_computation.89 | loop fusion | bytes 7077888 | tf_op jit(solution)/shard_map/slice | solution.py:166
  102.3 1.2 %fusion.20 = (bf16[1,1,144,1536]{3,2,1,0:T(8,128)(2,1)}, bf16[1,1,144,1536]{3,2,1,0:T(8,128)(2,1)}) fusion(f32[1,1,12,18,8,128]{5,4,3,2,1,0:T(8,128)S(1)} %copy-done.11, f32[1,1,144,1536]{3,0,2,1:T(1,128)S(1)} %bitcast.129, f32[1,1,144,1536]{3,0,2,1:T(1,128)S(1)} %bitcast.130, f32[1,1,12,18,8,128]{5,4,3,2,1,0:T(8,128)S(1)} %fusion.8), kind=kLoop, calls=%fused_computation.40 | loop fusion | flops 884736 | bytes 4423680 | tf_op jit(solution)/shard_map/convert_element_type | solution.py:166
  103.5 1.1 %fusion.22 = (bf16[1,1,144,1536]{3,2,1,0:T(8,128)(2,1)}, bf16[1,1,144,1536]{3,2,1,0:T(8,128)(2,1)}) fusion(f32[1,1,12,18,8,128]{5,4,3,2,1,0:T(8,128)S(1)} %fusion.7, f32[1,1,144,1536]{3,0,2,1:T(1,128)S(1)} %bitcast.127, f32[1,1,144,1536]{3,0,2,1:T(1,128)S(1)} %bitcast.128, f32[1,1,12,18,8,128]{5,4,3,2,1,0:T(8,128)S(1)} %copy-done.12), kind=kLoop, calls=%fused_computation.44 | loop fusion | flops 884736 | bytes 4423680 | tf_op jit(solution)/shard_map/convert_element_type | solution.py:164
  (54 shorter events, 0.5 us)
Async XLA Ops:
  0.6 19.3 %copy-start = (f32[12,16]{1,0:T(8,128)S(1)}, f32[12,16]{1,0:T(8,128)}, u32[]{:S(2)}) copy-start(f32[12,16]{1,0:T(8,128)} %param.13) | copy-start | bytes 2308
  0.6 2.5 %copy-start.8 = (bf16[1,1,144,1536]{3,2,1,0:T(8,128)(2,1)S(1)}, bf16[1,1,144,1536]{3,2,1,0:T(8,128)(2,1)}, u32[]{:S(2)}) copy-start(bf16[1,1,144,1536]{3,2,1,0:T(8,128)(2,1)} %param.9) | copy-start | bytes 1327108
  7.9 7.6 %copy-start.6 = (bf16[1,1,144,1536]{3,2,1,0:T(8,128)(2,1)S(1)}, bf16[1,1,144,1536]{3,2,1,0:T(8,128)(2,1)}, u32[]{:S(2)}) copy-start(bf16[1,1,144,1536]{3,2,1,0:T(8,128)(2,1)} %param.7) | copy-start | bytes 1327108
  7.9 7.9 %copy-start.7 = (bf16[1,1,144,1536]{3,2,1,0:T(8,128)(2,1)S(1)}, bf16[1,1,144,1536]{3,2,1,0:T(8,128)(2,1)}, u32[]{:S(2)}) copy-start(bf16[1,1,144,1536]{3,2,1,0:T(8,128)(2,1)} %param.8) | copy-start | bytes 1327108
  7.9 30.8 %all-to-all-start = ((bf16[16,9,4,1536]{3,2,1,0:T(4,128)(2,1)}), bf16[16,9,4,1536]{3,2,1,0:T(4,128)(2,1)S(1)}, u32[]{:S(2)}, u32[]{:S(2)}) async-start(bf16[16,9,4,1536]{3,2,1,0:T(4,128)(2,1)} %copy.94), calls=%async_computation | async-start | bytes 3538944 | tf_op jit(solution)/shard_map/all_to_all | solution.py:92
  15.9 12.5 %copy-start.3 = (bf16[144,12,128]{2,1,0:T(8,128)(2,1)}, bf16[144,12,128]{2,1,0:T(8,128)(2,1)S(1)}, u32[]{:S(2)}) copy-start(bf16[144,12,128]{2,1,0:T(8,128)(2,1)S(1)} %reshape.278) | copy-start | bytes 1327108
  16.2 12.2 %copy-start.1 = (bf16[144,12,128]{2,1,0:T(8,128)(2,1)}, bf16[144,12,128]{2,1,0:T(8,128)(2,1)S(1)}, u32[]{:S(2)}) copy-start(bf16[144,12,128]{2,1,0:T(8,128)(2,1)S(1)} %reshape.279) | copy-start | bytes 1327108
  19.9 8.5 %copy-start.14 = (bf16[144,12,128]{2,1,0:T(8,128)(2,1)}, bf16[144,12,128]{2,1,0:T(8,128)(2,1)S(1)}, u32[]{:S(2)}) copy-start(bf16[144,12,128]{2,1,0:T(8,128)(2,1)S(1)} %reshape.283) | copy-start | bytes 1327108
  45.0 1.3 %copy-start.16 = (f32[12,16,16]{1,2,0:T(8,128)S(1)}, f32[12,16,16]{1,2,0:T(8,128)}, u32[]{:S(2)}) copy-start(f32[12,16,16]{1,2,0:T(8,128)} %copy.98) | copy-start | bytes 36868
  45.0 1.3 %copy-start.18 = (pred[16,16]{0,1:T(8,128)(4,1)S(1)}, pred[16,16]{0,1:T(8,128)(4,1)}, u32[]{:S(2)}) copy-start(pred[16,16]{0,1:T(8,128)(4,1)} %broadcast_compare_fusion) | copy-start | bytes 772
  49.0 5.9 %collective-permute-start = (f32[12,16]{1,0:T(8,128)S(1)}, f32[12,16]{1,0:T(8,128)S(1)}, u32[]{:S(2)}, u32[]{:S(2)}) collective-permute-start(f32[12,16]{1,0:T(8,128)S(1)} %convolution_bitcast_fusion.3), channel_id=1, source_target_pairs={{0,1},{1,0},{2,3},{3,2},{4,5},{5,4},{6,7},{7,6},{8,9},{9,8},{10,11... | collective-permute-start | bytes 2312 | tf_op jit(solution)/shard_map/ppermute | solution.py:60
  49.7 5.2 %collective-permute-start.1 = (f32[12,16]{1,0:T(8,128)S(1)}, f32[12,16]{1,0:T(8,128)S(1)}, u32[]{:S(2)}, u32[]{:S(2)}) collective-permute-start(f32[12,16]{1,0:T(8,128)S(1)} %convolution_bitcast_fusion.3), channel_id=1, source_target_pairs={{0,2},{1,3},{2,0},{3,1},{4,6},{5,7},{6,4},{7,5},{8,10},{9,11},{10,... | collective-permute-start | bytes 2312 | tf_op jit(solution)/shard_map/ppermute | solution.py:60
  53.1 3.7 %collective-permute-start.2 = (f32[12,16]{1,0:T(8,128)S(1)}, f32[12,16]{1,0:T(8,128)S(1)}, u32[]{:S(2)}, u32[]{:S(2)}) collective-permute-start(f32[12,16]{1,0:T(8,128)S(1)} %convolution_bitcast_fusion.3), channel_id=1, source_target_pairs={{0,3},{1,2},{2,1},{3,0},{4,7},{5,6},{6,5},{7,4},{8,11},{9,10},{10,... | collective-permute-start | bytes 2312 | tf_op jit(solution)/shard_map/ppermute | solution.py:60
  56.8 5.5 %copy-start.10 = (bf16[9,12,16,128]{3,2,1,0:T(8,128)(2,1)S(1)}, bf16[9,12,16,128]{3,2,1,0:T(8,128)(2,1)}, u32[]{:S(2)}) copy-start(bf16[9,12,16,128]{3,2,1,0:T(8,128)(2,1)} %get-tuple-element.18) | copy-start | bytes 1327108
  56.8 10.1 %collective-permute-start.3 = (f32[12,16]{1,0:T(8,128)S(1)}, f32[12,16]{1,0:T(8,128)S(1)}, u32[]{:S(2)}, u32[]{:S(2)}) collective-permute-start(f32[12,16]{1,0:T(8,128)S(1)} %add_add_fusion.2), channel_id=1, source_target_pairs={{0,4},{1,5},{2,6},{3,7},{4,0},{5,1},{6,2},{7,3},{8,12},{9,13},{10,... | collective-permute-start | bytes 2312 | tf_op jit(solution)/shard_map/ppermute | solution.py:60
  57.0 9.9 %collective-permute-start.4 = (f32[12,16]{1,0:T(8,128)S(1)}, f32[12,16]{1,0:T(8,128)S(1)}, u32[]{:S(2)}, u32[]{:S(2)}) collective-permute-start(f32[12,16]{1,0:T(8,128)S(1)} %add_add_fusion.2), channel_id=1, source_target_pairs={{0,8},{1,9},{2,10},{3,11},{4,12},{5,13},{6,14},{7,15},{8,0},{9,1},... | collective-permute-start | bytes 2312 | tf_op jit(solution)/shard_map/ppermute | solution.py:60
  59.6 7.3 %collective-permute-start.5 = (f32[12,16]{1,0:T(8,128)S(1)}, f32[12,16]{1,0:T(8,128)S(1)}, u32[]{:S(2)}, u32[]{:S(2)}) collective-permute-start(f32[12,16]{1,0:T(8,128)S(1)} %add_add_fusion.2), channel_id=1, source_target_pairs={{0,12},{1,13},{2,14},{3,15},{4,8},{5,9},{6,10},{7,11},{8,4},{9,5},... | collective-permute-start | bytes 2312 | tf_op jit(solution)/shard_map/ppermute | solution.py:60
  65.7 1.0 copy-start.9
  69.6 8.0 %copy-start.5 = (f32[12,144,144]{1,2,0:T(8,128)S(1)}, f32[12,144,144]{1,2,0:T(8,128)}, u32[]{:S(2)}) copy-start(f32[12,144,144]{1,2,0:T(8,128)} %get-tuple-element.32) | copy-start | bytes 2985988
  69.6 29.6 %all-to-all-start.1 = ((bf16[16,9,4,1536]{3,2,1,0:T(4,128)(2,1)}), bf16[16,9,4,1536]{3,2,1,0:T(4,128)(2,1)S(1)}, u32[]{:S(2)}, u32[]{:S(2)}) async-start(bf16[16,9,4,1536]{3,2,1,0:T(4,128)(2,1)} %copy.106), calls=%async_computation.1 | async-start | bytes 3538944 | tf_op jit(solution)/shard_map/all_to_all | solution.py:150
  77.6 2.7 %copy-start.13 = (bf16[144,12,128]{2,1,0:T(8,128)(2,1)S(1)}, bf16[144,12,128]{2,1,0:T(8,128)(2,1)}, u32[]{:S(2)}) copy-start(bf16[144,12,128]{2,1,0:T(8,128)(2,1)} %reshape.280) | copy-start | bytes 1327108
  77.6 2.7 %copy-start.15 = (bf16[144,12,128]{2,1,0:T(8,128)(2,1)S(1)}, bf16[144,12,128]{2,1,0:T(8,128)(2,1)}, u32[]{:S(2)}) copy-start(bf16[144,12,128]{2,1,0:T(8,128)(2,1)} %copy-done.14) | copy-start | bytes 1327108
  77.6 2.7 %copy-start.17 = (f32[12,144]{1,0:T(8,128)S(1)}, f32[12,144]{1,0:T(8,128)}, u32[]{:S(2)}) copy-start(f32[12,144]{1,0:T(8,128)} %get-tuple-element.31) | copy-start | bytes 20740
  80.8 2.5 %copy-start.4 = (bf16[144,12,128]{2,1,0:T(8,128)(2,1)S(1)}, bf16[144,12,128]{2,1,0:T(8,128)(2,1)}, u32[]{:S(2)}) copy-start(bf16[144,12,128]{2,1,0:T(8,128)(2,1)} %copy-done.3) | copy-start | bytes 1327108
  81.2 13.0 %copy-start.2 = (bf16[144,12,128]{2,1,0:T(8,128)(2,1)S(1)}, bf16[144,12,128]{2,1,0:T(8,128)(2,1)}, u32[]{:S(2)}) copy-start(bf16[144,12,128]{2,1,0:T(8,128)(2,1)} %copy-done.1) | copy-start | bytes 1327108
  81.2 2.5 %collective-permute-start.6 = (f32[12,16]{1,0:T(8,128)S(1)}, f32[12,16]{1,0:T(8,128)S(1)}, u32[]{:S(2)}, u32[]{:S(2)}) collective-permute-start(f32[12,16]{1,0:T(8,128)S(1)} %add_add_fusion.1), channel_id=1, source_target_pairs={{0,16},{16,0},{32,48},{48,32},{64,80},{80,64},{96,112},{112,96},{1... | collective-permute-start | bytes 2312 | tf_op jit(solution)/shard_map/ppermute | solution.py:60
  81.3 3.7 %collective-permute-start.7 = (f32[12,16]{1,0:T(8,128)S(1)}, f32[12,16]{1,0:T(8,128)S(1)}, u32[]{:S(2)}, u32[]{:S(2)}) collective-permute-start(f32[12,16]{1,0:T(8,128)S(1)} %add_add_fusion.1), channel_id=1, source_target_pairs={{0,32},{16,48},{32,0},{48,16},{64,96},{80,112},{96,64},{112,80},{1... | collective-permute-start | bytes 2312 | tf_op jit(solution)/shard_map/ppermute | solution.py:60
  83.3 3.1 %collective-permute-start.8 = (f32[12,16]{1,0:T(8,128)S(1)}, f32[12,16]{1,0:T(8,128)S(1)}, u32[]{:S(2)}, u32[]{:S(2)}) collective-permute-start(f32[12,16]{1,0:T(8,128)S(1)} %add_add_fusion.1), channel_id=1, source_target_pairs={{0,48},{16,32},{32,16},{48,0},{64,112},{80,96},{96,80},{112,64},{1... | collective-permute-start | bytes 2312 | tf_op jit(solution)/shard_map/ppermute | solution.py:60
  86.4 8.4 %collective-permute-start.10 = (f32[12,16]{1,0:T(8,128)S(1)}, f32[12,16]{1,0:T(8,128)S(1)}, u32[]{:S(2)}, u32[]{:S(2)}) collective-permute-start(f32[12,16]{1,0:T(8,128)S(1)} %add_add_fusion), channel_id=1, source_target_pairs={{0,128},{16,144},{32,160},{48,176},{64,192},{80,208},{96,224},{112... | collective-permute-start | bytes 2312 | tf_op jit(solution)/shard_map/ppermute | solution.py:60
  92.8 5.8 %collective-permute-start.11 = (f32[12,16]{1,0:T(8,128)S(1)}, f32[12,16]{1,0:T(8,128)S(1)}, u32[]{:S(2)}, u32[]{:S(2)}) collective-permute-start(f32[12,16]{1,0:T(8,128)S(1)} %add_add_fusion), channel_id=1, source_target_pairs={{0,192},{16,208},{32,224},{48,240},{64,128},{80,144},{96,160},{112... | collective-permute-start | bytes 2312 | tf_op jit(solution)/shard_map/ppermute | solution.py:60
  93.2 5.3 %collective-permute-start.9 = (f32[12,16]{1,0:T(8,128)S(1)}, f32[12,16]{1,0:T(8,128)S(1)}, u32[]{:S(2)}, u32[]{:S(2)}) collective-permute-start(f32[12,16]{1,0:T(8,128)S(1)} %add_add_fusion), channel_id=1, source_target_pairs={{0,64},{16,80},{32,96},{48,112},{64,0},{80,16},{96,32},{112,48},{1... | collective-permute-start | bytes 2312 | tf_op jit(solution)/shard_map/ppermute | solution.py:60
  99.6 2.7 %copy-start.11 = (f32[1,1,12,18,8,128]{5,4,3,2,1,0:T(8,128)S(1)}, f32[1,1,12,18,8,128]{5,4,3,2,1,0:T(8,128)}, u32[]{:S(2)}) copy-start(f32[1,1,12,18,8,128]{5,4,3,2,1,0:T(8,128)} %convolution_bitcast_fusion) | copy-start | bytes 2654212
  102.3 1.2 %copy-start.12 = (f32[1,1,12,18,8,128]{5,4,3,2,1,0:T(8,128)S(1)}, f32[1,1,12,18,8,128]{5,4,3,2,1,0:T(8,128)}, u32[]{:S(2)}) copy-start(f32[1,1,12,18,8,128]{5,4,3,2,1,0:T(8,128)} %convolution_bitcast_fusion.1) | copy-start | bytes 2654212

commit v4 on v3

--- a/solution.py
+++ b/solution.py
@@ -115,11 +115,6 @@
         precision=lax.Precision.HIGHEST,
     )
     partial = quad_step(bias_part, "seq", seq_size, 1)
-    partial, shares, score_grad, query_part, key_part, value_part, slope_part = (
-        lax.optimization_barrier(
-            (partial, shares, score_grad, query_part, key_part, value_part, slope_part)
-        )
-    )
     shares_half = shares.astype(jnp.bfloat16)
     score_half = score_grad.astype(jnp.bfloat16)
     result = jnp.einsum(

time: 106 us -> 108 us (1.019)
  waiting for transfers between devices: 15.8 us -> 24.3 us
  local copies, waits for them, and re-layouts: 28.3 us -> 22.9 us
  matrix products: 15.6 us -> 14.5 us
    all_to_all x1, waiting for transfers between devices: 7.55 us -> 15.2 us  [on_device(): lax.all_to_all(stacked, 'seq', split_axis=0, concat_axis=0, tiled=True)]
    sub x1, matrix products: 3.27 us -> 0.77 us  [attend_forward(): weights = jnp.exp(scores - row_peak)]
    dot_general x1, matrix products: 0.32 us -> 2.25 us  [on_device(): jnp.einsum(TIME_PATTERNS[1], shares_half, value_part, preferred_element_t...]
    dot_general x1, matrix products: 0.35 us -> 2.19 us  [on_device(): jnp.einsum(TIME_PATTERNS[2], shares_half, slope_part, preferred_element_t...]
    sub x1, other arithmetic: 1.78 us -> 3.45 us  [on_device(): weights = jnp.exp(scores - row_peak)]
    dot_general x1, local copies, waits for them, and re-layouts: 1.72 us -> 0.19 us  [on_device(): jnp.tensordot(time_bias, onehot, axes=1, precision=lax.Precision.HIGHEST)]
    another operation x4, local copies, waits for them, and re-layouts: 4.31 us -> 2.88 us
    eq x1, other arithmetic: 1.38 us -> 0.07 us  [on_device(): same_clip = (clip_ids[:, :, None] == clip_ids[:, None, :])[:, None, None]]
  transfers between devices with their start and end apart: 14 -> 14, of which waited for: 5 -> 6; matrix products, arithmetic and copies ran while one was open for 25% -> 16% of each run, Pallas kernels for 0% -> 0%
where the time goes in v4:
time: 108 us; the launch traced here: 106 us
  starting transfers between devices  34.6 us (32%)
  waiting for transfers between devices  24.3 us (22%)
  local copies, waits for them, and re-layouts  22.9 us (21%)
  matrix products  14.5 us (13%)
  other arithmetic  8.4 us (8%)
  between operations  1.76 us (2%)
    ppermute x12, starting transfers between devices, quad_step(): lax.ppermute(value, axis, [(index, index ^ part * step) for index in rang...  19.3 us
    all_to_all x1, waiting for transfers between devices, on_device(): lax.all_to_all(stacked, 'seq', split_axis=0, concat_axis=0, tiled=True)  15.2 us
    ppermute x12, waiting for transfers between devices, quad_step(): lax.ppermute(value, axis, [(index, index ^ part * step) for index in rang...  9.09 us
    all_to_all x1, starting transfers between devices, on_device(): lax.all_to_all(back_rows, 'seq', split_axis=0, concat_axis=0, tiled=True)  7.76 us
    all_to_all x1, starting transfers between devices, on_device(): lax.all_to_all(stacked, 'seq', split_axis=0, concat_axis=0, tiled=True)  7.58 us
    another operation x5, local copies, waits for them, and re-layouts, on_device(): jnp.stack([tensor.reshape(seq_size, block, width) for tensor in (queries,...  6.61 us
    reshape x2, local copies, waits for them, and re-layouts, on_device(): rows = rows.reshape(seq_size, block, 4, head_count, width // head_count)  5.45 us
    sub x1, other arithmetic, on_device(): weights = jnp.exp(scores - row_peak)  3.45 us
  transfers between devices with their start and end apart: 14, of which 6 were waited for; matrix products, arithmetic and copies ran while one was open for 16% of the time, Pallas kernels for 0%

profile of v4, /device:TPU:4, one launch (start us, length us, event | category | flops | bytes accessed | tf_op | source)
XLA Modules:
  0.0 106.4 jit_solution(8878322446507777715)
XLA Ops:
  0.7 1.2 %stack_reshape.24 = bf16[16,9,1,1536]{3,1,0,2:T(8,128)(2,1)S(1)} reshape(bf16[1,1,144,1536]{3,2,1,0:T(8,128)(2,1)} %param.7) | data formatting | bytes 884736 | tf_op jit(solution)/shard_map/stack;reshape | solution.py:85
  1.9 1.2 %stack_reshape.25 = bf16[16,9,1,1536]{3,1,0,2:T(8,128)(2,1)S(1)} reshape(bf16[1,1,144,1536]{3,2,1,0:T(8,128)(2,1)} %param.8) | data formatting | bytes 884736 | tf_op jit(solution)/shard_map/stack;reshape | solution.py:85
  3.1 0.2 stack_reshape.26
  3.3 1.2 %stack_reshape.27 = bf16[16,9,1,1536]{3,1,0,2:T(8,128)(2,1)S(1)} reshape(bf16[1,1,144,1536]{3,2,1,0:T(8,128)(2,1)} %param.10) | data formatting | bytes 884736 | tf_op jit(solution)/shard_map/stack;reshape | solution.py:85
  4.5 0.6 pad_maximum_fusion
  5.1 2.8 %copy.94 = bf16[16,9,4,1536]{3,2,1,0:T(4,128)(2,1)} copy(bf16[16,9,4,1536]{3,1,0,2:T(8,128)(2,1)S(1)} %pad_maximum_fusion) | data formatting | bytes 3538944 | tf_op jit(solution)/shard_map/stack | solution.py:85
  7.9 7.6 %all-to-all-start = ((bf16[16,9,4,1536]{3,2,1,0:T(4,128)(2,1)}), bf16[16,9,4,1536]{3,2,1,0:T(4,128)(2,1)}, u32[]{:S(2)}, u32[]{:S(2)}) async-start(bf16[16,9,4,1536]{3,2,1,0:T(4,128)(2,1)} %copy.94), calls=%async_computation | async-start | bytes 3538944 | tf_op jit(solution)/shard_map/all_to_all | solution.py:92
  15.5 0.3 reshape.278
  15.9 0.3 reshape.279
  16.2 0.3 copy-done.9
  16.5 1.1 %reshape.280 = bf16[144,12,128]{2,1,0:T(8,128)(2,1)} reshape(bf16[1,1,144,1536]{3,2,1,0:T(8,128)(2,1)S(1)} %copy-done.9) | data formatting | bytes 884736 | tf_op jit(solution)/shard_map/reshape.7
  17.7 1.1 %reshape.283 = bf16[144,12,128]{2,1,0:T(8,128)(2,1)} reshape(bf16[1,1,144,1536]{3,2,1,0:T(8,128)(2,1)S(1)} %copy-done.10) | data formatting | bytes 884736 | tf_op jit(solution)/shard_map/reshape.22
  18.8 0.3 convolution_bitcast_fusion.2
  19.1 0.2 copy.98
  20.0 0.8 fusion.59
  20.8 2.8 %convolution_bitcast_fusion = f32[1,1,12,18,8,128]{5,4,3,2,1,0:T(8,128)} fusion(bf16[144,12,128]{2,1,0:T(8,128)(2,1)} %reshape.283, f32[12,144,144]{1,2,0:T(8,128)S(1)} %get-tuple-element.16, f32[12,144]{1,0:T(8,128)S(1)} %get-tuple-element.15), kind=kOutput, calls=%fused_computation.22 | convolution fusion | flops 64198656 | bytes 2329344 | tf_op jit(solution)/shard_map/bfhij,bfihe->bfjhe/dot_general | solution.py:39
  23.6 15.2 %all-to-all-done = bf16[16,9,4,1536]{3,2,1,0:T(4,128)(2,1)} async-done(((bf16[16,9,4,1536]{3,2,1,0:T(4,128)(2,1)}), bf16[16,9,4,1536]{3,2,1,0:T(4,128)(2,1)}, u32[]{:S(2)}, u32[]{:S(2)}) %all-to-all-start) | async-done | bytes 1769504 | tf_op jit(solution)/shard_map/all_to_all | solution.py:92
  38.8 3.4 %reshape.289 = bf16[16,9,4,12,128]{4,3,2,1,0:T(8,128)(2,1)S(1)} reshape(bf16[16,9,4,1536]{3,2,1,0:T(4,128)(2,1)} %all-to-all-done) | data formatting | bytes 3538944 | tf_op jit(solution)/shard_map/reshape | solution.py:93
  42.2 2.1 %copy.176 = bf16[16,9,4,12,128]{4,0,3,1,2:T(8,128)(2,1)S(1)} copy(bf16[16,9,4,12,128]{4,3,2,1,0:T(8,128)(2,1)S(1)} %reshape.289) | data formatting | bytes 3538944 | tf_op jit(solution)/shard_map/reshape | solution.py:93
  44.3 0.4 fusion.8
  44.6 3.5 %fusion.64 = (f32[9,12,16]{2,1,0:T(8,128)S(1)}, f32[9,12,16,16]{2,3,1,0:T(8,128)S(1)}) fusion(f32[9,12,16,16]{2,3,1,0:T(8,128)S(1)} %fusion.8), kind=kOutput, calls=%fused_computation.86 | output fusion | flops 55311 | bytes 228096 | tf_op jit(solution)/shard_map/sub | solution.py:104
  48.1 0.4 multiply_reduce_fusion.1
  48.5 0.3 fusion.35
  48.8 0.3 fusion.12
  49.1 0.4 fusion.11
  49.5 2.3 %fusion.13 = bf16[16,9,12,128]{3,0,2,1:T(8,128)(2,1)} fusion(bf16[4,9,12,16,128]{4,3,2,1,0:T(8,128)(2,1)} %bitcast.127, f32[9,12,16]{2,1,0:T(8,128)S(1)} %get-tuple-element.17, f32[9,12,16,16]{2,3,1,0:T(8,128)S(1)} %fusion.8), kind=kOutput, calls=%fused_computation.30 | convolution fusion | flops 7383759 | bytes 2727936 | tf_op jit(solution)/shard_map/phij,phje->phie/dot_general | solution.py:120
  51.9 0.2 convolution_bitcast_fusion.3
  52.1 0.7 collective-permute-start
  52.8 3.6 %collective-permute-start.1 = (f32[12,16]{1,0:T(8,128)S(1)}, f32[12,16]{1,0:T(8,128)S(1)}, u32[]{:S(2)}, u32[]{:S(2)}) collective-permute-start(f32[12,16]{1,0:T(8,128)S(1)} %convolution_bitcast_fusion.3), channel_id=1, source_target_pairs={{0,2},{1,3},{2,0},{3,1},{4,6},{5,7},{6,4},{7,5},{8,10},{9,11},{10,... | collective-permute-start | bytes 2312 | tf_op jit(solution)/shard_map/ppermute | solution.py:60
  56.4 0.3 collective-permute-start.2
  56.7 2.2 %fusion.14 = bf16[16,9,12,128]{3,0,2,1:T(8,128)(2,1)} fusion(bf16[4,9,12,16,128]{4,3,2,1,0:T(8,128)(2,1)} %bitcast.128, f32[9,12,16]{2,1,0:T(8,128)S(1)} %get-tuple-element.17, f32[9,12,16,16]{2,3,1,0:T(8,128)S(1)} %fusion.8), kind=kOutput, calls=%fused_computation.31 | convolution fusion | flops 7383759 | bytes 2727936 | tf_op jit(solution)/shard_map/phij,phie->phje/dot_general | solution.py:123
  58.9 0.1 copy.103
  59.0 0.3 stack_reshape.29
  59.3 0.1 copy.104
  59.5 0.3 stack_reshape.30
  59.8 0.2 copy-done.15
  60.0 0.1 copy.101
  60.2 0.3 stack_reshape.28
  60.7 0.3 stack_reshape.31
  61.0 1.1 collective-permute-start.3
  62.1 1.8 %collective-permute-start.4 = (f32[12,16]{1,0:T(8,128)S(1)}, f32[12,16]{1,0:T(8,128)S(1)}, u32[]{:S(2)}, u32[]{:S(2)}) collective-permute-start(f32[12,16]{1,0:T(8,128)S(1)} %add_add_fusion.2), channel_id=1, source_target_pairs={{0,8},{1,9},{2,10},{3,11},{4,12},{5,13},{6,14},{7,15},{8,0},{9,1},... | collective-permute-start | bytes 2312 | tf_op jit(solution)/shard_map/ppermute | solution.py:60
  63.9 1.9 %collective-permute-start.5 = (f32[12,16]{1,0:T(8,128)S(1)}, f32[12,16]{1,0:T(8,128)S(1)}, u32[]{:S(2)}, u32[]{:S(2)}) collective-permute-start(f32[12,16]{1,0:T(8,128)S(1)} %add_add_fusion.2), channel_id=1, source_target_pairs={{0,12},{1,13},{2,14},{3,15},{4,8},{5,9},{6,10},{7,11},{8,4},{9,5},... | collective-permute-start | bytes 2312 | tf_op jit(solution)/shard_map/ppermute | solution.py:60
  65.8 0.2 pad_maximum_fusion.1
  66.1 1.2 %collective-permute-done.4 = f32[12,16]{1,0:T(8,128)S(1)} collective-permute-done((f32[12,16]{1,0:T(8,128)S(1)}, f32[12,16]{1,0:T(8,128)S(1)}, u32[]{:S(2)}, u32[]{:S(2)}) %collective-permute-start.4) | collective-permute-done | bytes 800 | tf_op jit(solution)/shard_map/ppermute | solution.py:60
  67.2 1.5 %collective-permute-done.5 = f32[12,16]{1,0:T(8,128)S(1)} collective-permute-done((f32[12,16]{1,0:T(8,128)S(1)}, f32[12,16]{1,0:T(8,128)S(1)}, u32[]{:S(2)}, u32[]{:S(2)}) %collective-permute-start.5) | collective-permute-done | bytes 800 | tf_op jit(solution)/shard_map/ppermute | solution.py:60
  68.8 2.6 %copy.106 = bf16[16,9,4,1536]{3,2,1,0:T(4,128)(2,1)} copy(bf16[16,9,4,1536]{3,0,1,2:T(8,128)(2,1)S(1)} %pad_maximum_fusion.1) | data formatting | bytes 3538944 | tf_op jit(solution)/shard_map/optimization_barrier | solution.py:142
  71.4 7.8 %all-to-all-start.1 = ((bf16[16,9,4,1536]{3,2,1,0:T(4,128)(2,1)}), bf16[16,9,4,1536]{3,2,1,0:T(4,128)(2,1)S(1)}, u32[]{:S(2)}, u32[]{:S(2)}) async-start(bf16[16,9,4,1536]{3,2,1,0:T(4,128)(2,1)} %copy.106), calls=%async_computation.1 | async-start | bytes 3538944 | tf_op jit(solution)/shard_map/all_to_all | solution.py:145
  79.1 3.1 %convolution_bitcast_fusion.1 = f32[1,1,12,18,8,128]{5,4,3,2,1,0:T(8,128)} fusion(bf16[144,12,128]{2,1,0:T(8,128)(2,1)S(1)} %copy-done.13, f32[12,144,144]{1,2,0:T(8,128)} %copy-done.4, f32[12,144]{1,0:T(8,128)S(1)} %get-tuple-element.15), kind=kOutput, calls=%fused_computation.23 | convolution fusion | flops 64198656 | bytes 2329344 | tf_op jit(solution)/shard_map/bfhij,bfjhe->bfihe/dot_general | solution.py:31
  82.3 0.5 multiply_reduce_fusion
  82.8 0.3 multiply_convert_fusion
  83.2 2.0 %collective-permute-start.7 = (f32[12,16]{1,0:T(8,128)S(1)}, f32[12,16]{1,0:T(8,128)S(1)}, u32[]{:S(2)}, u32[]{:S(2)}) collective-permute-start(f32[12,16]{1,0:T(8,128)S(1)} %add_add_fusion.1), channel_id=1, source_target_pairs={{0,32},{16,48},{32,0},{48,16},{64,96},{80,112},{96,64},{112,80},{1... | collective-permute-start | bytes 2312 | tf_op jit(solution)/shard_map/ppermute | solution.py:60
  85.2 0.4 fusion.5
  85.6 1.3 %collective-permute-done.7 = f32[12,16]{1,0:T(8,128)S(1)} collective-permute-done((f32[12,16]{1,0:T(8,128)S(1)}, f32[12,16]{1,0:T(8,128)S(1)}, u32[]{:S(2)}, u32[]{:S(2)}) %collective-permute-start.7) | collective-permute-done | bytes 800 | tf_op jit(solution)/shard_map/ppermute | solution.py:60
  86.9 1.3 %collective-permute-done.8 = f32[12,16]{1,0:T(8,128)S(1)} collective-permute-done((f32[12,16]{1,0:T(8,128)S(1)}, f32[12,16]{1,0:T(8,128)S(1)}, u32[]{:S(2)}, u32[]{:S(2)}) %collective-permute-start.8) | collective-permute-done | bytes 800 | tf_op jit(solution)/shard_map/ppermute | solution.py:60
  88.3 6.3 %collective-permute-start.10 = (f32[12,16]{1,0:T(8,128)S(1)}, f32[12,16]{1,0:T(8,128)S(1)}, u32[]{:S(2)}, u32[]{:S(2)}) collective-permute-start(f32[12,16]{1,0:T(8,128)S(1)} %add_add_fusion), channel_id=1, source_target_pairs={{0,128},{16,144},{32,160},{48,176},{64,192},{80,208},{96,224},{112... | collective-permute-start | bytes 2312 | tf_op jit(solution)/shard_map/ppermute | solution.py:60
  94.6 0.5 collective-permute-start.11
  95.1 0.9 collective-permute-start.9
  96.0 0.6 fusion.4
  96.6 3.7 %collective-permute-done.11 = f32[12,16]{1,0:T(8,128)S(1)} collective-permute-done((f32[12,16]{1,0:T(8,128)S(1)}, f32[12,16]{1,0:T(8,128)S(1)}, u32[]{:S(2)}, u32[]{:S(2)}) %collective-permute-start.11) | collective-permute-done | bytes 800 | tf_op jit(solution)/shard_map/ppermute | solution.py:60
  100.3 0.6 add_multiply_fusion
  100.9 0.5 convert_bitcast_fusion
  101.4 2.6 %fusion.58 = (f32[1,16,9,1536]{3,0,2,1:T(1,128)S(1)}, f32[1,16,9,1536]{3,0,2,1:T(1,128)S(1)}, f32[1,16,9,1536]{3,0,2,1:T(1,128)S(1)}, f32[1,16,9,1536]{3,0,2,1:T(1,128)S(1)}) fusion(f32[4,16,9,1536]{3,0,2,1:T(4,128)S(1)} %convert_bitcast_fusion), kind=kLoop, calls=%fused_computation.84 | loop fusion | bytes 7077888 | tf_op jit(solution)/shard_map/slice | solution.py:161
  104.1 1.2 %fusion.15 = (bf16[1,1,144,1536]{3,2,1,0:T(8,128)(2,1)}, bf16[1,1,144,1536]{3,2,1,0:T(8,128)(2,1)}) fusion(f32[1,1,12,18,8,128]{5,4,3,2,1,0:T(8,128)S(1)} %copy-done.11, f32[1,1,144,1536]{3,0,2,1:T(1,128)S(1)} %bitcast.131, f32[1,1,144,1536]{3,0,2,1:T(1,128)S(1)} %bitcast.132, f32[1,1,12,18,8,128]{5,4,3,2,1,0:T(8,128)S(1)} %fusion.5), kind=kLoop, calls=%fused_computation.35 | loop fusion | flops 884736 | bytes 4423680 | tf_op jit(solution)/shard_map/convert_element_type | solution.py:161
  105.3 1.2 %fusion.17 = (bf16[1,1,144,1536]{3,2,1,0:T(8,128)(2,1)}, bf16[1,1,144,1536]{3,2,1,0:T(8,128)(2,1)}) fusion(f32[1,1,12,18,8,128]{5,4,3,2,1,0:T(8,128)S(1)} %fusion.4, f32[1,1,144,1536]{3,0,2,1:T(1,128)S(1)} %bitcast.129, f32[1,1,144,1536]{3,0,2,1:T(1,128)S(1)} %bitcast.130, f32[1,1,12,18,8,128]{5,4,3,2,1,0:T(8,128)S(1)} %copy-done.12), kind=kLoop, calls=%fused_computation.39 | loop fusion | flops 884736 | bytes 4423680 | tf_op jit(solution)/shard_map/convert_element_type | solution.py:159
  (52 shorter events, 0.6 us)
Async XLA Ops:
  0.6 18.2 %copy-start = (f32[12,16]{1,0:T(8,128)S(1)}, f32[12,16]{1,0:T(8,128)}, u32[]{:S(2)}) copy-start(f32[12,16]{1,0:T(8,128)} %param.13) | copy-start | bytes 2308
  0.6 2.5 %copy-start.8 = (bf16[1,1,144,1536]{3,2,1,0:T(8,128)(2,1)S(1)}, bf16[1,1,144,1536]{3,2,1,0:T(8,128)(2,1)}, u32[]{:S(2)}) copy-start(bf16[1,1,144,1536]{3,2,1,0:T(8,128)(2,1)} %param.9) | copy-start | bytes 1327108
  7.9 7.6 %copy-start.6 = (bf16[1,1,144,1536]{3,2,1,0:T(8,128)(2,1)S(1)}, bf16[1,1,144,1536]{3,2,1,0:T(8,128)(2,1)}, u32[]{:S(2)}) copy-start(bf16[1,1,144,1536]{3,2,1,0:T(8,128)(2,1)} %param.7) | copy-start | bytes 1327108
  7.9 7.9 %copy-start.7 = (bf16[1,1,144,1536]{3,2,1,0:T(8,128)(2,1)S(1)}, bf16[1,1,144,1536]{3,2,1,0:T(8,128)(2,1)}, u32[]{:S(2)}) copy-start(bf16[1,1,144,1536]{3,2,1,0:T(8,128)(2,1)} %param.8) | copy-start | bytes 1327108
  7.9 30.9 %all-to-all-start = ((bf16[16,9,4,1536]{3,2,1,0:T(4,128)(2,1)}), bf16[16,9,4,1536]{3,2,1,0:T(4,128)(2,1)}, u32[]{:S(2)}, u32[]{:S(2)}) async-start(bf16[16,9,4,1536]{3,2,1,0:T(4,128)(2,1)} %copy.94), calls=%async_computation | async-start | bytes 3538944 | tf_op jit(solution)/shard_map/all_to_all | solution.py:92
  15.5 1.0 copy-start.9
  15.5 2.1 %copy-start.10 = (bf16[1,1,144,1536]{3,2,1,0:T(8,128)(2,1)S(1)}, bf16[1,1,144,1536]{3,2,1,0:T(8,128)(2,1)}, u32[]{:S(2)}) copy-start(bf16[1,1,144,1536]{3,2,1,0:T(8,128)(2,1)} %param.10) | copy-start | bytes 1327108
  15.9 4.1 %copy-start.17 = (s32[1,16]{1,0:T(1,128)S(1)}, s32[1,16]{1,0:T(1,128)}, u32[]{:S(2)}) copy-start(s32[1,16]{1,0:T(1,128)} %param.12) | copy-start | bytes 196
  16.5 4.2 %copy-start.2 = (bf16[144,12,128]{2,1,0:T(8,128)(2,1)}, bf16[144,12,128]{2,1,0:T(8,128)(2,1)S(1)}, u32[]{:S(2)}) copy-start(bf16[144,12,128]{2,1,0:T(8,128)(2,1)S(1)} %reshape.279) | copy-start | bytes 1327108
  20.8 2.8 %copy-start.4 = (f32[12,144,144]{1,2,0:T(8,128)}, f32[12,144,144]{1,2,0:T(8,128)S(1)}, u32[]{:S(2)}) copy-start(f32[12,144,144]{1,2,0:T(8,128)S(1)} %get-tuple-element.16) | copy-start | bytes 2985988
  44.3 4.9 %copy-start.1 = (bf16[16,9,4,12,128]{4,0,3,1,2:T(8,128)(2,1)}, bf16[16,9,4,12,128]{4,0,3,1,2:T(8,128)(2,1)S(1)}, u32[]{:S(2)}) copy-start(bf16[16,9,4,12,128]{4,0,3,1,2:T(8,128)(2,1)S(1)} %copy.176) | copy-start | bytes 5308420
  52.1 8.9 %collective-permute-start = (f32[12,16]{1,0:T(8,128)S(1)}, f32[12,16]{1,0:T(8,128)S(1)}, u32[]{:S(2)}, u32[]{:S(2)}) collective-permute-start(f32[12,16]{1,0:T(8,128)S(1)} %convolution_bitcast_fusion.3), channel_id=1, source_target_pairs={{0,1},{1,0},{2,3},{3,2},{4,5},{5,4},{6,7},{7,6},{8,9},{9,8},{10,11... | collective-permute-start | bytes 2312 | tf_op jit(solution)/shard_map/ppermute | solution.py:60
  52.8 8.2 %collective-permute-start.1 = (f32[12,16]{1,0:T(8,128)S(1)}, f32[12,16]{1,0:T(8,128)S(1)}, u32[]{:S(2)}, u32[]{:S(2)}) collective-permute-start(f32[12,16]{1,0:T(8,128)S(1)} %convolution_bitcast_fusion.3), channel_id=1, source_target_pairs={{0,2},{1,3},{2,0},{3,1},{4,6},{5,7},{6,4},{7,5},{8,10},{9,11},{10,... | collective-permute-start | bytes 2312 | tf_op jit(solution)/shard_map/ppermute | solution.py:60
  56.4 4.6 %collective-permute-start.2 = (f32[12,16]{1,0:T(8,128)S(1)}, f32[12,16]{1,0:T(8,128)S(1)}, u32[]{:S(2)}, u32[]{:S(2)}) collective-permute-start(f32[12,16]{1,0:T(8,128)S(1)} %convolution_bitcast_fusion.3), channel_id=1, source_target_pairs={{0,3},{1,2},{2,1},{3,0},{4,7},{5,6},{6,5},{7,4},{8,11},{9,10},{10,... | collective-permute-start | bytes 2312 | tf_op jit(solution)/shard_map/ppermute | solution.py:60
  59.0 1.0 copy-start.15
  59.5 1.0 copy-start.16
  61.0 5.0 %collective-permute-start.3 = (f32[12,16]{1,0:T(8,128)S(1)}, f32[12,16]{1,0:T(8,128)S(1)}, u32[]{:S(2)}, u32[]{:S(2)}) collective-permute-start(f32[12,16]{1,0:T(8,128)S(1)} %add_add_fusion.2), channel_id=1, source_target_pairs={{0,4},{1,5},{2,6},{3,7},{4,0},{5,1},{6,2},{7,3},{8,12},{9,13},{10,... | collective-permute-start | bytes 2312 | tf_op jit(solution)/shard_map/ppermute | solution.py:60
  62.1 5.2 %collective-permute-start.4 = (f32[12,16]{1,0:T(8,128)S(1)}, f32[12,16]{1,0:T(8,128)S(1)}, u32[]{:S(2)}, u32[]{:S(2)}) collective-permute-start(f32[12,16]{1,0:T(8,128)S(1)} %add_add_fusion.2), channel_id=1, source_target_pairs={{0,8},{1,9},{2,10},{3,11},{4,12},{5,13},{6,14},{7,15},{8,0},{9,1},... | collective-permute-start | bytes 2312 | tf_op jit(solution)/shard_map/ppermute | solution.py:60
  63.9 4.9 %collective-permute-start.5 = (f32[12,16]{1,0:T(8,128)S(1)}, f32[12,16]{1,0:T(8,128)S(1)}, u32[]{:S(2)}, u32[]{:S(2)}) collective-permute-start(f32[12,16]{1,0:T(8,128)S(1)} %add_add_fusion.2), channel_id=1, source_target_pairs={{0,12},{1,13},{2,14},{3,15},{4,8},{5,9},{6,10},{7,11},{8,4},{9,5},... | collective-permute-start | bytes 2312 | tf_op jit(solution)/shard_map/ppermute | solution.py:60
  71.4 7.8 %copy-start.13 = (bf16[144,12,128]{2,1,0:T(8,128)(2,1)S(1)}, bf16[144,12,128]{2,1,0:T(8,128)(2,1)}, u32[]{:S(2)}) copy-start(bf16[144,12,128]{2,1,0:T(8,128)(2,1)} %reshape.280) | copy-start | bytes 1327108
  71.4 29.6 %all-to-all-start.1 = ((bf16[16,9,4,1536]{3,2,1,0:T(4,128)(2,1)}), bf16[16,9,4,1536]{3,2,1,0:T(4,128)(2,1)S(1)}, u32[]{:S(2)}, u32[]{:S(2)}) async-start(bf16[16,9,4,1536]{3,2,1,0:T(4,128)(2,1)} %copy.106), calls=%async_computation.1 | async-start | bytes 3538944 | tf_op jit(solution)/shard_map/all_to_all | solution.py:145
  79.1 3.1 %copy-start.5 = (f32[12,144,144]{1,2,0:T(8,128)S(1)}, f32[12,144,144]{1,2,0:T(8,128)}, u32[]{:S(2)}) copy-start(f32[12,144,144]{1,2,0:T(8,128)} %copy-done.4) | copy-start | bytes 2985988
  79.1 3.1 %copy-start.14 = (bf16[144,12,128]{2,1,0:T(8,128)(2,1)S(1)}, bf16[144,12,128]{2,1,0:T(8,128)(2,1)}, u32[]{:S(2)}) copy-start(bf16[144,12,128]{2,1,0:T(8,128)(2,1)} %reshape.283) | copy-start | bytes 1327108
  83.1 13.0 %copy-start.3 = (bf16[144,12,128]{2,1,0:T(8,128)(2,1)S(1)}, bf16[144,12,128]{2,1,0:T(8,128)(2,1)}, u32[]{:S(2)}) copy-start(bf16[144,12,128]{2,1,0:T(8,128)(2,1)} %copy-done.2) | copy-start | bytes 1327108
  83.1 2.5 %collective-permute-start.6 = (f32[12,16]{1,0:T(8,128)S(1)}, f32[12,16]{1,0:T(8,128)S(1)}, u32[]{:S(2)}, u32[]{:S(2)}) collective-permute-start(f32[12,16]{1,0:T(8,128)S(1)} %add_add_fusion.1), channel_id=1, source_target_pairs={{0,16},{16,0},{32,48},{48,32},{64,80},{80,64},{96,112},{112,96},{1... | collective-permute-start | bytes 2312 | tf_op jit(solution)/shard_map/ppermute | solution.py:60
  83.2 3.7 %collective-permute-start.7 = (f32[12,16]{1,0:T(8,128)S(1)}, f32[12,16]{1,0:T(8,128)S(1)}, u32[]{:S(2)}, u32[]{:S(2)}) collective-permute-start(f32[12,16]{1,0:T(8,128)S(1)} %add_add_fusion.1), channel_id=1, source_target_pairs={{0,32},{16,48},{32,0},{48,16},{64,96},{80,112},{96,64},{112,80},{1... | collective-permute-start | bytes 2312 | tf_op jit(solution)/shard_map/ppermute | solution.py:60
  85.2 3.1 %collective-permute-start.8 = (f32[12,16]{1,0:T(8,128)S(1)}, f32[12,16]{1,0:T(8,128)S(1)}, u32[]{:S(2)}, u32[]{:S(2)}) collective-permute-start(f32[12,16]{1,0:T(8,128)S(1)} %add_add_fusion.1), channel_id=1, source_target_pairs={{0,48},{16,32},{32,16},{48,0},{64,112},{80,96},{96,80},{112,64},{1... | collective-permute-start | bytes 2312 | tf_op jit(solution)/shard_map/ppermute | solution.py:60
  88.3 8.3 %collective-permute-start.10 = (f32[12,16]{1,0:T(8,128)S(1)}, f32[12,16]{1,0:T(8,128)S(1)}, u32[]{:S(2)}, u32[]{:S(2)}) collective-permute-start(f32[12,16]{1,0:T(8,128)S(1)} %add_add_fusion), channel_id=1, source_target_pairs={{0,128},{16,144},{32,160},{48,176},{64,192},{80,208},{96,224},{112... | collective-permute-start | bytes 2312 | tf_op jit(solution)/shard_map/ppermute | solution.py:60
  94.6 5.8 %collective-permute-start.11 = (f32[12,16]{1,0:T(8,128)S(1)}, f32[12,16]{1,0:T(8,128)S(1)}, u32[]{:S(2)}, u32[]{:S(2)}) collective-permute-start(f32[12,16]{1,0:T(8,128)S(1)} %add_add_fusion), channel_id=1, source_target_pairs={{0,192},{16,208},{32,224},{48,240},{64,128},{80,144},{96,160},{112... | collective-permute-start | bytes 2312 | tf_op jit(solution)/shard_map/ppermute | solution.py:60
  95.1 5.2 %collective-permute-start.9 = (f32[12,16]{1,0:T(8,128)S(1)}, f32[12,16]{1,0:T(8,128)S(1)}, u32[]{:S(2)}, u32[]{:S(2)}) collective-permute-start(f32[12,16]{1,0:T(8,128)S(1)} %add_add_fusion), channel_id=1, source_target_pairs={{0,64},{16,80},{32,96},{48,112},{64,0},{80,16},{96,32},{112,48},{1... | collective-permute-start | bytes 2312 | tf_op jit(solution)/shard_map/ppermute | solution.py:60
  101.4 2.7 %copy-start.11 = (f32[1,1,12,18,8,128]{5,4,3,2,1,0:T(8,128)S(1)}, f32[1,1,12,18,8,128]{5,4,3,2,1,0:T(8,128)}, u32[]{:S(2)}) copy-start(f32[1,1,12,18,8,128]{5,4,3,2,1,0:T(8,128)} %convolution_bitcast_fusion) | copy-start | bytes 2654212
  104.1 1.2 %copy-start.12 = (f32[1,1,12,18,8,128]{5,4,3,2,1,0:T(8,128)S(1)}, f32[1,1,12,18,8,128]{5,4,3,2,1,0:T(8,128)}, u32[]{:S(2)}) copy-start(f32[1,1,12,18,8,128]{5,4,3,2,1,0:T(8,128)} %convolution_bitcast_fusion.1) | copy-start | bytes 2654212

commit v5 on v3

--- a/solution.py
+++ b/solution.py
@@ -4,6 +4,7 @@
 import jax.numpy as jnp
 from jax import lax
 from jax.sharding import PartitionSpec as P
+from jax.experimental import pallas as pl
 
 SPACE_PATTERNS = ("bfihe,bfjhe->bfhij", "bfhij,bfjhe->bfihe", "bfhij,bfihe->bfjhe")
 TIME_PATTERNS = ("phie,phje->phij", "phij,phje->phie", "phij,phie->phje")
@@ -53,6 +54,25 @@
         * scaling
     )
     return (query_grad, key_grad, value_grad, score_grad)
+
+
+def regroup_kernel(x_ref, o_ref):
+    frames, block, tensors, width = x_ref.shape
+    heads, size = o_ref.shape[2], o_ref.shape[4]
+    for tensor in range(tensors):
+        for place in range(block):
+            row = x_ref[:, place, tensor, :]
+            for head in range(heads):
+                o_ref[tensor, place, head] = row[:, head * size : (head + 1) * size]
+
+
+def regroup(rows, heads):
+    frames, block, tensors, width = rows.shape
+    size = width // heads
+    return pl.pallas_call(
+        regroup_kernel,
+        out_shape=jax.ShapeDtypeStruct((tensors, block, heads, frames, size), rows.dtype),
+    )(rows)
 
 
 def quad_step(value, axis, size, step):
@@ -90,8 +110,7 @@
         axis=2,
     )
     rows = lax.all_to_all(stacked, "seq", split_axis=0, concat_axis=0, tiled=True)
-    rows = rows.reshape(seq_size, block, 4, head_count, width // head_count)
-    rows = jnp.transpose(rows, (2, 1, 3, 0, 4))
+    rows = regroup(rows, head_count)
     query_part, key_part, value_part, slope_part = rows[0], rows[1], rows[2], rows[3]
     scaling = 1.0 / math.sqrt(query_part.shape[-1])
     scores = (

time: 106 us -> 117 us (1.10)
  Pallas kernels: 0 us -> 7.27 us
  other arithmetic: 8.34 us -> 12.8 us
  local copies, waits for them, and re-layouts: 28.3 us -> 25.1 us
  matrix products: 15.6 us -> 17.8 us
    pallas_call x0 -> x1, Pallas kernels: none -> 7.27 us  [regroup(): pl.pallas_call(regroup_kernel, out_shape=jax.ShapeDtypeStruct((tensors, b...]
    reshape x2 -> x0, local copies, waits for them, and re-layouts: 6.25 us -> none  [on_device(): rows = rows.reshape(seq_size, block, 4, head_count, width // head_count)]
    another operation x1, other arithmetic: 0.61 us -> 5.07 us  [on_device(): jnp.stack([tensor.reshape(seq_size, block, width) for tensor in (queries,...]
    another operation x5 -> x4, local copies, waits for them, and re-layouts: 6.64 us -> 8.44 us  [on_device(): jnp.stack([tensor.reshape(seq_size, block, width) for tensor in (queries,...]
    dot_general x1, matrix products: 1.28 us -> 2.56 us  [on_device(): jnp.einsum(TIME_PATTERNS[0], slope_part, value_part, preferred_element_ty...]
    unnamed x38, local copies, waits for them, and re-layouts: 0.29 us -> 1.54 us
  transfers between devices with their start and end apart: 14 -> 14, of which waited for: 5 -> 5; matrix products, arithmetic and copies ran while one was open for 25% -> 23% of each run, Pallas kernels for 0% -> 0%
where the time goes in v5:
time: 117 us; the launch traced here: 115 us
  starting transfers between devices  34.8 us (30%)
  local copies, waits for them, and re-layouts  25.1 us (21%)
  matrix products  17.8 us (15%)
  waiting for transfers between devices  15.8 us (14%)
  other arithmetic  12.8 us (11%)
  Pallas kernels  7.27 us (6%)
  between operations  1.7 us (1%)
    ppermute x12, starting transfers between devices, quad_step(): lax.ppermute(value, axis, [(index, index ^ part * step) for index in rang...  19.2 us
    another operation x4, local copies, waits for them, and re-layouts, on_device(): jnp.stack([tensor.reshape(seq_size, block, width) for tensor in (queries,...  8.44 us
    ppermute x12, waiting for transfers between devices, quad_step(): lax.ppermute(value, axis, [(index, index ^ part * step) for index in rang...  8.26 us
    all_to_all x1, starting transfers between devices, on_device(): lax.all_to_all(back_rows, 'seq', split_axis=0, concat_axis=0, tiled=True)  8 us
    all_to_all x1, starting transfers between devices, on_device(): lax.all_to_all(stacked, 'seq', split_axis=0, concat_axis=0, tiled=True)  7.58 us
    all_to_all x1, waiting for transfers between devices, on_device(): lax.all_to_all(stacked, 'seq', split_axis=0, concat_axis=0, tiled=True)  7.52 us
    pallas_call x1, Pallas kernels, regroup(): pl.pallas_call(regroup_kernel, out_shape=jax.ShapeDtypeStruct((tensors, b...  7.27 us
    another operation x1, other arithmetic, on_device(): jnp.stack([tensor.reshape(seq_size, block, width) for tensor in (queries,...  5.07 us
  transfers between devices with their start and end apart: 14, of which 5 were waited for; matrix products, arithmetic and copies ran while one was open for 23% of the time, Pallas kernels for 0%

profile of v5, /device:TPU:4, one launch (start us, length us, event | category | flops | bytes accessed | tf_op | source)
XLA Modules:
  0.0 115.2 jit_solution(3448941202458451153)
XLA Ops:
  0.7 2.8 %stack_reshape.32 = bf16[16,9,1,1536]{3,2,1,0:T(2,128)(2,1)S(1)} reshape(bf16[1,1,144,1536]{3,2,1,0:T(8,128)(2,1)} %param.7) | data formatting | bytes 884736 | tf_op jit(solution)/shard_map/stack;reshape | solution.py:105
  3.4 2.7 %stack_reshape.33 = bf16[16,9,1,1536]{3,2,1,0:T(2,128)(2,1)S(1)} reshape(bf16[1,1,144,1536]{3,2,1,0:T(8,128)(2,1)} %param.8) | data formatting | bytes 884736 | tf_op jit(solution)/shard_map/stack;reshape | solution.py:105
  6.1 0.3 stack_reshape.34
  6.4 2.7 %stack_reshape.35 = bf16[16,9,1,1536]{3,2,1,0:T(2,128)(2,1)S(1)} reshape(bf16[1,1,144,1536]{3,2,1,0:T(8,128)(2,1)} %param.10) | data formatting | bytes 884736 | tf_op jit(solution)/shard_map/stack;reshape | solution.py:105
  9.1 5.1 %pad_maximum_fusion = bf16[16,9,4,1536]{3,2,1,0:T(4,128)(2,1)} fusion(bf16[16,9,1,1536]{3,2,1,0:T(2,128)(2,1)S(1)} %stack_reshape.35, bf16[16,9,1,1536]{3,2,1,0:T(2,128)(2,1)S(1)} %stack_reshape.34, bf16[16,9,1,1536]{3,2,1,0:T(2,128)(2,1)S(1)} %stack_reshape.33, bf16[16,9,1,1536]{3,2,1,0:T(2,128)(2,1)S(1)} %stack_reshape.32), kind=kLoop, calls=%fused_computation.5 | loop fusion | flops 7077888 | bytes 3538944 | tf_op jit(solution)/shard_map/stack | solution.py:105
  14.2 7.6 %all-to-all-start = ((bf16[16,9,4,1536]{3,2,1,0:T(4,128)(2,1)}), bf16[16,9,4,1536]{3,2,1,0:T(4,128)(2,1)S(1)}, u32[]{:S(2)}, u32[]{:S(2)}) async-start(bf16[16,9,4,1536]{3,2,1,0:T(4,128)(2,1)} %pad_maximum_fusion), calls=%async_computation | async-start | bytes 3538944 | tf_op jit(solution)/shard_map/all_to_all | solution.py:112
  21.8 0.3 reshape.275
  22.1 0.3 reshape.276
  22.5 2.4 %reshape.277 = bf16[144,12,128]{2,1,0:T(8,128)(2,1)} reshape(bf16[1,1,144,1536]{3,2,1,0:T(8,128)(2,1)} %param.9) | data formatting | bytes 884736 | tf_op jit(solution)/shard_map/reshape.7
  24.8 1.3 %reshape.279 = bf16[144,12,128]{2,1,0:T(8,128)(2,1)S(1)} reshape(bf16[1,1,144,1536]{3,2,1,0:T(8,128)(2,1)} %param.10) | data formatting | bytes 884736 | tf_op jit(solution)/shard_map/reshape.21
  26.2 0.9 convolution_bitcast_fusion.2
  27.1 1.7 %copy.102 = f32[12,16,16]{1,2,0:T(8,128)} copy(f32[12,16,16]{0,2,1:T(8,128)} %convolution_bitcast_fusion.2) | data formatting | bytes 24576 | tf_op jit(solution)/shard_map/dot_general | solution.py:97
  29.5 0.5 iota_compare_fusion.2
  30.0 1.4 %broadcast_compare_fusion = pred[16,16]{0,1:T(8,128)(4,1)} fusion(s32[16]{0:T(128)} %bitcast.125), kind=kLoop, calls=%fused_computation.82 | loop fusion | flops 256 | bytes 320 | tf_op jit(solution)/shard_map/eq | solution.py:100
  31.4 3.3 %fusion.66 = (f32[12,144]{1,0:T(8,128)}, f32[12,144,144]{1,2,0:T(8,128)}) fusion(pred[144]{0:T(512)(128)(4,1)} %iota_compare_fusion.2, bf16[144,12,128]{2,1,0:T(8,128)(2,1)S(1)} %reshape.276, bf16[144,12,128]{2,1,0:T(8,128)(2,1)S(1)} %reshape.275), kind=kOutput, calls=%fused_computation.89 | convolution fusion | flops 64696464 | bytes 1887120 | tf_op jit(solution)/shard_map/sub | solution.py:29
  34.7 2.8 %convolution_bitcast_fusion = f32[1,1,12,18,8,128]{5,4,3,2,1,0:T(8,128)} fusion(bf16[144,12,128]{2,1,0:T(8,128)(2,1)S(1)} %reshape.279, f32[12,144,144]{1,2,0:T(8,128)} %get-tuple-element.32, f32[12,144]{1,0:T(8,128)} %get-tuple-element.31), kind=kOutput, calls=%fused_computation.26 | convolution fusion | flops 64198656 | bytes 2329344 | tf_op jit(solution)/shard_map/bfhij,bfihe->bfjhe/dot_general | solution.py:40
  37.5 7.5 %all-to-all-done.x_ref = bf16[16,9,4,1536]{3,2,1,0:T(4,128)(2,1)S(1)} async-done(((bf16[16,9,4,1536]{3,2,1,0:T(4,128)(2,1)}), bf16[16,9,4,1536]{3,2,1,0:T(4,128)(2,1)S(1)}, u32[]{:S(2)}, u32[]{:S(2)}) %all-to-all-start) | async-done | bytes 1769504 | tf_op jit(solution)/shard_map/all_to_all | solution.py:112
  45.0 1.3 %copy-done.2 = bf16[16,9,4,1536]{3,2,1,0:T(4,128)(2,1)} copy-done((bf16[16,9,4,1536]{3,2,1,0:T(4,128)(2,1)}, bf16[16,9,4,1536]{3,2,1,0:T(4,128)(2,1)S(1)}, u32[]{:S(2)}) %copy-start.2) | copy-done | bytes 1769496
  46.3 7.3 %shard_map.110 = bf16[4,9,12,16,128]{4,3,2,1,0:T(8,128)(2,1)} custom-call(bf16[16,9,4,1536]{3,2,1,0:T(4,128)(2,1)} %copy-done.2), custom_call_target="tpu_custom_call" | custom-call | tf_op jit(solution)/shard_map/pallas_call | solution.py:72
  53.5 2.6 %fusion.64 = f32[9,12,16,16]{2,3,1,0:T(8,128)} fusion(bf16[4,9,12,16,128]{4,3,2,1,0:T(8,128)(2,1)} %shard_map.110), kind=kOutput, calls=%fused_computation.87 | convolution fusion | flops 7077888 | bytes 995328 | tf_op jit(solution)/shard_map/phie,phje->phij/dot_general | solution.py:125
  56.1 1.5 %fusion.6 = f32[9,12,16,16]{2,3,1,0:T(8,128)S(1)} fusion(f32[12,16,16]{1,2,0:T(8,128)} %copy.102, pred[16,16]{0,1:T(8,128)(4,1)} %broadcast_compare_fusion, bf16[4,9,12,16,128]{4,3,2,1,0:T(8,128)(2,1)S(1)} %copy-done.1), kind=kOutput, calls=%fused_computation.13 | convolution fusion | flops 7219614 | bytes 1007872 | tf_op jit(solution)/shard_map/div | solution.py:124
  57.6 1.8 %fusion.71 = (f32[12,16,16]{1,2,0:T(8,128)S(1)}, bf16[9,12,16,16]{2,3,1,0:T(8,128)(2,1)S(1)}) fusion(f32[9,12,16,16]{2,3,1,0:T(8,128)S(1)} %fusion.6, f32[9,12,16,16]{2,3,1,0:T(8,128)} %fusion.64), kind=kOutput, calls=%fused_computation.90 | output fusion | flops 136911 | bytes 288768 | tf_op jit(solution)/shard_map/sub | solution.py:129
  59.4 0.1 copy.103
  59.5 0.2 convolution_bitcast_fusion.3
  59.7 0.7 collective-permute-start
  60.4 3.4 %collective-permute-start.1 = (f32[12,16]{1,0:T(8,128)S(1)}, f32[12,16]{1,0:T(8,128)S(1)}, u32[]{:S(2)}, u32[]{:S(2)}) collective-permute-start(f32[12,16]{1,0:T(8,128)S(1)} %convolution_bitcast_fusion.3), channel_id=1, source_target_pairs={{0,2},{1,3},{2,0},{3,1},{4,6},{5,7},{6,4},{7,5},{8,10},{9,11},{10,... | collective-permute-start | bytes 2312 | tf_op jit(solution)/shard_map/ppermute | solution.py:80
  63.9 0.5 collective-permute-start.2
  64.3 1.3 %slice_bitcast_fusion.1 = (bf16[9,12,16,128]{3,2,1,0:T(8,128)(2,1)S(1)}, bf16[9,12,16,128]{3,2,1,0:T(8,128)(2,1)S(1)}, bf16[9,12,16,128]{3,2,1,0:T(8,128)(2,1)}, bf16[9,12,16,128]{3,2,1,0:T(8,128)(2,1)}) fusion(bf16[4,9,12,16,128]{4,3,2,1,0:T(8,128)(2,1)S(1)} %copy-done.1), kind=kLoop, calls=%fused_computation.53 | loop fusion | bytes 3538944 | tf_op jit(solution)/shard_map/squeeze | solution.py:114
  65.6 1.9 %collective-permute-done.2 = f32[12,16]{1,0:T(8,128)S(1)} collective-permute-done((f32[12,16]{1,0:T(8,128)S(1)}, f32[12,16]{1,0:T(8,128)S(1)}, u32[]{:S(2)}, u32[]{:S(2)}) %collective-permute-start.2) | collective-permute-done | bytes 800 | tf_op jit(solution)/shard_map/ppermute | solution.py:80
  67.6 2.7 %collective-permute-start.4 = (f32[12,16]{1,0:T(8,128)S(1)}, f32[12,16]{1,0:T(8,128)S(1)}, u32[]{:S(2)}, u32[]{:S(2)}) collective-permute-start(f32[12,16]{1,0:T(8,128)S(1)} %add_add_fusion.2), channel_id=1, source_target_pairs={{0,8},{1,9},{2,10},{3,11},{4,12},{5,13},{6,14},{7,15},{8,0},{9,1},... | collective-permute-start | bytes 2312 | tf_op jit(solution)/shard_map/ppermute | solution.py:80
  70.3 1.9 %collective-permute-start.5 = (f32[12,16]{1,0:T(8,128)S(1)}, f32[12,16]{1,0:T(8,128)S(1)}, u32[]{:S(2)}, u32[]{:S(2)}) collective-permute-start(f32[12,16]{1,0:T(8,128)S(1)} %add_add_fusion.2), channel_id=1, source_target_pairs={{0,12},{1,13},{2,14},{3,15},{4,8},{5,9},{6,10},{7,11},{8,4},{9,5},... | collective-permute-start | bytes 2312 | tf_op jit(solution)/shard_map/ppermute | solution.py:80
  72.2 0.3 fusion.18
  72.5 0.1 copy.105
  72.7 0.3 stack_reshape.28
  73.0 0.3 fusion.17
  73.3 0.1 copy.107
  73.5 0.3 stack_reshape.29
  73.8 1.4 %fusion.16 = bf16[16,9,12,128]{3,0,2,1:T(8,128)(2,1)S(1)} fusion(bf16[9,12,16,128]{3,2,1,0:T(8,128)(2,1)} %get-tuple-element.19, bf16[9,12,16,16]{2,3,1,0:T(8,128)(2,1)S(1)} %get-tuple-element.17), kind=kOutput, calls=%fused_computation.32 | convolution fusion | flops 7520256 | bytes 940032 | tf_op jit(solution)/shard_map/phij,phie->phje/dot_general | solution.py:155
  75.2 0.1 copy.108
  75.3 1.1 stack_reshape.30
  76.4 0.4 fusion.19
  76.7 0.1 copy.109
  76.9 0.3 stack_reshape.31
  77.2 0.2 copy-done.8
  77.4 0.2 pad_maximum_fusion.1
  77.7 2.6 %copy.110 = bf16[16,9,4,1536]{3,2,1,0:T(4,128)(2,1)} copy(bf16[16,9,4,1536]{3,0,1,2:T(8,128)(2,1)S(1)} %pad_maximum_fusion.1) | data formatting | bytes 3538944 | tf_op jit(solution)/shard_map/optimization_barrier | solution.py:166
  80.3 8.0 %all-to-all-start.1 = ((bf16[16,9,4,1536]{3,2,1,0:T(4,128)(2,1)}), bf16[16,9,4,1536]{3,2,1,0:T(4,128)(2,1)S(1)}, u32[]{:S(2)}, u32[]{:S(2)}) async-start(bf16[16,9,4,1536]{3,2,1,0:T(4,128)(2,1)} %copy.110), calls=%async_computation.1 | async-start | bytes 3538944 | tf_op jit(solution)/shard_map/all_to_all | solution.py:169
  88.3 2.7 %convolution_bitcast_fusion.1 = f32[1,1,12,18,8,128]{5,4,3,2,1,0:T(8,128)} fusion(bf16[144,12,128]{2,1,0:T(8,128)(2,1)} %reshape.277, f32[12,144,144]{1,2,0:T(8,128)S(1)} %copy-done.7, f32[12,144]{1,0:T(8,128)} %get-tuple-element.31), kind=kOutput, calls=%fused_computation.27 | convolution fusion | flops 64198656 | bytes 2329344 | tf_op jit(solution)/shard_map/bfhij,bfjhe->bfihe/dot_general | solution.py:32
  91.0 0.5 multiply_reduce_fusion
  91.5 0.4 multiply_convert_fusion
  92.0 2.0 %collective-permute-start.7 = (f32[12,16]{1,0:T(8,128)S(1)}, f32[12,16]{1,0:T(8,128)S(1)}, u32[]{:S(2)}, u32[]{:S(2)}) collective-permute-start(f32[12,16]{1,0:T(8,128)S(1)} %add_add_fusion.1), channel_id=1, source_target_pairs={{0,32},{16,48},{32,0},{48,16},{64,96},{80,112},{96,64},{112,80},{1... | collective-permute-start | bytes 2312 | tf_op jit(solution)/shard_map/ppermute | solution.py:80
  94.1 0.4 fusion.8
  94.5 1.3 %collective-permute-done.7 = f32[12,16]{1,0:T(8,128)S(1)} collective-permute-done((f32[12,16]{1,0:T(8,128)S(1)}, f32[12,16]{1,0:T(8,128)S(1)}, u32[]{:S(2)}, u32[]{:S(2)}) %collective-permute-start.7) | collective-permute-done | bytes 800 | tf_op jit(solution)/shard_map/ppermute | solution.py:80
  95.8 1.4 %collective-permute-done.8 = f32[12,16]{1,0:T(8,128)S(1)} collective-permute-done((f32[12,16]{1,0:T(8,128)S(1)}, f32[12,16]{1,0:T(8,128)S(1)}, u32[]{:S(2)}, u32[]{:S(2)}) %collective-permute-start.8) | collective-permute-done | bytes 800 | tf_op jit(solution)/shard_map/ppermute | solution.py:80
  97.1 6.3 %collective-permute-start.10 = (f32[12,16]{1,0:T(8,128)S(1)}, f32[12,16]{1,0:T(8,128)S(1)}, u32[]{:S(2)}, u32[]{:S(2)}) collective-permute-start(f32[12,16]{1,0:T(8,128)S(1)} %add_add_fusion), channel_id=1, source_target_pairs={{0,128},{16,144},{32,160},{48,176},{64,192},{80,208},{96,224},{112... | collective-permute-start | bytes 2312 | tf_op jit(solution)/shard_map/ppermute | solution.py:80
  103.4 0.6 collective-permute-start.11
  103.9 0.9 collective-permute-start.9
  104.9 0.6 fusion.7
  105.5 3.7 %collective-permute-done.11 = f32[12,16]{1,0:T(8,128)S(1)} collective-permute-done((f32[12,16]{1,0:T(8,128)S(1)}, f32[12,16]{1,0:T(8,128)S(1)}, u32[]{:S(2)}, u32[]{:S(2)}) %collective-permute-start.11) | collective-permute-done | bytes 800 | tf_op jit(solution)/shard_map/ppermute | solution.py:80
  109.2 0.6 add_multiply_fusion
  109.8 0.5 convert_bitcast_fusion
  110.3 2.6 %fusion.65 = (f32[1,16,9,1536]{3,0,2,1:T(1,128)S(1)}, f32[1,16,9,1536]{3,0,2,1:T(1,128)S(1)}, f32[1,16,9,1536]{3,0,2,1:T(1,128)S(1)}, f32[1,16,9,1536]{3,0,2,1:T(1,128)S(1)}) fusion(f32[4,16,9,1536]{3,0,2,1:T(4,128)S(1)} %convert_bitcast_fusion), kind=kLoop, calls=%fused_computation.88 | loop fusion | bytes 7077888 | tf_op jit(solution)/shard_map/slice | solution.py:185
  112.9 1.2 %fusion.20 = (bf16[1,1,144,1536]{3,2,1,0:T(8,128)(2,1)}, bf16[1,1,144,1536]{3,2,1,0:T(8,128)(2,1)}) fusion(f32[1,1,12,18,8,128]{5,4,3,2,1,0:T(8,128)S(1)} %copy-done.13, f32[1,1,144,1536]{3,0,2,1:T(1,128)S(1)} %bitcast.123, f32[1,1,144,1536]{3,0,2,1:T(1,128)S(1)} %bitcast.124, f32[1,1,12,18,8,128]{5,4,3,2,1,0:T(8,128)S(1)} %fusion.8), kind=kLoop, calls=%fused_computation.39 | loop fusion | flops 884736 | bytes 4423680 | tf_op jit(solution)/shard_map/convert_element_type | solution.py:185
  114.1 1.1 fusion.22
  (52 shorter events, 0.3 us)
Async XLA Ops:
  0.6 25.6 %copy-start = (f32[12,16]{1,0:T(8,128)S(1)}, f32[12,16]{1,0:T(8,128)}, u32[]{:S(2)}) copy-start(f32[12,16]{1,0:T(8,128)} %param.13) | copy-start | bytes 2308
  0.6 5.5 %copy-start.11 = (bf16[1,1,144,1536]{3,2,1,0:T(8,128)(2,1)S(1)}, bf16[1,1,144,1536]{3,2,1,0:T(8,128)(2,1)}, u32[]{:S(2)}) copy-start(bf16[1,1,144,1536]{3,2,1,0:T(8,128)(2,1)} %param.9) | copy-start | bytes 1327108
  14.2 7.6 %copy-start.9 = (bf16[1,1,144,1536]{3,2,1,0:T(8,128)(2,1)S(1)}, bf16[1,1,144,1536]{3,2,1,0:T(8,128)(2,1)}, u32[]{:S(2)}) copy-start(bf16[1,1,144,1536]{3,2,1,0:T(8,128)(2,1)} %param.7) | copy-start | bytes 1327108
  14.2 7.9 %copy-start.10 = (bf16[1,1,144,1536]{3,2,1,0:T(8,128)(2,1)S(1)}, bf16[1,1,144,1536]{3,2,1,0:T(8,128)(2,1)}, u32[]{:S(2)}) copy-start(bf16[1,1,144,1536]{3,2,1,0:T(8,128)(2,1)} %param.8) | copy-start | bytes 1327108
  14.2 30.8 %all-to-all-start = ((bf16[16,9,4,1536]{3,2,1,0:T(4,128)(2,1)}), bf16[16,9,4,1536]{3,2,1,0:T(4,128)(2,1)S(1)}, u32[]{:S(2)}, u32[]{:S(2)}) async-start(bf16[16,9,4,1536]{3,2,1,0:T(4,128)(2,1)} %pad_maximum_fusion), calls=%async_computation | async-start | bytes 3538944 | tf_op jit(solution)/shard_map/all_to_all | solution.py:112
  22.1 12.5 %copy-start.5 = (bf16[144,12,128]{2,1,0:T(8,128)(2,1)}, bf16[144,12,128]{2,1,0:T(8,128)(2,1)S(1)}, u32[]{:S(2)}) copy-start(bf16[144,12,128]{2,1,0:T(8,128)(2,1)S(1)} %reshape.275) | copy-start | bytes 1327108
  22.5 12.2 %copy-start.3 = (bf16[144,12,128]{2,1,0:T(8,128)(2,1)}, bf16[144,12,128]{2,1,0:T(8,128)(2,1)S(1)}, u32[]{:S(2)}) copy-start(bf16[144,12,128]{2,1,0:T(8,128)(2,1)S(1)} %reshape.276) | copy-start | bytes 1327108
  26.2 8.5 %copy-start.16 = (bf16[144,12,128]{2,1,0:T(8,128)(2,1)}, bf16[144,12,128]{2,1,0:T(8,128)(2,1)S(1)}, u32[]{:S(2)}) copy-start(bf16[144,12,128]{2,1,0:T(8,128)(2,1)S(1)} %reshape.279) | copy-start | bytes 1327108
  45.0 1.3 %copy-start.2 = (bf16[16,9,4,1536]{3,2,1,0:T(4,128)(2,1)}, bf16[16,9,4,1536]{3,2,1,0:T(4,128)(2,1)S(1)}, u32[]{:S(2)}) copy-start(bf16[16,9,4,1536]{3,2,1,0:T(4,128)(2,1)S(1)} %all-to-all-done.x_ref) | copy-start | bytes 5308420
  53.5 2.6 %copy-start.1 = (bf16[4,9,12,16,128]{4,3,2,1,0:T(8,128)(2,1)S(1)}, bf16[4,9,12,16,128]{4,3,2,1,0:T(8,128)(2,1)}, u32[]{:S(2)}) copy-start(bf16[4,9,12,16,128]{4,3,2,1,0:T(8,128)(2,1)} %shard_map.110) | copy-start | bytes 5308420
  59.7 5.9 %collective-permute-start = (f32[12,16]{1,0:T(8,128)S(1)}, f32[12,16]{1,0:T(8,128)S(1)}, u32[]{:S(2)}, u32[]{:S(2)}) collective-permute-start(f32[12,16]{1,0:T(8,128)S(1)} %convolution_bitcast_fusion.3), channel_id=1, source_target_pairs={{0,1},{1,0},{2,3},{3,2},{4,5},{5,4},{6,7},{7,6},{8,9},{9,8},{10,11... | collective-permute-start | bytes 2312 | tf_op jit(solution)/shard_map/ppermute | solution.py:80
  60.4 5.2 %collective-permute-start.1 = (f32[12,16]{1,0:T(8,128)S(1)}, f32[12,16]{1,0:T(8,128)S(1)}, u32[]{:S(2)}, u32[]{:S(2)}) collective-permute-start(f32[12,16]{1,0:T(8,128)S(1)} %convolution_bitcast_fusion.3), channel_id=1, source_target_pairs={{0,2},{1,3},{2,0},{3,1},{4,6},{5,7},{6,4},{7,5},{8,10},{9,11},{10,... | collective-permute-start | bytes 2312 | tf_op jit(solution)/shard_map/ppermute | solution.py:80
  63.9 3.7 %collective-permute-start.2 = (f32[12,16]{1,0:T(8,128)S(1)}, f32[12,16]{1,0:T(8,128)S(1)}, u32[]{:S(2)}, u32[]{:S(2)}) collective-permute-start(f32[12,16]{1,0:T(8,128)S(1)} %convolution_bitcast_fusion.3), channel_id=1, source_target_pairs={{0,3},{1,2},{2,1},{3,0},{4,7},{5,6},{6,5},{7,4},{8,11},{9,10},{10,... | collective-permute-start | bytes 2312 | tf_op jit(solution)/shard_map/ppermute | solution.py:80
  67.5 5.5 %copy-start.12 = (bf16[9,12,16,128]{3,2,1,0:T(8,128)(2,1)S(1)}, bf16[9,12,16,128]{3,2,1,0:T(8,128)(2,1)}, u32[]{:S(2)}) copy-start(bf16[9,12,16,128]{3,2,1,0:T(8,128)(2,1)} %get-tuple-element.18) | copy-start | bytes 1327108
  67.5 10.1 %collective-permute-start.3 = (f32[12,16]{1,0:T(8,128)S(1)}, f32[12,16]{1,0:T(8,128)S(1)}, u32[]{:S(2)}, u32[]{:S(2)}) collective-permute-start(f32[12,16]{1,0:T(8,128)S(1)} %add_add_fusion.2), channel_id=1, source_target_pairs={{0,4},{1,5},{2,6},{3,7},{4,0},{5,1},{6,2},{7,3},{8,12},{9,13},{10,... | collective-permute-start | bytes 2312 | tf_op jit(solution)/shard_map/ppermute | solution.py:80
  67.6 10.1 %collective-permute-start.4 = (f32[12,16]{1,0:T(8,128)S(1)}, f32[12,16]{1,0:T(8,128)S(1)}, u32[]{:S(2)}, u32[]{:S(2)}) collective-permute-start(f32[12,16]{1,0:T(8,128)S(1)} %add_add_fusion.2), channel_id=1, source_target_pairs={{0,8},{1,9},{2,10},{3,11},{4,12},{5,13},{6,14},{7,15},{8,0},{9,1},... | collective-permute-start | bytes 2312 | tf_op jit(solution)/shard_map/ppermute | solution.py:80
  70.3 7.3 %collective-permute-start.5 = (f32[12,16]{1,0:T(8,128)S(1)}, f32[12,16]{1,0:T(8,128)S(1)}, u32[]{:S(2)}, u32[]{:S(2)}) collective-permute-start(f32[12,16]{1,0:T(8,128)S(1)} %add_add_fusion.2), channel_id=1, source_target_pairs={{0,12},{1,13},{2,14},{3,15},{4,8},{5,9},{6,10},{7,11},{8,4},{9,5},... | collective-permute-start | bytes 2312 | tf_op jit(solution)/shard_map/ppermute | solution.py:80
  76.4 1.0 copy-start.8
  80.3 8.0 %copy-start.7 = (f32[12,144,144]{1,2,0:T(8,128)S(1)}, f32[12,144,144]{1,2,0:T(8,128)}, u32[]{:S(2)}) copy-start(f32[12,144,144]{1,2,0:T(8,128)} %get-tuple-element.32) | copy-start | bytes 2985988
  80.3 29.5 %all-to-all-start.1 = ((bf16[16,9,4,1536]{3,2,1,0:T(4,128)(2,1)}), bf16[16,9,4,1536]{3,2,1,0:T(4,128)(2,1)S(1)}, u32[]{:S(2)}, u32[]{:S(2)}) async-start(bf16[16,9,4,1536]{3,2,1,0:T(4,128)(2,1)} %copy.110), calls=%async_computation.1 | async-start | bytes 3538944 | tf_op jit(solution)/shard_map/all_to_all | solution.py:169
  88.3 2.7 %copy-start.15 = (bf16[144,12,128]{2,1,0:T(8,128)(2,1)S(1)}, bf16[144,12,128]{2,1,0:T(8,128)(2,1)}, u32[]{:S(2)}) copy-start(bf16[144,12,128]{2,1,0:T(8,128)(2,1)} %reshape.277) | copy-start | bytes 1327108
  88.3 2.7 %copy-start.17 = (bf16[144,12,128]{2,1,0:T(8,128)(2,1)S(1)}, bf16[144,12,128]{2,1,0:T(8,128)(2,1)}, u32[]{:S(2)}) copy-start(bf16[144,12,128]{2,1,0:T(8,128)(2,1)} %copy-done.16) | copy-start | bytes 1327108
  88.3 2.7 %copy-start.18 = (f32[12,144]{1,0:T(8,128)S(1)}, f32[12,144]{1,0:T(8,128)}, u32[]{:S(2)}) copy-start(f32[12,144]{1,0:T(8,128)} %get-tuple-element.31) | copy-start | bytes 20740
  91.5 2.6 %copy-start.6 = (bf16[144,12,128]{2,1,0:T(8,128)(2,1)S(1)}, bf16[144,12,128]{2,1,0:T(8,128)(2,1)}, u32[]{:S(2)}) copy-start(bf16[144,12,128]{2,1,0:T(8,128)(2,1)} %copy-done.5) | copy-start | bytes 1327108
  91.9 13.0 %copy-start.4 = (bf16[144,12,128]{2,1,0:T(8,128)(2,1)S(1)}, bf16[144,12,128]{2,1,0:T(8,128)(2,1)}, u32[]{:S(2)}) copy-start(bf16[144,12,128]{2,1,0:T(8,128)(2,1)} %copy-done.3) | copy-start | bytes 1327108
  91.9 2.5 %collective-permute-start.6 = (f32[12,16]{1,0:T(8,128)S(1)}, f32[12,16]{1,0:T(8,128)S(1)}, u32[]{:S(2)}, u32[]{:S(2)}) collective-permute-start(f32[12,16]{1,0:T(8,128)S(1)} %add_add_fusion.1), channel_id=1, source_target_pairs={{0,16},{16,0},{32,48},{48,32},{64,80},{80,64},{96,112},{112,96},{1... | collective-permute-start | bytes 2312 | tf_op jit(solution)/shard_map/ppermute | solution.py:80
  92.0 3.7 %collective-permute-start.7 = (f32[12,16]{1,0:T(8,128)S(1)}, f32[12,16]{1,0:T(8,128)S(1)}, u32[]{:S(2)}, u32[]{:S(2)}) collective-permute-start(f32[12,16]{1,0:T(8,128)S(1)} %add_add_fusion.1), channel_id=1, source_target_pairs={{0,32},{16,48},{32,0},{48,16},{64,96},{80,112},{96,64},{112,80},{1... | collective-permute-start | bytes 2312 | tf_op jit(solution)/shard_map/ppermute | solution.py:80
  94.0 3.1 %collective-permute-start.8 = (f32[12,16]{1,0:T(8,128)S(1)}, f32[12,16]{1,0:T(8,128)S(1)}, u32[]{:S(2)}, u32[]{:S(2)}) collective-permute-start(f32[12,16]{1,0:T(8,128)S(1)} %add_add_fusion.1), channel_id=1, source_target_pairs={{0,48},{16,32},{32,16},{48,0},{64,112},{80,96},{96,80},{112,64},{1... | collective-permute-start | bytes 2312 | tf_op jit(solution)/shard_map/ppermute | solution.py:80
  97.1 8.3 %collective-permute-start.10 = (f32[12,16]{1,0:T(8,128)S(1)}, f32[12,16]{1,0:T(8,128)S(1)}, u32[]{:S(2)}, u32[]{:S(2)}) collective-permute-start(f32[12,16]{1,0:T(8,128)S(1)} %add_add_fusion), channel_id=1, source_target_pairs={{0,128},{16,144},{32,160},{48,176},{64,192},{80,208},{96,224},{112... | collective-permute-start | bytes 2312 | tf_op jit(solution)/shard_map/ppermute | solution.py:80
  103.4 5.8 %collective-permute-start.11 = (f32[12,16]{1,0:T(8,128)S(1)}, f32[12,16]{1,0:T(8,128)S(1)}, u32[]{:S(2)}, u32[]{:S(2)}) collective-permute-start(f32[12,16]{1,0:T(8,128)S(1)} %add_add_fusion), channel_id=1, source_target_pairs={{0,192},{16,208},{32,224},{48,240},{64,128},{80,144},{96,160},{112... | collective-permute-start | bytes 2312 | tf_op jit(solution)/shard_map/ppermute | solution.py:80
  103.9 5.2 %collective-permute-start.9 = (f32[12,16]{1,0:T(8,128)S(1)}, f32[12,16]{1,0:T(8,128)S(1)}, u32[]{:S(2)}, u32[]{:S(2)}) collective-permute-start(f32[12,16]{1,0:T(8,128)S(1)} %add_add_fusion), channel_id=1, source_target_pairs={{0,64},{16,80},{32,96},{48,112},{64,0},{80,16},{96,32},{112,48},{1... | collective-permute-start | bytes 2312 | tf_op jit(solution)/shard_map/ppermute | solution.py:80
  110.3 2.7 %copy-start.13 = (f32[1,1,12,18,8,128]{5,4,3,2,1,0:T(8,128)S(1)}, f32[1,1,12,18,8,128]{5,4,3,2,1,0:T(8,128)}, u32[]{:S(2)}) copy-start(f32[1,1,12,18,8,128]{5,4,3,2,1,0:T(8,128)} %convolution_bitcast_fusion) | copy-start | bytes 2654212
  112.9 1.2 %copy-start.14 = (f32[1,1,12,18,8,128]{5,4,3,2,1,0:T(8,128)S(1)}, f32[1,1,12,18,8,128]{5,4,3,2,1,0:T(8,128)}, u32[]{:S(2)}) copy-start(f32[1,1,12,18,8,128]{5,4,3,2,1,0:T(8,128)} %convolution_bitcast_fusion.1) | copy-start | bytes 2654212

commit v6 on v4

--- a/solution.py
+++ b/solution.py
@@ -116,13 +116,18 @@
     )
     partial = quad_step(bias_part, "seq", seq_size, 1)
     shares_half = shares.astype(jnp.bfloat16)
-    score_half = score_grad.astype(jnp.bfloat16)
     result = jnp.einsum(
         TIME_PATTERNS[1], shares_half, value_part, preferred_element_type=jnp.float32
     )
     time_value_grad = jnp.einsum(
         TIME_PATTERNS[2], shares_half, slope_part, preferred_element_type=jnp.float32
     )
+    partial, result, time_value_grad, score_grad, query_part, key_part = (
+        lax.optimization_barrier(
+            (partial, result, time_value_grad, score_grad, query_part, key_part)
+        )
+    )
+    score_half = score_grad.astype(jnp.bfloat16)
     time_query_grad = (
         jnp.einsum(TIME_PATTERNS[1], score_half, key_part, preferred_element_type=jnp.float32)
         * scaling

time: 108 us -> 109 us (level)
  the two profiles are of different devices: /device:TPU:4 before, /device:TPU:160 now
where the time goes in v6:
time: 109 us; the launch traced here: 108 us
  starting transfers between devices  29 us (27%)
  waiting for transfers between devices  28.7 us (26%)
  local copies, waits for them, and re-layouts  23.9 us (22%)
  matrix products  15.6 us (14%)
  other arithmetic  9.11 us (8%)
  between operations  1.84 us (2%)
    all_to_all x1, waiting for transfers between devices, on_device(): lax.all_to_all(stacked, 'seq', split_axis=0, concat_axis=0, tiled=True)  19 us
    ppermute x12, starting transfers between devices, quad_step(): lax.ppermute(value, axis, [(index, index ^ part * step) for index in rang...  18 us
    all_to_all x1, starting transfers between devices, on_device(): lax.all_to_all(stacked, 'seq', split_axis=0, concat_axis=0, tiled=True)  7.21 us
    another operation x5, local copies, waits for them, and re-layouts, on_device(): jnp.stack([tensor.reshape(seq_size, block, width) for tensor in (queries,...  6.65 us
    reshape x2, local copies, waits for them, and re-layouts, on_device(): rows = rows.reshape(seq_size, block, 4, head_count, width // head_count)  5.45 us
    all_to_all x1, waiting for transfers between devices, on_device(): lax.all_to_all(back_rows, 'seq', split_axis=0, concat_axis=0, tiled=True)  5.29 us
    ppermute x12, waiting for transfers between devices, quad_step(): lax.ppermute(value, axis, [(index, index ^ part * step) for index in rang...  4.44 us
    all_to_all x1, starting transfers between devices, on_device(): lax.all_to_all(back_rows, 'seq', split_axis=0, concat_axis=0, tiled=True)  3.84 us
  transfers between devices with their start and end apart: 14, of which 6 were waited for; matrix products, arithmetic and copies ran while one was open for 19% of the time, Pallas kernels for 0%

profile of v6, /device:TPU:160, one launch (start us, length us, event | category | flops | bytes accessed | tf_op | source)
XLA Modules:
  0.0 108.3 jit_solution(4151164306109169732)
XLA Ops:
  0.7 1.2 %stack_reshape.24 = bf16[16,9,1,1536]{3,1,0,2:T(8,128)(2,1)S(1)} reshape(bf16[1,1,144,1536]{3,2,1,0:T(8,128)(2,1)} %param.7) | data formatting | bytes 884736 | tf_op jit(solution)/shard_map/stack;reshape | solution.py:85
  1.9 1.2 %stack_reshape.25 = bf16[16,9,1,1536]{3,1,0,2:T(8,128)(2,1)S(1)} reshape(bf16[1,1,144,1536]{3,2,1,0:T(8,128)(2,1)} %param.8) | data formatting | bytes 884736 | tf_op jit(solution)/shard_map/stack;reshape | solution.py:85
  3.1 0.2 stack_reshape.26
  3.3 1.2 %stack_reshape.27 = bf16[16,9,1,1536]{3,1,0,2:T(8,128)(2,1)S(1)} reshape(bf16[1,1,144,1536]{3,2,1,0:T(8,128)(2,1)} %param.10) | data formatting | bytes 884736 | tf_op jit(solution)/shard_map/stack;reshape | solution.py:85
  4.5 0.6 pad_maximum_fusion
  5.1 2.8 %copy.94 = bf16[16,9,4,1536]{3,2,1,0:T(4,128)(2,1)} copy(bf16[16,9,4,1536]{3,1,0,2:T(8,128)(2,1)S(1)} %pad_maximum_fusion) | data formatting | bytes 3538944 | tf_op jit(solution)/shard_map/stack | solution.py:85
  8.0 7.2 %all-to-all-start = ((bf16[16,9,4,1536]{3,2,1,0:T(4,128)(2,1)}), bf16[16,9,4,1536]{3,2,1,0:T(4,128)(2,1)}, u32[]{:S(2)}, u32[]{:S(2)}) async-start(bf16[16,9,4,1536]{3,2,1,0:T(4,128)(2,1)} %copy.94), calls=%async_computation | async-start | bytes 3538944 | tf_op jit(solution)/shard_map/all_to_all | solution.py:92
  15.2 0.3 reshape.278
  15.6 0.3 reshape.279
  15.9 0.3 copy-done.10
  16.2 1.1 %reshape.280 = bf16[144,12,128]{2,1,0:T(8,128)(2,1)} reshape(bf16[1,1,144,1536]{3,2,1,0:T(8,128)(2,1)S(1)} %copy-done.10) | data formatting | bytes 884736 | tf_op jit(solution)/shard_map/reshape.7
  17.3 1.1 %reshape.283 = bf16[144,12,128]{2,1,0:T(8,128)(2,1)} reshape(bf16[1,1,144,1536]{3,2,1,0:T(8,128)(2,1)S(1)} %copy-done.11) | data formatting | bytes 884736 | tf_op jit(solution)/shard_map/reshape.22
  18.5 0.3 convolution_bitcast_fusion.2
  18.7 0.2 copy.98
  19.7 0.8 fusion.63
  20.5 2.8 %convolution_bitcast_fusion = f32[1,1,12,18,8,128]{5,4,3,2,1,0:T(8,128)} fusion(bf16[144,12,128]{2,1,0:T(8,128)(2,1)} %reshape.283, f32[12,144,144]{1,2,0:T(8,128)S(1)} %get-tuple-element.28, f32[12,144]{1,0:T(8,128)S(1)} %get-tuple-element.27), kind=kOutput, calls=%fused_computation.25 | convolution fusion | flops 64198656 | bytes 2329344 | tf_op jit(solution)/shard_map/bfhij,bfihe->bfjhe/dot_general | solution.py:39
  23.3 19.0 %all-to-all-done = bf16[16,9,4,1536]{3,2,1,0:T(4,128)(2,1)} async-done(((bf16[16,9,4,1536]{3,2,1,0:T(4,128)(2,1)}), bf16[16,9,4,1536]{3,2,1,0:T(4,128)(2,1)}, u32[]{:S(2)}, u32[]{:S(2)}) %all-to-all-start) | async-done | bytes 1769504 | tf_op jit(solution)/shard_map/all_to_all | solution.py:92
  42.3 3.4 %reshape.289 = bf16[16,9,4,12,128]{4,3,2,1,0:T(8,128)(2,1)S(1)} reshape(bf16[16,9,4,1536]{3,2,1,0:T(4,128)(2,1)} %all-to-all-done) | data formatting | bytes 3538944 | tf_op jit(solution)/shard_map/reshape | solution.py:93
  45.7 2.1 %copy.176 = bf16[16,9,4,12,128]{4,0,3,1,2:T(8,128)(2,1)S(1)} copy(bf16[16,9,4,12,128]{4,3,2,1,0:T(8,128)(2,1)S(1)} %reshape.289) | data formatting | bytes 3538944 | tf_op jit(solution)/shard_map/reshape | solution.py:93
  47.8 0.4 fusion.27
  48.2 0.4 fusion.11
  48.5 0.5 copy-done.1
  49.0 3.4 %fusion.68 = (f32[9,12,16]{2,1,0:T(8,128)S(1)}, f32[9,12,16,16]{2,3,1,0:T(8,128)S(1)}) fusion(f32[9,12,16,16]{2,3,1,0:T(8,128)S(1)} %fusion.11), kind=kOutput, calls=%fused_computation.89 | output fusion | flops 55311 | bytes 228096 | tf_op jit(solution)/shard_map/sub | solution.py:104
  52.4 1.1 %fusion.69 = (f32[12,16,16]{1,2,0:T(8,128)S(1)}, bf16[9,12,16,16]{2,3,1,0:T(8,128)(2,1)}) fusion(f32[9,12,16,16]{2,3,1,0:T(8,128)S(1)} %fusion.27, f32[9,12,16,16]{2,3,1,0:T(8,128)S(1)} %get-tuple-element.30, f32[9,12,16]{2,1,0:T(8,128)S(1)} %get-tuple-element.29), kind=kOutput, calls=%fused_computation.90 | output fusion | flops 192207 | bytes 295680 | tf_op jit(solution)/shard_map/sub | solution.py:110
  53.7 0.9 convolution_bitcast_fusion.3
  54.6 0.2 collective-permute-start.1
  54.8 4.5 %collective-permute-start.2 = (f32[12,16]{1,0:T(8,128)S(1)}, f32[12,16]{1,0:T(8,128)S(1)}, u32[]{:S(2)}, u32[]{:S(2)}) collective-permute-start(f32[12,16]{1,0:T(8,128)S(1)} %convolution_bitcast_fusion.3), channel_id=1, source_target_pairs={{0,3},{1,2},{2,1},{3,0},{4,7},{5,6},{6,5},{7,4},{8,11},{9,10},{10,... | collective-permute-start | bytes 2312 | tf_op jit(solution)/shard_map/ppermute | solution.py:60
  59.3 1.2 %fusion.26 = bf16[9,12,16,128]{3,2,1,0:T(8,128)(2,1)} fusion(bf16[4,9,12,16,128]{4,3,2,1,0:T(8,128)(2,1)S(1)} %bitcast.123, f32[9,12,16]{2,1,0:T(8,128)S(1)} %get-tuple-element.29, f32[9,12,16,16]{2,3,1,0:T(8,128)S(1)} %fusion.11), kind=kOutput, calls=%fused_computation.56 | convolution fusion | flops 7162575 | bytes 2727936 | tf_op jit(solution)/shard_map/phij,phie->phje/dot_general | solution.py:122
  60.5 0.2 slice_bitcast_fusion.2
  60.6 2.7 %fusion.28 = bf16[9,12,16,128]{3,2,1,0:T(8,128)(2,1)} fusion(bf16[4,9,12,16,128]{4,3,2,1,0:T(8,128)(2,1)S(1)} %bitcast.125, f32[9,12,16]{2,1,0:T(8,128)S(1)} %get-tuple-element.29, f32[9,12,16,16]{2,3,1,0:T(8,128)} %copy-done.13), kind=kOutput, calls=%fused_computation.58 | convolution fusion | flops 7162575 | bytes 2727936 | tf_op jit(solution)/shard_map/phij,phje->phie/dot_general | solution.py:119
  63.4 0.2 collective-permute-start.3
  63.5 2.7 %collective-permute-start.4 = (f32[12,16]{1,0:T(8,128)S(1)}, f32[12,16]{1,0:T(8,128)S(1)}, u32[]{:S(2)}, u32[]{:S(2)}) collective-permute-start(f32[12,16]{1,0:T(8,128)S(1)} %add_add_fusion.2), channel_id=1, source_target_pairs={{0,8},{1,9},{2,10},{3,11},{4,12},{5,13},{6,14},{7,15},{8,0},{9,1},... | collective-permute-start | bytes 2312 | tf_op jit(solution)/shard_map/ppermute | solution.py:60
  66.2 1.9 %collective-permute-start.5 = (f32[12,16]{1,0:T(8,128)S(1)}, f32[12,16]{1,0:T(8,128)S(1)}, u32[]{:S(2)}, u32[]{:S(2)}) collective-permute-start(f32[12,16]{1,0:T(8,128)S(1)} %add_add_fusion.2), channel_id=1, source_target_pairs={{0,12},{1,13},{2,14},{3,15},{4,8},{5,9},{6,10},{7,11},{8,4},{9,5},... | collective-permute-start | bytes 2312 | tf_op jit(solution)/shard_map/ppermute | solution.py:60
  68.2 1.3 %fusion.15 = bf16[16,9,12,128]{3,0,2,1:T(8,128)(2,1)S(1)} fusion(bf16[9,12,16,128]{3,2,1,0:T(8,128)(2,1)S(1)} %get-tuple-element.16, bf16[9,12,16,16]{2,3,1,0:T(8,128)(2,1)} %get-tuple-element.15), kind=kOutput, calls=%fused_computation.30 | convolution fusion | flops 7520256 | bytes 940032 | tf_op jit(solution)/shard_map/phij,phje->phie/dot_general | solution.py:132
  69.5 0.1 copy.103
  69.6 0.3 stack_reshape.29
  70.0 0.4 fusion.14
  70.3 0.1 copy.104
  70.5 0.3 stack_reshape.30
  70.8 0.5 copy-done.19
  71.5 0.3 stack_reshape.28
  72.0 0.3 stack_reshape.31
  72.3 0.2 pad_maximum_fusion.1
  72.5 2.6 %copy.106 = bf16[16,9,4,1536]{3,2,1,0:T(4,128)(2,1)} copy(bf16[16,9,4,1536]{3,0,1,2:T(8,128)(2,1)S(1)} %pad_maximum_fusion.1) | data formatting | bytes 3538944 | tf_op jit(solution)/shard_map/optimization_barrier | solution.py:147
  75.1 3.8 %all-to-all-start.1 = ((bf16[16,9,4,1536]{3,2,1,0:T(4,128)(2,1)}), bf16[16,9,4,1536]{3,2,1,0:T(4,128)(2,1)S(1)}, u32[]{:S(2)}, u32[]{:S(2)}) async-start(bf16[16,9,4,1536]{3,2,1,0:T(4,128)(2,1)} %copy.106), calls=%async_computation.1 | async-start | bytes 3538944 | tf_op jit(solution)/shard_map/all_to_all | solution.py:150
  79.0 3.1 %convolution_bitcast_fusion.1 = f32[1,1,12,18,8,128]{5,4,3,2,1,0:T(8,128)} fusion(bf16[144,12,128]{2,1,0:T(8,128)(2,1)S(1)} %copy-done.16, f32[12,144,144]{1,2,0:T(8,128)} %copy-done.5, f32[12,144]{1,0:T(8,128)S(1)} %copy-done.22), kind=kOutput, calls=%fused_computation.26 | convolution fusion | flops 64198656 | bytes 2329344 | tf_op jit(solution)/shard_map/bfhij,bfjhe->bfihe/dot_general | solution.py:31
  82.2 0.5 multiply_reduce_fusion
  82.7 0.3 multiply_convert_fusion
  83.1 1.1 %collective-permute-start.7 = (f32[12,16]{1,0:T(8,128)S(1)}, f32[12,16]{1,0:T(8,128)S(1)}, u32[]{:S(2)}, u32[]{:S(2)}) collective-permute-start(f32[12,16]{1,0:T(8,128)S(1)} %add_add_fusion.1), channel_id=1, source_target_pairs={{0,32},{16,48},{32,0},{48,16},{64,96},{80,112},{96,64},{112,80},{1... | collective-permute-start | bytes 2312 | tf_op jit(solution)/shard_map/ppermute | solution.py:60
  84.2 0.8 collective-permute-start.8
  85.0 0.4 fusion.6
  85.4 1.5 %collective-permute-done.7 = f32[12,16]{1,0:T(8,128)S(1)} collective-permute-done((f32[12,16]{1,0:T(8,128)S(1)}, f32[12,16]{1,0:T(8,128)S(1)}, u32[]{:S(2)}, u32[]{:S(2)}) %collective-permute-start.7) | collective-permute-done | bytes 800 | tf_op jit(solution)/shard_map/ppermute | solution.py:60
  86.9 0.4 collective-permute-done.8
  87.3 5.1 %collective-permute-start.11 = (f32[12,16]{1,0:T(8,128)S(1)}, f32[12,16]{1,0:T(8,128)S(1)}, u32[]{:S(2)}, u32[]{:S(2)}) collective-permute-start(f32[12,16]{1,0:T(8,128)S(1)} %add_add_fusion), channel_id=1, source_target_pairs={{0,192},{16,208},{32,224},{48,240},{64,128},{80,144},{96,160},{112... | collective-permute-start | bytes 2312 | tf_op jit(solution)/shard_map/ppermute | solution.py:60
  92.4 1.4 %collective-permute-start.9 = (f32[12,16]{1,0:T(8,128)S(1)}, f32[12,16]{1,0:T(8,128)S(1)}, u32[]{:S(2)}, u32[]{:S(2)}) collective-permute-start(f32[12,16]{1,0:T(8,128)S(1)} %add_add_fusion), channel_id=1, source_target_pairs={{0,64},{16,80},{32,96},{48,112},{64,0},{80,16},{96,32},{112,48},{1... | collective-permute-start | bytes 2312 | tf_op jit(solution)/shard_map/ppermute | solution.py:60
  93.8 0.6 fusion.5
  94.4 0.5 collective-permute-done.10
  94.9 2.0 %collective-permute-done.9 = f32[12,16]{1,0:T(8,128)S(1)} collective-permute-done((f32[12,16]{1,0:T(8,128)S(1)}, f32[12,16]{1,0:T(8,128)S(1)}, u32[]{:S(2)}, u32[]{:S(2)}) %collective-permute-start.9) | collective-permute-done | bytes 800 | tf_op jit(solution)/shard_map/ppermute | solution.py:60
  96.9 0.6 add_multiply_fusion
  97.5 5.3 %all-to-all-done.1 = bf16[16,9,4,1536]{3,2,1,0:T(4,128)(2,1)S(1)} async-done(((bf16[16,9,4,1536]{3,2,1,0:T(4,128)(2,1)}), bf16[16,9,4,1536]{3,2,1,0:T(4,128)(2,1)S(1)}, u32[]{:S(2)}, u32[]{:S(2)}) %all-to-all-start.1) | async-done | bytes 1769504 | tf_op jit(solution)/shard_map/all_to_all | solution.py:150
  102.8 0.5 convert_bitcast_fusion
  103.3 2.6 %fusion.62 = (f32[1,16,9,1536]{3,0,2,1:T(1,128)S(1)}, f32[1,16,9,1536]{3,0,2,1:T(1,128)S(1)}, f32[1,16,9,1536]{3,0,2,1:T(1,128)S(1)}, f32[1,16,9,1536]{3,0,2,1:T(1,128)S(1)}) fusion(f32[4,16,9,1536]{3,0,2,1:T(4,128)S(1)} %convert_bitcast_fusion), kind=kLoop, calls=%fused_computation.87 | loop fusion | bytes 7077888 | tf_op jit(solution)/shard_map/slice | solution.py:166
  106.0 1.1 %fusion.16 = (bf16[1,1,144,1536]{3,2,1,0:T(8,128)(2,1)}, bf16[1,1,144,1536]{3,2,1,0:T(8,128)(2,1)}) fusion(f32[1,1,12,18,8,128]{5,4,3,2,1,0:T(8,128)S(1)} %copy-done.14, f32[1,1,144,1536]{3,0,2,1:T(1,128)S(1)} %bitcast.128, f32[1,1,144,1536]{3,0,2,1:T(1,128)S(1)} %bitcast.129, f32[1,1,12,18,8,128]{5,4,3,2,1,0:T(8,128)S(1)} %fusion.6), kind=kLoop, calls=%fused_computation.34 | loop fusion | flops 884736 | bytes 4423680 | tf_op jit(solution)/shard_map/convert_element_type | solution.py:166
  107.2 1.1 %fusion.18 = (bf16[1,1,144,1536]{3,2,1,0:T(8,128)(2,1)}, bf16[1,1,144,1536]{3,2,1,0:T(8,128)(2,1)}) fusion(f32[1,1,12,18,8,128]{5,4,3,2,1,0:T(8,128)S(1)} %fusion.5, f32[1,1,144,1536]{3,0,2,1:T(1,128)S(1)} %bitcast.126, f32[1,1,144,1536]{3,0,2,1:T(1,128)S(1)} %bitcast.127, f32[1,1,12,18,8,128]{5,4,3,2,1,0:T(8,128)S(1)} %copy-done.15), kind=kLoop, calls=%fused_computation.38 | loop fusion | flops 884736 | bytes 4423680 | tf_op jit(solution)/shard_map/convert_element_type | solution.py:164
  (65 shorter events, 0.9 us)
Async XLA Ops:
  0.6 17.8 %copy-start = (f32[12,16]{1,0:T(8,128)S(1)}, f32[12,16]{1,0:T(8,128)}, u32[]{:S(2)}) copy-start(f32[12,16]{1,0:T(8,128)} %param.13) | copy-start | bytes 2308
  0.6 2.5 %copy-start.9 = (bf16[1,1,144,1536]{3,2,1,0:T(8,128)(2,1)S(1)}, bf16[1,1,144,1536]{3,2,1,0:T(8,128)(2,1)}, u32[]{:S(2)}) copy-start(bf16[1,1,144,1536]{3,2,1,0:T(8,128)(2,1)} %param.9) | copy-start | bytes 1327108
  8.0 7.2 %copy-start.7 = (bf16[1,1,144,1536]{3,2,1,0:T(8,128)(2,1)S(1)}, bf16[1,1,144,1536]{3,2,1,0:T(8,128)(2,1)}, u32[]{:S(2)}) copy-start(bf16[1,1,144,1536]{3,2,1,0:T(8,128)(2,1)} %param.7) | copy-start | bytes 1327108
  8.0 7.6 %copy-start.8 = (bf16[1,1,144,1536]{3,2,1,0:T(8,128)(2,1)S(1)}, bf16[1,1,144,1536]{3,2,1,0:T(8,128)(2,1)}, u32[]{:S(2)}) copy-start(bf16[1,1,144,1536]{3,2,1,0:T(8,128)(2,1)} %param.8) | copy-start | bytes 1327108
  8.0 34.4 %all-to-all-start = ((bf16[16,9,4,1536]{3,2,1,0:T(4,128)(2,1)}), bf16[16,9,4,1536]{3,2,1,0:T(4,128)(2,1)}, u32[]{:S(2)}, u32[]{:S(2)}) async-start(bf16[16,9,4,1536]{3,2,1,0:T(4,128)(2,1)} %copy.94), calls=%async_computation | async-start | bytes 3538944 | tf_op jit(solution)/shard_map/all_to_all | solution.py:92
  15.2 1.0 copy-start.10
  15.2 2.1 %copy-start.11 = (bf16[1,1,144,1536]{3,2,1,0:T(8,128)(2,1)S(1)}, bf16[1,1,144,1536]{3,2,1,0:T(8,128)(2,1)}, u32[]{:S(2)}) copy-start(bf16[1,1,144,1536]{3,2,1,0:T(8,128)(2,1)} %param.10) | copy-start | bytes 1327108
  15.5 4.1 %copy-start.23 = (s32[1,16]{1,0:T(1,128)S(1)}, s32[1,16]{1,0:T(1,128)}, u32[]{:S(2)}) copy-start(s32[1,16]{1,0:T(1,128)} %param.12) | copy-start | bytes 196
  16.2 4.3 %copy-start.3 = (bf16[144,12,128]{2,1,0:T(8,128)(2,1)}, bf16[144,12,128]{2,1,0:T(8,128)(2,1)S(1)}, u32[]{:S(2)}) copy-start(bf16[144,12,128]{2,1,0:T(8,128)(2,1)S(1)} %reshape.279) | copy-start | bytes 1327108
  18.5 1.1 %copy-start.20 = (s32[16,16]{1,0:T(8,128)}, s32[16,16]{1,0:T(8,128)S(1)}, u32[]{:S(2)}) copy-start(s32[16,16]{1,0:T(8,128)S(1)} %subtract_abs_fusion) | copy-start | bytes 3076
  20.5 2.9 %copy-start.5 = (f32[12,144,144]{1,2,0:T(8,128)}, f32[12,144,144]{1,2,0:T(8,128)S(1)}, u32[]{:S(2)}) copy-start(f32[12,144,144]{1,2,0:T(8,128)S(1)} %get-tuple-element.28) | copy-start | bytes 2985988
  20.5 2.9 %copy-start.21 = (f32[12,144]{1,0:T(8,128)}, f32[12,144]{1,0:T(8,128)S(1)}, u32[]{:S(2)}) copy-start(f32[12,144]{1,0:T(8,128)S(1)} %get-tuple-element.27) | copy-start | bytes 20740
  47.8 1.2 %copy-start.1 = (bf16[16,9,4,12,128]{4,0,3,1,2:T(8,128)(2,1)}, bf16[16,9,4,12,128]{4,0,3,1,2:T(8,128)(2,1)S(1)}, u32[]{:S(2)}) copy-start(bf16[16,9,4,12,128]{4,0,3,1,2:T(8,128)(2,1)S(1)} %copy.176) | copy-start | bytes 5308420
  49.0 10.3 %copy-start.13 = (f32[9,12,16,16]{2,3,1,0:T(8,128)}, f32[9,12,16,16]{2,3,1,0:T(8,128)S(1)}, u32[]{:S(2)}) copy-start(f32[9,12,16,16]{2,3,1,0:T(8,128)S(1)} %fusion.11) | copy-start | bytes 331780
  52.4 6.9 %copy-start.2 = (bf16[16,9,4,12,128]{4,0,3,1,2:T(8,128)(2,1)S(1)}, bf16[16,9,4,12,128]{4,0,3,1,2:T(8,128)(2,1)}, u32[]{:S(2)}) copy-start(bf16[16,9,4,12,128]{4,0,3,1,2:T(8,128)(2,1)} %copy-done.1) | copy-start | bytes 5308420
  54.5 8.8 %collective-permute-start = (f32[12,16]{1,0:T(8,128)S(1)}, f32[12,16]{1,0:T(8,128)S(1)}, u32[]{:S(2)}, u32[]{:S(2)}) collective-permute-start(f32[12,16]{1,0:T(8,128)S(1)} %convolution_bitcast_fusion.3), channel_id=1, source_target_pairs={{0,1},{1,0},{2,3},{3,2},{4,5},{5,4},{6,7},{7,6},{8,9},{9,8},{10,11... | collective-permute-start | bytes 2312 | tf_op jit(solution)/shard_map/ppermute | solution.py:60
  54.6 8.7 %collective-permute-start.1 = (f32[12,16]{1,0:T(8,128)S(1)}, f32[12,16]{1,0:T(8,128)S(1)}, u32[]{:S(2)}, u32[]{:S(2)}) collective-permute-start(f32[12,16]{1,0:T(8,128)S(1)} %convolution_bitcast_fusion.3), channel_id=1, source_target_pairs={{0,2},{1,3},{2,0},{3,1},{4,6},{5,7},{6,4},{7,5},{8,10},{9,11},{10,... | collective-permute-start | bytes 2312 | tf_op jit(solution)/shard_map/ppermute | solution.py:60
  54.8 8.6 %collective-permute-start.2 = (f32[12,16]{1,0:T(8,128)S(1)}, f32[12,16]{1,0:T(8,128)S(1)}, u32[]{:S(2)}, u32[]{:S(2)}) collective-permute-start(f32[12,16]{1,0:T(8,128)S(1)} %convolution_bitcast_fusion.3), channel_id=1, source_target_pairs={{0,3},{1,2},{2,1},{3,0},{4,7},{5,6},{6,5},{7,4},{8,11},{9,10},{10,... | collective-permute-start | bytes 2312 | tf_op jit(solution)/shard_map/ppermute | solution.py:60
  63.3 6.6 %copy-start.12 = (bf16[9,12,16,16]{2,3,1,0:T(8,128)(2,1)S(1)}, bf16[9,12,16,16]{2,3,1,0:T(8,128)(2,1)}, u32[]{:S(2)}) copy-start(bf16[9,12,16,16]{2,3,1,0:T(8,128)(2,1)} %get-tuple-element.15) | copy-start | bytes 165892
  63.4 9.1 %collective-permute-start.3 = (f32[12,16]{1,0:T(8,128)S(1)}, f32[12,16]{1,0:T(8,128)S(1)}, u32[]{:S(2)}, u32[]{:S(2)}) collective-permute-start(f32[12,16]{1,0:T(8,128)S(1)} %add_add_fusion.2), channel_id=1, source_target_pairs={{0,4},{1,5},{2,6},{3,7},{4,0},{5,1},{6,2},{7,3},{8,12},{9,13},{10,... | collective-permute-start | bytes 2312 | tf_op jit(solution)/shard_map/ppermute | solution.py:60
  63.5 9.0 %collective-permute-start.4 = (f32[12,16]{1,0:T(8,128)S(1)}, f32[12,16]{1,0:T(8,128)S(1)}, u32[]{:S(2)}, u32[]{:S(2)}) collective-permute-start(f32[12,16]{1,0:T(8,128)S(1)} %add_add_fusion.2), channel_id=1, source_target_pairs={{0,8},{1,9},{2,10},{3,11},{4,12},{5,13},{6,14},{7,15},{8,0},{9,1},... | collective-permute-start | bytes 2312 | tf_op jit(solution)/shard_map/ppermute | solution.py:60
  66.2 6.3 %collective-permute-start.5 = (f32[12,16]{1,0:T(8,128)S(1)}, f32[12,16]{1,0:T(8,128)S(1)}, u32[]{:S(2)}, u32[]{:S(2)}) collective-permute-start(f32[12,16]{1,0:T(8,128)S(1)} %add_add_fusion.2), channel_id=1, source_target_pairs={{0,12},{1,13},{2,14},{3,15},{4,8},{5,9},{6,10},{7,11},{8,4},{9,5},... | collective-permute-start | bytes 2312 | tf_op jit(solution)/shard_map/ppermute | solution.py:60
  70.3 1.0 copy-start.19
  70.5 1.3 %copy-start.18 = (bf16[9,12,16,128]{3,2,1,0:T(8,128)(2,1)S(1)}, bf16[9,12,16,128]{3,2,1,0:T(8,128)(2,1)}, u32[]{:S(2)}) copy-start(bf16[9,12,16,128]{3,2,1,0:T(8,128)(2,1)} %fusion.26) | copy-start | bytes 1327108
  75.1 3.9 %copy-start.16 = (bf16[144,12,128]{2,1,0:T(8,128)(2,1)S(1)}, bf16[144,12,128]{2,1,0:T(8,128)(2,1)}, u32[]{:S(2)}) copy-start(bf16[144,12,128]{2,1,0:T(8,128)(2,1)} %reshape.280) | copy-start | bytes 1327108
  75.1 3.9 %copy-start.22 = (f32[12,144]{1,0:T(8,128)S(1)}, f32[12,144]{1,0:T(8,128)}, u32[]{:S(2)}) copy-start(f32[12,144]{1,0:T(8,128)} %copy-done.21) | copy-start | bytes 20740
  75.1 27.7 %all-to-all-start.1 = ((bf16[16,9,4,1536]{3,2,1,0:T(4,128)(2,1)}), bf16[16,9,4,1536]{3,2,1,0:T(4,128)(2,1)S(1)}, u32[]{:S(2)}, u32[]{:S(2)}) async-start(bf16[16,9,4,1536]{3,2,1,0:T(4,128)(2,1)} %copy.106), calls=%async_computation.1 | async-start | bytes 3538944 | tf_op jit(solution)/shard_map/all_to_all | solution.py:150
  79.0 3.2 %copy-start.6 = (f32[12,144,144]{1,2,0:T(8,128)S(1)}, f32[12,144,144]{1,2,0:T(8,128)}, u32[]{:S(2)}) copy-start(f32[12,144,144]{1,2,0:T(8,128)} %copy-done.5) | copy-start | bytes 2985988
  79.0 3.2 %copy-start.17 = (bf16[144,12,128]{2,1,0:T(8,128)(2,1)S(1)}, bf16[144,12,128]{2,1,0:T(8,128)(2,1)}, u32[]{:S(2)}) copy-start(bf16[144,12,128]{2,1,0:T(8,128)(2,1)} %reshape.283) | copy-start | bytes 1327108
  83.0 10.8 %copy-start.4 = (bf16[144,12,128]{2,1,0:T(8,128)(2,1)S(1)}, bf16[144,12,128]{2,1,0:T(8,128)(2,1)}, u32[]{:S(2)}) copy-start(bf16[144,12,128]{2,1,0:T(8,128)(2,1)} %copy-done.3) | copy-start | bytes 1327108
  83.0 2.3 %collective-permute-start.6 = (f32[12,16]{1,0:T(8,128)S(1)}, f32[12,16]{1,0:T(8,128)S(1)}, u32[]{:S(2)}, u32[]{:S(2)}) collective-permute-start(f32[12,16]{1,0:T(8,128)S(1)} %add_add_fusion.1), channel_id=1, source_target_pairs={{0,16},{16,0},{32,48},{48,32},{64,80},{80,64},{96,112},{112,96},{1... | collective-permute-start | bytes 2312 | tf_op jit(solution)/shard_map/ppermute | solution.py:60
  83.1 3.7 %collective-permute-start.7 = (f32[12,16]{1,0:T(8,128)S(1)}, f32[12,16]{1,0:T(8,128)S(1)}, u32[]{:S(2)}, u32[]{:S(2)}) collective-permute-start(f32[12,16]{1,0:T(8,128)S(1)} %add_add_fusion.1), channel_id=1, source_target_pairs={{0,32},{16,48},{32,0},{48,16},{64,96},{80,112},{96,64},{112,80},{1... | collective-permute-start | bytes 2312 | tf_op jit(solution)/shard_map/ppermute | solution.py:60
  84.2 3.1 %collective-permute-start.8 = (f32[12,16]{1,0:T(8,128)S(1)}, f32[12,16]{1,0:T(8,128)S(1)}, u32[]{:S(2)}, u32[]{:S(2)}) collective-permute-start(f32[12,16]{1,0:T(8,128)S(1)} %add_add_fusion.1), channel_id=1, source_target_pairs={{0,48},{16,32},{32,16},{48,0},{64,112},{80,96},{96,80},{112,64},{1... | collective-permute-start | bytes 2312 | tf_op jit(solution)/shard_map/ppermute | solution.py:60
  87.3 7.6 %collective-permute-start.10 = (f32[12,16]{1,0:T(8,128)S(1)}, f32[12,16]{1,0:T(8,128)S(1)}, u32[]{:S(2)}, u32[]{:S(2)}) collective-permute-start(f32[12,16]{1,0:T(8,128)S(1)} %add_add_fusion), channel_id=1, source_target_pairs={{0,128},{16,144},{32,160},{48,176},{64,192},{80,208},{96,224},{112... | collective-permute-start | bytes 2312 | tf_op jit(solution)/shard_map/ppermute | solution.py:60
  87.3 7.6 %collective-permute-start.11 = (f32[12,16]{1,0:T(8,128)S(1)}, f32[12,16]{1,0:T(8,128)S(1)}, u32[]{:S(2)}, u32[]{:S(2)}) collective-permute-start(f32[12,16]{1,0:T(8,128)S(1)} %add_add_fusion), channel_id=1, source_target_pairs={{0,192},{16,208},{32,224},{48,240},{64,128},{80,144},{96,160},{112... | collective-permute-start | bytes 2312 | tf_op jit(solution)/shard_map/ppermute | solution.py:60
  92.4 4.6 %collective-permute-start.9 = (f32[12,16]{1,0:T(8,128)S(1)}, f32[12,16]{1,0:T(8,128)S(1)}, u32[]{:S(2)}, u32[]{:S(2)}) collective-permute-start(f32[12,16]{1,0:T(8,128)S(1)} %add_add_fusion), channel_id=1, source_target_pairs={{0,64},{16,80},{32,96},{48,112},{64,0},{80,16},{96,32},{112,48},{1... | collective-permute-start | bytes 2312 | tf_op jit(solution)/shard_map/ppermute | solution.py:60
  103.3 2.7 %copy-start.14 = (f32[1,1,12,18,8,128]{5,4,3,2,1,0:T(8,128)S(1)}, f32[1,1,12,18,8,128]{5,4,3,2,1,0:T(8,128)}, u32[]{:S(2)}) copy-start(f32[1,1,12,18,8,128]{5,4,3,2,1,0:T(8,128)} %convolution_bitcast_fusion) | copy-start | bytes 2654212
  106.0 1.2 %copy-start.15 = (f32[1,1,12,18,8,128]{5,4,3,2,1,0:T(8,128)S(1)}, f32[1,1,12,18,8,128]{5,4,3,2,1,0:T(8,128)}, u32[]{:S(2)}) copy-start(f32[1,1,12,18,8,128]{5,4,3,2,1,0:T(8,128)} %convolution_bitcast_fusion.1) | copy-start | bytes 2654212

commit v7 on v4

--- a/solution.py
+++ b/solution.py
@@ -85,27 +85,23 @@
     stacked = jnp.stack(
         [
             tensor.reshape(seq_size, block, width)
-            for tensor in (queries, keys, values, cotangent)
+            for tensor in (keys, values, queries, cotangent)
         ],
         axis=2,
     )
     rows = lax.all_to_all(stacked, "seq", split_axis=0, concat_axis=0, tiled=True)
     rows = rows.reshape(seq_size, block, 4, head_count, width // head_count)
     rows = jnp.transpose(rows, (2, 1, 3, 0, 4))
-    query_part, key_part, value_part, slope_part = rows[0], rows[1], rows[2], rows[3]
-    scaling = 1.0 / math.sqrt(query_part.shape[-1])
-    scores = (
-        jnp.einsum(TIME_PATTERNS[0], query_part, key_part, preferred_element_type=jnp.float32)
-        * scaling
-        + bias_table[0]
+    scaling = 1.0 / math.sqrt(rows.shape[-1])
+    pair = jnp.einsum(
+        "tphie,tphje->tphij", rows[2:4], rows[0:2], preferred_element_type=jnp.float32
     )
+    scores = pair[0] * scaling + bias_table[0]
     scores = jnp.where(same_clip[0], scores, -1e30)
     row_peak = jnp.max(scores, axis=-1, keepdims=True)
     weights = jnp.exp(scores - row_peak)
     shares = weights / jnp.sum(weights, axis=-1, keepdims=True)
-    share_grad = jnp.einsum(
-        TIME_PATTERNS[0], slope_part, value_part, preferred_element_type=jnp.float32
-    )
+    share_grad = pair[1]
     spread = jnp.sum(shares * share_grad, axis=-1, keepdims=True)
     score_grad = shares * (share_grad - spread)
     bias_part = jnp.tensordot(
@@ -115,29 +111,25 @@
         precision=lax.Precision.HIGHEST,
     )
     partial = quad_step(bias_part, "seq", seq_size, 1)
+    partial, shares, score_grad, rows = lax.optimization_barrier(
+        (partial, shares, score_grad, rows)
+    )
     shares_half = shares.astype(jnp.bfloat16)
     score_half = score_grad.astype(jnp.bfloat16)
-    result = jnp.einsum(
-        TIME_PATTERNS[1], shares_half, value_part, preferred_element_type=jnp.float32
+    mixers = jnp.stack(
+        [
+            score_half,
+            shares_half,
+            jnp.swapaxes(score_half, -1, -2),
+            jnp.swapaxes(shares_half, -1, -2),
+        ]
     )
-    time_value_grad = jnp.einsum(
-        TIME_PATTERNS[2], shares_half, slope_part, preferred_element_type=jnp.float32
-    )
-    time_query_grad = (
-        jnp.einsum(TIME_PATTERNS[1], score_half, key_part, preferred_element_type=jnp.float32)
-        * scaling
-    )
-    time_key_grad = (
-        jnp.einsum(TIME_PATTERNS[2], score_half, query_part, preferred_element_type=jnp.float32)
-        * scaling
-    )
+    outs = jnp.einsum("tphij,tphje->tphie", mixers, rows, preferred_element_type=jnp.float32)
+    factor = jnp.array([scaling, 1.0, scaling, 1.0], jnp.float32)[:, None, None, None, None]
+    outs = outs * factor
     partial = quad_step(partial, "seq", seq_size, 4)
-    back_rows = jnp.stack(
-        [
-            jnp.transpose(tensor.astype(jnp.bfloat16), (2, 0, 1, 3)).reshape(seq_size, block, width)
-            for tensor in (result, time_query_grad, time_key_grad, time_value_grad)
-        ],
-        axis=2,
+    back_rows = jnp.transpose(outs.astype(jnp.bfloat16), (3, 1, 0, 2, 4)).reshape(
+        seq_size, block, 4, width
     )
     partial, back_rows = lax.optimization_barrier((partial, back_rows))
     summed = quad_step(quad_step(partial, "dp", dp_size, 1), "dp", dp_size, 4)
@@ -155,8 +147,8 @@
     space_grads = attend_backward(
         SPACE_PATTERNS, space_query, space_key, space_value, space_slope, space_shares, space_half
     )
-    attended = (join_heads(space_out) + back[0]).astype(jnp.bfloat16)
-    query_grad = (join_heads(space_grads[0]) + back[1]).astype(jnp.bfloat16)
+    attended = (join_heads(space_out) + back[1]).astype(jnp.bfloat16)
+    query_grad = (join_heads(space_grads[0]) + back[0]).astype(jnp.bfloat16)
     key_grad = (join_heads(space_grads[1]) + back[2]).astype(jnp.bfloat16)
     value_grad = (join_heads(space_grads[2]) + back[3]).astype(jnp.bfloat16)
     return (attended, query_grad, key_grad, value_grad, bias_grad)

time: 108 us -> 117 us (1.083)
  the two profiles are of different devices: /device:TPU:4 before, /device:TPU:160 now
where the time goes in v7:
time: 117 us
  local copies, waits for them, and re-layouts  30.4 us (26%)
  starting transfers between devices  29.1 us (25%)
  waiting for transfers between devices  29.1 us (25%)
  matrix products  13.2 us (11%)
  other arithmetic  13.1 us (11%)
  between operations  1.65 us (1%)
    all_to_all x1, waiting for transfers between devices, on_device(): lax.all_to_all(stacked, 'seq', split_axis=0, concat_axis=0, tiled=True)  19 us
    ppermute x12, starting transfers between devices, quad_step(): lax.ppermute(value, axis, [(index, index ^ part * step) for index in rang...  18.1 us
    all_to_all x1, starting transfers between devices, on_device(): lax.all_to_all(stacked, 'seq', split_axis=0, concat_axis=0, tiled=True)  7.17 us
    another operation x5, local copies, waits for them, and re-layouts, on_device(): jnp.stack([tensor.reshape(seq_size, block, width) for tensor in (keys, va...  6.64 us
    reshape x2, local copies, waits for them, and re-layouts, on_device(): rows = rows.reshape(seq_size, block, 4, head_count, width // head_count)  6.32 us
    all_to_all x1, waiting for transfers between devices, on_device(): lax.all_to_all(back_rows, 'seq', split_axis=0, concat_axis=0, tiled=True)  5.69 us
    ppermute x12, waiting for transfers between devices, quad_step(): lax.ppermute(value, axis, [(index, index ^ part * step) for index in rang...  4.42 us
    another operation x4, local copies, waits for them, and re-layouts  4.11 us
  transfers between devices with their start and end apart: 14, of which 6 were waited for; matrix products, arithmetic and copies ran while one was open for 20% of the time, Pallas kernels for 0%

profile of v7, /device:TPU:160, one launch (start us, length us, event | category | flops | bytes accessed | tf_op | source)
XLA Modules:
  0.0 116.5 jit_solution(1961073091295417267)
XLA Ops:
  0.6 0.0 copy-start
  0.6 0.0 copy-start.7
  0.7 1.2 %stack_reshape.12 = bf16[16,9,1,1536]{3,1,0,2:T(8,128)(2,1)S(1)} reshape(bf16[1,1,144,1536]{3,2,1,0:T(8,128)(2,1)} %param.9) | data formatting | bytes 884736 | tf_op jit(solution)/shard_map/stack;reshape | solution.py:85
  1.9 1.2 %stack_reshape.13 = bf16[16,9,1,1536]{3,1,0,2:T(8,128)(2,1)S(1)} reshape(bf16[1,1,144,1536]{3,2,1,0:T(8,128)(2,1)} %param.10) | data formatting | bytes 884736 | tf_op jit(solution)/shard_map/stack;reshape | solution.py:85
  3.1 0.2 stack_reshape.14
  3.3 1.2 %stack_reshape.15 = bf16[16,9,1,1536]{3,1,0,2:T(8,128)(2,1)S(1)} reshape(bf16[1,1,144,1536]{3,2,1,0:T(8,128)(2,1)} %param.11) | data formatting | bytes 884736 | tf_op jit(solution)/shard_map/stack;reshape | solution.py:85
  4.5 0.6 pad_maximum_fusion
  5.1 2.8 %copy.60 = bf16[16,9,4,1536]{3,2,1,0:T(4,128)(2,1)} copy(bf16[16,9,4,1536]{3,1,0,2:T(8,128)(2,1)S(1)} %pad_maximum_fusion) | data formatting | bytes 3538944 | tf_op jit(solution)/shard_map/stack | solution.py:85
  8.0 7.2 %all-to-all-start = ((bf16[16,9,4,1536]{3,2,1,0:T(4,128)(2,1)}), bf16[16,9,4,1536]{3,2,1,0:T(4,128)(2,1)S(1)}, u32[]{:S(2)}, u32[]{:S(2)}) async-start(bf16[16,9,4,1536]{3,2,1,0:T(4,128)(2,1)} %copy.60), calls=%async_computation | async-start | bytes 3538944 | tf_op jit(solution)/shard_map/all_to_all | solution.py:92
  15.1 0.0 copy-start.21
  15.1 0.3 reshape.284
  15.5 0.3 reshape.285
  15.8 2.3 %reshape.290 = bf16[144,12,128]{2,1,0:T(8,128)(2,1)} reshape(bf16[1,1,144,1536]{3,2,1,0:T(8,128)(2,1)} %param.11) | data formatting | bytes 884736 | tf_op jit(solution)/shard_map/reshape.23
  18.2 0.3 convolution_bitcast_fusion.2
  18.4 0.8 copy.64
  19.9 0.7 broadcast_compare_fusion
  20.6 2.6 %fusion.85 = (f32[12,144]{1,0:T(8,128)}, f32[12,144,144]{1,2,0:T(8,128)}) fusion(pred[144]{0:T(512)(128)(4,1)S(1)} %iota_compare_fusion.2, bf16[144,12,128]{2,1,0:T(8,128)(2,1)S(1)} %reshape.285, bf16[144,12,128]{2,1,0:T(8,128)(2,1)S(1)} %reshape.284), kind=kOutput, calls=%fused_computation.95 | convolution fusion | flops 64696464 | bytes 1887120 | tf_op jit(solution)/shard_map/sub | solution.py:28
  23.2 19.0 %all-to-all-done = bf16[16,9,4,1536]{3,2,1,0:T(4,128)(2,1)S(1)} async-done(((bf16[16,9,4,1536]{3,2,1,0:T(4,128)(2,1)}), bf16[16,9,4,1536]{3,2,1,0:T(4,128)(2,1)S(1)}, u32[]{:S(2)}, u32[]{:S(2)}) %all-to-all-start) | async-done | bytes 1769504 | tf_op jit(solution)/shard_map/all_to_all | solution.py:92
  42.2 2.6 %reshape.296 = bf16[16,9,4,12,128]{4,3,2,1,0:T(8,128)(2,1)} reshape(bf16[16,9,4,1536]{3,2,1,0:T(4,128)(2,1)S(1)} %all-to-all-done) | data formatting | bytes 3538944 | tf_op jit(solution)/shard_map/reshape | solution.py:93
  44.8 3.7 %copy.137 = bf16[16,9,4,12,128]{4,0,3,1,2:T(8,128)(2,1)S(1)} copy(bf16[16,9,4,12,128]{4,3,2,1,0:T(8,128)(2,1)} %reshape.296) | data formatting | bytes 3538944 | tf_op jit(solution)/shard_map/reshape | solution.py:93
  48.5 0.6 fusion.29
  49.1 2.3 %fusion.16 = f32[9,12,16,16]{2,3,1,0:T(8,128)} fusion(f32[2,9,12,16,16]{3,4,2,1,0:T(8,128)S(1)} %fusion.29, f32[12,16,16]{1,2,0:T(8,128)} %copy.64, pred[16,16]{0,1:T(8,128)(4,1)} %broadcast_compare_fusion), kind=kOutput, calls=%fused_computation.22 | output fusion | flops 141726 | bytes 1007872 | tf_op jit(solution)/shard_map/div | solution.py:103
  51.4 3.3 %fusion.90 = (f32[12,16,16]{1,2,0:T(8,128)}, bf16[9,12,16,16]{2,3,1,0:T(8,128)(2,1)}) fusion(f32[9,12,16,16]{2,3,1,0:T(8,128)} %fusion.16, f32[2,9,12,16,16]{3,4,2,1,0:T(8,128)S(1)} %fusion.29), kind=kOutput, calls=%fused_computation.96 | output fusion | flops 136911 | bytes 2058240 | tf_op jit(solution)/shard_map/sub | solution.py:106
  54.7 1.0 copy.65
  55.7 0.8 convolution_bitcast_fusion.3
  56.5 0.2 collective-permute-start.1
  56.7 4.5 %collective-permute-start.2 = (f32[12,16]{1,0:T(8,128)}, f32[12,16]{1,0:T(8,128)}, u32[]{:S(2)}, u32[]{:S(2)}) collective-permute-start(f32[12,16]{1,0:T(8,128)} %convolution_bitcast_fusion.3), channel_id=1, source_target_pairs={{0,3},{1,2},{2,1},{3,0},{4,7},{5,6},{6,5},{7,4},{8,11},{9,10},{10,... | collective-permute-start | bytes 2312 | tf_op jit(solution)/shard_map/ppermute | solution.py:60
  61.2 3.0 %convolution_bitcast_fusion = f32[1,1,12,18,8,128]{5,4,3,2,1,0:T(8,128)} fusion(bf16[144,12,128]{2,1,0:T(8,128)(2,1)} %reshape.290, f32[12,144,144]{1,2,0:T(8,128)} %get-tuple-element.24, f32[12,144]{1,0:T(8,128)} %get-tuple-element.23), kind=kOutput, calls=%fused_computation.30 | convolution fusion | flops 64198656 | bytes 2329344 | tf_op jit(solution)/shard_map/bfhij,bfihe->bfjhe/dot_general | solution.py:39
  64.3 1.1 reshape.286
  65.4 0.6 copy-done.20
  66.0 0.8 add_add_fusion.2
  66.8 0.3 collective-permute-start.3
  67.1 2.7 %collective-permute-start.4 = (f32[12,16]{1,0:T(8,128)S(1)}, f32[12,16]{1,0:T(8,128)}, u32[]{:S(2)}, u32[]{:S(2)}) collective-permute-start(f32[12,16]{1,0:T(8,128)S(1)} %add_add_fusion.2), channel_id=1, source_target_pairs={{0,8},{1,9},{2,10},{3,11},{4,12},{5,13},{6,14},{7,15},{8,0},{9,1},... | collective-permute-start | bytes 2312 | tf_op jit(solution)/shard_map/ppermute | solution.py:60
  69.8 1.9 %collective-permute-start.5 = (f32[12,16]{1,0:T(8,128)S(1)}, f32[12,16]{1,0:T(8,128)}, u32[]{:S(2)}, u32[]{:S(2)}) collective-permute-start(f32[12,16]{1,0:T(8,128)S(1)} %add_add_fusion.2), channel_id=1, source_target_pairs={{0,12},{1,13},{2,14},{3,15},{4,8},{5,9},{6,10},{7,11},{8,4},{9,5},... | collective-permute-start | bytes 2312 | tf_op jit(solution)/shard_map/ppermute | solution.py:60
  71.7 0.9 convert_bitcast_fusion.2
  72.7 0.2 copy.67
  72.9 0.2 copy.66
  73.2 0.5 copy-done.16
  73.7 1.7 %fusion.12 = bf16[16,9,4,12,128]{4,0,3,1,2:T(8,128)(2,1)S(1)} fusion(f32[4]{0:T(128)} %constant.5.clone, bf16[4,9,12,16,128]{4,3,2,1,0:T(8,128)(2,1)S(1)} %bitcast.121, bf16[1,9,12,16,16]{4,3,2,1,0:T(8,128)(2,1)S(1)} %copy-done.16, bf16[1,9,12,16,16]{4,3,2,1,0:T(8,128)(2,1)S(1)} %bitcast.126, bf16[1,9,12,16,16]{4,3,2,1,0:T(8,128)(2,1)S(1)} %copy.67, ...), kind=kOutput, calls=%fused_computation.20 | convolution fusion | flops 30412800 | bytes 3760144 | tf_op jit(solution)/shard_map/tphij,tphje->tphie/dot_general | solution.py:127
  75.4 0.6 copy.68
  76.0 2.5 %reshape.289 = bf16[16,9,4,1536]{3,0,2,1:T(8,128)(2,1)} reshape(bf16[16,9,4,12,128]{4,3,0,2,1:T(8,128)(2,1)S(1)} %copy.68) | data formatting | bytes 3538944 | tf_op jit(solution)/shard_map/reshape | solution.py:131
  78.6 0.7 add_add_fusion.1
  79.3 4.1 %copy.69 = bf16[16,9,4,1536]{3,2,1,0:T(4,128)(2,1)} copy(bf16[16,9,4,1536]{3,0,2,1:T(8,128)(2,1)} %reshape.289) | data formatting | bytes 3538944 | tf_op jit(solution)/shard_map/optimization_barrier | solution.py:134
  83.4 3.8 %all-to-all-start.1 = ((bf16[16,9,4,1536]{3,2,1,0:T(4,128)(2,1)}), bf16[16,9,4,1536]{3,2,1,0:T(4,128)(2,1)S(1)}, u32[]{:S(2)}, u32[]{:S(2)}) async-start(bf16[16,9,4,1536]{3,2,1,0:T(4,128)(2,1)} %copy.69), calls=%async_computation.1 | async-start | bytes 3538944 | tf_op jit(solution)/shard_map/all_to_all | solution.py:137
  87.3 2.7 %convolution_bitcast_fusion.1 = f32[1,1,12,18,8,128]{5,4,3,2,1,0:T(8,128)} fusion(bf16[144,12,128]{2,1,0:T(8,128)(2,1)} %reshape.286, f32[12,144,144]{1,2,0:T(8,128)S(1)} %copy-done.6, f32[12,144]{1,0:T(8,128)} %get-tuple-element.23), kind=kOutput, calls=%fused_computation.31 | convolution fusion | flops 64198656 | bytes 2329344 | tf_op jit(solution)/shard_map/bfhij,bfjhe->bfihe/dot_general | solution.py:31
  90.0 0.5 multiply_reduce_fusion
  90.5 0.4 multiply_convert_fusion.1
  90.9 0.1 collective-permute-start.6
  91.0 1.1 collective-permute-start.7
  92.1 0.8 collective-permute-start.8
  92.8 0.4 fusion.18
  93.2 1.5 %collective-permute-done.7 = f32[12,16]{1,0:T(8,128)S(1)} collective-permute-done((f32[12,16]{1,0:T(8,128)S(1)}, f32[12,16]{1,0:T(8,128)S(1)}, u32[]{:S(2)}, u32[]{:S(2)}) %collective-permute-start.7) | collective-permute-done | bytes 800 | tf_op jit(solution)/shard_map/ppermute | solution.py:60
  94.7 0.4 collective-permute-done.8
  95.2 5.0 %collective-permute-start.11 = (f32[12,16]{1,0:T(8,128)S(1)}, f32[12,16]{1,0:T(8,128)S(1)}, u32[]{:S(2)}, u32[]{:S(2)}) collective-permute-start(f32[12,16]{1,0:T(8,128)S(1)} %add_add_fusion), channel_id=1, source_target_pairs={{0,192},{16,208},{32,224},{48,240},{64,128},{80,144},{96,160},{112... | collective-permute-start | bytes 2312 | tf_op jit(solution)/shard_map/ppermute | solution.py:60
  100.2 1.5 %collective-permute-start.9 = (f32[12,16]{1,0:T(8,128)S(1)}, f32[12,16]{1,0:T(8,128)S(1)}, u32[]{:S(2)}, u32[]{:S(2)}) collective-permute-start(f32[12,16]{1,0:T(8,128)S(1)} %add_add_fusion), channel_id=1, source_target_pairs={{0,64},{16,80},{32,96},{48,112},{64,0},{80,16},{96,32},{112,48},{1... | collective-permute-start | bytes 2312 | tf_op jit(solution)/shard_map/ppermute | solution.py:60
  101.7 0.6 fusion.17
  102.3 0.5 collective-permute-done.10
  102.7 2.0 %collective-permute-done.9 = f32[12,16]{1,0:T(8,128)S(1)} collective-permute-done((f32[12,16]{1,0:T(8,128)S(1)}, f32[12,16]{1,0:T(8,128)S(1)}, u32[]{:S(2)}, u32[]{:S(2)}) %collective-permute-start.9) | collective-permute-done | bytes 800 | tf_op jit(solution)/shard_map/ppermute | solution.py:60
  104.7 0.6 add_multiply_fusion
  105.4 5.7 %all-to-all-done.1 = bf16[16,9,4,1536]{3,2,1,0:T(4,128)(2,1)S(1)} async-done(((bf16[16,9,4,1536]{3,2,1,0:T(4,128)(2,1)}), bf16[16,9,4,1536]{3,2,1,0:T(4,128)(2,1)S(1)}, u32[]{:S(2)}, u32[]{:S(2)}) %all-to-all-start.1) | async-done | bytes 1769504 | tf_op jit(solution)/shard_map/all_to_all | solution.py:137
  111.0 0.5 convert_bitcast_fusion
  111.5 2.6 %fusion.84 = (f32[1,16,9,1536]{3,0,2,1:T(1,128)S(1)}, f32[1,16,9,1536]{3,0,2,1:T(1,128)S(1)}, f32[1,16,9,1536]{3,0,2,1:T(1,128)S(1)}, f32[1,16,9,1536]{3,0,2,1:T(1,128)S(1)}) fusion(f32[4,16,9,1536]{3,0,2,1:T(4,128)S(1)} %convert_bitcast_fusion), kind=kLoop, calls=%fused_computation.94 | loop fusion | bytes 7077888 | tf_op jit(solution)/shard_map/slice | solution.py:153
  114.2 1.2 %fusion.22 = (bf16[1,1,144,1536]{3,2,1,0:T(8,128)(2,1)}, bf16[1,1,144,1536]{3,2,1,0:T(8,128)(2,1)}) fusion(f32[1,1,12,18,8,128]{5,4,3,2,1,0:T(8,128)S(1)} %copy-done.12, f32[1,1,144,1536]{3,0,2,1:T(1,128)S(1)} %bitcast.124, f32[1,1,144,1536]{3,0,2,1:T(1,128)S(1)} %bitcast.125, f32[1,1,12,18,8,128]{5,4,3,2,1,0:T(8,128)S(1)} %fusion.18), kind=kLoop, calls=%fused_computation.35 | loop fusion | flops 884736 | bytes 4423680 | tf_op jit(solution)/shard_map/convert_element_type | solution.py:153
  115.4 1.1 fusion.24
  (52 shorter events, 0.1 us)
Async XLA Ops:
  0.6 17.5 %copy-start = (f32[12,16]{1,0:T(8,128)S(1)}, f32[12,16]{1,0:T(8,128)}, u32[]{:S(2)}) copy-start(f32[12,16]{1,0:T(8,128)} %param.14) | copy-start | bytes 2308
  0.6 2.5 %copy-start.7 = (bf16[1,1,144,1536]{3,2,1,0:T(8,128)(2,1)S(1)}, bf16[1,1,144,1536]{3,2,1,0:T(8,128)(2,1)}, u32[]{:S(2)}) copy-start(bf16[1,1,144,1536]{3,2,1,0:T(8,128)(2,1)} %param.8) | copy-start | bytes 1327108
  7.9 7.2 %copy-start.8 = (bf16[1,1,144,1536]{3,2,1,0:T(8,128)(2,1)S(1)}, bf16[1,1,144,1536]{3,2,1,0:T(8,128)(2,1)}, u32[]{:S(2)}) copy-start(bf16[1,1,144,1536]{3,2,1,0:T(8,128)(2,1)} %param.8) | copy-start | bytes 1327108
  7.9 7.5 %copy-start.9 = (bf16[1,1,144,1536]{3,2,1,0:T(8,128)(2,1)S(1)}, bf16[1,1,144,1536]{3,2,1,0:T(8,128)(2,1)}, u32[]{:S(2)}) copy-start(bf16[1,1,144,1536]{3,2,1,0:T(8,128)(2,1)} %param.9) | copy-start | bytes 1327108
  8.0 34.3 %all-to-all-start = ((bf16[16,9,4,1536]{3,2,1,0:T(4,128)(2,1)}), bf16[16,9,4,1536]{3,2,1,0:T(4,128)(2,1)S(1)}, u32[]{:S(2)}, u32[]{:S(2)}) async-start(bf16[16,9,4,1536]{3,2,1,0:T(4,128)(2,1)} %copy.60), calls=%async_computation | async-start | bytes 3538944 | tf_op jit(solution)/shard_map/all_to_all | solution.py:92
  15.1 4.8 %copy-start.21 = (s32[1,16]{1,0:T(1,128)S(1)}, s32[1,16]{1,0:T(1,128)}, u32[]{:S(2)}) copy-start(s32[1,16]{1,0:T(1,128)} %param.13) | copy-start | bytes 196
  15.5 7.7 %copy-start.4 = (bf16[144,12,128]{2,1,0:T(8,128)(2,1)}, bf16[144,12,128]{2,1,0:T(8,128)(2,1)S(1)}, u32[]{:S(2)}) copy-start(bf16[144,12,128]{2,1,0:T(8,128)(2,1)S(1)} %reshape.284) | copy-start | bytes 1327108
  15.8 7.4 %copy-start.2 = (bf16[144,12,128]{2,1,0:T(8,128)(2,1)}, bf16[144,12,128]{2,1,0:T(8,128)(2,1)S(1)}, u32[]{:S(2)}) copy-start(bf16[144,12,128]{2,1,0:T(8,128)(2,1)S(1)} %reshape.285) | copy-start | bytes 1327108
  56.5 8.9 %collective-permute-start = (f32[12,16]{1,0:T(8,128)}, f32[12,16]{1,0:T(8,128)S(1)}, u32[]{:S(2)}, u32[]{:S(2)}) collective-permute-start(f32[12,16]{1,0:T(8,128)} %convolution_bitcast_fusion.3), channel_id=1, source_target_pairs={{0,1},{1,0},{2,3},{3,2},{4,5},{5,4},{6,7},{7,6},{8,9},{9,8},{10,11... | collective-permute-start | bytes 2312 | tf_op jit(solution)/shard_map/ppermute | solution.py:60
  56.5 8.9 %collective-permute-start.1 = (f32[12,16]{1,0:T(8,128)}, f32[12,16]{1,0:T(8,128)}, u32[]{:S(2)}, u32[]{:S(2)}) collective-permute-start(f32[12,16]{1,0:T(8,128)} %convolution_bitcast_fusion.3), channel_id=1, source_target_pairs={{0,2},{1,3},{2,0},{3,1},{4,6},{5,7},{6,4},{7,5},{8,10},{9,11},{10,... | collective-permute-start | bytes 2312 | tf_op jit(solution)/shard_map/ppermute | solution.py:60
  56.7 9.3 %collective-permute-start.2 = (f32[12,16]{1,0:T(8,128)}, f32[12,16]{1,0:T(8,128)}, u32[]{:S(2)}, u32[]{:S(2)}) collective-permute-start(f32[12,16]{1,0:T(8,128)} %convolution_bitcast_fusion.3), channel_id=1, source_target_pairs={{0,3},{1,2},{2,1},{3,0},{4,7},{5,6},{6,5},{7,4},{8,11},{9,10},{10,... | collective-permute-start | bytes 2312 | tf_op jit(solution)/shard_map/ppermute | solution.py:60
  61.2 3.0 %copy-start.10 = (bf16[1,1,144,1536]{3,2,1,0:T(8,128)(2,1)S(1)}, bf16[1,1,144,1536]{3,2,1,0:T(8,128)(2,1)}, u32[]{:S(2)}) copy-start(bf16[1,1,144,1536]{3,2,1,0:T(8,128)(2,1)} %param.10) | copy-start | bytes 1327108
  61.2 10.5 %copy-start.1 = (f32[9,12,16,16]{2,3,1,0:T(8,128)S(1)}, f32[9,12,16,16]{2,3,1,0:T(8,128)}, u32[]{:S(2)}) copy-start(f32[9,12,16,16]{2,3,1,0:T(8,128)} %fusion.16) | copy-start | bytes 331780
  64.3 8.6 %copy-start.11 = (bf16[9,12,16,16]{2,3,1,0:T(8,128)(2,1)S(1)}, bf16[9,12,16,16]{2,3,1,0:T(8,128)(2,1)}, u32[]{:S(2)}) copy-start(bf16[9,12,16,16]{2,3,1,0:T(8,128)(2,1)} %get-tuple-element.12) | copy-start | bytes 165892
  65.4 0.6 copy-start.20
  66.8 6.4 %copy-start.17 = (f32[12,16]{1,0:T(8,128)}, f32[12,16]{1,0:T(8,128)S(1)}, u32[]{:S(2)}) copy-start(f32[12,16]{1,0:T(8,128)S(1)} %add_add_fusion.2) | copy-start | bytes 2308
  66.8 11.8 %collective-permute-start.3 = (f32[12,16]{1,0:T(8,128)S(1)}, f32[12,16]{1,0:T(8,128)}, u32[]{:S(2)}, u32[]{:S(2)}) collective-permute-start(f32[12,16]{1,0:T(8,128)S(1)} %add_add_fusion.2), channel_id=1, source_target_pairs={{0,4},{1,5},{2,6},{3,7},{4,0},{5,1},{6,2},{7,3},{8,12},{9,13},{10,... | collective-permute-start | bytes 2312 | tf_op jit(solution)/shard_map/ppermute | solution.py:60
  67.1 11.5 %collective-permute-start.4 = (f32[12,16]{1,0:T(8,128)S(1)}, f32[12,16]{1,0:T(8,128)}, u32[]{:S(2)}, u32[]{:S(2)}) collective-permute-start(f32[12,16]{1,0:T(8,128)S(1)} %add_add_fusion.2), channel_id=1, source_target_pairs={{0,8},{1,9},{2,10},{3,11},{4,12},{5,13},{6,14},{7,15},{8,0},{9,1},... | collective-permute-start | bytes 2312 | tf_op jit(solution)/shard_map/ppermute | solution.py:60
  69.8 8.7 %collective-permute-start.5 = (f32[12,16]{1,0:T(8,128)S(1)}, f32[12,16]{1,0:T(8,128)}, u32[]{:S(2)}, u32[]{:S(2)}) collective-permute-start(f32[12,16]{1,0:T(8,128)S(1)} %add_add_fusion.2), channel_id=1, source_target_pairs={{0,12},{1,13},{2,14},{3,15},{4,8},{5,9},{6,10},{7,11},{8,4},{9,5},... | collective-permute-start | bytes 2312 | tf_op jit(solution)/shard_map/ppermute | solution.py:60
  72.7 1.0 copy-start.16
  76.0 2.5 %copy-start.18 = (f32[12,16]{1,0:T(8,128)S(1)}, f32[12,16]{1,0:T(8,128)}, u32[]{:S(2)}) copy-start(f32[12,16]{1,0:T(8,128)} %copy-done.17) | copy-start | bytes 2308
  83.4 3.9 %copy-start.6 = (f32[12,144,144]{1,2,0:T(8,128)S(1)}, f32[12,144,144]{1,2,0:T(8,128)}, u32[]{:S(2)}) copy-start(f32[12,144,144]{1,2,0:T(8,128)} %get-tuple-element.24) | copy-start | bytes 2985988
  83.4 27.7 %all-to-all-start.1 = ((bf16[16,9,4,1536]{3,2,1,0:T(4,128)(2,1)}), bf16[16,9,4,1536]{3,2,1,0:T(4,128)(2,1)S(1)}, u32[]{:S(2)}, u32[]{:S(2)}) async-start(bf16[16,9,4,1536]{3,2,1,0:T(4,128)(2,1)} %copy.69), calls=%async_computation.1 | async-start | bytes 3538944 | tf_op jit(solution)/shard_map/all_to_all | solution.py:137
  87.2 2.7 %copy-start.14 = (bf16[144,12,128]{2,1,0:T(8,128)(2,1)S(1)}, bf16[144,12,128]{2,1,0:T(8,128)(2,1)}, u32[]{:S(2)}) copy-start(bf16[144,12,128]{2,1,0:T(8,128)(2,1)} %reshape.290) | copy-start | bytes 1327108
  87.3 2.7 %copy-start.15 = (bf16[144,12,128]{2,1,0:T(8,128)(2,1)S(1)}, bf16[144,12,128]{2,1,0:T(8,128)(2,1)}, u32[]{:S(2)}) copy-start(bf16[144,12,128]{2,1,0:T(8,128)(2,1)} %reshape.286) | copy-start | bytes 1327108
  87.3 2.7 %copy-start.19 = (f32[12,144]{1,0:T(8,128)S(1)}, f32[12,144]{1,0:T(8,128)}, u32[]{:S(2)}) copy-start(f32[12,144]{1,0:T(8,128)} %get-tuple-element.23) | copy-start | bytes 20740
  90.5 2.4 %copy-start.5 = (bf16[144,12,128]{2,1,0:T(8,128)(2,1)S(1)}, bf16[144,12,128]{2,1,0:T(8,128)(2,1)}, u32[]{:S(2)}) copy-start(bf16[144,12,128]{2,1,0:T(8,128)(2,1)} %copy-done.4) | copy-start | bytes 1327108
  90.9 10.8 %copy-start.3 = (bf16[144,12,128]{2,1,0:T(8,128)(2,1)S(1)}, bf16[144,12,128]{2,1,0:T(8,128)(2,1)}, u32[]{:S(2)}) copy-start(bf16[144,12,128]{2,1,0:T(8,128)(2,1)} %copy-done.2) | copy-start | bytes 1327108
  90.9 2.3 %collective-permute-start.6 = (f32[12,16]{1,0:T(8,128)S(1)}, f32[12,16]{1,0:T(8,128)S(1)}, u32[]{:S(2)}, u32[]{:S(2)}) collective-permute-start(f32[12,16]{1,0:T(8,128)S(1)} %add_add_fusion.1), channel_id=1, source_target_pairs={{0,16},{16,0},{32,48},{48,32},{64,80},{80,64},{96,112},{112,96},{1... | collective-permute-start | bytes 2312 | tf_op jit(solution)/shard_map/ppermute | solution.py:60
  91.0 3.7 %collective-permute-start.7 = (f32[12,16]{1,0:T(8,128)S(1)}, f32[12,16]{1,0:T(8,128)S(1)}, u32[]{:S(2)}, u32[]{:S(2)}) collective-permute-start(f32[12,16]{1,0:T(8,128)S(1)} %add_add_fusion.1), channel_id=1, source_target_pairs={{0,32},{16,48},{32,0},{48,16},{64,96},{80,112},{96,64},{112,80},{1... | collective-permute-start | bytes 2312 | tf_op jit(solution)/shard_map/ppermute | solution.py:60
  92.1 3.1 %collective-permute-start.8 = (f32[12,16]{1,0:T(8,128)S(1)}, f32[12,16]{1,0:T(8,128)S(1)}, u32[]{:S(2)}, u32[]{:S(2)}) collective-permute-start(f32[12,16]{1,0:T(8,128)S(1)} %add_add_fusion.1), channel_id=1, source_target_pairs={{0,48},{16,32},{32,16},{48,0},{64,112},{80,96},{96,80},{112,64},{1... | collective-permute-start | bytes 2312 | tf_op jit(solution)/shard_map/ppermute | solution.py:60
  95.2 7.6 %collective-permute-start.10 = (f32[12,16]{1,0:T(8,128)S(1)}, f32[12,16]{1,0:T(8,128)S(1)}, u32[]{:S(2)}, u32[]{:S(2)}) collective-permute-start(f32[12,16]{1,0:T(8,128)S(1)} %add_add_fusion), channel_id=1, source_target_pairs={{0,128},{16,144},{32,160},{48,176},{64,192},{80,208},{96,224},{112... | collective-permute-start | bytes 2312 | tf_op jit(solution)/shard_map/ppermute | solution.py:60
  95.2 7.6 %collective-permute-start.11 = (f32[12,16]{1,0:T(8,128)S(1)}, f32[12,16]{1,0:T(8,128)S(1)}, u32[]{:S(2)}, u32[]{:S(2)}) collective-permute-start(f32[12,16]{1,0:T(8,128)S(1)} %add_add_fusion), channel_id=1, source_target_pairs={{0,192},{16,208},{32,224},{48,240},{64,128},{80,144},{96,160},{112... | collective-permute-start | bytes 2312 | tf_op jit(solution)/shard_map/ppermute | solution.py:60
  100.2 4.6 %collective-permute-start.9 = (f32[12,16]{1,0:T(8,128)S(1)}, f32[12,16]{1,0:T(8,128)S(1)}, u32[]{:S(2)}, u32[]{:S(2)}) collective-permute-start(f32[12,16]{1,0:T(8,128)S(1)} %add_add_fusion), channel_id=1, source_target_pairs={{0,64},{16,80},{32,96},{48,112},{64,0},{80,16},{96,32},{112,48},{1... | collective-permute-start | bytes 2312 | tf_op jit(solution)/shard_map/ppermute | solution.py:60
  111.5 2.7 %copy-start.12 = (f32[1,1,12,18,8,128]{5,4,3,2,1,0:T(8,128)S(1)}, f32[1,1,12,18,8,128]{5,4,3,2,1,0:T(8,128)}, u32[]{:S(2)}) copy-start(f32[1,1,12,18,8,128]{5,4,3,2,1,0:T(8,128)} %convolution_bitcast_fusion) | copy-start | bytes 2654212
  114.2 1.2 %copy-start.13 = (f32[1,1,12,18,8,128]{5,4,3,2,1,0:T(8,128)S(1)}, f32[1,1,12,18,8,128]{5,4,3,2,1,0:T(8,128)}, u32[]{:S(2)}) copy-start(f32[1,1,12,18,8,128]{5,4,3,2,1,0:T(8,128)} %convolution_bitcast_fusion.1) | copy-start | bytes 2654212

commit v8 on v3

--- a/solution.py
+++ b/solution.py
@@ -136,7 +136,6 @@
         jnp.einsum(TIME_PATTERNS[2], score_half, query_part, preferred_element_type=jnp.float32)
         * scaling
     )
-    partial = quad_step(partial, "seq", seq_size, 4)
     back_rows = jnp.stack(
         [
             jnp.transpose(tensor.astype(jnp.bfloat16), (2, 0, 1, 3)).reshape(seq_size, block, width)
@@ -145,6 +144,7 @@
         axis=2,
     )
     partial, back_rows = lax.optimization_barrier((partial, back_rows))
+    partial = quad_step(partial, "seq", seq_size, 4)
     summed = quad_step(quad_step(partial, "dp", dp_size, 1), "dp", dp_size, 4)
     bias_grad = summed / math.sqrt(dp_size * queries.shape[0] * frames_all * positions)
     back = lax.all_to_all(back_rows, "seq", split_axis=0, concat_axis=0, tiled=True)

time: 106 us -> 124 us (1.17)
  waiting for transfers between devices: 15.8 us -> 27.5 us
  local copies, waits for them, and re-layouts: 28.3 us -> 33.5 us
  matrix products: 15.6 us -> 17.3 us
    ppermute x12, waiting for transfers between devices: 8.27 us -> 18 us  [quad_step(): lax.ppermute(value, axis, [(index, index ^ part * step) for index in rang...]
    another operation x4, local copies, waits for them, and re-layouts: 4.31 us -> 6.36 us
    all_to_all x1, waiting for transfers between devices: 7.55 us -> 9.59 us  [on_device(): lax.all_to_all(stacked, 'seq', split_axis=0, concat_axis=0, tiled=True)]
    dot_general x1, matrix products: 0.48 us -> 2.42 us  [attend_backward(): jnp.einsum(patterns[0], cotangent_part, value_part, preferred_element_typ...]
    reduce_sum x1, local copies, waits for them, and re-layouts: 0.11 us -> 1.65 us  [on_device(): jnp.sum(score_grad, axis=0)]
    another operation x4, local copies, waits for them, and re-layouts: 1.97 us -> 3.5 us  [on_device(): jnp.stack([jnp.transpose(tensor.astype(jnp.bfloat16), (2, 0, 1, 3)).resha...]
    sub x1, other arithmetic: 1.78 us -> 3.21 us  [on_device(): score_grad = shares * (share_grad - spread)]
    sub x1, matrix products: 3.27 us -> 1.98 us  [attend_forward(): weights = jnp.exp(scores - row_peak)]
  transfers between devices with their start and end apart: 14 -> 14, of which waited for: 5 -> 7; matrix products, arithmetic and copies ran while one was open for 25% -> 17% of each run, Pallas kernels for 0% -> 0%
where the time goes in v8:
time: 124 us; the launch traced here: 123 us
  starting transfers between devices  34.8 us (28%)
  local copies, waits for them, and re-layouts  33.5 us (27%)
  waiting for transfers between devices  27.5 us (22%)
  matrix products  17.3 us (14%)
  other arithmetic  8.49 us (7%)
  between operations  1.64 us (1%)
    ppermute x12, starting transfers between devices, quad_step(): lax.ppermute(value, axis, [(index, index ^ part * step) for index in rang...  19.2 us
    ppermute x12, waiting for transfers between devices, quad_step(): lax.ppermute(value, axis, [(index, index ^ part * step) for index in rang...  18 us
    all_to_all x1, waiting for transfers between devices, on_device(): lax.all_to_all(stacked, 'seq', split_axis=0, concat_axis=0, tiled=True)  9.59 us
    all_to_all x1, starting transfers between devices, on_device(): lax.all_to_all(back_rows, 'seq', split_axis=0, concat_axis=0, tiled=True)  8 us
    all_to_all x1, starting transfers between devices, on_device(): lax.all_to_all(stacked, 'seq', split_axis=0, concat_axis=0, tiled=True)  7.58 us
    another operation x5, local copies, waits for them, and re-layouts, on_device(): jnp.stack([tensor.reshape(seq_size, block, width) for tensor in (queries,...  6.63 us
    another operation x4, local copies, waits for them, and re-layouts  6.36 us
    reshape x2, local copies, waits for them, and re-layouts, on_device(): rows = rows.reshape(seq_size, block, 4, head_count, width // head_count)  6.26 us
  transfers between devices with their start and end apart: 14, of which 7 were waited for; matrix products, arithmetic and copies ran while one was open for 17% of the time, Pallas kernels for 0%

profile of v8, /device:TPU:4, one launch (start us, length us, event | category | flops | bytes accessed | tf_op | source)
XLA Modules:
  0.0 123.2 jit_solution(12244834710607072135)
XLA Ops:
  0.7 1.2 %stack_reshape.24 = bf16[16,9,1,1536]{3,1,0,2:T(8,128)(2,1)S(1)} reshape(bf16[1,1,144,1536]{3,2,1,0:T(8,128)(2,1)} %param.7) | data formatting | bytes 884736 | tf_op jit(solution)/shard_map/stack;reshape | solution.py:85
  1.9 1.2 stack_reshape.25
  3.3 1.2 stack_reshape.27
  4.5 0.6 pad_maximum_fusion
  5.1 2.8 %copy.94 = bf16[16,9,4,1536]{3,2,1,0:T(4,128)(2,1)} copy(bf16[16,9,4,1536]{3,1,0,2:T(8,128)(2,1)S(1)} %pad_maximum_fusion) | data formatting | bytes 3538944 | tf_op jit(solution)/shard_map/stack | solution.py:85
  7.9 7.6 %all-to-all-start = ((bf16[16,9,4,1536]{3,2,1,0:T(4,128)(2,1)}), bf16[16,9,4,1536]{3,2,1,0:T(4,128)(2,1)S(1)}, u32[]{:S(2)}, u32[]{:S(2)}) async-start(bf16[16,9,4,1536]{3,2,1,0:T(4,128)(2,1)} %copy.94), calls=%async_computation | async-start | bytes 3538944 | tf_op jit(solution)/shard_map/all_to_all | solution.py:92
  15.5 0.3 reshape.278
  15.9 1.5 %reshape.279 = bf16[144,12,128]{2,1,0:T(8,128)(2,1)S(1)} reshape(bf16[1,1,144,1536]{3,2,1,0:T(8,128)(2,1)} %param.8) | data formatting | bytes 884736 | tf_op jit(solution)/shard_map/reshape.3
  17.4 2.4 %reshape.280 = bf16[144,12,128]{2,1,0:T(8,128)(2,1)} reshape(bf16[1,1,144,1536]{3,2,1,0:T(8,128)(2,1)} %param.9) | data formatting | bytes 884736 | tf_op jit(solution)/shard_map/reshape.7
  19.8 2.1 %reshape.283 = bf16[144,12,128]{2,1,0:T(8,128)(2,1)} reshape(bf16[1,1,144,1536]{3,2,1,0:T(8,128)(2,1)} %param.10) | data formatting | bytes 884736 | tf_op jit(solution)/shard_map/reshape.22
  21.9 0.3 convolution_bitcast_fusion.2
  22.2 0.8 copy.98
  23.7 0.7 broadcast_compare_fusion
  24.4 2.0 %fusion.66 = (f32[12,144]{1,0:T(8,128)S(1)}, f32[12,144,144]{1,2,0:T(8,128)}) fusion(pred[144]{0:T(512)(128)(4,1)S(1)} %iota_compare_fusion.2, bf16[144,12,128]{2,1,0:T(8,128)(2,1)S(1)} %reshape.279, bf16[144,12,128]{2,1,0:T(8,128)(2,1)S(1)} %reshape.278), kind=kOutput, calls=%fused_computation.90 | convolution fusion | flops 64696464 | bytes 1887120 | tf_op jit(solution)/shard_map/sub | solution.py:28
  26.4 2.4 %multiply_reduce_fusion = (f32[12,144]{1,0:T(8,128)S(1)}, f32[12,144,144]{1,2,0:T(8,128)S(1)}) fusion(f32[12,144,144]{1,2,0:T(8,128)} %get-tuple-element.32, f32[12,144]{1,0:T(8,128)S(1)} %get-tuple-element.31, bf16[144,12,128]{2,1,0:T(8,128)(2,1)} %reshape.280, bf16[144,12,128]{2,1,0:T(8,128)(2,1)} %reshape.283), kind=kOutput, calls=%fused_computation.9 | convolution fusion | flops 64445760 | bytes 2889216 | tf_op jit(solution)/shard_map/bfihe,bfjhe->bfhij/dot_general | solution.py:42
  28.8 0.3 multiply_convert_fusion
  29.1 9.6 %all-to-all-done = bf16[16,9,4,1536]{3,2,1,0:T(4,128)(2,1)S(1)} async-done(((bf16[16,9,4,1536]{3,2,1,0:T(4,128)(2,1)}), bf16[16,9,4,1536]{3,2,1,0:T(4,128)(2,1)S(1)}, u32[]{:S(2)}, u32[]{:S(2)}) %all-to-all-start) | async-done | bytes 1769504 | tf_op jit(solution)/shard_map/all_to_all | solution.py:92
  38.7 2.5 %reshape.289 = bf16[16,9,4,12,128]{4,3,2,1,0:T(8,128)(2,1)} reshape(bf16[16,9,4,1536]{3,2,1,0:T(4,128)(2,1)S(1)} %all-to-all-done) | data formatting | bytes 3538944 | tf_op jit(solution)/shard_map/reshape | solution.py:93
  41.3 3.7 %copy.176 = bf16[16,9,4,12,128]{4,0,3,1,2:T(8,128)(2,1)S(1)} copy(bf16[16,9,4,12,128]{4,3,2,1,0:T(8,128)(2,1)} %reshape.289) | data formatting | bytes 3538944 | tf_op jit(solution)/shard_map/reshape | solution.py:93
  45.0 1.3 %fusion.64 = f32[9,12,16,16]{2,3,1,0:T(8,128)} fusion(bf16[4,9,12,16,128]{4,3,2,1,0:T(8,128)(2,1)S(1)} %bitcast.124), kind=kOutput, calls=%fused_computation.88 | convolution fusion | flops 7077888 | bytes 995328 | tf_op jit(solution)/shard_map/phie,phje->phij/dot_general | solution.py:106
  46.3 1.5 %fusion.6 = f32[9,12,16,16]{2,3,1,0:T(8,128)S(1)} fusion(f32[12,16,16]{1,2,0:T(8,128)} %copy.98, pred[16,16]{0,1:T(8,128)(4,1)} %broadcast_compare_fusion, bf16[4,9,12,16,128]{4,3,2,1,0:T(8,128)(2,1)S(1)} %bitcast.125), kind=kOutput, calls=%fused_computation.14 | convolution fusion | flops 7219614 | bytes 1007872 | tf_op jit(solution)/shard_map/div | solution.py:105
  47.8 3.2 %fusion.71 = (f32[12,16,16]{1,2,0:T(8,128)}, bf16[9,12,16,16]{2,3,1,0:T(8,128)(2,1)}) fusion(f32[9,12,16,16]{2,3,1,0:T(8,128)S(1)} %fusion.6, f32[9,12,16,16]{2,3,1,0:T(8,128)} %fusion.64), kind=kOutput, calls=%fused_computation.91 | output fusion | flops 136911 | bytes 288768 | tf_op jit(solution)/shard_map/sub | solution.py:110
  51.0 1.6 %copy.99 = f32[12,16,16]{2,0,1:T(8,128)} copy(f32[12,16,16]{1,2,0:T(8,128)} %get-tuple-element.33) | data formatting | bytes 24576 | tf_op jit(solution)/shard_map/reduce_sum | solution.py:112
  52.6 1.1 convolution_bitcast_fusion.3
  53.7 0.7 collective-permute-start
  54.4 3.5 %collective-permute-start.1 = (f32[12,16]{1,0:T(8,128)S(1)}, f32[12,16]{1,0:T(8,128)S(1)}, u32[]{:S(2)}, u32[]{:S(2)}) collective-permute-start(f32[12,16]{1,0:T(8,128)S(1)} %convolution_bitcast_fusion.3), channel_id=1, source_target_pairs={{0,2},{1,3},{2,0},{3,1},{4,6},{5,7},{6,4},{7,5},{8,10},{9,11},{10,... | collective-permute-start | bytes 2312 | tf_op jit(solution)/shard_map/ppermute | solution.py:60
  57.9 0.5 collective-permute-start.2
  58.4 1.2 slice_bitcast_fusion.1
  59.6 2.0 %collective-permute-done.2 = f32[12,16]{1,0:T(8,128)S(1)} collective-permute-done((f32[12,16]{1,0:T(8,128)S(1)}, f32[12,16]{1,0:T(8,128)S(1)}, u32[]{:S(2)}, u32[]{:S(2)}) %collective-permute-start.2) | collective-permute-done | bytes 800 | tf_op jit(solution)/shard_map/ppermute | solution.py:60
  61.5 0.3 fusion.18
  62.0 1.1 stack_reshape.28
  63.1 1.4 %fusion.17 = bf16[16,9,12,128]{3,0,2,1:T(8,128)(2,1)S(1)} fusion(bf16[9,12,16,128]{3,2,1,0:T(8,128)(2,1)} %get-tuple-element.18, bf16[9,12,16,16]{2,3,1,0:T(8,128)(2,1)S(1)} %copy-done.1), kind=kOutput, calls=%fused_computation.34 | convolution fusion | flops 7520256 | bytes 940032 | tf_op jit(solution)/shard_map/phij,phje->phie/dot_general | solution.py:132
  64.6 1.1 stack_reshape.29
  65.7 0.4 fusion.16
  66.2 1.1 stack_reshape.30
  67.3 0.4 fusion.19
  67.8 0.3 stack_reshape.31
  68.1 0.2 copy-done.12
  68.4 0.3 copy-done.14
  68.7 0.2 pad_maximum_fusion.1
  68.9 2.6 %copy.106 = bf16[16,9,4,1536]{3,2,1,0:T(4,128)(2,1)} copy(bf16[16,9,4,1536]{3,0,1,2:T(8,128)(2,1)S(1)} %pad_maximum_fusion.1) | data formatting | bytes 3538944 | tf_op jit(solution)/shard_map/optimization_barrier | solution.py:146
  71.6 8.0 %all-to-all-start.1 = ((bf16[16,9,4,1536]{3,2,1,0:T(4,128)(2,1)}), bf16[16,9,4,1536]{3,2,1,0:T(4,128)(2,1)S(1)}, u32[]{:S(2)}, u32[]{:S(2)}) async-start(bf16[16,9,4,1536]{3,2,1,0:T(4,128)(2,1)} %copy.106), calls=%async_computation.1 | async-start | bytes 3538944 | tf_op jit(solution)/shard_map/all_to_all | solution.py:150
  79.6 2.9 %convolution_bitcast_fusion = f32[1,1,12,18,8,128]{5,4,3,2,1,0:T(8,128)} fusion(bf16[144,12,128]{2,1,0:T(8,128)(2,1)S(1)} %copy-done.19, f32[12,144,144]{1,2,0:T(8,128)} %get-tuple-element.32, f32[12,144]{1,0:T(8,128)S(1)} %copy-done.21), kind=kOutput, calls=%fused_computation.27 | convolution fusion | flops 64198656 | bytes 2329344 | tf_op jit(solution)/shard_map/bfhij,bfihe->bfjhe/dot_general | solution.py:39
  82.5 1.5 %collective-permute-start.3 = (f32[12,16]{1,0:T(8,128)S(1)}, f32[12,16]{1,0:T(8,128)S(1)}, u32[]{:S(2)}, u32[]{:S(2)}) collective-permute-start(f32[12,16]{1,0:T(8,128)S(1)} %add_add_fusion.2), channel_id=1, source_target_pairs={{0,4},{1,5},{2,6},{3,7},{4,0},{5,1},{6,2},{7,3},{8,12},{9,13},{10,... | collective-permute-start | bytes 2312 | tf_op jit(solution)/shard_map/ppermute | solution.py:60
  84.0 2.7 %collective-permute-start.4 = (f32[12,16]{1,0:T(8,128)S(1)}, f32[12,16]{1,0:T(8,128)S(1)}, u32[]{:S(2)}, u32[]{:S(2)}) collective-permute-start(f32[12,16]{1,0:T(8,128)S(1)} %add_add_fusion.2), channel_id=1, source_target_pairs={{0,8},{1,9},{2,10},{3,11},{4,12},{5,13},{6,14},{7,15},{8,0},{9,1},... | collective-permute-start | bytes 2312 | tf_op jit(solution)/shard_map/ppermute | solution.py:60
  86.7 0.6 collective-permute-start.5
  87.2 1.5 %convolution_bitcast_fusion.1 = f32[1,1,12,18,8,128]{5,4,3,2,1,0:T(8,128)} fusion(bf16[144,12,128]{2,1,0:T(8,128)(2,1)S(1)} %copy-done.18, f32[12,144,144]{1,2,0:T(8,128)S(1)} %copy-done.9, f32[12,144]{1,0:T(8,128)S(1)} %copy-done.21), kind=kOutput, calls=%fused_computation.28 | convolution fusion | flops 64198656 | bytes 2329344 | tf_op jit(solution)/shard_map/bfhij,bfjhe->bfihe/dot_general | solution.py:31
  88.8 6.8 %collective-permute-done.3 = f32[12,16]{1,0:T(8,128)S(1)} collective-permute-done((f32[12,16]{1,0:T(8,128)S(1)}, f32[12,16]{1,0:T(8,128)S(1)}, u32[]{:S(2)}, u32[]{:S(2)}) %collective-permute-start.3) | collective-permute-done | bytes 800 | tf_op jit(solution)/shard_map/ppermute | solution.py:60
  95.6 3.7 %collective-permute-done.4 = f32[12,16]{1,0:T(8,128)S(1)} collective-permute-done((f32[12,16]{1,0:T(8,128)S(1)}, f32[12,16]{1,0:T(8,128)S(1)}, u32[]{:S(2)}, u32[]{:S(2)}) %collective-permute-start.4) | collective-permute-done | bytes 800 | tf_op jit(solution)/shard_map/ppermute | solution.py:60
  99.4 2.0 %collective-permute-start.7 = (f32[12,16]{1,0:T(8,128)S(1)}, f32[12,16]{1,0:T(8,128)S(1)}, u32[]{:S(2)}, u32[]{:S(2)}) collective-permute-start(f32[12,16]{1,0:T(8,128)S(1)} %add_add_fusion.1), channel_id=1, source_target_pairs={{0,32},{16,48},{32,0},{48,16},{64,96},{80,112},{96,64},{112,80},{1... | collective-permute-start | bytes 2312 | tf_op jit(solution)/shard_map/ppermute | solution.py:60
  101.4 0.4 fusion.8
  101.8 1.3 %collective-permute-done.7 = f32[12,16]{1,0:T(8,128)S(1)} collective-permute-done((f32[12,16]{1,0:T(8,128)S(1)}, f32[12,16]{1,0:T(8,128)S(1)}, u32[]{:S(2)}, u32[]{:S(2)}) %collective-permute-start.7) | collective-permute-done | bytes 800 | tf_op jit(solution)/shard_map/ppermute | solution.py:60
  103.1 1.3 %collective-permute-done.8 = f32[12,16]{1,0:T(8,128)S(1)} collective-permute-done((f32[12,16]{1,0:T(8,128)S(1)}, f32[12,16]{1,0:T(8,128)S(1)}, u32[]{:S(2)}, u32[]{:S(2)}) %collective-permute-start.8) | collective-permute-done | bytes 800 | tf_op jit(solution)/shard_map/ppermute | solution.py:60
  104.5 6.3 %collective-permute-start.10 = (f32[12,16]{1,0:T(8,128)S(1)}, f32[12,16]{1,0:T(8,128)S(1)}, u32[]{:S(2)}, u32[]{:S(2)}) collective-permute-start(f32[12,16]{1,0:T(8,128)S(1)} %add_add_fusion), channel_id=1, source_target_pairs={{0,128},{16,144},{32,160},{48,176},{64,192},{80,208},{96,224},{112... | collective-permute-start | bytes 2312 | tf_op jit(solution)/shard_map/ppermute | solution.py:60
  110.8 0.6 collective-permute-start.11
  111.3 0.9 collective-permute-start.9
  112.3 1.5 %fusion.7 = f32[1,1,12,18,8,128]{5,4,3,2,1,0:T(8,128)} fusion(bf16[12,144,144]{1,2,0:T(8,128)(2,1)S(1)} %multiply_convert_fusion, bf16[144,12,128]{2,1,0:T(8,128)(2,1)S(1)} %copy-done.4), kind=kOutput, calls=%fused_computation.17 | convolution fusion | flops 63922176 | bytes 1824768 | tf_op jit(solution)/shard_map/bfhij,bfjhe->bfihe/dot_general | solution.py:49
  113.8 2.8 %collective-permute-done.11 = f32[12,16]{1,0:T(8,128)S(1)} collective-permute-done((f32[12,16]{1,0:T(8,128)S(1)}, f32[12,16]{1,0:T(8,128)S(1)}, u32[]{:S(2)}, u32[]{:S(2)}) %collective-permute-start.11) | collective-permute-done | bytes 800 | tf_op jit(solution)/shard_map/ppermute | solution.py:60
  116.5 0.6 add_multiply_fusion
  117.2 0.5 convert_bitcast_fusion
  117.7 2.6 %fusion.65 = (f32[1,16,9,1536]{3,0,2,1:T(1,128)S(1)}, f32[1,16,9,1536]{3,0,2,1:T(1,128)S(1)}, f32[1,16,9,1536]{3,0,2,1:T(1,128)S(1)}, f32[1,16,9,1536]{3,0,2,1:T(1,128)S(1)}) fusion(f32[4,16,9,1536]{3,0,2,1:T(4,128)S(1)} %convert_bitcast_fusion), kind=kLoop, calls=%fused_computation.89 | loop fusion | bytes 7077888 | tf_op jit(solution)/shard_map/slice | solution.py:166
  120.3 1.2 fusion.20
  121.5 0.6 copy-done.17
  122.1 1.2 fusion.22
  (62 shorter events, 1.1 us)
Async XLA Ops:
  0.6 21.3 %copy-start = (f32[12,16]{1,0:T(8,128)S(1)}, f32[12,16]{1,0:T(8,128)}, u32[]{:S(2)}) copy-start(f32[12,16]{1,0:T(8,128)} %param.13) | copy-start | bytes 2308
  0.6 2.5 %copy-start.11 = (bf16[1,1,144,1536]{3,2,1,0:T(8,128)(2,1)S(1)}, bf16[1,1,144,1536]{3,2,1,0:T(8,128)(2,1)}, u32[]{:S(2)}) copy-start(bf16[1,1,144,1536]{3,2,1,0:T(8,128)(2,1)} %param.9) | copy-start | bytes 1327108
  7.9 7.6 %copy-start.10 = (bf16[1,1,144,1536]{3,2,1,0:T(8,128)(2,1)S(1)}, bf16[1,1,144,1536]{3,2,1,0:T(8,128)(2,1)}, u32[]{:S(2)}) copy-start(bf16[1,1,144,1536]{3,2,1,0:T(8,128)(2,1)} %param.7) | copy-start | bytes 1327108
  7.9 30.8 %all-to-all-start = ((bf16[16,9,4,1536]{3,2,1,0:T(4,128)(2,1)}), bf16[16,9,4,1536]{3,2,1,0:T(4,128)(2,1)S(1)}, u32[]{:S(2)}, u32[]{:S(2)}) async-start(bf16[16,9,4,1536]{3,2,1,0:T(4,128)(2,1)} %copy.94), calls=%async_computation | async-start | bytes 3538944 | tf_op jit(solution)/shard_map/all_to_all | solution.py:92
  15.9 10.5 %copy-start.5 = (bf16[144,12,128]{2,1,0:T(8,128)(2,1)}, bf16[144,12,128]{2,1,0:T(8,128)(2,1)S(1)}, u32[]{:S(2)}) copy-start(bf16[144,12,128]{2,1,0:T(8,128)(2,1)S(1)} %reshape.278) | copy-start | bytes 1327108
  15.9 7.8 %copy-start.22 = (s32[1,16]{1,0:T(1,128)S(1)}, s32[1,16]{1,0:T(1,128)}, u32[]{:S(2)}) copy-start(s32[1,16]{1,0:T(1,128)} %param.12) | copy-start | bytes 196
  17.4 8.9 %copy-start.3 = (bf16[144,12,128]{2,1,0:T(8,128)(2,1)}, bf16[144,12,128]{2,1,0:T(8,128)(2,1)S(1)}, u32[]{:S(2)}) copy-start(bf16[144,12,128]{2,1,0:T(8,128)(2,1)S(1)} %reshape.279) | copy-start | bytes 1327108
  26.4 2.4 %copy-start.20 = (f32[12,144]{1,0:T(8,128)}, f32[12,144]{1,0:T(8,128)S(1)}, u32[]{:S(2)}) copy-start(f32[12,144]{1,0:T(8,128)S(1)} %get-tuple-element.31) | copy-start | bytes 20740
  26.4 2.4 %copy-start.8 = (f32[12,144,144]{1,2,0:T(8,128)S(1)}, f32[12,144,144]{1,2,0:T(8,128)}, u32[]{:S(2)}) copy-start(f32[12,144,144]{1,2,0:T(8,128)} %get-tuple-element.32) | copy-start | bytes 2985988
  53.7 5.8 %collective-permute-start = (f32[12,16]{1,0:T(8,128)S(1)}, f32[12,16]{1,0:T(8,128)S(1)}, u32[]{:S(2)}, u32[]{:S(2)}) collective-permute-start(f32[12,16]{1,0:T(8,128)S(1)} %convolution_bitcast_fusion.3), channel_id=1, source_target_pairs={{0,1},{1,0},{2,3},{3,2},{4,5},{5,4},{6,7},{7,6},{8,9},{9,8},{10,11... | collective-permute-start | bytes 2312 | tf_op jit(solution)/shard_map/ppermute | solution.py:60
  54.4 5.2 %collective-permute-start.1 = (f32[12,16]{1,0:T(8,128)S(1)}, f32[12,16]{1,0:T(8,128)S(1)}, u32[]{:S(2)}, u32[]{:S(2)}) collective-permute-start(f32[12,16]{1,0:T(8,128)S(1)} %convolution_bitcast_fusion.3), channel_id=1, source_target_pairs={{0,2},{1,3},{2,0},{3,1},{4,6},{5,7},{6,4},{7,5},{8,10},{9,11},{10,... | collective-permute-start | bytes 2312 | tf_op jit(solution)/shard_map/ppermute | solution.py:60
  57.9 3.7 %collective-permute-start.2 = (f32[12,16]{1,0:T(8,128)S(1)}, f32[12,16]{1,0:T(8,128)S(1)}, u32[]{:S(2)}, u32[]{:S(2)}) collective-permute-start(f32[12,16]{1,0:T(8,128)S(1)} %convolution_bitcast_fusion.3), channel_id=1, source_target_pairs={{0,3},{1,2},{2,1},{3,0},{4,7},{5,6},{6,5},{7,4},{8,11},{9,10},{10,... | collective-permute-start | bytes 2312 | tf_op jit(solution)/shard_map/ppermute | solution.py:60
  61.5 1.5 %copy-start.1 = (bf16[9,12,16,16]{2,3,1,0:T(8,128)(2,1)S(1)}, bf16[9,12,16,16]{2,3,1,0:T(8,128)(2,1)}, u32[]{:S(2)}) copy-start(bf16[9,12,16,16]{2,3,1,0:T(8,128)(2,1)} %get-tuple-element.17) | copy-start | bytes 165892
  63.1 2.6 %copy-start.15 = (bf16[9,12,16,128]{3,2,1,0:T(8,128)(2,1)S(1)}, bf16[9,12,16,128]{3,2,1,0:T(8,128)(2,1)}, u32[]{:S(2)}) copy-start(bf16[9,12,16,128]{3,2,1,0:T(8,128)(2,1)} %get-tuple-element.19) | copy-start | bytes 1327108
  65.7 1.6 %copy-start.7 = (bf16[9,12,16,128]{3,2,1,0:T(8,128)(2,1)S(1)}, bf16[9,12,16,128]{3,2,1,0:T(8,128)(2,1)}, u32[]{:S(2)}) copy-start(bf16[9,12,16,128]{3,2,1,0:T(8,128)(2,1)} %get-tuple-element.20) | copy-start | bytes 1327108
  67.3 1.0 copy-start.12
  67.3 1.1 copy-start.13
  67.6 1.1 copy-start.14
  71.5 8.0 %copy-start.19 = (bf16[144,12,128]{2,1,0:T(8,128)(2,1)S(1)}, bf16[144,12,128]{2,1,0:T(8,128)(2,1)}, u32[]{:S(2)}) copy-start(bf16[144,12,128]{2,1,0:T(8,128)(2,1)} %reshape.283) | copy-start | bytes 1327108
  71.5 8.0 %copy-start.21 = (f32[12,144]{1,0:T(8,128)S(1)}, f32[12,144]{1,0:T(8,128)}, u32[]{:S(2)}) copy-start(f32[12,144]{1,0:T(8,128)} %copy-done.20) | copy-start | bytes 20740
  71.6 45.6 %all-to-all-start.1 = ((bf16[16,9,4,1536]{3,2,1,0:T(4,128)(2,1)}), bf16[16,9,4,1536]{3,2,1,0:T(4,128)(2,1)S(1)}, u32[]{:S(2)}, u32[]{:S(2)}) async-start(bf16[16,9,4,1536]{3,2,1,0:T(4,128)(2,1)} %copy.106), calls=%async_computation.1 | async-start | bytes 3538944 | tf_op jit(solution)/shard_map/all_to_all | solution.py:150
  79.6 7.7 %copy-start.9 = (f32[12,144,144]{1,2,0:T(8,128)S(1)}, f32[12,144,144]{1,2,0:T(8,128)}, u32[]{:S(2)}) copy-start(f32[12,144,144]{1,2,0:T(8,128)} %get-tuple-element.32) | copy-start | bytes 2985988
  79.6 7.7 %copy-start.18 = (bf16[144,12,128]{2,1,0:T(8,128)(2,1)S(1)}, bf16[144,12,128]{2,1,0:T(8,128)(2,1)}, u32[]{:S(2)}) copy-start(bf16[144,12,128]{2,1,0:T(8,128)(2,1)} %reshape.280) | copy-start | bytes 1327108
  82.5 18.9 %copy-start.6 = (bf16[144,12,128]{2,1,0:T(8,128)(2,1)S(1)}, bf16[144,12,128]{2,1,0:T(8,128)(2,1)}, u32[]{:S(2)}) copy-start(bf16[144,12,128]{2,1,0:T(8,128)(2,1)} %copy-done.5) | copy-start | bytes 1327108
  82.5 13.1 %collective-permute-start.3 = (f32[12,16]{1,0:T(8,128)S(1)}, f32[12,16]{1,0:T(8,128)S(1)}, u32[]{:S(2)}, u32[]{:S(2)}) collective-permute-start(f32[12,16]{1,0:T(8,128)S(1)} %add_add_fusion.2), channel_id=1, source_target_pairs={{0,4},{1,5},{2,6},{3,7},{4,0},{5,1},{6,2},{7,3},{8,12},{9,13},{10,... | collective-permute-start | bytes 2312 | tf_op jit(solution)/shard_map/ppermute | solution.py:60
  84.0 15.3 %collective-permute-start.4 = (f32[12,16]{1,0:T(8,128)S(1)}, f32[12,16]{1,0:T(8,128)S(1)}, u32[]{:S(2)}, u32[]{:S(2)}) collective-permute-start(f32[12,16]{1,0:T(8,128)S(1)} %add_add_fusion.2), channel_id=1, source_target_pairs={{0,8},{1,9},{2,10},{3,11},{4,12},{5,13},{6,14},{7,15},{8,0},{9,1},... | collective-permute-start | bytes 2312 | tf_op jit(solution)/shard_map/ppermute | solution.py:60
  86.7 12.6 %collective-permute-start.5 = (f32[12,16]{1,0:T(8,128)S(1)}, f32[12,16]{1,0:T(8,128)S(1)}, u32[]{:S(2)}, u32[]{:S(2)}) collective-permute-start(f32[12,16]{1,0:T(8,128)S(1)} %add_add_fusion.2), channel_id=1, source_target_pairs={{0,12},{1,13},{2,14},{3,15},{4,8},{5,9},{6,10},{7,11},{8,4},{9,5},... | collective-permute-start | bytes 2312 | tf_op jit(solution)/shard_map/ppermute | solution.py:60
  88.8 23.5 %copy-start.4 = (bf16[144,12,128]{2,1,0:T(8,128)(2,1)S(1)}, bf16[144,12,128]{2,1,0:T(8,128)(2,1)}, u32[]{:S(2)}) copy-start(bf16[144,12,128]{2,1,0:T(8,128)(2,1)} %copy-done.3) | copy-start | bytes 1327108
  99.3 2.5 %collective-permute-start.6 = (f32[12,16]{1,0:T(8,128)S(1)}, f32[12,16]{1,0:T(8,128)S(1)}, u32[]{:S(2)}, u32[]{:S(2)}) collective-permute-start(f32[12,16]{1,0:T(8,128)S(1)} %add_add_fusion.1), channel_id=1, source_target_pairs={{0,16},{16,0},{32,48},{48,32},{64,80},{80,64},{96,112},{112,96},{1... | collective-permute-start | bytes 2312 | tf_op jit(solution)/shard_map/ppermute | solution.py:60
  99.4 3.7 %collective-permute-start.7 = (f32[12,16]{1,0:T(8,128)S(1)}, f32[12,16]{1,0:T(8,128)S(1)}, u32[]{:S(2)}, u32[]{:S(2)}) collective-permute-start(f32[12,16]{1,0:T(8,128)S(1)} %add_add_fusion.1), channel_id=1, source_target_pairs={{0,32},{16,48},{32,0},{48,16},{64,96},{80,112},{96,64},{112,80},{1... | collective-permute-start | bytes 2312 | tf_op jit(solution)/shard_map/ppermute | solution.py:60
  101.4 3.1 %collective-permute-start.8 = (f32[12,16]{1,0:T(8,128)S(1)}, f32[12,16]{1,0:T(8,128)S(1)}, u32[]{:S(2)}, u32[]{:S(2)}) collective-permute-start(f32[12,16]{1,0:T(8,128)S(1)} %add_add_fusion.1), channel_id=1, source_target_pairs={{0,48},{16,32},{32,16},{48,0},{64,112},{80,96},{96,80},{112,64},{1... | collective-permute-start | bytes 2312 | tf_op jit(solution)/shard_map/ppermute | solution.py:60
  104.5 9.3 %collective-permute-start.10 = (f32[12,16]{1,0:T(8,128)S(1)}, f32[12,16]{1,0:T(8,128)S(1)}, u32[]{:S(2)}, u32[]{:S(2)}) collective-permute-start(f32[12,16]{1,0:T(8,128)S(1)} %add_add_fusion), channel_id=1, source_target_pairs={{0,128},{16,144},{32,160},{48,176},{64,192},{80,208},{96,224},{112... | collective-permute-start | bytes 2312 | tf_op jit(solution)/shard_map/ppermute | solution.py:60
  110.8 5.8 %collective-permute-start.11 = (f32[12,16]{1,0:T(8,128)S(1)}, f32[12,16]{1,0:T(8,128)S(1)}, u32[]{:S(2)}, u32[]{:S(2)}) collective-permute-start(f32[12,16]{1,0:T(8,128)S(1)} %add_add_fusion), channel_id=1, source_target_pairs={{0,192},{16,208},{32,224},{48,240},{64,128},{80,144},{96,160},{112... | collective-permute-start | bytes 2312 | tf_op jit(solution)/shard_map/ppermute | solution.py:60
  111.3 5.2 %collective-permute-start.9 = (f32[12,16]{1,0:T(8,128)S(1)}, f32[12,16]{1,0:T(8,128)S(1)}, u32[]{:S(2)}, u32[]{:S(2)}) collective-permute-start(f32[12,16]{1,0:T(8,128)S(1)} %add_add_fusion), channel_id=1, source_target_pairs={{0,64},{16,80},{32,96},{48,112},{64,0},{80,16},{96,32},{112,48},{1... | collective-permute-start | bytes 2312 | tf_op jit(solution)/shard_map/ppermute | solution.py:60
  117.6 2.7 %copy-start.16 = (f32[1,1,12,18,8,128]{5,4,3,2,1,0:T(8,128)S(1)}, f32[1,1,12,18,8,128]{5,4,3,2,1,0:T(8,128)}, u32[]{:S(2)}) copy-start(f32[1,1,12,18,8,128]{5,4,3,2,1,0:T(8,128)} %convolution_bitcast_fusion) | copy-start | bytes 2654212
  120.3 1.2 copy-start.2
  120.3 1.7 %copy-start.17 = (f32[1,1,12,18,8,128]{5,4,3,2,1,0:T(8,128)S(1)}, f32[1,1,12,18,8,128]{5,4,3,2,1,0:T(8,128)}, u32[]{:S(2)}) copy-start(f32[1,1,12,18,8,128]{5,4,3,2,1,0:T(8,128)} %convolution_bitcast_fusion.1) | copy-start | bytes 2654212

commit v9 on v3

--- a/solution.py
+++ b/solution.py
@@ -84,7 +84,7 @@
     block = positions // seq_size
     stacked = jnp.stack(
         [
-            tensor.reshape(seq_size, block, width)
+            jnp.swapaxes(tensor.reshape(block, seq_size, width), 0, 1)
             for tensor in (queries, keys, values, cotangent)
         ],
         axis=2,
@@ -148,7 +148,7 @@
     summed = quad_step(quad_step(partial, "dp", dp_size, 1), "dp", dp_size, 4)
     bias_grad = summed / math.sqrt(dp_size * queries.shape[0] * frames_all * positions)
     back = lax.all_to_all(back_rows, "seq", split_axis=0, concat_axis=0, tiled=True)
-    back = jnp.moveaxis(back, 2, 0).reshape(4, 1, 1, positions, width).astype(jnp.float32)
+    back = jnp.transpose(back, (2, 1, 0, 3)).reshape(4, 1, 1, positions, width).astype(jnp.float32)
 
     space_query = split_heads(queries, head_count)
     space_key = split_heads(keys, head_count)

time: 106 us -> 105 us (level)
  local copies, waits for them, and re-layouts: 28.3 us -> 25.7 us
    another operation x9 -> x5, local copies, waits for them, and re-layouts: 10.9 us -> 6.96 us  [the longest x5 6.64 us: on_device(): jnp.stack([tensor.reshape(seq_size, block, width) for tensor in (queries,...]
    slice x1 -> x2, local copies, waits for them, and re-layouts: 2.64 us -> 2.7 us  [on_device(): value_grad = (join_heads(space_grads[2]) + back[3]).astype(jnp.bfloat16)]
  transfers between devices with their start and end apart: 14 -> 14, of which waited for: 5 -> 5; matrix products, arithmetic and copies ran while one was open for 25% -> 26% of each run, Pallas kernels for 0% -> 0%
where the time goes in v9:
time: 105 us; the launch traced here: 103 us
  starting transfers between devices  34.8 us (33%)
  local copies, waits for them, and re-layouts  25.7 us (24%)
  matrix products  16.1 us (15%)
  waiting for transfers between devices  15.8 us (15%)
  other arithmetic  9.28 us (9%)
  between operations  1.69 us (2%)
    ppermute x12, starting transfers between devices, quad_step(): lax.ppermute(value, axis, [(index, index ^ part * step) for index in rang...  19.2 us
    ppermute x12, waiting for transfers between devices, quad_step(): lax.ppermute(value, axis, [(index, index ^ part * step) for index in rang...  8.25 us
    all_to_all x1, starting transfers between devices, on_device(): lax.all_to_all(back_rows, 'seq', split_axis=0, concat_axis=0, tiled=True)  7.99 us
    all_to_all x1, starting transfers between devices, on_device(): lax.all_to_all(stacked, 'seq', split_axis=0, concat_axis=0, tiled=True)  7.58 us
    all_to_all x1, waiting for transfers between devices, on_device(): lax.all_to_all(stacked, 'seq', split_axis=0, concat_axis=0, tiled=True)  7.5 us
    reshape x2, local copies, waits for them, and re-layouts, on_device(): rows = rows.reshape(seq_size, block, 4, head_count, width // head_count)  6.25 us
    another operation x4, local copies, waits for them, and re-layouts  4.35 us
    sub x1, matrix products, attend_forward(): weights = jnp.exp(scores - row_peak)  3.27 us
  transfers between devices with their start and end apart: 14, of which 5 were waited for; matrix products, arithmetic and copies ran while one was open for 26% of the time, Pallas kernels for 0%

profile of v9, /device:TPU:4, one launch (start us, length us, event | category | flops | bytes accessed | tf_op | source)
XLA Modules:
  0.0 103.2 jit_solution(12160425400553442015)
XLA Ops:
  0.6 1.6 %pad_maximum_fusion = bf16[16,9,4,1536]{3,0,2,1:T(8,128)(2,1)S(1)} fusion(bf16[16,9,1,1536]{3,0,2,1:T(8,128)(2,1)} %bitcast.152, bf16[16,9,1,1536]{3,0,2,1:T(8,128)(2,1)} %bitcast.151, bf16[16,9,1,1536]{3,0,2,1:T(8,128)(2,1)} %bitcast.150, bf16[16,9,1,1536]{3,0,2,1:T(8,128)(2,1)} %bitcast.149), kind=kLoop, calls=%fused_computation.5 | loop fusion | flops 2654208 | bytes 3538944 | tf_op jit(solution)/shard_map/stack | solution.py:85
  2.3 2.6 %copy.115 = bf16[16,9,4,1536]{3,2,1,0:T(4,128)(2,1)} copy(bf16[16,9,4,1536]{3,0,2,1:T(8,128)(2,1)S(1)} %pad_maximum_fusion) | data formatting | bytes 3538944 | tf_op jit(solution)/shard_map/stack | solution.py:85
  4.9 7.6 %all-to-all-start = ((bf16[16,9,4,1536]{3,2,1,0:T(4,128)(2,1)}), bf16[16,9,4,1536]{3,2,1,0:T(4,128)(2,1)S(1)}, u32[]{:S(2)}, u32[]{:S(2)}) async-start(bf16[16,9,4,1536]{3,2,1,0:T(4,128)(2,1)} %copy.115), calls=%async_computation | async-start | bytes 3538944 | tf_op jit(solution)/shard_map/all_to_all | solution.py:92
  12.5 0.3 reshape.290
  12.8 0.3 reshape.291
  13.2 2.4 %reshape.292 = bf16[144,12,128]{2,1,0:T(8,128)(2,1)} reshape(bf16[1,1,144,1536]{3,2,1,0:T(8,128)(2,1)} %param.9) | data formatting | bytes 884736 | tf_op jit(solution)/shard_map/reshape.7
  15.6 1.3 %reshape.299 = bf16[144,12,128]{2,1,0:T(8,128)(2,1)S(1)} reshape(bf16[1,1,144,1536]{3,2,1,0:T(8,128)(2,1)} %param.10) | data formatting | bytes 884736 | tf_op jit(solution)/shard_map/reshape.12
  16.9 0.9 convolution_bitcast_fusion.2
  17.8 1.7 %copy.119 = f32[12,16,16]{1,2,0:T(8,128)} copy(f32[12,16,16]{0,2,1:T(8,128)} %convolution_bitcast_fusion.2) | data formatting | bytes 24576 | tf_op jit(solution)/shard_map/dot_general | solution.py:77
  20.2 0.5 iota_compare_fusion.2
  20.7 1.4 %broadcast_compare_fusion = pred[16,16]{0,1:T(8,128)(4,1)} fusion(s32[16]{0:T(128)} %bitcast.153), kind=kLoop, calls=%fused_computation.83 | loop fusion | flops 256 | bytes 320 | tf_op jit(solution)/shard_map/eq | solution.py:80
  22.1 3.3 %fusion.66 = (f32[12,144]{1,0:T(8,128)}, f32[12,144,144]{1,2,0:T(8,128)}) fusion(pred[144]{0:T(512)(128)(4,1)} %iota_compare_fusion.2, bf16[144,12,128]{2,1,0:T(8,128)(2,1)S(1)} %reshape.291, bf16[144,12,128]{2,1,0:T(8,128)(2,1)S(1)} %reshape.290), kind=kOutput, calls=%fused_computation.90 | convolution fusion | flops 64696464 | bytes 1887120 | tf_op jit(solution)/shard_map/sub | solution.py:28
  25.4 2.8 %convolution_bitcast_fusion = f32[1,1,12,18,8,128]{5,4,3,2,1,0:T(8,128)} fusion(bf16[144,12,128]{2,1,0:T(8,128)(2,1)S(1)} %reshape.299, f32[12,144,144]{1,2,0:T(8,128)} %get-tuple-element.32, f32[12,144]{1,0:T(8,128)} %get-tuple-element.31), kind=kOutput, calls=%fused_computation.27 | convolution fusion | flops 64198656 | bytes 2329344 | tf_op jit(solution)/shard_map/bfhij,bfihe->bfjhe/dot_general | solution.py:39
  28.2 7.5 %all-to-all-done = bf16[16,9,4,1536]{3,2,1,0:T(4,128)(2,1)S(1)} async-done(((bf16[16,9,4,1536]{3,2,1,0:T(4,128)(2,1)}), bf16[16,9,4,1536]{3,2,1,0:T(4,128)(2,1)S(1)}, u32[]{:S(2)}, u32[]{:S(2)}) %all-to-all-start) | async-done | bytes 1769504 | tf_op jit(solution)/shard_map/all_to_all | solution.py:92
  35.7 2.5 %reshape.305 = bf16[16,9,4,12,128]{4,3,2,1,0:T(8,128)(2,1)} reshape(bf16[16,9,4,1536]{3,2,1,0:T(4,128)(2,1)S(1)} %all-to-all-done) | data formatting | bytes 3538944 | tf_op jit(solution)/shard_map/reshape | solution.py:93
  38.2 3.7 %copy.193 = bf16[16,9,4,12,128]{4,0,3,1,2:T(8,128)(2,1)S(1)} copy(bf16[16,9,4,12,128]{4,3,2,1,0:T(8,128)(2,1)} %reshape.305) | data formatting | bytes 3538944 | tf_op jit(solution)/shard_map/reshape | solution.py:93
  42.0 1.3 %fusion.64 = f32[9,12,16,16]{2,3,1,0:T(8,128)} fusion(bf16[4,9,12,16,128]{4,3,2,1,0:T(8,128)(2,1)S(1)} %bitcast.142), kind=kOutput, calls=%fused_computation.88 | convolution fusion | flops 7077888 | bytes 995328 | tf_op jit(solution)/shard_map/phie,phje->phij/dot_general | solution.py:106
  43.3 0.6 fusion.6
  43.9 1.8 %fusion.71 = (f32[12,16,16]{1,2,0:T(8,128)S(1)}, bf16[9,12,16,16]{2,3,1,0:T(8,128)(2,1)S(1)}) fusion(f32[9,12,16,16]{2,3,1,0:T(8,128)S(1)} %fusion.6, f32[9,12,16,16]{2,3,1,0:T(8,128)} %fusion.64), kind=kOutput, calls=%fused_computation.91 | output fusion | flops 136911 | bytes 288768 | tf_op jit(solution)/shard_map/sub | solution.py:110
  45.6 0.1 copy.120
  45.8 0.2 convolution_bitcast_fusion.3
  46.0 0.7 collective-permute-start
  46.6 3.5 %collective-permute-start.1 = (f32[12,16]{1,0:T(8,128)S(1)}, f32[12,16]{1,0:T(8,128)S(1)}, u32[]{:S(2)}, u32[]{:S(2)}) collective-permute-start(f32[12,16]{1,0:T(8,128)S(1)} %convolution_bitcast_fusion.3), channel_id=1, source_target_pairs={{0,2},{1,3},{2,0},{3,1},{4,6},{5,7},{6,4},{7,5},{8,10},{9,11},{10,... | collective-permute-start | bytes 2312 | tf_op jit(solution)/shard_map/ppermute | solution.py:60
  50.1 0.5 collective-permute-start.2
  50.6 1.3 %slice_bitcast_fusion.1 = (bf16[9,12,16,128]{3,2,1,0:T(8,128)(2,1)S(1)}, bf16[9,12,16,128]{3,2,1,0:T(8,128)(2,1)S(1)}, bf16[9,12,16,128]{3,2,1,0:T(8,128)(2,1)}, bf16[9,12,16,128]{3,2,1,0:T(8,128)(2,1)}) fusion(bf16[4,9,12,16,128]{4,3,2,1,0:T(8,128)(2,1)S(1)} %bitcast.144), kind=kLoop, calls=%fused_computation.54 | loop fusion | bytes 3538944 | tf_op jit(solution)/shard_map/squeeze | solution.py:95
  51.8 1.9 %collective-permute-done.2 = f32[12,16]{1,0:T(8,128)S(1)} collective-permute-done((f32[12,16]{1,0:T(8,128)S(1)}, f32[12,16]{1,0:T(8,128)S(1)}, u32[]{:S(2)}, u32[]{:S(2)}) %collective-permute-start.2) | collective-permute-done | bytes 800 | tf_op jit(solution)/shard_map/ppermute | solution.py:60
  53.8 0.1 collective-permute-start.3
  53.8 2.7 %collective-permute-start.4 = (f32[12,16]{1,0:T(8,128)S(1)}, f32[12,16]{1,0:T(8,128)S(1)}, u32[]{:S(2)}, u32[]{:S(2)}) collective-permute-start(f32[12,16]{1,0:T(8,128)S(1)} %add_add_fusion.2), channel_id=1, source_target_pairs={{0,8},{1,9},{2,10},{3,11},{4,12},{5,13},{6,14},{7,15},{8,0},{9,1},... | collective-permute-start | bytes 2312 | tf_op jit(solution)/shard_map/ppermute | solution.py:60
  56.6 1.9 %collective-permute-start.5 = (f32[12,16]{1,0:T(8,128)S(1)}, f32[12,16]{1,0:T(8,128)S(1)}, u32[]{:S(2)}, u32[]{:S(2)}) collective-permute-start(f32[12,16]{1,0:T(8,128)S(1)} %add_add_fusion.2), channel_id=1, source_target_pairs={{0,12},{1,13},{2,14},{3,15},{4,8},{5,9},{6,10},{7,11},{8,4},{9,5},... | collective-permute-start | bytes 2312 | tf_op jit(solution)/shard_map/ppermute | solution.py:60
  58.5 0.3 fusion.18
  58.8 0.1 copy.122
  58.9 0.3 stack_reshape.12
  59.3 0.3 fusion.17
  59.6 0.1 copy.124
  59.7 0.3 stack_reshape.13
  60.0 1.4 %fusion.16 = bf16[16,9,12,128]{3,0,2,1:T(8,128)(2,1)S(1)} fusion(bf16[9,12,16,128]{3,2,1,0:T(8,128)(2,1)} %get-tuple-element.19, bf16[9,12,16,16]{2,3,1,0:T(8,128)(2,1)S(1)} %get-tuple-element.17), kind=kOutput, calls=%fused_computation.33 | convolution fusion | flops 7520256 | bytes 940032 | tf_op jit(solution)/shard_map/phij,phie->phje/dot_general | solution.py:136
  61.4 0.1 copy.125
  61.6 1.1 %stack_reshape.14 = bf16[16,9,1,1536]{3,0,1,2:T(8,128)(2,1)} reshape(bf16[16,9,12,128]{3,2,0,1:T(8,128)(2,1)S(1)} %copy.125) | data formatting | bytes 884736 | tf_op jit(solution)/shard_map/stack;reshape | solution.py:140
  62.6 0.4 fusion.19
  63.0 0.1 copy.126
  63.1 0.3 stack_reshape.15
  63.5 0.2 copy-done.8
  63.7 0.2 pad_maximum_fusion.1
  63.9 2.6 %copy.127 = bf16[16,9,4,1536]{3,2,1,0:T(4,128)(2,1)} copy(bf16[16,9,4,1536]{3,0,1,2:T(8,128)(2,1)S(1)} %pad_maximum_fusion.1) | data formatting | bytes 3538944 | tf_op jit(solution)/shard_map/optimization_barrier | solution.py:147
  66.5 8.0 %all-to-all-start.1 = ((bf16[16,9,4,1536]{3,2,1,0:T(4,128)(2,1)}), bf16[16,9,4,1536]{3,2,1,0:T(4,128)(2,1)S(1)}, u32[]{:S(2)}, u32[]{:S(2)}) async-start(bf16[16,9,4,1536]{3,2,1,0:T(4,128)(2,1)} %copy.127), calls=%async_computation.1 | async-start | bytes 3538944 | tf_op jit(solution)/shard_map/all_to_all | solution.py:150
  74.6 3.2 %convolution_bitcast_fusion.1 = f32[1,1,12,18,8,128]{5,4,3,2,1,0:T(8,128)} fusion(bf16[144,12,128]{2,1,0:T(8,128)(2,1)S(1)} %copy-done.12, f32[12,144,144]{1,2,0:T(8,128)} %get-tuple-element.32, f32[12,144]{1,0:T(8,128)S(1)} %copy-done.16), kind=kOutput, calls=%fused_computation.28 | convolution fusion | flops 64198656 | bytes 2329344 | tf_op jit(solution)/shard_map/bfhij,bfjhe->bfihe/dot_general | solution.py:31
  77.8 0.5 multiply_reduce_fusion
  78.2 0.3 multiply_convert_fusion
  78.6 0.1 collective-permute-start.6
  78.7 2.0 %collective-permute-start.7 = (f32[12,16]{1,0:T(8,128)S(1)}, f32[12,16]{1,0:T(8,128)S(1)}, u32[]{:S(2)}, u32[]{:S(2)}) collective-permute-start(f32[12,16]{1,0:T(8,128)S(1)} %add_add_fusion.1), channel_id=1, source_target_pairs={{0,32},{16,48},{32,0},{48,16},{64,96},{80,112},{96,64},{112,80},{1... | collective-permute-start | bytes 2312 | tf_op jit(solution)/shard_map/ppermute | solution.py:60
  80.7 0.4 fusion.8
  81.1 1.3 %collective-permute-done.7 = f32[12,16]{1,0:T(8,128)S(1)} collective-permute-done((f32[12,16]{1,0:T(8,128)S(1)}, f32[12,16]{1,0:T(8,128)S(1)}, u32[]{:S(2)}, u32[]{:S(2)}) %collective-permute-start.7) | collective-permute-done | bytes 800 | tf_op jit(solution)/shard_map/ppermute | solution.py:60
  82.4 1.3 %collective-permute-done.8 = f32[12,16]{1,0:T(8,128)S(1)} collective-permute-done((f32[12,16]{1,0:T(8,128)S(1)}, f32[12,16]{1,0:T(8,128)S(1)}, u32[]{:S(2)}, u32[]{:S(2)}) %collective-permute-start.8) | collective-permute-done | bytes 800 | tf_op jit(solution)/shard_map/ppermute | solution.py:60
  83.8 6.3 %collective-permute-start.10 = (f32[12,16]{1,0:T(8,128)S(1)}, f32[12,16]{1,0:T(8,128)S(1)}, u32[]{:S(2)}, u32[]{:S(2)}) collective-permute-start(f32[12,16]{1,0:T(8,128)S(1)} %add_add_fusion), channel_id=1, source_target_pairs={{0,128},{16,144},{32,160},{48,176},{64,192},{80,208},{96,224},{112... | collective-permute-start | bytes 2312 | tf_op jit(solution)/shard_map/ppermute | solution.py:60
  90.1 0.6 collective-permute-start.11
  90.6 0.9 collective-permute-start.9
  91.5 0.6 fusion.7
  92.1 3.7 %collective-permute-done.11 = f32[12,16]{1,0:T(8,128)S(1)} collective-permute-done((f32[12,16]{1,0:T(8,128)S(1)}, f32[12,16]{1,0:T(8,128)S(1)}, u32[]{:S(2)}, u32[]{:S(2)}) %collective-permute-start.11) | collective-permute-done | bytes 800 | tf_op jit(solution)/shard_map/ppermute | solution.py:60
  95.8 0.6 add_multiply_fusion
  96.4 0.5 convert_bitcast_fusion
  96.9 2.6 %fusion.65 = (f32[1,9,16,1536]{3,0,1,2:T(1,128)S(1)}, f32[1,9,16,1536]{3,0,1,2:T(1,128)S(1)}, f32[1,9,16,1536]{3,0,1,2:T(1,128)S(1)}, f32[1,9,16,1536]{3,0,1,2:T(1,128)S(1)}) fusion(f32[4,9,16,1536]{3,0,1,2:T(4,128)S(1)} %convert_bitcast_fusion), kind=kLoop, calls=%fused_computation.89 | loop fusion | bytes 7077888 | tf_op jit(solution)/shard_map/slice | solution.py:166
  99.9 1.0 copy-done.10
  100.9 1.1 %fusion.20 = (bf16[1,1,144,1536]{3,2,1,0:T(8,128)(2,1)}, bf16[1,1,144,1536]{3,2,1,0:T(8,128)(2,1)}) fusion(f32[1,1,12,18,8,128]{5,4,3,2,1,0:T(8,128)S(1)} %copy-done.10, f32[1,1,12,18,8,128]{5,4,3,2,1,0:T(8,128)S(1)} %fusion.8, f32[1,1,144,1536]{3,2,1,0:T(8,128)S(1)} %bitcast.148, f32[1,1,144,1536]{3,2,1,0:T(8,128)S(1)} %bitcast.147), kind=kLoop, calls=%fused_computation.40 | loop fusion | flops 884736 | bytes 4423680 | tf_op jit(solution)/shard_map/convert_element_type | solution.py:166
  102.1 1.2 %fusion.22 = (bf16[1,1,144,1536]{3,2,1,0:T(8,128)(2,1)}, bf16[1,1,144,1536]{3,2,1,0:T(8,128)(2,1)}) fusion(f32[1,1,12,18,8,128]{5,4,3,2,1,0:T(8,128)S(1)} %fusion.7, f32[1,1,12,18,8,128]{5,4,3,2,1,0:T(8,128)S(1)} %copy-done.11, f32[1,1,144,1536]{3,2,1,0:T(8,128)S(1)} %bitcast.146, f32[1,1,144,1536]{3,2,1,0:T(8,128)S(1)} %bitcast.145), kind=kLoop, calls=%fused_computation.44 | loop fusion | flops 884736 | bytes 4423680 | tf_op jit(solution)/shard_map/convert_element_type | solution.py:164
  (52 shorter events, 0.4 us)
Async XLA Ops:
  0.6 16.3 %copy-start = (f32[12,16]{1,0:T(8,128)S(1)}, f32[12,16]{1,0:T(8,128)}, u32[]{:S(2)}) copy-start(f32[12,16]{1,0:T(8,128)} %param.13) | copy-start | bytes 2308
  4.9 7.6 %copy-start.6 = (bf16[1,1,144,1536]{3,2,1,0:T(8,128)(2,1)S(1)}, bf16[1,1,144,1536]{3,2,1,0:T(8,128)(2,1)}, u32[]{:S(2)}) copy-start(bf16[1,1,144,1536]{3,2,1,0:T(8,128)(2,1)} %param.7) | copy-start | bytes 1327108
  4.9 7.9 %copy-start.7 = (bf16[1,1,144,1536]{3,2,1,0:T(8,128)(2,1)S(1)}, bf16[1,1,144,1536]{3,2,1,0:T(8,128)(2,1)}, u32[]{:S(2)}) copy-start(bf16[1,1,144,1536]{3,2,1,0:T(8,128)(2,1)} %param.8) | copy-start | bytes 1327108
  4.9 30.8 %all-to-all-start = ((bf16[16,9,4,1536]{3,2,1,0:T(4,128)(2,1)}), bf16[16,9,4,1536]{3,2,1,0:T(4,128)(2,1)S(1)}, u32[]{:S(2)}, u32[]{:S(2)}) async-start(bf16[16,9,4,1536]{3,2,1,0:T(4,128)(2,1)} %copy.115), calls=%async_computation | async-start | bytes 3538944 | tf_op jit(solution)/shard_map/all_to_all | solution.py:92
  12.8 12.6 %copy-start.3 = (bf16[144,12,128]{2,1,0:T(8,128)(2,1)}, bf16[144,12,128]{2,1,0:T(8,128)(2,1)S(1)}, u32[]{:S(2)}) copy-start(bf16[144,12,128]{2,1,0:T(8,128)(2,1)S(1)} %reshape.290) | copy-start | bytes 1327108
  13.2 12.2 %copy-start.1 = (bf16[144,12,128]{2,1,0:T(8,128)(2,1)}, bf16[144,12,128]{2,1,0:T(8,128)(2,1)S(1)}, u32[]{:S(2)}) copy-start(bf16[144,12,128]{2,1,0:T(8,128)(2,1)S(1)} %reshape.291) | copy-start | bytes 1327108
  16.9 8.5 %copy-start.13 = (bf16[144,12,128]{2,1,0:T(8,128)(2,1)}, bf16[144,12,128]{2,1,0:T(8,128)(2,1)S(1)}, u32[]{:S(2)}) copy-start(bf16[144,12,128]{2,1,0:T(8,128)(2,1)S(1)} %reshape.299) | copy-start | bytes 1327108
  41.9 1.3 %copy-start.15 = (f32[12,16,16]{1,2,0:T(8,128)S(1)}, f32[12,16,16]{1,2,0:T(8,128)}, u32[]{:S(2)}) copy-start(f32[12,16,16]{1,2,0:T(8,128)} %copy.119) | copy-start | bytes 36868
  42.0 1.3 %copy-start.17 = (pred[16,16]{0,1:T(8,128)(4,1)S(1)}, pred[16,16]{0,1:T(8,128)(4,1)}, u32[]{:S(2)}) copy-start(pred[16,16]{0,1:T(8,128)(4,1)} %broadcast_compare_fusion) | copy-start | bytes 772
  46.0 5.9 %collective-permute-start = (f32[12,16]{1,0:T(8,128)S(1)}, f32[12,16]{1,0:T(8,128)S(1)}, u32[]{:S(2)}, u32[]{:S(2)}) collective-permute-start(f32[12,16]{1,0:T(8,128)S(1)} %convolution_bitcast_fusion.3), channel_id=1, source_target_pairs={{0,1},{1,0},{2,3},{3,2},{4,5},{5,4},{6,7},{7,6},{8,9},{9,8},{10,11... | collective-permute-start | bytes 2312 | tf_op jit(solution)/shard_map/ppermute | solution.py:60
  46.6 5.2 %collective-permute-start.1 = (f32[12,16]{1,0:T(8,128)S(1)}, f32[12,16]{1,0:T(8,128)S(1)}, u32[]{:S(2)}, u32[]{:S(2)}) collective-permute-start(f32[12,16]{1,0:T(8,128)S(1)} %convolution_bitcast_fusion.3), channel_id=1, source_target_pairs={{0,2},{1,3},{2,0},{3,1},{4,6},{5,7},{6,4},{7,5},{8,10},{9,11},{10,... | collective-permute-start | bytes 2312 | tf_op jit(solution)/shard_map/ppermute | solution.py:60
  50.1 3.7 %collective-permute-start.2 = (f32[12,16]{1,0:T(8,128)S(1)}, f32[12,16]{1,0:T(8,128)S(1)}, u32[]{:S(2)}, u32[]{:S(2)}) collective-permute-start(f32[12,16]{1,0:T(8,128)S(1)} %convolution_bitcast_fusion.3), channel_id=1, source_target_pairs={{0,3},{1,2},{2,1},{3,0},{4,7},{5,6},{6,5},{7,4},{8,11},{9,10},{10,... | collective-permute-start | bytes 2312 | tf_op jit(solution)/shard_map/ppermute | solution.py:60
  53.8 5.5 %copy-start.9 = (bf16[9,12,16,128]{3,2,1,0:T(8,128)(2,1)S(1)}, bf16[9,12,16,128]{3,2,1,0:T(8,128)(2,1)}, u32[]{:S(2)}) copy-start(bf16[9,12,16,128]{3,2,1,0:T(8,128)(2,1)} %get-tuple-element.18) | copy-start | bytes 1327108
  53.8 10.1 %collective-permute-start.3 = (f32[12,16]{1,0:T(8,128)S(1)}, f32[12,16]{1,0:T(8,128)S(1)}, u32[]{:S(2)}, u32[]{:S(2)}) collective-permute-start(f32[12,16]{1,0:T(8,128)S(1)} %add_add_fusion.2), channel_id=1, source_target_pairs={{0,4},{1,5},{2,6},{3,7},{4,0},{5,1},{6,2},{7,3},{8,12},{9,13},{10,... | collective-permute-start | bytes 2312 | tf_op jit(solution)/shard_map/ppermute | solution.py:60
  53.8 10.1 %collective-permute-start.4 = (f32[12,16]{1,0:T(8,128)S(1)}, f32[12,16]{1,0:T(8,128)S(1)}, u32[]{:S(2)}, u32[]{:S(2)}) collective-permute-start(f32[12,16]{1,0:T(8,128)S(1)} %add_add_fusion.2), channel_id=1, source_target_pairs={{0,8},{1,9},{2,10},{3,11},{4,12},{5,13},{6,14},{7,15},{8,0},{9,1},... | collective-permute-start | bytes 2312 | tf_op jit(solution)/shard_map/ppermute | solution.py:60
  56.6 7.3 %collective-permute-start.5 = (f32[12,16]{1,0:T(8,128)S(1)}, f32[12,16]{1,0:T(8,128)S(1)}, u32[]{:S(2)}, u32[]{:S(2)}) collective-permute-start(f32[12,16]{1,0:T(8,128)S(1)} %add_add_fusion.2), channel_id=1, source_target_pairs={{0,12},{1,13},{2,14},{3,15},{4,8},{5,9},{6,10},{7,11},{8,4},{9,5},... | collective-permute-start | bytes 2312 | tf_op jit(solution)/shard_map/ppermute | solution.py:60
  62.6 1.0 copy-start.8
  66.5 8.0 %copy-start.12 = (bf16[144,12,128]{2,1,0:T(8,128)(2,1)S(1)}, bf16[144,12,128]{2,1,0:T(8,128)(2,1)}, u32[]{:S(2)}) copy-start(bf16[144,12,128]{2,1,0:T(8,128)(2,1)} %reshape.292) | copy-start | bytes 1327108
  66.5 8.0 %copy-start.16 = (f32[12,144]{1,0:T(8,128)S(1)}, f32[12,144]{1,0:T(8,128)}, u32[]{:S(2)}) copy-start(f32[12,144]{1,0:T(8,128)} %get-tuple-element.31) | copy-start | bytes 20740
  66.5 29.9 %all-to-all-start.1 = ((bf16[16,9,4,1536]{3,2,1,0:T(4,128)(2,1)}), bf16[16,9,4,1536]{3,2,1,0:T(4,128)(2,1)S(1)}, u32[]{:S(2)}, u32[]{:S(2)}) async-start(bf16[16,9,4,1536]{3,2,1,0:T(4,128)(2,1)} %copy.127), calls=%async_computation.1 | async-start | bytes 3538944 | tf_op jit(solution)/shard_map/all_to_all | solution.py:150
  74.6 3.2 %copy-start.5 = (f32[12,144,144]{1,2,0:T(8,128)S(1)}, f32[12,144,144]{1,2,0:T(8,128)}, u32[]{:S(2)}) copy-start(f32[12,144,144]{1,2,0:T(8,128)} %get-tuple-element.32) | copy-start | bytes 2985988
  74.6 3.2 %copy-start.14 = (bf16[144,12,128]{2,1,0:T(8,128)(2,1)S(1)}, bf16[144,12,128]{2,1,0:T(8,128)(2,1)}, u32[]{:S(2)}) copy-start(bf16[144,12,128]{2,1,0:T(8,128)(2,1)} %copy-done.13) | copy-start | bytes 1327108
  78.2 2.5 %copy-start.4 = (bf16[144,12,128]{2,1,0:T(8,128)(2,1)S(1)}, bf16[144,12,128]{2,1,0:T(8,128)(2,1)}, u32[]{:S(2)}) copy-start(bf16[144,12,128]{2,1,0:T(8,128)(2,1)} %copy-done.3) | copy-start | bytes 1327108
  78.6 13.0 %copy-start.2 = (bf16[144,12,128]{2,1,0:T(8,128)(2,1)S(1)}, bf16[144,12,128]{2,1,0:T(8,128)(2,1)}, u32[]{:S(2)}) copy-start(bf16[144,12,128]{2,1,0:T(8,128)(2,1)} %copy-done.1) | copy-start | bytes 1327108
  78.6 2.5 %collective-permute-start.6 = (f32[12,16]{1,0:T(8,128)S(1)}, f32[12,16]{1,0:T(8,128)S(1)}, u32[]{:S(2)}, u32[]{:S(2)}) collective-permute-start(f32[12,16]{1,0:T(8,128)S(1)} %add_add_fusion.1), channel_id=1, source_target_pairs={{0,16},{16,0},{32,48},{48,32},{64,80},{80,64},{96,112},{112,96},{1... | collective-permute-start | bytes 2312 | tf_op jit(solution)/shard_map/ppermute | solution.py:60
  78.7 3.7 %collective-permute-start.7 = (f32[12,16]{1,0:T(8,128)S(1)}, f32[12,16]{1,0:T(8,128)S(1)}, u32[]{:S(2)}, u32[]{:S(2)}) collective-permute-start(f32[12,16]{1,0:T(8,128)S(1)} %add_add_fusion.1), channel_id=1, source_target_pairs={{0,32},{16,48},{32,0},{48,16},{64,96},{80,112},{96,64},{112,80},{1... | collective-permute-start | bytes 2312 | tf_op jit(solution)/shard_map/ppermute | solution.py:60
  80.7 3.1 %collective-permute-start.8 = (f32[12,16]{1,0:T(8,128)S(1)}, f32[12,16]{1,0:T(8,128)S(1)}, u32[]{:S(2)}, u32[]{:S(2)}) collective-permute-start(f32[12,16]{1,0:T(8,128)S(1)} %add_add_fusion.1), channel_id=1, source_target_pairs={{0,48},{16,32},{32,16},{48,0},{64,112},{80,96},{96,80},{112,64},{1... | collective-permute-start | bytes 2312 | tf_op jit(solution)/shard_map/ppermute | solution.py:60
  83.8 8.4 %collective-permute-start.10 = (f32[12,16]{1,0:T(8,128)S(1)}, f32[12,16]{1,0:T(8,128)S(1)}, u32[]{:S(2)}, u32[]{:S(2)}) collective-permute-start(f32[12,16]{1,0:T(8,128)S(1)} %add_add_fusion), channel_id=1, source_target_pairs={{0,128},{16,144},{32,160},{48,176},{64,192},{80,208},{96,224},{112... | collective-permute-start | bytes 2312 | tf_op jit(solution)/shard_map/ppermute | solution.py:60
  90.1 5.8 %collective-permute-start.11 = (f32[12,16]{1,0:T(8,128)S(1)}, f32[12,16]{1,0:T(8,128)S(1)}, u32[]{:S(2)}, u32[]{:S(2)}) collective-permute-start(f32[12,16]{1,0:T(8,128)S(1)} %add_add_fusion), channel_id=1, source_target_pairs={{0,192},{16,208},{32,224},{48,240},{64,128},{80,144},{96,160},{112... | collective-permute-start | bytes 2312 | tf_op jit(solution)/shard_map/ppermute | solution.py:60
  90.6 5.2 %collective-permute-start.9 = (f32[12,16]{1,0:T(8,128)S(1)}, f32[12,16]{1,0:T(8,128)S(1)}, u32[]{:S(2)}, u32[]{:S(2)}) collective-permute-start(f32[12,16]{1,0:T(8,128)S(1)} %add_add_fusion), channel_id=1, source_target_pairs={{0,64},{16,80},{32,96},{48,112},{64,0},{80,16},{96,32},{112,48},{1... | collective-permute-start | bytes 2312 | tf_op jit(solution)/shard_map/ppermute | solution.py:60
  99.7 1.2 %copy-start.10 = (f32[1,1,12,18,8,128]{5,4,3,2,1,0:T(8,128)S(1)}, f32[1,1,12,18,8,128]{5,4,3,2,1,0:T(8,128)}, u32[]{:S(2)}) copy-start(f32[1,1,12,18,8,128]{5,4,3,2,1,0:T(8,128)} %convolution_bitcast_fusion) | copy-start | bytes 2654212
  100.9 1.2 %copy-start.11 = (f32[1,1,12,18,8,128]{5,4,3,2,1,0:T(8,128)S(1)}, f32[1,1,12,18,8,128]{5,4,3,2,1,0:T(8,128)}, u32[]{:S(2)}) copy-start(f32[1,1,12,18,8,128]{5,4,3,2,1,0:T(8,128)} %convolution_bitcast_fusion.1) | copy-start | bytes 2654212

commit v10 on v9

--- a/solution.py
+++ b/solution.py
@@ -148,7 +148,6 @@
     summed = quad_step(quad_step(partial, "dp", dp_size, 1), "dp", dp_size, 4)
     bias_grad = summed / math.sqrt(dp_size * queries.shape[0] * frames_all * positions)
     back = lax.all_to_all(back_rows, "seq", split_axis=0, concat_axis=0, tiled=True)
-    back = jnp.transpose(back, (2, 1, 0, 3)).reshape(4, 1, 1, positions, width).astype(jnp.float32)
 
     space_query = split_heads(queries, head_count)
     space_key = split_heads(keys, head_count)
@@ -160,10 +159,15 @@
     space_grads = attend_backward(
         SPACE_PATTERNS, space_query, space_key, space_value, space_slope, space_shares, space_half
     )
-    attended = (join_heads(space_out) + back[0]).astype(jnp.bfloat16)
-    query_grad = (join_heads(space_grads[0]) + back[1]).astype(jnp.bfloat16)
-    key_grad = (join_heads(space_grads[1]) + back[2]).astype(jnp.bfloat16)
-    value_grad = (join_heads(space_grads[2]) + back[3]).astype(jnp.bfloat16)
+    def combine(space_part, tensor):
+        space_rows = join_heads(space_part).reshape(block, seq_size, width)
+        total = space_rows + jnp.swapaxes(back[:, :, tensor, :], 0, 1).astype(jnp.float32)
+        return total.astype(jnp.bfloat16).reshape(1, 1, positions, width)
+
+    attended = combine(space_out, 0)
+    query_grad = combine(space_grads[0], 1)
+    key_grad = combine(space_grads[1], 2)
+    value_grad = combine(space_grads[2], 3)
     return (attended, query_grad, key_grad, value_grad, bias_grad)
 
 

time: 105 us -> 109 us (1.038)
  local copies, waits for them, and re-layouts: 25.7 us -> 33.8 us
  waiting for transfers between devices: 15.8 us -> 12.1 us
    another operation x4 -> x8, local copies, waits for them, and re-layouts: 4.35 us -> 8.55 us
    ppermute x12, waiting for transfers between devices: 8.25 us -> 4.58 us  [quad_step(): lax.ppermute(value, axis, [(index, index ^ part * step) for index in rang...]
    transpose x0 -> x2, local copies, waits for them, and re-layouts: none -> 2.94 us  [the longest x1 1.47 us: attend_forward(): jnp.einsum(patterns[1], shares_half, value_part, preferred_element_type=j...]
    mul x0 -> x2, local copies, waits for them, and re-layouts: none -> 1.77 us  [the longest x1 1.47 us: attend_backward(): jnp.einsum(patterns[1], score_half, key_part, preferred_element_type=jnp....]
    convert_element_type x3 -> x2, other arithmetic: 2.79 us -> 2.27 us  [combine(): return total.astype(jnp.bfloat16).reshape(1, 1, positions, width)]
    slice x5 -> x1, local copies, waits for them, and re-layouts: 2.89 us -> 2.56 us  [combine(): back[:, :, tensor, :]]
  transfers between devices with their start and end apart: 14 -> 14, of which waited for: 5 -> 4; matrix products, arithmetic and copies ran while one was open for 26% -> 34% of each run, Pallas kernels for 0% -> 0%
where the time goes in v10:
time: 109 us; the launch traced here: 108 us
  starting transfers between devices  34.8 us (32%)
  local copies, waits for them, and re-layouts  33.8 us (31%)
  matrix products  16.5 us (15%)
  waiting for transfers between devices  12.1 us (11%)
  other arithmetic  8.85 us (8%)
  between operations  1.68 us (2%)
    ppermute x12, starting transfers between devices, quad_step(): lax.ppermute(value, axis, [(index, index ^ part * step) for index in rang...  19.2 us
    all_to_all x1, starting transfers between devices, on_device(): lax.all_to_all(back_rows, 'seq', split_axis=0, concat_axis=0, tiled=True)  8 us
    all_to_all x1, starting transfers between devices, on_device(): lax.all_to_all(stacked, 'seq', split_axis=0, concat_axis=0, tiled=True)  7.58 us
    all_to_all x1, waiting for transfers between devices, on_device(): lax.all_to_all(stacked, 'seq', split_axis=0, concat_axis=0, tiled=True)  7.55 us
    reshape x2, local copies, waits for them, and re-layouts, on_device(): rows = rows.reshape(seq_size, block, 4, head_count, width // head_count)  6.28 us
    ppermute x12, waiting for transfers between devices, quad_step(): lax.ppermute(value, axis, [(index, index ^ part * step) for index in rang...  4.58 us
    another operation x4, local copies, waits for them, and re-layouts  4.31 us
    another operation x4, local copies, waits for them, and re-layouts, combine(): space_rows = join_heads(space_part).reshape(block, seq_size, width)  4.24 us
  transfers between devices with their start and end apart: 14, of which 4 were waited for; matrix products, arithmetic and copies ran while one was open for 34% of the time, Pallas kernels for 0%

profile of v10, /device:TPU:4, one launch (start us, length us, event | category | flops | bytes accessed | tf_op | source)
XLA Modules:
  0.0 107.8 jit_solution(16623335752375120544)
XLA Ops:
  0.6 1.6 %pad_maximum_fusion = bf16[16,9,4,1536]{3,0,2,1:T(8,128)(2,1)S(1)} fusion(bf16[16,9,1,1536]{3,0,2,1:T(8,128)(2,1)} %bitcast.164, bf16[16,9,1,1536]{3,0,2,1:T(8,128)(2,1)} %bitcast.163, bf16[16,9,1,1536]{3,0,2,1:T(8,128)(2,1)} %bitcast.162, bf16[16,9,1,1536]{3,0,2,1:T(8,128)(2,1)} %bitcast.161), kind=kLoop, calls=%fused_computation.4 | loop fusion | flops 2654208 | bytes 3538944 | tf_op jit(solution)/shard_map/stack | solution.py:85
  2.3 2.6 %copy.115 = bf16[16,9,4,1536]{3,2,1,0:T(4,128)(2,1)} copy(bf16[16,9,4,1536]{3,0,2,1:T(8,128)(2,1)S(1)} %pad_maximum_fusion) | data formatting | bytes 3538944 | tf_op jit(solution)/shard_map/stack | solution.py:85
  4.9 7.6 %all-to-all-start = ((bf16[16,9,4,1536]{3,2,1,0:T(4,128)(2,1)}), bf16[16,9,4,1536]{3,2,1,0:T(4,128)(2,1)S(1)}, u32[]{:S(2)}, u32[]{:S(2)}) async-start(bf16[16,9,4,1536]{3,2,1,0:T(4,128)(2,1)} %copy.115), calls=%async_computation | async-start | bytes 3538944 | tf_op jit(solution)/shard_map/all_to_all | solution.py:92
  12.5 0.3 reshape.180
  12.8 0.3 reshape.181
  13.2 2.4 %reshape.182 = bf16[144,12,128]{2,1,0:T(8,128)(2,1)} reshape(bf16[1,1,144,1536]{3,2,1,0:T(8,128)(2,1)} %param.9) | data formatting | bytes 884736 | tf_op jit(solution)/shard_map/reshape.7
  15.5 1.3 %reshape.189 = bf16[144,12,128]{2,1,0:T(8,128)(2,1)S(1)} reshape(bf16[1,1,144,1536]{3,2,1,0:T(8,128)(2,1)} %param.10) | data formatting | bytes 884736 | tf_op jit(solution)/shard_map/reshape.12
  16.9 0.9 convolution_bitcast_fusion.2
  17.8 1.7 %copy.119 = f32[12,16,16]{1,2,0:T(8,128)} copy(f32[12,16,16]{0,2,1:T(8,128)} %convolution_bitcast_fusion.2) | data formatting | bytes 24576 | tf_op jit(solution)/shard_map/dot_general | solution.py:77
  20.2 0.5 iota_compare_fusion.2
  20.7 1.4 %broadcast_compare_fusion = pred[16,16]{0,1:T(8,128)(4,1)} fusion(s32[16]{0:T(128)} %bitcast.169), kind=kLoop, calls=%fused_computation.90 | loop fusion | flops 256 | bytes 320 | tf_op jit(solution)/shard_map/eq | solution.py:80
  22.1 3.3 %fusion.70 = (f32[12,144]{1,0:T(8,128)}, f32[12,144,144]{1,2,0:T(8,128)}) fusion(pred[144]{0:T(512)(128)(4,1)} %iota_compare_fusion.2, bf16[144,12,128]{2,1,0:T(8,128)(2,1)S(1)} %reshape.181, bf16[144,12,128]{2,1,0:T(8,128)(2,1)S(1)} %reshape.180), kind=kOutput, calls=%fused_computation.97 | convolution fusion | flops 64696464 | bytes 1887120 | tf_op jit(solution)/shard_map/sub | solution.py:28
  25.3 2.8 %convolution_bitcast_fusion = f32[1,1,144,12,128]{4,2,3,1,0:T(8,128)} fusion(bf16[144,12,128]{2,1,0:T(8,128)(2,1)S(1)} %reshape.189, f32[12,144,144]{1,2,0:T(8,128)} %get-tuple-element.32, f32[12,144]{1,0:T(8,128)} %get-tuple-element.31), kind=kOutput, calls=%fused_computation.26 | convolution fusion | flops 64198656 | bytes 2329344 | tf_op jit(solution)/shard_map/bfhij,bfihe->bfjhe/dot_general | solution.py:39
  28.1 7.6 %all-to-all-done = bf16[16,9,4,1536]{3,2,1,0:T(4,128)(2,1)S(1)} async-done(((bf16[16,9,4,1536]{3,2,1,0:T(4,128)(2,1)}), bf16[16,9,4,1536]{3,2,1,0:T(4,128)(2,1)S(1)}, u32[]{:S(2)}, u32[]{:S(2)}) %all-to-all-start) | async-done | bytes 1769504 | tf_op jit(solution)/shard_map/all_to_all | solution.py:92
  35.7 2.6 %reshape.199 = bf16[16,9,4,12,128]{4,3,2,1,0:T(8,128)(2,1)} reshape(bf16[16,9,4,1536]{3,2,1,0:T(4,128)(2,1)S(1)} %all-to-all-done) | data formatting | bytes 3538944 | tf_op jit(solution)/shard_map/reshape | solution.py:93
  38.2 3.7 %copy.201 = bf16[16,9,4,12,128]{4,0,3,1,2:T(8,128)(2,1)S(1)} copy(bf16[16,9,4,12,128]{4,3,2,1,0:T(8,128)(2,1)} %reshape.199) | data formatting | bytes 3538944 | tf_op jit(solution)/shard_map/reshape | solution.py:93
  42.0 1.3 %fusion.68 = f32[9,12,16,16]{2,3,1,0:T(8,128)} fusion(bf16[4,9,12,16,128]{4,3,2,1,0:T(8,128)(2,1)S(1)} %bitcast.158), kind=kOutput, calls=%fused_computation.95 | convolution fusion | flops 7077888 | bytes 995328 | tf_op jit(solution)/shard_map/phie,phje->phij/dot_general | solution.py:106
  43.3 0.6 fusion.6
  43.9 1.8 %fusion.75 = (f32[12,16,16]{1,2,0:T(8,128)S(1)}, bf16[9,12,16,16]{2,3,1,0:T(8,128)(2,1)S(1)}) fusion(f32[9,12,16,16]{2,3,1,0:T(8,128)S(1)} %fusion.6, f32[9,12,16,16]{2,3,1,0:T(8,128)} %fusion.68), kind=kOutput, calls=%fused_computation.98 | output fusion | flops 136911 | bytes 288768 | tf_op jit(solution)/shard_map/sub | solution.py:110
  45.8 0.2 convolution_bitcast_fusion.3
  46.0 0.7 collective-permute-start
  46.7 3.5 %collective-permute-start.1 = (f32[12,16]{1,0:T(8,128)S(1)}, f32[12,16]{1,0:T(8,128)S(1)}, u32[]{:S(2)}, u32[]{:S(2)}) collective-permute-start(f32[12,16]{1,0:T(8,128)S(1)} %convolution_bitcast_fusion.3), channel_id=1, source_target_pairs={{0,2},{1,3},{2,0},{3,1},{4,6},{5,7},{6,4},{7,5},{8,10},{9,11},{10,... | collective-permute-start | bytes 2312 | tf_op jit(solution)/shard_map/ppermute | solution.py:60
  50.1 0.5 collective-permute-start.2
  50.6 1.3 %slice_bitcast_fusion.1 = (bf16[9,12,16,128]{3,2,1,0:T(8,128)(2,1)S(1)}, bf16[9,12,16,128]{3,2,1,0:T(8,128)(2,1)S(1)}, bf16[9,12,16,128]{3,2,1,0:T(8,128)(2,1)}, bf16[9,12,16,128]{3,2,1,0:T(8,128)(2,1)}) fusion(bf16[4,9,12,16,128]{4,3,2,1,0:T(8,128)(2,1)S(1)} %bitcast.160), kind=kLoop, calls=%fused_computation.57 | loop fusion | bytes 3538944 | tf_op jit(solution)/shard_map/squeeze | solution.py:95
  51.9 1.9 %collective-permute-done.2 = f32[12,16]{1,0:T(8,128)S(1)} collective-permute-done((f32[12,16]{1,0:T(8,128)S(1)}, f32[12,16]{1,0:T(8,128)S(1)}, u32[]{:S(2)}, u32[]{:S(2)}) %collective-permute-start.2) | collective-permute-done | bytes 800 | tf_op jit(solution)/shard_map/ppermute | solution.py:60
  53.9 2.7 %collective-permute-start.4 = (f32[12,16]{1,0:T(8,128)S(1)}, f32[12,16]{1,0:T(8,128)S(1)}, u32[]{:S(2)}, u32[]{:S(2)}) collective-permute-start(f32[12,16]{1,0:T(8,128)S(1)} %add_add_fusion.2), channel_id=1, source_target_pairs={{0,8},{1,9},{2,10},{3,11},{4,12},{5,13},{6,14},{7,15},{8,0},{9,1},... | collective-permute-start | bytes 2312 | tf_op jit(solution)/shard_map/ppermute | solution.py:60
  56.6 1.9 %collective-permute-start.5 = (f32[12,16]{1,0:T(8,128)S(1)}, f32[12,16]{1,0:T(8,128)S(1)}, u32[]{:S(2)}, u32[]{:S(2)}) collective-permute-start(f32[12,16]{1,0:T(8,128)S(1)} %add_add_fusion.2), channel_id=1, source_target_pairs={{0,12},{1,13},{2,14},{3,15},{4,8},{5,9},{6,10},{7,11},{8,4},{9,5},... | collective-permute-start | bytes 2312 | tf_op jit(solution)/shard_map/ppermute | solution.py:60
  58.5 0.3 fusion.18
  59.0 0.3 stack_reshape.12
  59.3 0.3 fusion.17
  59.7 0.3 stack_reshape.13
  60.1 1.4 %fusion.16 = bf16[16,9,12,128]{3,0,2,1:T(8,128)(2,1)S(1)} fusion(bf16[9,12,16,128]{3,2,1,0:T(8,128)(2,1)} %get-tuple-element.19, bf16[9,12,16,16]{2,3,1,0:T(8,128)(2,1)S(1)} %get-tuple-element.17), kind=kOutput, calls=%fused_computation.32 | convolution fusion | flops 7520256 | bytes 940032 | tf_op jit(solution)/shard_map/phij,phie->phje/dot_general | solution.py:136
  61.6 1.1 stack_reshape.14
  62.7 0.4 fusion.19
  63.0 0.1 copy.126
  63.2 0.3 stack_reshape.15
  63.5 0.2 copy-done.12
  63.7 0.2 pad_maximum_fusion.1
  63.9 2.6 %copy.127 = bf16[16,9,4,1536]{3,2,1,0:T(4,128)(2,1)} copy(bf16[16,9,4,1536]{3,0,1,2:T(8,128)(2,1)S(1)} %pad_maximum_fusion.1) | data formatting | bytes 3538944 | tf_op jit(solution)/shard_map/optimization_barrier | solution.py:147
  66.5 8.0 %all-to-all-start.1 = ((bf16[16,9,4,1536]{3,2,1,0:T(4,128)(2,1)}), bf16[16,9,4,1536]{3,2,1,0:T(4,128)(2,1)S(1)}, u32[]{:S(2)}, u32[]{:S(2)}) async-start(bf16[16,9,4,1536]{3,2,1,0:T(4,128)(2,1)} %copy.127), calls=%async_computation.1 | async-start | bytes 3538944 | tf_op jit(solution)/shard_map/all_to_all | solution.py:150
  74.6 2.7 %convolution_bitcast_fusion.1 = f32[1,1,144,12,128]{4,2,3,1,0:T(8,128)} fusion(bf16[144,12,128]{2,1,0:T(8,128)(2,1)} %reshape.182, f32[12,144,144]{1,2,0:T(8,128)S(1)} %copy-done.9, f32[12,144]{1,0:T(8,128)} %get-tuple-element.31), kind=kOutput, calls=%fused_computation.27 | convolution fusion | flops 64198656 | bytes 2329344 | tf_op jit(solution)/shard_map/bfhij,bfjhe->bfihe/dot_general | solution.py:31
  77.3 0.5 multiply_reduce_fusion
  77.8 0.4 multiply_convert_fusion
  78.3 2.0 %collective-permute-start.7 = (f32[12,16]{1,0:T(8,128)S(1)}, f32[12,16]{1,0:T(8,128)S(1)}, u32[]{:S(2)}, u32[]{:S(2)}) collective-permute-start(f32[12,16]{1,0:T(8,128)S(1)} %add_add_fusion.1), channel_id=1, source_target_pairs={{0,32},{16,48},{32,0},{48,16},{64,96},{80,112},{96,64},{112,80},{1... | collective-permute-start | bytes 2312 | tf_op jit(solution)/shard_map/ppermute | solution.py:60
  80.3 0.4 fusion.8
  80.7 1.3 %collective-permute-done.7 = f32[12,16]{1,0:T(8,128)S(1)} collective-permute-done((f32[12,16]{1,0:T(8,128)S(1)}, f32[12,16]{1,0:T(8,128)S(1)}, u32[]{:S(2)}, u32[]{:S(2)}) %collective-permute-start.7) | collective-permute-done | bytes 800 | tf_op jit(solution)/shard_map/ppermute | solution.py:60
  82.0 1.3 %collective-permute-done.8 = f32[12,16]{1,0:T(8,128)S(1)} collective-permute-done((f32[12,16]{1,0:T(8,128)S(1)}, f32[12,16]{1,0:T(8,128)S(1)}, u32[]{:S(2)}, u32[]{:S(2)}) %collective-permute-start.8) | collective-permute-done | bytes 800 | tf_op jit(solution)/shard_map/ppermute | solution.py:60
  83.4 6.3 %collective-permute-start.10 = (f32[12,16]{1,0:T(8,128)S(1)}, f32[12,16]{1,0:T(8,128)S(1)}, u32[]{:S(2)}, u32[]{:S(2)}) collective-permute-start(f32[12,16]{1,0:T(8,128)S(1)} %add_add_fusion), channel_id=1, source_target_pairs={{0,128},{16,144},{32,160},{48,176},{64,192},{80,208},{96,224},{112... | collective-permute-start | bytes 2312 | tf_op jit(solution)/shard_map/ppermute | solution.py:60
  89.7 0.6 collective-permute-start.11
  90.2 0.9 collective-permute-start.9
  91.2 1.5 %fusion.7 = f32[1,1,144,12,128]{4,2,3,1,0:T(8,128)} fusion(bf16[12,144,144]{1,2,0:T(8,128)(2,1)S(1)} %multiply_convert_fusion, bf16[144,12,128]{2,1,0:T(8,128)(2,1)S(1)} %copy-done.6), kind=kOutput, calls=%fused_computation.16 | convolution fusion | flops 63922176 | bytes 1824768 | tf_op jit(solution)/shard_map/bfhij,bfjhe->bfihe/dot_general | solution.py:49
  92.7 0.3 copy.136
  93.0 1.1 reshape_reshape.14
  94.1 1.5 %copy.139 = f32[1,1,144,12,128]{4,3,2,1,0:T(8,128)S(1)} copy(f32[1,1,144,12,128]{4,2,3,1,0:T(8,128)} %convolution_bitcast_fusion) | data formatting | bytes 1769472 | tf_op jit(solution)/shard_map/bfhij,bfihe->bfjhe/transpose | solution.py:39
  95.5 1.1 reshape_reshape.15
  96.6 1.5 %copy.133 = f32[1,1,144,12,128]{4,3,2,1,0:T(8,128)S(1)} copy(f32[1,1,144,12,128]{4,2,3,1,0:T(8,128)} %fusion.7) | data formatting | bytes 1769472 | tf_op jit(solution)/shard_map/mul | solution.py:49
  98.1 1.1 %reshape_reshape.13 = f32[9,16,1536]{2,1,0:T(8,128)} reshape(f32[1,1,144,12,128]{4,3,2,1,0:T(8,128)S(1)} %copy.133) | data formatting | bytes 1769472 | tf_op jit(solution)/shard_map/reshape;reshape | solution.py:163
  99.1 1.5 %copy.114 = f32[1,1,144,12,128]{4,3,2,1,0:T(8,128)S(1)} copy(f32[1,1,144,12,128]{4,2,3,1,0:T(8,128)} %convolution_bitcast_fusion.1) | data formatting | bytes 1769472 | tf_op jit(solution)/shard_map/bfhij,bfjhe->bfihe/transpose | solution.py:31
  100.6 1.1 reshape_reshape.12
  101.7 0.6 add_multiply_fusion
  102.3 2.6 %fusion.69 = (bf16[16,9,1,1536]{3,2,1,0:T(2,128)(2,1)S(1)}, bf16[16,9,1,1536]{3,2,1,0:T(2,128)(2,1)S(1)}, bf16[16,9,1,1536]{3,2,1,0:T(2,128)(2,1)S(1)}, bf16[16,9,1,1536]{3,2,1,0:T(2,128)(2,1)S(1)}) fusion(bf16[16,9,4,1536]{3,2,1,0:T(4,128)(2,1)S(1)} %all-to-all-done.1), kind=kLoop, calls=%fused_computation.96 | loop fusion | bytes 3538944 | tf_op jit(solution)/shard_map/slice | solution.py:164
  104.9 1.1 %fusion.21 = (bf16[9,16,1536]{2,1,0:T(8,128)(2,1)}, bf16[9,16,1536]{2,1,0:T(8,128)(2,1)}) fusion(f32[9,16,1536]{2,1,0:T(8,128)S(1)} %copy-done.3, bf16[16,9,1,1536]{3,2,1,0:T(2,128)(2,1)S(1)} %get-tuple-element.23, f32[9,16,1536]{2,1,0:T(8,128)S(1)} %copy-done.1, bf16[16,9,1,1536]{3,2,1,0:T(2,128)(2,1)S(1)} %get-tuple-element.24), kind=kLoop, calls=%fused_computation.40 | loop fusion | flops 1327104 | bytes 3538944 | tf_op jit(solution)/shard_map/convert_element_type | solution.py:165
  106.1 0.6 copy-done.4
  106.6 1.1 %fusion.25 = (bf16[9,16,1536]{2,1,0:T(8,128)(2,1)}, bf16[9,16,1536]{2,1,0:T(8,128)(2,1)}) fusion(f32[9,16,1536]{2,1,0:T(8,128)S(1)} %copy-done.2, bf16[16,9,1,1536]{3,2,1,0:T(2,128)(2,1)S(1)} %get-tuple-element.25, f32[9,16,1536]{2,1,0:T(8,128)S(1)} %copy-done.4, bf16[16,9,1,1536]{3,2,1,0:T(2,128)(2,1)S(1)} %get-tuple-element.26), kind=kLoop, calls=%fused_computation.46 | loop fusion | flops 1327104 | bytes 3538944 | tf_op jit(solution)/shard_map/convert_element_type | solution.py:165
  (59 shorter events, 0.8 us)
Async XLA Ops:
  0.6 16.2 %copy-start = (f32[12,16]{1,0:T(8,128)S(1)}, f32[12,16]{1,0:T(8,128)}, u32[]{:S(2)}) copy-start(f32[12,16]{1,0:T(8,128)} %param.13) | copy-start | bytes 2308
  4.9 7.6 %copy-start.10 = (bf16[1,1,144,1536]{3,2,1,0:T(8,128)(2,1)S(1)}, bf16[1,1,144,1536]{3,2,1,0:T(8,128)(2,1)}, u32[]{:S(2)}) copy-start(bf16[1,1,144,1536]{3,2,1,0:T(8,128)(2,1)} %param.7) | copy-start | bytes 1327108
  4.9 7.9 %copy-start.11 = (bf16[1,1,144,1536]{3,2,1,0:T(8,128)(2,1)S(1)}, bf16[1,1,144,1536]{3,2,1,0:T(8,128)(2,1)}, u32[]{:S(2)}) copy-start(bf16[1,1,144,1536]{3,2,1,0:T(8,128)(2,1)} %param.8) | copy-start | bytes 1327108
  4.9 30.8 %all-to-all-start = ((bf16[16,9,4,1536]{3,2,1,0:T(4,128)(2,1)}), bf16[16,9,4,1536]{3,2,1,0:T(4,128)(2,1)S(1)}, u32[]{:S(2)}, u32[]{:S(2)}) async-start(bf16[16,9,4,1536]{3,2,1,0:T(4,128)(2,1)} %copy.115), calls=%async_computation | async-start | bytes 3538944 | tf_op jit(solution)/shard_map/all_to_all | solution.py:92
  12.8 12.5 %copy-start.7 = (bf16[144,12,128]{2,1,0:T(8,128)(2,1)}, bf16[144,12,128]{2,1,0:T(8,128)(2,1)S(1)}, u32[]{:S(2)}) copy-start(bf16[144,12,128]{2,1,0:T(8,128)(2,1)S(1)} %reshape.180) | copy-start | bytes 1327108
  13.1 12.2 %copy-start.5 = (bf16[144,12,128]{2,1,0:T(8,128)(2,1)}, bf16[144,12,128]{2,1,0:T(8,128)(2,1)S(1)}, u32[]{:S(2)}) copy-start(bf16[144,12,128]{2,1,0:T(8,128)(2,1)S(1)} %reshape.181) | copy-start | bytes 1327108
  16.8 8.5 %copy-start.15 = (bf16[144,12,128]{2,1,0:T(8,128)(2,1)}, bf16[144,12,128]{2,1,0:T(8,128)(2,1)S(1)}, u32[]{:S(2)}) copy-start(bf16[144,12,128]{2,1,0:T(8,128)(2,1)S(1)} %reshape.189) | copy-start | bytes 1327108
  42.0 1.3 %copy-start.17 = (f32[12,16,16]{1,2,0:T(8,128)S(1)}, f32[12,16,16]{1,2,0:T(8,128)}, u32[]{:S(2)}) copy-start(f32[12,16,16]{1,2,0:T(8,128)} %copy.119) | copy-start | bytes 36868
  42.0 1.3 %copy-start.19 = (pred[16,16]{0,1:T(8,128)(4,1)S(1)}, pred[16,16]{0,1:T(8,128)(4,1)}, u32[]{:S(2)}) copy-start(pred[16,16]{0,1:T(8,128)(4,1)} %broadcast_compare_fusion) | copy-start | bytes 772
  46.0 5.9 %collective-permute-start = (f32[12,16]{1,0:T(8,128)S(1)}, f32[12,16]{1,0:T(8,128)S(1)}, u32[]{:S(2)}, u32[]{:S(2)}) collective-permute-start(f32[12,16]{1,0:T(8,128)S(1)} %convolution_bitcast_fusion.3), channel_id=1, source_target_pairs={{0,1},{1,0},{2,3},{3,2},{4,5},{5,4},{6,7},{7,6},{8,9},{9,8},{10,11... | collective-permute-start | bytes 2312 | tf_op jit(solution)/shard_map/ppermute | solution.py:60
  46.7 5.2 %collective-permute-start.1 = (f32[12,16]{1,0:T(8,128)S(1)}, f32[12,16]{1,0:T(8,128)S(1)}, u32[]{:S(2)}, u32[]{:S(2)}) collective-permute-start(f32[12,16]{1,0:T(8,128)S(1)} %convolution_bitcast_fusion.3), channel_id=1, source_target_pairs={{0,2},{1,3},{2,0},{3,1},{4,6},{5,7},{6,4},{7,5},{8,10},{9,11},{10,... | collective-permute-start | bytes 2312 | tf_op jit(solution)/shard_map/ppermute | solution.py:60
  50.1 3.7 %collective-permute-start.2 = (f32[12,16]{1,0:T(8,128)S(1)}, f32[12,16]{1,0:T(8,128)S(1)}, u32[]{:S(2)}, u32[]{:S(2)}) collective-permute-start(f32[12,16]{1,0:T(8,128)S(1)} %convolution_bitcast_fusion.3), channel_id=1, source_target_pairs={{0,3},{1,2},{2,1},{3,0},{4,7},{5,6},{6,5},{7,4},{8,11},{9,10},{10,... | collective-permute-start | bytes 2312 | tf_op jit(solution)/shard_map/ppermute | solution.py:60
  53.8 5.5 %copy-start.13 = (bf16[9,12,16,128]{3,2,1,0:T(8,128)(2,1)S(1)}, bf16[9,12,16,128]{3,2,1,0:T(8,128)(2,1)}, u32[]{:S(2)}) copy-start(bf16[9,12,16,128]{3,2,1,0:T(8,128)(2,1)} %get-tuple-element.18) | copy-start | bytes 1327108
  53.8 10.1 %collective-permute-start.3 = (f32[12,16]{1,0:T(8,128)S(1)}, f32[12,16]{1,0:T(8,128)S(1)}, u32[]{:S(2)}, u32[]{:S(2)}) collective-permute-start(f32[12,16]{1,0:T(8,128)S(1)} %add_add_fusion.2), channel_id=1, source_target_pairs={{0,4},{1,5},{2,6},{3,7},{4,0},{5,1},{6,2},{7,3},{8,12},{9,13},{10,... | collective-permute-start | bytes 2312 | tf_op jit(solution)/shard_map/ppermute | solution.py:60
  53.9 10.0 %collective-permute-start.4 = (f32[12,16]{1,0:T(8,128)S(1)}, f32[12,16]{1,0:T(8,128)S(1)}, u32[]{:S(2)}, u32[]{:S(2)}) collective-permute-start(f32[12,16]{1,0:T(8,128)S(1)} %add_add_fusion.2), channel_id=1, source_target_pairs={{0,8},{1,9},{2,10},{3,11},{4,12},{5,13},{6,14},{7,15},{8,0},{9,1},... | collective-permute-start | bytes 2312 | tf_op jit(solution)/shard_map/ppermute | solution.py:60
  56.6 7.3 %collective-permute-start.5 = (f32[12,16]{1,0:T(8,128)S(1)}, f32[12,16]{1,0:T(8,128)S(1)}, u32[]{:S(2)}, u32[]{:S(2)}) collective-permute-start(f32[12,16]{1,0:T(8,128)S(1)} %add_add_fusion.2), channel_id=1, source_target_pairs={{0,12},{1,13},{2,14},{3,15},{4,8},{5,9},{6,10},{7,11},{8,4},{9,5},... | collective-permute-start | bytes 2312 | tf_op jit(solution)/shard_map/ppermute | solution.py:60
  62.7 1.0 copy-start.12
  66.5 8.0 %copy-start.9 = (f32[12,144,144]{1,2,0:T(8,128)S(1)}, f32[12,144,144]{1,2,0:T(8,128)}, u32[]{:S(2)}) copy-start(f32[12,144,144]{1,2,0:T(8,128)} %get-tuple-element.32) | copy-start | bytes 2985988
  66.5 35.8 %all-to-all-start.1 = ((bf16[16,9,4,1536]{3,2,1,0:T(4,128)(2,1)}), bf16[16,9,4,1536]{3,2,1,0:T(4,128)(2,1)S(1)}, u32[]{:S(2)}, u32[]{:S(2)}) async-start(bf16[16,9,4,1536]{3,2,1,0:T(4,128)(2,1)} %copy.127), calls=%async_computation.1 | async-start | bytes 3538944 | tf_op jit(solution)/shard_map/all_to_all | solution.py:150
  74.5 2.7 %copy-start.14 = (bf16[144,12,128]{2,1,0:T(8,128)(2,1)S(1)}, bf16[144,12,128]{2,1,0:T(8,128)(2,1)}, u32[]{:S(2)}) copy-start(bf16[144,12,128]{2,1,0:T(8,128)(2,1)} %reshape.182) | copy-start | bytes 1327108
  74.6 2.7 %copy-start.16 = (bf16[144,12,128]{2,1,0:T(8,128)(2,1)S(1)}, bf16[144,12,128]{2,1,0:T(8,128)(2,1)}, u32[]{:S(2)}) copy-start(bf16[144,12,128]{2,1,0:T(8,128)(2,1)} %copy-done.15) | copy-start | bytes 1327108
  74.6 2.7 %copy-start.18 = (f32[12,144]{1,0:T(8,128)S(1)}, f32[12,144]{1,0:T(8,128)}, u32[]{:S(2)}) copy-start(f32[12,144]{1,0:T(8,128)} %get-tuple-element.31) | copy-start | bytes 20740
  77.8 2.6 %copy-start.8 = (bf16[144,12,128]{2,1,0:T(8,128)(2,1)S(1)}, bf16[144,12,128]{2,1,0:T(8,128)(2,1)}, u32[]{:S(2)}) copy-start(bf16[144,12,128]{2,1,0:T(8,128)(2,1)} %copy-done.7) | copy-start | bytes 1327108
  78.2 13.0 %copy-start.6 = (bf16[144,12,128]{2,1,0:T(8,128)(2,1)S(1)}, bf16[144,12,128]{2,1,0:T(8,128)(2,1)}, u32[]{:S(2)}) copy-start(bf16[144,12,128]{2,1,0:T(8,128)(2,1)} %copy-done.5) | copy-start | bytes 1327108
  78.2 2.5 %collective-permute-start.6 = (f32[12,16]{1,0:T(8,128)S(1)}, f32[12,16]{1,0:T(8,128)S(1)}, u32[]{:S(2)}, u32[]{:S(2)}) collective-permute-start(f32[12,16]{1,0:T(8,128)S(1)} %add_add_fusion.1), channel_id=1, source_target_pairs={{0,16},{16,0},{32,48},{48,32},{64,80},{80,64},{96,112},{112,96},{1... | collective-permute-start | bytes 2312 | tf_op jit(solution)/shard_map/ppermute | solution.py:60
  78.3 3.7 %collective-permute-start.7 = (f32[12,16]{1,0:T(8,128)S(1)}, f32[12,16]{1,0:T(8,128)S(1)}, u32[]{:S(2)}, u32[]{:S(2)}) collective-permute-start(f32[12,16]{1,0:T(8,128)S(1)} %add_add_fusion.1), channel_id=1, source_target_pairs={{0,32},{16,48},{32,0},{48,16},{64,96},{80,112},{96,64},{112,80},{1... | collective-permute-start | bytes 2312 | tf_op jit(solution)/shard_map/ppermute | solution.py:60
  80.3 3.1 %collective-permute-start.8 = (f32[12,16]{1,0:T(8,128)S(1)}, f32[12,16]{1,0:T(8,128)S(1)}, u32[]{:S(2)}, u32[]{:S(2)}) collective-permute-start(f32[12,16]{1,0:T(8,128)S(1)} %add_add_fusion.1), channel_id=1, source_target_pairs={{0,48},{16,32},{32,16},{48,0},{64,112},{80,96},{96,80},{112,64},{1... | collective-permute-start | bytes 2312 | tf_op jit(solution)/shard_map/ppermute | solution.py:60
  83.4 18.3 %collective-permute-start.10 = (f32[12,16]{1,0:T(8,128)S(1)}, f32[12,16]{1,0:T(8,128)S(1)}, u32[]{:S(2)}, u32[]{:S(2)}) collective-permute-start(f32[12,16]{1,0:T(8,128)S(1)} %add_add_fusion), channel_id=1, source_target_pairs={{0,128},{16,144},{32,160},{48,176},{64,192},{80,208},{96,224},{112... | collective-permute-start | bytes 2312 | tf_op jit(solution)/shard_map/ppermute | solution.py:60
  89.7 12.0 %collective-permute-start.11 = (f32[12,16]{1,0:T(8,128)S(1)}, f32[12,16]{1,0:T(8,128)S(1)}, u32[]{:S(2)}, u32[]{:S(2)}) collective-permute-start(f32[12,16]{1,0:T(8,128)S(1)} %add_add_fusion), channel_id=1, source_target_pairs={{0,192},{16,208},{32,224},{48,240},{64,128},{80,144},{96,160},{112... | collective-permute-start | bytes 2312 | tf_op jit(solution)/shard_map/ppermute | solution.py:60
  90.2 11.5 %collective-permute-start.9 = (f32[12,16]{1,0:T(8,128)S(1)}, f32[12,16]{1,0:T(8,128)S(1)}, u32[]{:S(2)}, u32[]{:S(2)}) collective-permute-start(f32[12,16]{1,0:T(8,128)S(1)} %add_add_fusion), channel_id=1, source_target_pairs={{0,64},{16,80},{32,96},{48,112},{64,0},{80,16},{96,32},{112,48},{1... | collective-permute-start | bytes 2312 | tf_op jit(solution)/shard_map/ppermute | solution.py:60
  102.3 2.6 %copy-start.1 = (f32[9,16,1536]{2,1,0:T(8,128)S(1)}, f32[9,16,1536]{2,1,0:T(8,128)}, u32[]{:S(2)}) copy-start(f32[9,16,1536]{2,1,0:T(8,128)} %reshape_reshape.14) | copy-start | bytes 2654212
  102.3 2.6 %copy-start.3 = (f32[9,16,1536]{2,1,0:T(8,128)S(1)}, f32[9,16,1536]{2,1,0:T(8,128)}, u32[]{:S(2)}) copy-start(f32[9,16,1536]{2,1,0:T(8,128)} %reshape_reshape.15) | copy-start | bytes 2654212
  104.9 1.2 %copy-start.2 = (f32[9,16,1536]{2,1,0:T(8,128)S(1)}, f32[9,16,1536]{2,1,0:T(8,128)}, u32[]{:S(2)}) copy-start(f32[9,16,1536]{2,1,0:T(8,128)} %reshape_reshape.13) | copy-start | bytes 2654212
  104.9 1.7 %copy-start.4 = (f32[9,16,1536]{2,1,0:T(8,128)S(1)}, f32[9,16,1536]{2,1,0:T(8,128)}, u32[]{:S(2)}) copy-start(f32[9,16,1536]{2,1,0:T(8,128)} %reshape_reshape.12) | copy-start | bytes 2654212

commit v11 on v9

--- a/solution.py
+++ b/solution.py
@@ -148,7 +148,8 @@
     summed = quad_step(quad_step(partial, "dp", dp_size, 1), "dp", dp_size, 4)
     bias_grad = summed / math.sqrt(dp_size * queries.shape[0] * frames_all * positions)
     back = lax.all_to_all(back_rows, "seq", split_axis=0, concat_axis=0, tiled=True)
-    back = jnp.transpose(back, (2, 1, 0, 3)).reshape(4, 1, 1, positions, width).astype(jnp.float32)
+    back = lax.optimization_barrier(jnp.transpose(back, (2, 1, 0, 3)))
+    back = back.reshape(4, 1, 1, positions, width).astype(jnp.float32)
 
     space_query = split_heads(queries, head_count)
     space_key = split_heads(keys, head_count)

time: 105 us -> 104 us (level)
  no operation moved by 1% of the time
where the time goes in v11:
time: 104 us; the launch traced here: 103 us
  starting transfers between devices  34.8 us (33%)
  local copies, waits for them, and re-layouts  25.6 us (25%)
  matrix products  16.1 us (15%)
  waiting for transfers between devices  15.8 us (15%)
  other arithmetic  8.74 us (8%)
  between operations  1.68 us (2%)
    ppermute x12, starting transfers between devices, quad_step(): lax.ppermute(value, axis, [(index, index ^ part * step) for index in rang...  19.2 us
    ppermute x12, waiting for transfers between devices, quad_step(): lax.ppermute(value, axis, [(index, index ^ part * step) for index in rang...  8.25 us
    all_to_all x1, starting transfers between devices, on_device(): lax.all_to_all(back_rows, 'seq', split_axis=0, concat_axis=0, tiled=True)  7.99 us
    all_to_all x1, starting transfers between devices, on_device(): lax.all_to_all(stacked, 'seq', split_axis=0, concat_axis=0, tiled=True)  7.58 us
    all_to_all x1, waiting for transfers between devices, on_device(): lax.all_to_all(stacked, 'seq', split_axis=0, concat_axis=0, tiled=True)  7.5 us
    reshape x2, local copies, waits for them, and re-layouts, on_device(): rows = rows.reshape(seq_size, block, 4, head_count, width // head_count)  6.25 us
    another operation x4, local copies, waits for them, and re-layouts  4.35 us
    sub x1, matrix products, attend_forward(): weights = jnp.exp(scores - row_peak)  3.27 us
  transfers between devices with their start and end apart: 14, of which 5 were waited for; matrix products, arithmetic and copies ran while one was open for 26% of the time, Pallas kernels for 0%

profile of v11, /device:TPU:4, one launch (start us, length us, event | category | flops | bytes accessed | tf_op | source)
XLA Modules:
  0.0 102.6 jit_solution(2942280030017305155)
XLA Ops:
  0.6 1.6 %pad_maximum_fusion = bf16[16,9,4,1536]{3,0,2,1:T(8,128)(2,1)S(1)} fusion(bf16[16,9,1,1536]{3,0,2,1:T(8,128)(2,1)} %bitcast.152, bf16[16,9,1,1536]{3,0,2,1:T(8,128)(2,1)} %bitcast.151, bf16[16,9,1,1536]{3,0,2,1:T(8,128)(2,1)} %bitcast.150, bf16[16,9,1,1536]{3,0,2,1:T(8,128)(2,1)} %bitcast.149), kind=kLoop, calls=%fused_computation.4 | loop fusion | flops 2654208 | bytes 3538944 | tf_op jit(solution)/shard_map/stack | solution.py:85
  2.3 2.6 %copy.115 = bf16[16,9,4,1536]{3,2,1,0:T(4,128)(2,1)} copy(bf16[16,9,4,1536]{3,0,2,1:T(8,128)(2,1)S(1)} %pad_maximum_fusion) | data formatting | bytes 3538944 | tf_op jit(solution)/shard_map/stack | solution.py:85
  4.9 7.6 %all-to-all-start = ((bf16[16,9,4,1536]{3,2,1,0:T(4,128)(2,1)}), bf16[16,9,4,1536]{3,2,1,0:T(4,128)(2,1)S(1)}, u32[]{:S(2)}, u32[]{:S(2)}) async-start(bf16[16,9,4,1536]{3,2,1,0:T(4,128)(2,1)} %copy.115), calls=%async_computation | async-start | bytes 3538944 | tf_op jit(solution)/shard_map/all_to_all | solution.py:92
  12.5 0.3 reshape.290
  12.8 0.3 reshape.291
  13.2 2.4 %reshape.292 = bf16[144,12,128]{2,1,0:T(8,128)(2,1)} reshape(bf16[1,1,144,1536]{3,2,1,0:T(8,128)(2,1)} %param.9) | data formatting | bytes 884736 | tf_op jit(solution)/shard_map/reshape.7
  15.6 1.3 %reshape.299 = bf16[144,12,128]{2,1,0:T(8,128)(2,1)S(1)} reshape(bf16[1,1,144,1536]{3,2,1,0:T(8,128)(2,1)} %param.10) | data formatting | bytes 884736 | tf_op jit(solution)/shard_map/reshape.12
  16.9 0.9 convolution_bitcast_fusion.2
  17.8 1.7 %copy.119 = f32[12,16,16]{1,2,0:T(8,128)} copy(f32[12,16,16]{0,2,1:T(8,128)} %convolution_bitcast_fusion.2) | data formatting | bytes 24576 | tf_op jit(solution)/shard_map/dot_general | solution.py:77
  20.2 0.5 iota_compare_fusion.2
  20.7 1.4 %broadcast_compare_fusion = pred[16,16]{0,1:T(8,128)(4,1)} fusion(s32[16]{0:T(128)} %bitcast.153), kind=kLoop, calls=%fused_computation.82 | loop fusion | flops 256 | bytes 320 | tf_op jit(solution)/shard_map/eq | solution.py:80
  22.1 3.3 %fusion.66 = (f32[12,144]{1,0:T(8,128)}, f32[12,144,144]{1,2,0:T(8,128)}) fusion(pred[144]{0:T(512)(128)(4,1)} %iota_compare_fusion.2, bf16[144,12,128]{2,1,0:T(8,128)(2,1)S(1)} %reshape.291, bf16[144,12,128]{2,1,0:T(8,128)(2,1)S(1)} %reshape.290), kind=kOutput, calls=%fused_computation.89 | convolution fusion | flops 64696464 | bytes 1887120 | tf_op jit(solution)/shard_map/sub | solution.py:28
  25.4 2.8 %convolution_bitcast_fusion = f32[1,1,12,18,8,128]{5,4,3,2,1,0:T(8,128)} fusion(bf16[144,12,128]{2,1,0:T(8,128)(2,1)S(1)} %reshape.299, f32[12,144,144]{1,2,0:T(8,128)} %get-tuple-element.32, f32[12,144]{1,0:T(8,128)} %get-tuple-element.31), kind=kOutput, calls=%fused_computation.26 | convolution fusion | flops 64198656 | bytes 2329344 | tf_op jit(solution)/shard_map/bfhij,bfihe->bfjhe/dot_general | solution.py:39
  28.2 7.5 %all-to-all-done = bf16[16,9,4,1536]{3,2,1,0:T(4,128)(2,1)S(1)} async-done(((bf16[16,9,4,1536]{3,2,1,0:T(4,128)(2,1)}), bf16[16,9,4,1536]{3,2,1,0:T(4,128)(2,1)S(1)}, u32[]{:S(2)}, u32[]{:S(2)}) %all-to-all-start) | async-done | bytes 1769504 | tf_op jit(solution)/shard_map/all_to_all | solution.py:92
  35.7 2.5 %reshape.305 = bf16[16,9,4,12,128]{4,3,2,1,0:T(8,128)(2,1)} reshape(bf16[16,9,4,1536]{3,2,1,0:T(4,128)(2,1)S(1)} %all-to-all-done) | data formatting | bytes 3538944 | tf_op jit(solution)/shard_map/reshape | solution.py:93
  38.2 3.7 %copy.193 = bf16[16,9,4,12,128]{4,0,3,1,2:T(8,128)(2,1)S(1)} copy(bf16[16,9,4,12,128]{4,3,2,1,0:T(8,128)(2,1)} %reshape.305) | data formatting | bytes 3538944 | tf_op jit(solution)/shard_map/reshape | solution.py:93
  42.0 1.3 %fusion.64 = f32[9,12,16,16]{2,3,1,0:T(8,128)} fusion(bf16[4,9,12,16,128]{4,3,2,1,0:T(8,128)(2,1)S(1)} %bitcast.142), kind=kOutput, calls=%fused_computation.87 | convolution fusion | flops 7077888 | bytes 995328 | tf_op jit(solution)/shard_map/phie,phje->phij/dot_general | solution.py:106
  43.3 0.6 fusion.6
  43.9 1.8 %fusion.71 = (f32[12,16,16]{1,2,0:T(8,128)S(1)}, bf16[9,12,16,16]{2,3,1,0:T(8,128)(2,1)S(1)}) fusion(f32[9,12,16,16]{2,3,1,0:T(8,128)S(1)} %fusion.6, f32[9,12,16,16]{2,3,1,0:T(8,128)} %fusion.64), kind=kOutput, calls=%fused_computation.90 | output fusion | flops 136911 | bytes 288768 | tf_op jit(solution)/shard_map/sub | solution.py:110
  45.6 0.1 copy.120
  45.8 0.2 convolution_bitcast_fusion.3
  46.0 0.7 collective-permute-start
  46.6 3.5 %collective-permute-start.1 = (f32[12,16]{1,0:T(8,128)S(1)}, f32[12,16]{1,0:T(8,128)S(1)}, u32[]{:S(2)}, u32[]{:S(2)}) collective-permute-start(f32[12,16]{1,0:T(8,128)S(1)} %convolution_bitcast_fusion.3), channel_id=1, source_target_pairs={{0,2},{1,3},{2,0},{3,1},{4,6},{5,7},{6,4},{7,5},{8,10},{9,11},{10,... | collective-permute-start | bytes 2312 | tf_op jit(solution)/shard_map/ppermute | solution.py:60
  50.1 0.5 collective-permute-start.2
  50.6 1.3 %slice_bitcast_fusion.1 = (bf16[9,12,16,128]{3,2,1,0:T(8,128)(2,1)S(1)}, bf16[9,12,16,128]{3,2,1,0:T(8,128)(2,1)S(1)}, bf16[9,12,16,128]{3,2,1,0:T(8,128)(2,1)}, bf16[9,12,16,128]{3,2,1,0:T(8,128)(2,1)}) fusion(bf16[4,9,12,16,128]{4,3,2,1,0:T(8,128)(2,1)S(1)} %bitcast.144), kind=kLoop, calls=%fused_computation.53 | loop fusion | bytes 3538944 | tf_op jit(solution)/shard_map/squeeze | solution.py:95
  51.8 1.9 %collective-permute-done.2 = f32[12,16]{1,0:T(8,128)S(1)} collective-permute-done((f32[12,16]{1,0:T(8,128)S(1)}, f32[12,16]{1,0:T(8,128)S(1)}, u32[]{:S(2)}, u32[]{:S(2)}) %collective-permute-start.2) | collective-permute-done | bytes 800 | tf_op jit(solution)/shard_map/ppermute | solution.py:60
  53.8 0.1 collective-permute-start.3
  53.8 2.7 %collective-permute-start.4 = (f32[12,16]{1,0:T(8,128)S(1)}, f32[12,16]{1,0:T(8,128)S(1)}, u32[]{:S(2)}, u32[]{:S(2)}) collective-permute-start(f32[12,16]{1,0:T(8,128)S(1)} %add_add_fusion.2), channel_id=1, source_target_pairs={{0,8},{1,9},{2,10},{3,11},{4,12},{5,13},{6,14},{7,15},{8,0},{9,1},... | collective-permute-start | bytes 2312 | tf_op jit(solution)/shard_map/ppermute | solution.py:60
  56.6 1.9 %collective-permute-start.5 = (f32[12,16]{1,0:T(8,128)S(1)}, f32[12,16]{1,0:T(8,128)S(1)}, u32[]{:S(2)}, u32[]{:S(2)}) collective-permute-start(f32[12,16]{1,0:T(8,128)S(1)} %add_add_fusion.2), channel_id=1, source_target_pairs={{0,12},{1,13},{2,14},{3,15},{4,8},{5,9},{6,10},{7,11},{8,4},{9,5},... | collective-permute-start | bytes 2312 | tf_op jit(solution)/shard_map/ppermute | solution.py:60
  58.5 0.3 fusion.18
  58.8 0.1 copy.122
  58.9 0.3 stack_reshape.12
  59.3 0.3 fusion.17
  59.6 0.1 copy.124
  59.7 0.3 stack_reshape.13
  60.0 1.4 %fusion.16 = bf16[16,9,12,128]{3,0,2,1:T(8,128)(2,1)S(1)} fusion(bf16[9,12,16,128]{3,2,1,0:T(8,128)(2,1)} %get-tuple-element.19, bf16[9,12,16,16]{2,3,1,0:T(8,128)(2,1)S(1)} %get-tuple-element.17), kind=kOutput, calls=%fused_computation.32 | convolution fusion | flops 7520256 | bytes 940032 | tf_op jit(solution)/shard_map/phij,phie->phje/dot_general | solution.py:136
  61.4 0.1 copy.125
  61.6 1.1 %stack_reshape.14 = bf16[16,9,1,1536]{3,0,1,2:T(8,128)(2,1)} reshape(bf16[16,9,12,128]{3,2,0,1:T(8,128)(2,1)S(1)} %copy.125) | data formatting | bytes 884736 | tf_op jit(solution)/shard_map/stack;reshape | solution.py:140
  62.6 0.4 fusion.19
  63.0 0.1 copy.126
  63.1 0.3 stack_reshape.15
  63.5 0.2 copy-done.8
  63.7 0.2 pad_maximum_fusion.1
  63.9 2.6 %copy.127 = bf16[16,9,4,1536]{3,2,1,0:T(4,128)(2,1)} copy(bf16[16,9,4,1536]{3,0,1,2:T(8,128)(2,1)S(1)} %pad_maximum_fusion.1) | data formatting | bytes 3538944 | tf_op jit(solution)/shard_map/optimization_barrier | solution.py:147
  66.5 8.0 %all-to-all-start.1 = ((bf16[16,9,4,1536]{3,2,1,0:T(4,128)(2,1)}), bf16[16,9,4,1536]{3,2,1,0:T(4,128)(2,1)S(1)}, u32[]{:S(2)}, u32[]{:S(2)}) async-start(bf16[16,9,4,1536]{3,2,1,0:T(4,128)(2,1)} %copy.127), calls=%async_computation.1 | async-start | bytes 3538944 | tf_op jit(solution)/shard_map/all_to_all | solution.py:150
  74.6 3.2 %convolution_bitcast_fusion.1 = f32[1,1,12,18,8,128]{5,4,3,2,1,0:T(8,128)} fusion(bf16[144,12,128]{2,1,0:T(8,128)(2,1)S(1)} %copy-done.12, f32[12,144,144]{1,2,0:T(8,128)} %get-tuple-element.32, f32[12,144]{1,0:T(8,128)S(1)} %copy-done.16), kind=kOutput, calls=%fused_computation.27 | convolution fusion | flops 64198656 | bytes 2329344 | tf_op jit(solution)/shard_map/bfhij,bfjhe->bfihe/dot_general | solution.py:31
  77.8 0.5 multiply_reduce_fusion
  78.2 0.3 multiply_convert_fusion
  78.6 0.1 collective-permute-start.6
  78.7 2.0 %collective-permute-start.7 = (f32[12,16]{1,0:T(8,128)S(1)}, f32[12,16]{1,0:T(8,128)S(1)}, u32[]{:S(2)}, u32[]{:S(2)}) collective-permute-start(f32[12,16]{1,0:T(8,128)S(1)} %add_add_fusion.1), channel_id=1, source_target_pairs={{0,32},{16,48},{32,0},{48,16},{64,96},{80,112},{96,64},{112,80},{1... | collective-permute-start | bytes 2312 | tf_op jit(solution)/shard_map/ppermute | solution.py:60
  80.7 0.4 fusion.8
  81.1 1.3 %collective-permute-done.7 = f32[12,16]{1,0:T(8,128)S(1)} collective-permute-done((f32[12,16]{1,0:T(8,128)S(1)}, f32[12,16]{1,0:T(8,128)S(1)}, u32[]{:S(2)}, u32[]{:S(2)}) %collective-permute-start.7) | collective-permute-done | bytes 800 | tf_op jit(solution)/shard_map/ppermute | solution.py:60
  82.4 1.3 %collective-permute-done.8 = f32[12,16]{1,0:T(8,128)S(1)} collective-permute-done((f32[12,16]{1,0:T(8,128)S(1)}, f32[12,16]{1,0:T(8,128)S(1)}, u32[]{:S(2)}, u32[]{:S(2)}) %collective-permute-start.8) | collective-permute-done | bytes 800 | tf_op jit(solution)/shard_map/ppermute | solution.py:60
  83.8 6.3 %collective-permute-start.10 = (f32[12,16]{1,0:T(8,128)S(1)}, f32[12,16]{1,0:T(8,128)S(1)}, u32[]{:S(2)}, u32[]{:S(2)}) collective-permute-start(f32[12,16]{1,0:T(8,128)S(1)} %add_add_fusion), channel_id=1, source_target_pairs={{0,128},{16,144},{32,160},{48,176},{64,192},{80,208},{96,224},{112... | collective-permute-start | bytes 2312 | tf_op jit(solution)/shard_map/ppermute | solution.py:60
  90.1 0.6 collective-permute-start.11
  90.6 0.9 collective-permute-start.9
  91.5 0.6 fusion.7
  92.1 3.7 %collective-permute-done.11 = f32[12,16]{1,0:T(8,128)S(1)} collective-permute-done((f32[12,16]{1,0:T(8,128)S(1)}, f32[12,16]{1,0:T(8,128)S(1)}, u32[]{:S(2)}, u32[]{:S(2)}) %collective-permute-start.11) | collective-permute-done | bytes 800 | tf_op jit(solution)/shard_map/ppermute | solution.py:60
  95.8 0.6 add_multiply_fusion
  96.4 2.5 %fusion.65 = (f32[1,9,16,1536]{3,0,1,2:T(1,128)S(1)}, f32[1,9,16,1536]{3,0,1,2:T(1,128)S(1)}, f32[1,9,16,1536]{3,0,1,2:T(1,128)S(1)}, f32[1,9,16,1536]{3,0,1,2:T(1,128)S(1)}) fusion(bf16[4,9,16,1536]{3,0,1,2:T(4,128)(2,1)S(1)} %bitcast.141), kind=kLoop, calls=%fused_computation.88 | loop fusion | bytes 7077888 | tf_op jit(solution)/shard_map/slice | solution.py:167
  99.2 1.0 copy-done.10
  100.2 1.1 %fusion.20 = (bf16[1,1,144,1536]{3,2,1,0:T(8,128)(2,1)}, bf16[1,1,144,1536]{3,2,1,0:T(8,128)(2,1)}) fusion(f32[1,1,12,18,8,128]{5,4,3,2,1,0:T(8,128)S(1)} %copy-done.10, f32[1,1,12,18,8,128]{5,4,3,2,1,0:T(8,128)S(1)} %fusion.8, f32[1,1,144,1536]{3,2,1,0:T(8,128)S(1)} %bitcast.147, f32[1,1,144,1536]{3,2,1,0:T(8,128)S(1)} %bitcast.148), kind=kLoop, calls=%fused_computation.39 | loop fusion | flops 884736 | bytes 4423680 | tf_op jit(solution)/shard_map/convert_element_type | solution.py:167
  101.3 0.1 copy-done.11
  101.4 1.1 %fusion.22 = (bf16[1,1,144,1536]{3,2,1,0:T(8,128)(2,1)}, bf16[1,1,144,1536]{3,2,1,0:T(8,128)(2,1)}) fusion(f32[1,1,12,18,8,128]{5,4,3,2,1,0:T(8,128)S(1)} %fusion.7, f32[1,1,12,18,8,128]{5,4,3,2,1,0:T(8,128)S(1)} %copy-done.11, f32[1,1,144,1536]{3,2,1,0:T(8,128)S(1)} %bitcast.146, f32[1,1,144,1536]{3,2,1,0:T(8,128)S(1)} %bitcast.145), kind=kLoop, calls=%fused_computation.43 | loop fusion | flops 884736 | bytes 4423680 | tf_op jit(solution)/shard_map/convert_element_type | solution.py:165
  (51 shorter events, 0.4 us)
Async XLA Ops:
  0.6 16.3 %copy-start = (f32[12,16]{1,0:T(8,128)S(1)}, f32[12,16]{1,0:T(8,128)}, u32[]{:S(2)}) copy-start(f32[12,16]{1,0:T(8,128)} %param.13) | copy-start | bytes 2308
  4.9 7.6 %copy-start.6 = (bf16[1,1,144,1536]{3,2,1,0:T(8,128)(2,1)S(1)}, bf16[1,1,144,1536]{3,2,1,0:T(8,128)(2,1)}, u32[]{:S(2)}) copy-start(bf16[1,1,144,1536]{3,2,1,0:T(8,128)(2,1)} %param.7) | copy-start | bytes 1327108
  4.9 7.9 %copy-start.7 = (bf16[1,1,144,1536]{3,2,1,0:T(8,128)(2,1)S(1)}, bf16[1,1,144,1536]{3,2,1,0:T(8,128)(2,1)}, u32[]{:S(2)}) copy-start(bf16[1,1,144,1536]{3,2,1,0:T(8,128)(2,1)} %param.8) | copy-start | bytes 1327108
  4.9 30.8 %all-to-all-start = ((bf16[16,9,4,1536]{3,2,1,0:T(4,128)(2,1)}), bf16[16,9,4,1536]{3,2,1,0:T(4,128)(2,1)S(1)}, u32[]{:S(2)}, u32[]{:S(2)}) async-start(bf16[16,9,4,1536]{3,2,1,0:T(4,128)(2,1)} %copy.115), calls=%async_computation | async-start | bytes 3538944 | tf_op jit(solution)/shard_map/all_to_all | solution.py:92
  12.8 12.6 %copy-start.3 = (bf16[144,12,128]{2,1,0:T(8,128)(2,1)}, bf16[144,12,128]{2,1,0:T(8,128)(2,1)S(1)}, u32[]{:S(2)}) copy-start(bf16[144,12,128]{2,1,0:T(8,128)(2,1)S(1)} %reshape.290) | copy-start | bytes 1327108
  13.2 12.2 %copy-start.1 = (bf16[144,12,128]{2,1,0:T(8,128)(2,1)}, bf16[144,12,128]{2,1,0:T(8,128)(2,1)S(1)}, u32[]{:S(2)}) copy-start(bf16[144,12,128]{2,1,0:T(8,128)(2,1)S(1)} %reshape.291) | copy-start | bytes 1327108
  16.9 8.5 %copy-start.13 = (bf16[144,12,128]{2,1,0:T(8,128)(2,1)}, bf16[144,12,128]{2,1,0:T(8,128)(2,1)S(1)}, u32[]{:S(2)}) copy-start(bf16[144,12,128]{2,1,0:T(8,128)(2,1)S(1)} %reshape.299) | copy-start | bytes 1327108
  41.9 1.3 %copy-start.15 = (f32[12,16,16]{1,2,0:T(8,128)S(1)}, f32[12,16,16]{1,2,0:T(8,128)}, u32[]{:S(2)}) copy-start(f32[12,16,16]{1,2,0:T(8,128)} %copy.119) | copy-start | bytes 36868
  42.0 1.3 %copy-start.17 = (pred[16,16]{0,1:T(8,128)(4,1)S(1)}, pred[16,16]{0,1:T(8,128)(4,1)}, u32[]{:S(2)}) copy-start(pred[16,16]{0,1:T(8,128)(4,1)} %broadcast_compare_fusion) | copy-start | bytes 772
  46.0 5.9 %collective-permute-start = (f32[12,16]{1,0:T(8,128)S(1)}, f32[12,16]{1,0:T(8,128)S(1)}, u32[]{:S(2)}, u32[]{:S(2)}) collective-permute-start(f32[12,16]{1,0:T(8,128)S(1)} %convolution_bitcast_fusion.3), channel_id=1, source_target_pairs={{0,1},{1,0},{2,3},{3,2},{4,5},{5,4},{6,7},{7,6},{8,9},{9,8},{10,11... | collective-permute-start | bytes 2312 | tf_op jit(solution)/shard_map/ppermute | solution.py:60
  46.6 5.2 %collective-permute-start.1 = (f32[12,16]{1,0:T(8,128)S(1)}, f32[12,16]{1,0:T(8,128)S(1)}, u32[]{:S(2)}, u32[]{:S(2)}) collective-permute-start(f32[12,16]{1,0:T(8,128)S(1)} %convolution_bitcast_fusion.3), channel_id=1, source_target_pairs={{0,2},{1,3},{2,0},{3,1},{4,6},{5,7},{6,4},{7,5},{8,10},{9,11},{10,... | collective-permute-start | bytes 2312 | tf_op jit(solution)/shard_map/ppermute | solution.py:60
  50.1 3.7 %collective-permute-start.2 = (f32[12,16]{1,0:T(8,128)S(1)}, f32[12,16]{1,0:T(8,128)S(1)}, u32[]{:S(2)}, u32[]{:S(2)}) collective-permute-start(f32[12,16]{1,0:T(8,128)S(1)} %convolution_bitcast_fusion.3), channel_id=1, source_target_pairs={{0,3},{1,2},{2,1},{3,0},{4,7},{5,6},{6,5},{7,4},{8,11},{9,10},{10,... | collective-permute-start | bytes 2312 | tf_op jit(solution)/shard_map/ppermute | solution.py:60
  53.8 5.5 %copy-start.9 = (bf16[9,12,16,128]{3,2,1,0:T(8,128)(2,1)S(1)}, bf16[9,12,16,128]{3,2,1,0:T(8,128)(2,1)}, u32[]{:S(2)}) copy-start(bf16[9,12,16,128]{3,2,1,0:T(8,128)(2,1)} %get-tuple-element.18) | copy-start | bytes 1327108
  53.8 10.1 %collective-permute-start.3 = (f32[12,16]{1,0:T(8,128)S(1)}, f32[12,16]{1,0:T(8,128)S(1)}, u32[]{:S(2)}, u32[]{:S(2)}) collective-permute-start(f32[12,16]{1,0:T(8,128)S(1)} %add_add_fusion.2), channel_id=1, source_target_pairs={{0,4},{1,5},{2,6},{3,7},{4,0},{5,1},{6,2},{7,3},{8,12},{9,13},{10,... | collective-permute-start | bytes 2312 | tf_op jit(solution)/shard_map/ppermute | solution.py:60
  53.8 10.1 %collective-permute-start.4 = (f32[12,16]{1,0:T(8,128)S(1)}, f32[12,16]{1,0:T(8,128)S(1)}, u32[]{:S(2)}, u32[]{:S(2)}) collective-permute-start(f32[12,16]{1,0:T(8,128)S(1)} %add_add_fusion.2), channel_id=1, source_target_pairs={{0,8},{1,9},{2,10},{3,11},{4,12},{5,13},{6,14},{7,15},{8,0},{9,1},... | collective-permute-start | bytes 2312 | tf_op jit(solution)/shard_map/ppermute | solution.py:60
  56.6 7.3 %collective-permute-start.5 = (f32[12,16]{1,0:T(8,128)S(1)}, f32[12,16]{1,0:T(8,128)S(1)}, u32[]{:S(2)}, u32[]{:S(2)}) collective-permute-start(f32[12,16]{1,0:T(8,128)S(1)} %add_add_fusion.2), channel_id=1, source_target_pairs={{0,12},{1,13},{2,14},{3,15},{4,8},{5,9},{6,10},{7,11},{8,4},{9,5},... | collective-permute-start | bytes 2312 | tf_op jit(solution)/shard_map/ppermute | solution.py:60
  62.6 1.0 copy-start.8
  66.5 8.0 %copy-start.12 = (bf16[144,12,128]{2,1,0:T(8,128)(2,1)S(1)}, bf16[144,12,128]{2,1,0:T(8,128)(2,1)}, u32[]{:S(2)}) copy-start(bf16[144,12,128]{2,1,0:T(8,128)(2,1)} %reshape.292) | copy-start | bytes 1327108
  66.5 8.0 %copy-start.16 = (f32[12,144]{1,0:T(8,128)S(1)}, f32[12,144]{1,0:T(8,128)}, u32[]{:S(2)}) copy-start(f32[12,144]{1,0:T(8,128)} %get-tuple-element.31) | copy-start | bytes 20740
  66.5 29.9 %all-to-all-start.1 = ((bf16[16,9,4,1536]{3,2,1,0:T(4,128)(2,1)}), bf16[16,9,4,1536]{3,2,1,0:T(4,128)(2,1)S(1)}, u32[]{:S(2)}, u32[]{:S(2)}) async-start(bf16[16,9,4,1536]{3,2,1,0:T(4,128)(2,1)} %copy.127), calls=%async_computation.1 | async-start | bytes 3538944 | tf_op jit(solution)/shard_map/all_to_all | solution.py:150
  74.6 3.2 %copy-start.5 = (f32[12,144,144]{1,2,0:T(8,128)S(1)}, f32[12,144,144]{1,2,0:T(8,128)}, u32[]{:S(2)}) copy-start(f32[12,144,144]{1,2,0:T(8,128)} %get-tuple-element.32) | copy-start | bytes 2985988
  74.6 3.2 %copy-start.14 = (bf16[144,12,128]{2,1,0:T(8,128)(2,1)S(1)}, bf16[144,12,128]{2,1,0:T(8,128)(2,1)}, u32[]{:S(2)}) copy-start(bf16[144,12,128]{2,1,0:T(8,128)(2,1)} %copy-done.13) | copy-start | bytes 1327108
  78.2 2.5 %copy-start.4 = (bf16[144,12,128]{2,1,0:T(8,128)(2,1)S(1)}, bf16[144,12,128]{2,1,0:T(8,128)(2,1)}, u32[]{:S(2)}) copy-start(bf16[144,12,128]{2,1,0:T(8,128)(2,1)} %copy-done.3) | copy-start | bytes 1327108
  78.6 13.0 %copy-start.2 = (bf16[144,12,128]{2,1,0:T(8,128)(2,1)S(1)}, bf16[144,12,128]{2,1,0:T(8,128)(2,1)}, u32[]{:S(2)}) copy-start(bf16[144,12,128]{2,1,0:T(8,128)(2,1)} %copy-done.1) | copy-start | bytes 1327108
  78.6 2.5 %collective-permute-start.6 = (f32[12,16]{1,0:T(8,128)S(1)}, f32[12,16]{1,0:T(8,128)S(1)}, u32[]{:S(2)}, u32[]{:S(2)}) collective-permute-start(f32[12,16]{1,0:T(8,128)S(1)} %add_add_fusion.1), channel_id=1, source_target_pairs={{0,16},{16,0},{32,48},{48,32},{64,80},{80,64},{96,112},{112,96},{1... | collective-permute-start | bytes 2312 | tf_op jit(solution)/shard_map/ppermute | solution.py:60
  78.7 3.7 %collective-permute-start.7 = (f32[12,16]{1,0:T(8,128)S(1)}, f32[12,16]{1,0:T(8,128)S(1)}, u32[]{:S(2)}, u32[]{:S(2)}) collective-permute-start(f32[12,16]{1,0:T(8,128)S(1)} %add_add_fusion.1), channel_id=1, source_target_pairs={{0,32},{16,48},{32,0},{48,16},{64,96},{80,112},{96,64},{112,80},{1... | collective-permute-start | bytes 2312 | tf_op jit(solution)/shard_map/ppermute | solution.py:60
  80.7 3.1 %collective-permute-start.8 = (f32[12,16]{1,0:T(8,128)S(1)}, f32[12,16]{1,0:T(8,128)S(1)}, u32[]{:S(2)}, u32[]{:S(2)}) collective-permute-start(f32[12,16]{1,0:T(8,128)S(1)} %add_add_fusion.1), channel_id=1, source_target_pairs={{0,48},{16,32},{32,16},{48,0},{64,112},{80,96},{96,80},{112,64},{1... | collective-permute-start | bytes 2312 | tf_op jit(solution)/shard_map/ppermute | solution.py:60
  83.8 8.4 %collective-permute-start.10 = (f32[12,16]{1,0:T(8,128)S(1)}, f32[12,16]{1,0:T(8,128)S(1)}, u32[]{:S(2)}, u32[]{:S(2)}) collective-permute-start(f32[12,16]{1,0:T(8,128)S(1)} %add_add_fusion), channel_id=1, source_target_pairs={{0,128},{16,144},{32,160},{48,176},{64,192},{80,208},{96,224},{112... | collective-permute-start | bytes 2312 | tf_op jit(solution)/shard_map/ppermute | solution.py:60
  90.1 5.8 %collective-permute-start.11 = (f32[12,16]{1,0:T(8,128)S(1)}, f32[12,16]{1,0:T(8,128)S(1)}, u32[]{:S(2)}, u32[]{:S(2)}) collective-permute-start(f32[12,16]{1,0:T(8,128)S(1)} %add_add_fusion), channel_id=1, source_target_pairs={{0,192},{16,208},{32,224},{48,240},{64,128},{80,144},{96,160},{112... | collective-permute-start | bytes 2312 | tf_op jit(solution)/shard_map/ppermute | solution.py:60
  90.6 5.2 %collective-permute-start.9 = (f32[12,16]{1,0:T(8,128)S(1)}, f32[12,16]{1,0:T(8,128)S(1)}, u32[]{:S(2)}, u32[]{:S(2)}) collective-permute-start(f32[12,16]{1,0:T(8,128)S(1)} %add_add_fusion), channel_id=1, source_target_pairs={{0,64},{16,80},{32,96},{48,112},{64,0},{80,16},{96,32},{112,48},{1... | collective-permute-start | bytes 2312 | tf_op jit(solution)/shard_map/ppermute | solution.py:60
  99.0 1.2 %copy-start.10 = (f32[1,1,12,18,8,128]{5,4,3,2,1,0:T(8,128)S(1)}, f32[1,1,12,18,8,128]{5,4,3,2,1,0:T(8,128)}, u32[]{:S(2)}) copy-start(f32[1,1,12,18,8,128]{5,4,3,2,1,0:T(8,128)} %convolution_bitcast_fusion) | copy-start | bytes 2654212
  100.2 1.2 %copy-start.11 = (f32[1,1,12,18,8,128]{5,4,3,2,1,0:T(8,128)S(1)}, f32[1,1,12,18,8,128]{5,4,3,2,1,0:T(8,128)}, u32[]{:S(2)}) copy-start(f32[1,1,12,18,8,128]{5,4,3,2,1,0:T(8,128)} %convolution_bitcast_fusion.1) | copy-start | bytes 2654212
